TPU v7x, 32 devices: a whole 2x2x4 slice. The times are simulated.
32 devices in a mesh: ta: 4 (over z), xyz: 8 (over y, x, core).
Axes of the slice: x: 2, y: 2, z: 4, core: 2. Of those that a mesh axis runs over, the one named last changes fastest.
Arguments:
- right_side: float32 [32, 4, 8, 4, 2, 2, 128], P(None, 'ta', 'xyz'), may hold values from -6 to 6
- coarse_links: bfloat16 [4, 8, 4, 2, 2, 9, 64, 128], P('ta', 'xyz'), may hold values from -3 to 3
- null_vectors: bfloat16 [4, 8, 4, 2, 2, 48, 128], P('ta', 'xyz'), may hold values from -0.29882812 to 0.29882812
- coarse_inverse: bfloat16 [4, 384, 384], P('ta', 'xyz'), may hold values from -2 to 2
Outputs:
- solution: float32 [32, 4, 8, 4, 2, 2, 128], P(None, 'ta', 'xyz')
- residual: float32 [32, 4, 8, 4, 2, 2, 128], P(None, 'ta', 'xyz')
All inputs are finite; a program needn't handle non-finite values.
Results may differ from a plain program's by a relative error of at most 0.0075.
Values may be sent and summed in bfloat16 or wider, within the bound.
No kernel may reach another device: no remote copies, remote signals or barrier semaphores. Data moves between devices by JAX's collectives and lax.ppermute only.
A program may use at most 64 MiB of HBM per device.

v0:
```python
import jax
import jax.numpy as jnp
from jax import lax
from jax.sharding import PartitionSpec as P

OMEGA = 0.4
EPS = 1e-06


def from_behind(x, axis, by):
    length = lax.axis_size(axis)
    return lax.ppermute(x, axis, [(i, (i + by) % length) for i in range(length)])


def with_halo(cells, sides, width):
    for axis, dim in sides:
        count = lax.axis_size(axis)
        head = lax.slice_in_dim(cells, 0, width, axis=dim)
        tail = lax.slice_in_dim(cells, cells.shape[dim] - width, cells.shape[dim], axis=dim)
        cells = jnp.concatenate(
            [
                lax.ppermute(tail, axis, [(i, (i + 1) % count) for i in range(count)]),
                cells,
                lax.ppermute(head, axis, [((i + 1) % count, i) for i in range(count)]),
            ],
            axis=dim,
        )
    return cells


def fetch_face(face, stride, extent, toward):
    nearby = from_behind(face, "xyz", -toward * stride)
    across = from_behind(face, "xyz", toward * stride * (extent - 1))
    coord = lax.axis_index("xyz") // stride % extent
    boundary = extent - 1 if toward > 0 else 0
    return jnp.where(coord == boundary, across, nearby)


def both_sides(lowered, which, stride, extent):
    length = lowered.shape[which]
    from_upper = fetch_face(lax.slice_in_dim(lowered, 0, 1, axis=which), stride, extent, 1)
    from_lower = fetch_face(
        lax.slice_in_dim(lowered, length - 1, length, axis=which), stride, extent, -1
    )
    upper = jnp.concatenate([lax.slice_in_dim(lowered, 1, length, axis=which), from_upper], which)
    lower = jnp.concatenate(
        [from_lower, lax.slice_in_dim(lowered, 0, length - 1, axis=which)], which
    )
    return (upper, lower)


def apply_links(coarse_links, lowered):
    blocks_total = lax.axis_size("xyz")
    across_x = 2 + 2 * min(blocks_total // 64, 1)
    across_z = blocks_total // (across_x * across_x)
    upper_x, lower_x = both_sides(lowered, 5, 1, across_x)
    upper_y, lower_y = both_sides(lowered, 4, across_x, across_x)
    upper_z, lower_z = both_sides(lowered, 3, across_x * across_x, across_z)
    padded = with_halo(lowered, (("ta", 1),), 1)
    upper_t = padded[:, 2:]
    lower_t = padded[:, :-2]
    stacked = jnp.stack(
        [lowered, upper_x, lower_x, upper_y, lower_y, upper_z, lower_z, upper_t, lower_t], 2
    )
    half_width = lowered.shape[-1] // 2
    real_part = stacked[..., :half_width]
    imag_part = stacked[..., half_width:]
    real_input = jnp.concatenate([real_part, -imag_part], -1)
    imag_input = jnp.concatenate([imag_part, real_part], -1)
    inputs = jnp.stack([real_input, imag_input], 0)
    result = jnp.einsum(
        "tbzyxdik,pntdbzyxk->pntbzyxi", coarse_links, inputs, preferred_element_type=jnp.float32
    )
    return jnp.concatenate([result[0], result[1]], -1)


def precondition(vector_in, null_vectors, coarse_inverse):
    lowered = vector_in.astype(jnp.bfloat16)
    coarse = jnp.einsum(
        "tbzyxjk,ntbzyxk->nj", null_vectors, lowered, preferred_element_type=jnp.float32
    ).astype(jnp.bfloat16)
    inverse_rows = coarse_inverse[0]
    correction = lax.dot_general(
        lax.all_gather(coarse, "xyz", axis=1, tiled=True),
        inverse_rows,
        (((1,), (1,)), ((), ())),
        preferred_element_type=jnp.float32,
    ).astype(jnp.bfloat16)
    prolonged = jnp.einsum(
        "tbzyxjk,nj->ntbzyxk", null_vectors, correction, preferred_element_type=jnp.float32
    )
    return OMEGA * vector_in + prolonged


def inner_rows(left_vec, right_vec):
    return jnp.sum(left_vec * right_vec, axis=(1, 2, 3, 4, 5, 6))


def scaled(weights, vector_in):
    return weights[:, None, None, None, None, None, None] * vector_in


def pair_products(image, residual):
    return lax.psum((inner_rows(image, image), inner_rows(image, residual)), ("ta", "xyz"))


def shards(right_side, coarse_links, null_vectors, coarse_inverse):
    residual = right_side
    direction_a = precondition(residual, null_vectors, coarse_inverse)
    image_a = apply_links(coarse_links, direction_a.astype(jnp.bfloat16))
    norm_a, correlation_a = pair_products(image_a, residual)
    step_a = correlation_a / (norm_a + EPS)
    solution = scaled(step_a, direction_a)
    residual = residual - scaled(step_a, image_a)
    direction_b = precondition(residual, null_vectors, coarse_inverse)
    image_b = apply_links(coarse_links, direction_b.astype(jnp.bfloat16))
    projection_sum = lax.psum(inner_rows(image_a, image_b), ("ta", "xyz"))
    beta_coef = projection_sum / (norm_a + EPS)
    image_b = image_b - scaled(beta_coef, image_a)
    direction_b = direction_b - scaled(beta_coef, direction_a)
    norm_b, correlation_b = pair_products(image_b, residual)
    step_b = correlation_b / (norm_b + EPS)
    solution = solution + scaled(step_b, direction_b)
    residual = residual - scaled(step_b, image_b)
    return (solution, residual)


def solution(mesh):
    in_specs = (
        P(None, "ta", "xyz", None, None, None, None),
        P("ta", "xyz", None, None, None, None, None, None),
        P("ta", "xyz", None, None, None, None, None),
        P("ta", "xyz", None),
    )
    out_specs = (
        P(None, "ta", "xyz", None, None, None, None),
        P(None, "ta", "xyz", None, None, None, None),
    )
    return jax.shard_map(shards, mesh=mesh, in_specs=in_specs, out_specs=out_specs, check_vma=False)
```

profile of v0, /device:TPU:0, one launch (start us, length us, event | category | flops | bytes accessed | tf_op | source)
XLA Modules:
  0.0 213.9 jit_solution(7676962154770344067)
XLA Ops:
  2.9 10.7 %all-gather = bf16[8,48,32]{1,2,0:T(8,128)(2,1)S(1)} all-gather(bf16[1,48,32]{1,2,0:T(8,128)(2,1)S(1)} %fusion.23), channel_id=1, replica_groups=mesh['ta'=4,'xyz'=8] {'xyz'}, dimensions={0}, use_global_device_ids=true | all-gather | bytes 27648 | tf_op jit(solution)/shard_map/all_gather | solution.py:84
  14.4 2.1 bitcast_dynamic-update-slice_fusion.5
  16.5 1.5 fusion.54
  18.0 1.5 collective-permute-start.7
  19.5 1.4 collective-permute-start.6
  20.9 1.5 fusion.55
  24.0 1.7 fusion.53
  25.7 1.4 fusion.52
  27.1 1.7 collective-permute-start.2
  32.6 3.6 %collective-permute-start.10 = (bf16[32,1,1,4,2,2,128]{6,0,5,4,3,2,1:T(8,128)(2,1)}, bf16[32,1,1,4,2,2,128]{6,0,5,4,3,2,1:T(8,128)(2,1)S(1)}, u32[]{:S(2)}, u32[]{:S(2)}) collective-permute-start(bf16[32,1,1,4,2,2,128]{6,0,5,4,3,2,1:T(8,128)(2,1)} %get-tuple-element.23), channel_id=1, source_target_pairs={{8,0},{16,8},{24,16},{0,24},{9,1},{17,9},{25,17},{1,25},{10,2},{18... | collective-permute-start | bytes 393224 | tf_op jit(solution)/shard_map/ppermute | solution.py:24
  37.1 1.5 collective-permute-start.9
  41.1 2.5 %collective-permute-done.8 = bf16[32,1,1,1,2,2,128]{6,0,5,4,3,2,1:T(8,128)(2,1)S(1)} collective-permute-done((bf16[32,1,1,1,2,2,128]{6,0,5,4,3,2,1:T(8,128)(2,1)S(1)}, bf16[32,1,1,1,2,2,128]{6,0,5,4,3,2,1:T(8,128)(2,1)S(1)}, u32[]{:S(2)}, u32[]{:S(2)}) %collective-permute-start.8) | collective-permute-done | bytes 32800 | tf_op jit(solution)/shard_map/ppermute | solution.py:12
  48.6 38.7 %all-reduce.1 = (f32[32]{0:T(128)S(1)}, f32[32]{0:T(128)S(1)}) all-reduce(f32[32]{0:T(128)S(1)} %get-tuple-element.11, f32[32]{0:T(128)S(1)} %get-tuple-element.10), channel_id=1, replica_groups=mesh['ta'=4,'xyz'=8] {'ta','xyz'}, use_global_device_ids=true, to_apply=%region_1.2 | all-reduce | flops 64 | bytes 512 | tf_op jit(solution)/shard_map/psum | solution.py:104
  88.3 10.0 %all-gather.1 = bf16[8,48,32]{1,2,0:T(8,128)(2,1)S(1)} all-gather(bf16[1,48,32]{1,2,0:T(8,128)(2,1)S(1)} %fusion.22), channel_id=1, replica_groups=mesh['ta'=4,'xyz'=8] {'xyz'}, dimensions={0}, use_global_device_ids=true | all-gather | bytes 27648 | tf_op jit(solution)/shard_map/all_gather | solution.py:84
  99.0 2.1 bitcast_dynamic-update-slice_fusion.2
  103.0 1.4 collective-permute-start.13
  106.8 2.4 %collective-permute-start.18 = (bf16[32,1,1,4,1,2,128]{6,0,5,4,3,2,1:T(8,128)(2,1)S(1)}, bf16[32,1,1,4,1,2,128]{6,0,5,4,3,2,1:T(8,128)(2,1)S(1)}, u32[]{:S(2)}, u32[]{:S(2)}) collective-permute-start(bf16[32,1,1,4,1,2,128]{6,0,5,4,3,2,1:T(8,128)(2,1)S(1)} %get-tuple-element.36), channel_id=1, source_target_pairs={{0,6},{1,7},{2,0},{3,1},{4,2},{5,3},{6,4},{7,5},{8,14},{9,15},{10,... | collective-permute-start | bytes 196616 | tf_op jit(solution)/shard_map/ppermute | solution.py:12
  109.2 2.6 %collective-permute-start.14 = (bf16[32,1,1,4,2,1,128]{6,0,5,4,3,2,1:T(8,128)(2,1)S(1)}, bf16[32,1,1,4,2,1,128]{6,0,5,4,3,2,1:T(8,128)(2,1)S(1)}, u32[]{:S(2)}, u32[]{:S(2)}) collective-permute-start(bf16[32,1,1,4,2,1,128]{6,0,5,4,3,2,1:T(8,128)(2,1)S(1)} %get-tuple-element.38), channel_id=1, source_target_pairs={{0,7},{1,0},{2,1},{3,2},{4,3},{5,4},{6,5},{7,6},{8,15},{9,8},{10,9... | collective-permute-start | bytes 196616 | tf_op jit(solution)/shard_map/ppermute | solution.py:12
  111.8 2.7 %collective-permute-done.15 = bf16[32,1,1,4,2,1,128]{6,0,5,4,3,2,1:T(8,128)(2,1)S(1)} collective-permute-done((bf16[32,1,1,4,2,1,128]{6,0,5,4,3,2,1:T(8,128)(2,1)S(1)}, bf16[32,1,1,4,2,1,128]{6,0,5,4,3,2,1:T(8,128)(2,1)S(1)}, u32[]{:S(2)}, u32[]{:S(2)}) %collective-permute-start.15) | collective-permute-done | bytes 65568 | tf_op jit(solution)/shard_map/ppermute | solution.py:12
  114.5 2.1 %collective-permute-start.22 = (bf16[32,1,1,4,2,2,128]{6,0,5,4,3,2,1:T(8,128)(2,1)S(1)}, bf16[32,1,1,4,2,2,128]{6,0,5,4,3,2,1:T(8,128)(2,1)S(1)}, u32[]{:S(2)}, u32[]{:S(2)}) collective-permute-start(bf16[32,1,1,4,2,2,128]{6,0,5,4,3,2,1:T(8,128)(2,1)S(1)} %copy-done.5), channel_id=1, source_target_pairs={{8,0},{16,8},{24,16},{0,24},{9,1},{17,9},{25,17},{1,25},{10,2},{18... | collective-permute-start | bytes 393224 | tf_op jit(solution)/shard_map/ppermute | solution.py:24
  116.7 2.0 collective-permute-start.23
  121.9 3.0 %collective-permute-done.20 = bf16[32,1,1,1,2,2,128]{6,0,5,4,3,2,1:T(8,128)(2,1)S(1)} collective-permute-done((bf16[32,1,1,1,2,2,128]{6,0,5,4,3,2,1:T(8,128)(2,1)S(1)}, bf16[32,1,1,1,2,2,128]{6,0,5,4,3,2,1:T(8,128)(2,1)S(1)}, u32[]{:S(2)}, u32[]{:S(2)}) %collective-permute-start.20) | collective-permute-done | bytes 32800 | tf_op jit(solution)/shard_map/ppermute | solution.py:12
  129.9 39.7 %psum.37 = f32[32]{0:T(128)S(1)} all-reduce(f32[32]{0:T(128)S(1)} %multiply_reduce_fusion.2), channel_id=1, replica_groups=mesh['ta'=4,'xyz'=8] {'ta','xyz'}, use_global_device_ids=true, to_apply=%region_5.6 | all-reduce | flops 32 | bytes 256 | tf_op jit(solution)/shard_map/psum | solution.py:117
  170.6 40.1 %all-reduce = (f32[32]{0:T(128)S(1)}, f32[32]{0:T(128)S(1)}) all-reduce(f32[32]{0:T(128)S(1)} %get-tuple-element.9, f32[32]{0:T(128)S(1)} %get-tuple-element.8), channel_id=1, replica_groups=mesh['ta'=4,'xyz'=8] {'ta','xyz'}, use_global_device_ids=true, to_apply=%region_7.8 | all-reduce | flops 64 | bytes 512 | tf_op jit(solution)/shard_map/psum | solution.py:104
  (115 shorter events, 34.7 us)
Async XLA Ops:
  18.0 21.6 %collective-permute-start.7 = (bf16[32,1,1,4,1,2,128]{6,0,5,4,3,2,1:T(8,128)(2,1)}, bf16[32,1,1,4,1,2,128]{6,0,5,4,3,2,1:T(8,128)(2,1)}, u32[]{:S(2)}, u32[]{:S(2)}) collective-permute-start(bf16[32,1,1,4,1,2,128]{6,0,5,4,3,2,1:T(8,128)(2,1)} %get-tuple-element.44), channel_id=1, source_target_pairs={{0,2},{1,3},{2,4},{3,5},{4,6},{5,7},{6,0},{7,1},{8,10},{9,11},{10,... | collective-permute-start | bytes 196616 | tf_op jit(solution)/shard_map/ppermute | solution.py:12
  19.5 20.7 %collective-permute-start.6 = (bf16[32,1,1,4,1,2,128]{6,0,5,4,3,2,1:T(8,128)(2,1)}, bf16[32,1,1,4,1,2,128]{6,0,5,4,3,2,1:T(8,128)(2,1)}, u32[]{:S(2)}, u32[]{:S(2)}) collective-permute-start(bf16[32,1,1,4,1,2,128]{6,0,5,4,3,2,1:T(8,128)(2,1)} %get-tuple-element.44), channel_id=1, source_target_pairs={{0,6},{1,7},{2,0},{3,1},{4,2},{5,3},{6,4},{7,5},{8,14},{9,15},{10,... | collective-permute-start | bytes 196616 | tf_op jit(solution)/shard_map/ppermute | solution.py:12
  22.5 4.6 %collective-permute-start.1 = (bf16[32,1,1,4,2,1,128]{6,0,5,4,3,2,1:T(8,128)(2,1)}, bf16[32,1,1,4,2,1,128]{6,0,5,4,3,2,1:T(8,128)(2,1)}, u32[]{:S(2)}, u32[]{:S(2)}) collective-permute-start(bf16[32,1,1,4,2,1,128]{6,0,5,4,3,2,1:T(8,128)(2,1)} %get-tuple-element.47), channel_id=1, source_target_pairs={{0,7},{1,0},{2,1},{3,2},{4,3},{5,4},{6,5},{7,6},{8,15},{9,8},{10,9... | collective-permute-start | bytes 196616 | tf_op jit(solution)/shard_map/ppermute | solution.py:12
  22.5 6.3 %collective-permute-start = (bf16[32,1,1,4,2,1,128]{6,0,5,4,3,2,1:T(8,128)(2,1)}, bf16[32,1,1,4,2,1,128]{6,0,5,4,3,2,1:T(8,128)(2,1)}, u32[]{:S(2)}, u32[]{:S(2)}) collective-permute-start(bf16[32,1,1,4,2,1,128]{6,0,5,4,3,2,1:T(8,128)(2,1)} %get-tuple-element.47), channel_id=1, source_target_pairs={{0,1},{1,2},{2,3},{3,4},{4,5},{5,6},{6,7},{7,0},{8,9},{9,10},{10,1... | collective-permute-start | bytes 196616 | tf_op jit(solution)/shard_map/ppermute | solution.py:12
  23.0 8.5 %collective-permute-start.3 = (bf16[32,1,1,4,2,1,128]{6,0,5,4,3,2,1:T(8,128)(2,1)}, bf16[32,1,1,4,2,1,128]{6,0,5,4,3,2,1:T(8,128)(2,1)}, u32[]{:S(2)}, u32[]{:S(2)}) collective-permute-start(bf16[32,1,1,4,2,1,128]{6,0,5,4,3,2,1:T(8,128)(2,1)} %get-tuple-element.46), channel_id=1, source_target_pairs={{0,1},{1,2},{2,3},{3,4},{4,5},{5,6},{6,7},{7,0},{8,9},{9,10},{10,1... | collective-permute-start | bytes 196616 | tf_op jit(solution)/shard_map/ppermute | solution.py:12
  27.1 5.5 %collective-permute-start.2 = (bf16[32,1,1,4,2,1,128]{6,0,5,4,3,2,1:T(8,128)(2,1)}, bf16[32,1,1,4,2,1,128]{6,0,5,4,3,2,1:T(8,128)(2,1)S(1)}, u32[]{:S(2)}, u32[]{:S(2)}) collective-permute-start(bf16[32,1,1,4,2,1,128]{6,0,5,4,3,2,1:T(8,128)(2,1)} %get-tuple-element.46), channel_id=1, source_target_pairs={{0,7},{1,0},{2,1},{3,2},{4,3},{5,4},{6,5},{7,6},{8,15},{9,8},{10,9... | collective-permute-start | bytes 196616 | tf_op jit(solution)/shard_map/ppermute | solution.py:12
  28.8 8.3 %collective-permute-start.5 = (bf16[32,1,1,4,1,2,128]{6,0,5,4,3,2,1:T(8,128)(2,1)}, bf16[32,1,1,4,1,2,128]{6,0,5,4,3,2,1:T(8,128)(2,1)S(1)}, u32[]{:S(2)}, u32[]{:S(2)}) collective-permute-start(bf16[32,1,1,4,1,2,128]{6,0,5,4,3,2,1:T(8,128)(2,1)} %get-tuple-element.45), channel_id=1, source_target_pairs={{0,6},{1,7},{2,0},{3,1},{4,2},{5,3},{6,4},{7,5},{8,14},{9,15},{10,... | collective-permute-start | bytes 196616 | tf_op jit(solution)/shard_map/ppermute | solution.py:12
  31.5 5.6 %collective-permute-start.4 = (bf16[32,1,1,4,1,2,128]{6,0,5,4,3,2,1:T(8,128)(2,1)}, bf16[32,1,1,4,1,2,128]{6,0,5,4,3,2,1:T(8,128)(2,1)S(1)}, u32[]{:S(2)}, u32[]{:S(2)}) collective-permute-start(bf16[32,1,1,4,1,2,128]{6,0,5,4,3,2,1:T(8,128)(2,1)} %get-tuple-element.45), channel_id=1, source_target_pairs={{0,2},{1,3},{2,4},{3,5},{4,6},{5,7},{6,0},{7,1},{8,10},{9,11},{10,... | collective-permute-start | bytes 196616 | tf_op jit(solution)/shard_map/ppermute | solution.py:12
  32.6 11.1 %collective-permute-start.10 = (bf16[32,1,1,4,2,2,128]{6,0,5,4,3,2,1:T(8,128)(2,1)}, bf16[32,1,1,4,2,2,128]{6,0,5,4,3,2,1:T(8,128)(2,1)S(1)}, u32[]{:S(2)}, u32[]{:S(2)}) collective-permute-start(bf16[32,1,1,4,2,2,128]{6,0,5,4,3,2,1:T(8,128)(2,1)} %get-tuple-element.23), channel_id=1, source_target_pairs={{8,0},{16,8},{24,16},{0,24},{9,1},{17,9},{25,17},{1,25},{10,2},{18... | collective-permute-start | bytes 393224 | tf_op jit(solution)/shard_map/ppermute | solution.py:24
  37.1 7.1 %collective-permute-start.11 = (bf16[32,1,1,4,2,2,128]{6,0,5,4,3,2,1:T(8,128)(2,1)}, bf16[32,1,1,4,2,2,128]{6,0,5,4,3,2,1:T(8,128)(2,1)S(1)}, u32[]{:S(2)}, u32[]{:S(2)}) collective-permute-start(bf16[32,1,1,4,2,2,128]{6,0,5,4,3,2,1:T(8,128)(2,1)} %get-tuple-element.23), channel_id=1, source_target_pairs={{0,8},{8,16},{16,24},{24,0},{1,9},{9,17},{17,25},{25,1},{2,10},{10... | collective-permute-start | bytes 393224 | tf_op jit(solution)/shard_map/ppermute | solution.py:22
  37.1 6.5 %collective-permute-start.9 = (bf16[32,1,1,1,2,2,128]{6,0,5,4,3,2,1:T(8,128)(2,1)}, bf16[32,1,1,1,2,2,128]{6,0,5,4,3,2,1:T(8,128)(2,1)S(1)}, u32[]{:S(2)}, u32[]{:S(2)}) collective-permute-start(bf16[32,1,1,1,2,2,128]{6,0,5,4,3,2,1:T(8,128)(2,1)} %get-tuple-element.40), channel_id=1, source_target_pairs={{0,4},{1,5},{2,6},{3,7},{4,0},{5,1},{6,2},{7,3},{8,12},{9,13},{10,... | collective-permute-start | bytes 98312 | tf_op jit(solution)/shard_map/ppermute | solution.py:12
  39.6 4.0 %collective-permute-start.8 = (bf16[32,1,1,1,2,2,128]{6,0,5,4,3,2,1:T(8,128)(2,1)S(1)}, bf16[32,1,1,1,2,2,128]{6,0,5,4,3,2,1:T(8,128)(2,1)S(1)}, u32[]{:S(2)}, u32[]{:S(2)}) collective-permute-start(bf16[32,1,1,1,2,2,128]{6,0,5,4,3,2,1:T(8,128)(2,1)S(1)} %copy-done.10), channel_id=1, source_target_pairs={{0,4},{1,5},{2,6},{3,7},{4,0},{5,1},{6,2},{7,3},{8,12},{9,13},{10,... | collective-permute-start | bytes 98312 | tf_op jit(solution)/shard_map/ppermute | solution.py:12
  103.0 6.3 %collective-permute-start.13 = (bf16[32,1,1,4,2,1,128]{6,0,5,4,3,2,1:T(8,128)(2,1)S(1)}, bf16[32,1,1,4,2,1,128]{6,0,5,4,3,2,1:T(8,128)(2,1)S(1)}, u32[]{:S(2)}, u32[]{:S(2)}) collective-permute-start(bf16[32,1,1,4,2,1,128]{6,0,5,4,3,2,1:T(8,128)(2,1)S(1)} %get-tuple-element.39), channel_id=1, source_target_pairs={{0,7},{1,0},{2,1},{3,2},{4,3},{5,4},{6,5},{7,6},{8,15},{9,8},{10,9... | collective-permute-start | bytes 196616 | tf_op jit(solution)/shard_map/ppermute | solution.py:12
  104.4 7.4 %collective-permute-start.12 = (bf16[32,1,1,4,2,1,128]{6,0,5,4,3,2,1:T(8,128)(2,1)S(1)}, bf16[32,1,1,4,2,1,128]{6,0,5,4,3,2,1:T(8,128)(2,1)S(1)}, u32[]{:S(2)}, u32[]{:S(2)}) collective-permute-start(bf16[32,1,1,4,2,1,128]{6,0,5,4,3,2,1:T(8,128)(2,1)S(1)} %get-tuple-element.39), channel_id=1, source_target_pairs={{0,1},{1,2},{2,3},{3,4},{4,5},{5,6},{6,7},{7,0},{8,9},{9,10},{10,1... | collective-permute-start | bytes 196616 | tf_op jit(solution)/shard_map/ppermute | solution.py:12
  106.2 14.8 %collective-permute-start.19 = (bf16[32,1,1,4,1,2,128]{6,0,5,4,3,2,1:T(8,128)(2,1)S(1)}, bf16[32,1,1,4,1,2,128]{6,0,5,4,3,2,1:T(8,128)(2,1)S(1)}, u32[]{:S(2)}, u32[]{:S(2)}) collective-permute-start(bf16[32,1,1,4,1,2,128]{6,0,5,4,3,2,1:T(8,128)(2,1)S(1)} %get-tuple-element.36), channel_id=1, source_target_pairs={{0,2},{1,3},{2,4},{3,5},{4,6},{5,7},{6,0},{7,1},{8,10},{9,11},{10,... | collective-permute-start | bytes 196616 | tf_op jit(solution)/shard_map/ppermute | solution.py:12
  106.8 15.1 %collective-permute-start.18 = (bf16[32,1,1,4,1,2,128]{6,0,5,4,3,2,1:T(8,128)(2,1)S(1)}, bf16[32,1,1,4,1,2,128]{6,0,5,4,3,2,1:T(8,128)(2,1)S(1)}, u32[]{:S(2)}, u32[]{:S(2)}) collective-permute-start(bf16[32,1,1,4,1,2,128]{6,0,5,4,3,2,1:T(8,128)(2,1)S(1)} %get-tuple-element.36), channel_id=1, source_target_pairs={{0,6},{1,7},{2,0},{3,1},{4,2},{5,3},{6,4},{7,5},{8,14},{9,15},{10,... | collective-permute-start | bytes 196616 | tf_op jit(solution)/shard_map/ppermute | solution.py:12
  109.2 5.4 %collective-permute-start.15 = (bf16[32,1,1,4,2,1,128]{6,0,5,4,3,2,1:T(8,128)(2,1)S(1)}, bf16[32,1,1,4,2,1,128]{6,0,5,4,3,2,1:T(8,128)(2,1)S(1)}, u32[]{:S(2)}, u32[]{:S(2)}) collective-permute-start(bf16[32,1,1,4,2,1,128]{6,0,5,4,3,2,1:T(8,128)(2,1)S(1)} %get-tuple-element.38), channel_id=1, source_target_pairs={{0,1},{1,2},{2,3},{3,4},{4,5},{5,6},{6,7},{7,0},{8,9},{9,10},{10,1... | collective-permute-start | bytes 196616 | tf_op jit(solution)/shard_map/ppermute | solution.py:12
  109.2 5.3 %collective-permute-start.14 = (bf16[32,1,1,4,2,1,128]{6,0,5,4,3,2,1:T(8,128)(2,1)S(1)}, bf16[32,1,1,4,2,1,128]{6,0,5,4,3,2,1:T(8,128)(2,1)S(1)}, u32[]{:S(2)}, u32[]{:S(2)}) collective-permute-start(bf16[32,1,1,4,2,1,128]{6,0,5,4,3,2,1:T(8,128)(2,1)S(1)} %get-tuple-element.38), channel_id=1, source_target_pairs={{0,7},{1,0},{2,1},{3,2},{4,3},{5,4},{6,5},{7,6},{8,15},{9,8},{10,9... | collective-permute-start | bytes 196616 | tf_op jit(solution)/shard_map/ppermute | solution.py:12
  111.8 4.9 %collective-permute-start.17 = (bf16[32,1,1,4,1,2,128]{6,0,5,4,3,2,1:T(8,128)(2,1)S(1)}, bf16[32,1,1,4,1,2,128]{6,0,5,4,3,2,1:T(8,128)(2,1)S(1)}, u32[]{:S(2)}, u32[]{:S(2)}) collective-permute-start(bf16[32,1,1,4,1,2,128]{6,0,5,4,3,2,1:T(8,128)(2,1)S(1)} %get-tuple-element.37), channel_id=1, source_target_pairs={{0,6},{1,7},{2,0},{3,1},{4,2},{5,3},{6,4},{7,5},{8,14},{9,15},{10,... | collective-permute-start | bytes 196616 | tf_op jit(solution)/shard_map/ppermute | solution.py:12
  114.5 5.2 %collective-permute-start.16 = (bf16[32,1,1,4,1,2,128]{6,0,5,4,3,2,1:T(8,128)(2,1)S(1)}, bf16[32,1,1,4,1,2,128]{6,0,5,4,3,2,1:T(8,128)(2,1)S(1)}, u32[]{:S(2)}, u32[]{:S(2)}) collective-permute-start(bf16[32,1,1,4,1,2,128]{6,0,5,4,3,2,1:T(8,128)(2,1)S(1)} %get-tuple-element.37), channel_id=1, source_target_pairs={{0,2},{1,3},{2,4},{3,5},{4,6},{5,7},{6,0},{7,1},{8,10},{9,11},{10,... | collective-permute-start | bytes 196616 | tf_op jit(solution)/shard_map/ppermute | solution.py:12
  114.5 10.5 %collective-permute-start.22 = (bf16[32,1,1,4,2,2,128]{6,0,5,4,3,2,1:T(8,128)(2,1)S(1)}, bf16[32,1,1,4,2,2,128]{6,0,5,4,3,2,1:T(8,128)(2,1)S(1)}, u32[]{:S(2)}, u32[]{:S(2)}) collective-permute-start(bf16[32,1,1,4,2,2,128]{6,0,5,4,3,2,1:T(8,128)(2,1)S(1)} %copy-done.5), channel_id=1, source_target_pairs={{8,0},{16,8},{24,16},{0,24},{9,1},{17,9},{25,17},{1,25},{10,2},{18... | collective-permute-start | bytes 393224 | tf_op jit(solution)/shard_map/ppermute | solution.py:24
  116.7 8.3 %collective-permute-start.23 = (bf16[32,1,1,4,2,2,128]{6,0,5,4,3,2,1:T(8,128)(2,1)S(1)}, bf16[32,1,1,4,2,2,128]{6,0,5,4,3,2,1:T(8,128)(2,1)S(1)}, u32[]{:S(2)}, u32[]{:S(2)}) collective-permute-start(bf16[32,1,1,4,2,2,128]{6,0,5,4,3,2,1:T(8,128)(2,1)S(1)} %copy-done.5), channel_id=1, source_target_pairs={{0,8},{8,16},{16,24},{24,0},{1,9},{9,17},{17,25},{25,1},{2,10},{10... | collective-permute-start | bytes 393224 | tf_op jit(solution)/shard_map/ppermute | solution.py:22
  119.7 5.3 %collective-permute-start.21 = (bf16[32,1,1,1,2,2,128]{6,0,5,4,3,2,1:T(8,128)(2,1)S(1)}, bf16[32,1,1,1,2,2,128]{6,0,5,4,3,2,1:T(8,128)(2,1)S(1)}, u32[]{:S(2)}, u32[]{:S(2)}) collective-permute-start(bf16[32,1,1,1,2,2,128]{6,0,5,4,3,2,1:T(8,128)(2,1)S(1)} %get-tuple-element.32), channel_id=1, source_target_pairs={{0,4},{1,5},{2,6},{3,7},{4,0},{5,1},{6,2},{7,3},{8,12},{9,13},{10,... | collective-permute-start | bytes 98312 | tf_op jit(solution)/shard_map/ppermute | solution.py:12
  121.0 4.0 %collective-permute-start.20 = (bf16[32,1,1,1,2,2,128]{6,0,5,4,3,2,1:T(8,128)(2,1)S(1)}, bf16[32,1,1,1,2,2,128]{6,0,5,4,3,2,1:T(8,128)(2,1)S(1)}, u32[]{:S(2)}, u32[]{:S(2)}) collective-permute-start(bf16[32,1,1,1,2,2,128]{6,0,5,4,3,2,1:T(8,128)(2,1)S(1)} %get-tuple-element.33), channel_id=1, source_target_pairs={{0,4},{1,5},{2,6},{3,7},{4,0},{5,1},{6,2},{7,3},{8,12},{9,13},{10,... | collective-permute-start | bytes 98312 | tf_op jit(solution)/shard_map/ppermute | solution.py:12
  (11 other events, 252.8 us)
where the time goes:
time: 215 us; the launch traced here: 214 us
  blocking collectives  139 us (65%)
  starting transfers between devices  27.3 us (13%)
  local copies, waits for them, and re-layouts  16.4 us (8%)
  other arithmetic  12.9 us (6%)
  waiting for transfers between devices  9.75 us (5%)
  matrix products  7.22 us (3%)
    psum x2, blocking collectives, pair_products(): lax.psum((inner_rows(image, image), inner_rows(image, residual)), ('ta',...  78.8 us
    psum x1, blocking collectives, shards(): projection_sum = lax.psum(inner_rows(image_a, image_b), ('ta', 'xyz'))  39.7 us
    all_gather x2, blocking collectives, precondition(): lax.all_gather(coarse, 'xyz', axis=1, tiled=True)  20.7 us
    ppermute x20, starting transfers between devices, from_behind(): lax.ppermute(x, axis, [(i, (i + by) % length) for i in range(length)])  19.5 us
    ppermute x20, waiting for transfers between devices, from_behind(): lax.ppermute(x, axis, [(i, (i + by) % length) for i in range(length)])  9.27 us
    ppermute x2, starting transfers between devices, with_halo(): lax.ppermute(head, axis, [((i + 1) % count, i) for i in range(count)])  5.75 us
    unnamed x28, local copies, waits for them, and re-layouts  5.09 us
    slice x4, local copies, waits for them, and re-layouts, both_sides(): lax.slice_in_dim(lowered, 1, length, axis=which)  4.87 us
  transfers between devices with their start and end apart: 24, of which 5 were waited for; matrix products, arithmetic and copies ran while one was open for 5% of the time, Pallas kernels for 0%

commit v1 on v0

--- a/solution.py
+++ b/solution.py
@@ -7,41 +7,72 @@
 EPS = 1e-06
 
 
-def from_behind(x, axis, by):
-    length = lax.axis_size(axis)
-    return lax.ppermute(x, axis, [(i, (i + by) % length) for i in range(length)])
+def is_power_of_two(count):
+    return count & (count - 1) == 0
 
 
-def with_halo(cells, sides, width):
-    for axis, dim in sides:
-        count = lax.axis_size(axis)
-        head = lax.slice_in_dim(cells, 0, width, axis=dim)
-        tail = lax.slice_in_dim(cells, cells.shape[dim] - width, cells.shape[dim], axis=dim)
-        cells = jnp.concatenate(
-            [
-                lax.ppermute(tail, axis, [(i, (i + 1) % count) for i in range(count)]),
-                cells,
-                lax.ppermute(head, axis, [((i + 1) % count, i) for i in range(count)]),
-            ],
-            axis=dim,
-        )
-    return cells
+def exchange(x, axis, bit):
+    count = lax.axis_size(axis)
+    return lax.ppermute(x, axis, [(i, i ^ bit) for i in range(count)])
 
 
-def fetch_face(face, stride, extent, toward):
-    nearby = from_behind(face, "xyz", -toward * stride)
-    across = from_behind(face, "xyz", toward * stride * (extent - 1))
-    coord = lax.axis_index("xyz") // stride % extent
-    boundary = extent - 1 if toward > 0 else 0
-    return jnp.where(coord == boundary, across, nearby)
+def axis_sum(x, axis):
+    count = lax.axis_size(axis)
+    if not is_power_of_two(count):
+        return lax.psum(x, axis)
+    bit = 1
+    while bit < count:
+        x = x + exchange(x, axis, bit)
+        bit *= 2
+    return x
 
 
-def both_sides(lowered, which, stride, extent):
+def total_sum(x):
+    return axis_sum(axis_sum(x, "xyz"), "ta")
+
+
+def gather_tiled(x, axis, dim):
+    count = lax.axis_size(axis)
+    if not is_power_of_two(count):
+        return lax.all_gather(x, axis, axis=dim, tiled=True)
+    me = lax.axis_index(axis)
+    bit = 1
+    while bit < count:
+        other = exchange(x, axis, bit)
+        x = jnp.where(
+            me // bit % 2 == 0,
+            jnp.concatenate([x, other], dim),
+            jnp.concatenate([other, x], dim),
+        )
+        bit *= 2
+    return x
+
+
+def neighbour_source(device, stride, extent, step):
+    coord = device // stride % extent
+    return device + ((coord + step) % extent - coord) * stride
+
+
+def both_sides(lowered, which, axis, stride, extent):
     length = lowered.shape[which]
-    from_upper = fetch_face(lax.slice_in_dim(lowered, 0, 1, axis=which), stride, extent, 1)
-    from_lower = fetch_face(
-        lax.slice_in_dim(lowered, length - 1, length, axis=which), stride, extent, -1
-    )
+    count = lax.axis_size(axis)
+    first = lax.slice_in_dim(lowered, 0, 1, axis=which)
+    last = lax.slice_in_dim(lowered, length - 1, length, axis=which)
+    if extent == 1:
+        from_upper, from_lower = first, last
+    elif extent == 2:
+        perm = [(neighbour_source(d, stride, extent, 1), d) for d in range(count)]
+        if length == 1:
+            from_upper = from_lower = lax.ppermute(first, axis, perm)
+        else:
+            pair = lax.ppermute(jnp.concatenate([first, last], which), axis, perm)
+            from_upper = lax.slice_in_dim(pair, 0, 1, axis=which)
+            from_lower = lax.slice_in_dim(pair, 1, 2, axis=which)
+    else:
+        up = [(neighbour_source(d, stride, extent, 1), d) for d in range(count)]
+        down = [(neighbour_source(d, stride, extent, -1), d) for d in range(count)]
+        from_upper = lax.ppermute(first, axis, up)
+        from_lower = lax.ppermute(last, axis, down)
     upper = jnp.concatenate([lax.slice_in_dim(lowered, 1, length, axis=which), from_upper], which)
     lower = jnp.concatenate(
         [from_lower, lax.slice_in_dim(lowered, 0, length - 1, axis=which)], which
@@ -53,12 +84,10 @@
     blocks_total = lax.axis_size("xyz")
     across_x = 2 + 2 * min(blocks_total // 64, 1)
     across_z = blocks_total // (across_x * across_x)
-    upper_x, lower_x = both_sides(lowered, 5, 1, across_x)
-    upper_y, lower_y = both_sides(lowered, 4, across_x, across_x)
-    upper_z, lower_z = both_sides(lowered, 3, across_x * across_x, across_z)
-    padded = with_halo(lowered, (("ta", 1),), 1)
-    upper_t = padded[:, 2:]
-    lower_t = padded[:, :-2]
+    upper_x, lower_x = both_sides(lowered, 5, "xyz", 1, across_x)
+    upper_y, lower_y = both_sides(lowered, 4, "xyz", across_x, across_x)
+    upper_z, lower_z = both_sides(lowered, 3, "xyz", across_x * across_x, across_z)
+    upper_t, lower_t = both_sides(lowered, 1, "ta", 1, lax.axis_size("ta"))
     stacked = jnp.stack(
         [lowered, upper_x, lower_x, upper_y, lower_y, upper_z, lower_z, upper_t, lower_t], 2
     )
@@ -81,7 +110,7 @@
     ).astype(jnp.bfloat16)
     inverse_rows = coarse_inverse[0]
     correction = lax.dot_general(
-        lax.all_gather(coarse, "xyz", axis=1, tiled=True),
+        gather_tiled(coarse, "xyz", 1),
         inverse_rows,
         (((1,), (1,)), ((), ())),
         preferred_element_type=jnp.float32,
@@ -101,7 +130,8 @@
 
 
 def pair_products(image, residual):
-    return lax.psum((inner_rows(image, image), inner_rows(image, residual)), ("ta", "xyz"))
+    both = total_sum(jnp.stack([inner_rows(image, image), inner_rows(image, residual)]))
+    return (both[0], both[1])
 
 
 def shards(right_side, coarse_links, null_vectors, coarse_inverse):
@@ -114,7 +144,7 @@
     residual = residual - scaled(step_a, image_a)
     direction_b = precondition(residual, null_vectors, coarse_inverse)
     image_b = apply_links(coarse_links, direction_b.astype(jnp.bfloat16))
-    projection_sum = lax.psum(inner_rows(image_a, image_b), ("ta", "xyz"))
+    projection_sum = total_sum(inner_rows(image_a, image_b))
     beta_coef = projection_sum / (norm_a + EPS)
     image_b = image_b - scaled(beta_coef, image_a)
     direction_b = direction_b - scaled(beta_coef, direction_a)

time: 215 us -> 117 us (0.54)
  blocking collectives: 139 us -> 0 us
  waiting for transfers between devices: 9.75 us -> 59 us
  other arithmetic: 12.9 us -> 7.26 us
  local copies, waits for them, and re-layouts: 16.4 us -> 13.5 us
    psum x3 -> x0, blocking collectives: 119 us -> none  [the longest x2 78.8 us: pair_products(): lax.psum((inner_rows(image, image), inner_rows(image, residual)), ('ta',...]
    ppermute x24 -> x31, waiting for transfers between devices: 9.75 us -> 59 us  [the longest x21 51.2 us: exchange(): return lax.ppermute(x, axis, [(i, i ^ bit) for i in range(count)])]
    all_gather x2 -> x0, blocking collectives: 20.7 us -> none  [precondition(): lax.all_gather(coarse, 'xyz', axis=1, tiled=True)]
    unnamed x12, other arithmetic: 2.77 us -> 0.24 us
    slice x6 -> x12, local copies, waits for them, and re-layouts: 7.04 us -> 5.14 us  [the longest x6 5.08 us: both_sides(): first = lax.slice_in_dim(lowered, 0, 1, axis=which)]
    ppermute x24 -> x31, starting transfers between devices: 27.3 us -> 27.9 us  [the longest x21 16.4 us: exchange(): return lax.ppermute(x, axis, [(i, i ^ bit) for i in range(count)])]
    unnamed x28 -> x30, local copies, waits for them, and re-layouts: 5.09 us -> 4.8 us
  transfers between devices with their start and end apart: 24 -> 31, of which waited for: 5 -> 25; matrix products, arithmetic and copies ran while one was open for 5% -> 4% of each run, Pallas kernels for 0% -> 0%
where the time goes in v1:
time: 117 us; the launch traced here: 116 us
  waiting for transfers between devices  59 us (50%)
  starting transfers between devices  27.9 us (24%)
  local copies, waits for them, and re-layouts  13.5 us (12%)
  matrix products  7.4 us (6%)
  other arithmetic  7.26 us (6%)
  between operations  1.18 us (1%)
    ppermute x21, waiting for transfers between devices, exchange(): return lax.ppermute(x, axis, [(i, i ^ bit) for i in range(count)])  51.2 us
    ppermute x21, starting transfers between devices, exchange(): return lax.ppermute(x, axis, [(i, i ^ bit) for i in range(count)])  16.4 us
    ppermute x6, starting transfers between devices, both_sides(): pair = lax.ppermute(jnp.concatenate([first, last], which), axis, perm)  5.83 us
    ppermute x2, starting transfers between devices, both_sides(): from_upper = lax.ppermute(first, axis, up)  5.12 us
    slice x6, local copies, waits for them, and re-layouts, both_sides(): first = lax.slice_in_dim(lowered, 0, 1, axis=which)  5.08 us
    unnamed x30, local copies, waits for them, and re-layouts  4.8 us
    dot_general x2, matrix products, precondition(): jnp.einsum('tbzyxjk,nj->ntbzyxk', null_vectors, correction, preferred_ele...  4.46 us
    ppermute x6, waiting for transfers between devices, both_sides(): pair = lax.ppermute(jnp.concatenate([first, last], which), axis, perm)  3.95 us
  transfers between devices with their start and end apart: 31, of which 25 were waited for; matrix products, arithmetic and copies ran while one was open for 4% of the time, Pallas kernels for 0%

profile of v1, /device:TPU:0, one launch (start us, length us, event | category | flops | bytes accessed | tf_op | source)
XLA Modules:
  0.0 116.2 jit_solution(13113688960027791123)
XLA Ops:
  4.3 2.8 %collective-permute-start.1 = (bf16[32,96]{1,0:T(8,128)(2,1)S(1)}, bf16[32,96]{1,0:T(8,128)(2,1)S(1)}, u32[]{:S(2)}, u32[]{:S(2)}) collective-permute-start(bf16[32,96]{1,0:T(8,128)(2,1)S(1)} %maximum_select_fusion.8), channel_id=1, source_target_pairs={{0,2},{1,3},{2,0},{3,1},{4,6},{5,7},{6,4},{7,5},{8,10},{9,11},{10,... | collective-permute-start | bytes 18440 | tf_op jit(solution)/shard_map/ppermute | solution.py:16
  8.9 2.1 %collective-permute-start.2 = (bf16[32,192]{1,0:T(8,128)(2,1)S(1)}, bf16[32,192]{1,0:T(8,128)(2,1)}, u32[]{:S(2)}, u32[]{:S(2)}) collective-permute-start(bf16[32,192]{1,0:T(8,128)(2,1)S(1)} %maximum_select_fusion.6), channel_id=1, source_target_pairs={{0,4},{1,5},{2,6},{3,7},{4,0},{5,1},{6,2},{7,3},{8,12},{9,13},{10,... | collective-permute-start | bytes 36872 | tf_op jit(solution)/shard_map/ppermute | solution.py:16
  11.0 1.8 %collective-permute-done.2 = bf16[32,192]{1,0:T(8,128)(2,1)} collective-permute-done((bf16[32,192]{1,0:T(8,128)(2,1)S(1)}, bf16[32,192]{1,0:T(8,128)(2,1)}, u32[]{:S(2)}, u32[]{:S(2)}) %collective-permute-start.2) | collective-permute-done | bytes 12320 | tf_op jit(solution)/shard_map/ppermute | solution.py:16
  12.8 2.2 %bitcast_dynamic-update-slice_fusion.5 = (bf16[32,1,9,1,4,2,2,128]{7,0,6,5,4,3,2,1:T(8,128)(2,1)S(1)}, bf16[32,1,1,4,2,2,128]{6,0,5,4,3,2,1:T(8,128)(2,1)}, f32[32,1,1,4,2,2,128]{6,0,5,4,3,2,1:T(8,128)}) fusion(bf16[1,1,4,2,2,48,128]{6,5,4,3,2,1,0:T(8,128)(2,1)} %param.6, bf16[1,48,384]{2,1,0:T(8,128)(2,1)} %param.7, ...), kind=kOutput, calls=%fused_computation.74 | convolution fusion | flops 7779839 | bytes 1044481 | tf_op jit(solution)/shard_map/tbzyxjk,nj->ntbzyxk/dot_general | solution.py:118
  16.7 2.1 %collective-permute-start.4 = (bf16[32,1,1,4,2,2,128]{6,0,5,4,3,2,1:T(8,128)(2,1)}, bf16[32,1,1,4,2,2,128]{6,0,5,4,3,2,1:T(8,128)(2,1)S(1)}, u32[]{:S(2)}, u32[]{:S(2)}) collective-permute-start(bf16[32,1,1,4,2,2,128]{6,0,5,4,3,2,1:T(8,128)(2,1)} %get-tuple-element.15), channel_id=1, source_target_pairs={{2,0},{3,1},{0,2},{1,3},{6,4},{7,5},{4,6},{5,7},{10,8},{11,9},{8,1... | collective-permute-start | bytes 393224 | tf_op jit(solution)/shard_map/ppermute | solution.py:68
  18.7 3.6 %collective-permute-start.6 = (bf16[32,1,1,4,2,2,128]{6,0,5,4,3,2,1:T(8,128)(2,1)}, bf16[32,1,1,4,2,2,128]{6,0,5,4,3,2,1:T(8,128)(2,1)S(1)}, u32[]{:S(2)}, u32[]{:S(2)}) collective-permute-start(bf16[32,1,1,4,2,2,128]{6,0,5,4,3,2,1:T(8,128)(2,1)} %get-tuple-element.15), channel_id=1, source_target_pairs={{8,0},{16,8},{24,16},{0,24},{9,1},{17,9},{25,17},{1,25},{10,2},{18... | collective-permute-start | bytes 393224 | tf_op jit(solution)/shard_map/ppermute | solution.py:74
  25.9 2.1 %collective-permute-done.5 = bf16[32,1,1,2,2,2,128]{6,0,5,4,3,2,1:T(8,128)(2,1)S(1)} collective-permute-done((bf16[32,1,1,2,2,2,128]{6,0,5,4,3,2,1:T(8,128)(2,1)S(1)}, bf16[32,1,1,2,2,2,128]{6,0,5,4,3,2,1:T(8,128)(2,1)S(1)}, u32[]{:S(2)}, u32[]{:S(2)}) %collective-permute-start.5) | collective-permute-done | bytes 65568 | tf_op jit(solution)/shard_map/ppermute | solution.py:68
  28.2 2.1 %collective-permute-done.7 = bf16[32,1,1,4,2,2,128]{6,0,5,4,3,2,1:T(8,128)(2,1)S(1)} collective-permute-done((bf16[32,1,1,4,2,2,128]{6,0,5,4,3,2,1:T(8,128)(2,1)}, bf16[32,1,1,4,2,2,128]{6,0,5,4,3,2,1:T(8,128)(2,1)S(1)}, u32[]{:S(2)}, u32[]{:S(2)}) %collective-permute-start.7) | collective-permute-done | bytes 131104 | tf_op jit(solution)/shard_map/ppermute | solution.py:75
  36.5 3.0 %collective-permute-done.9 = f32[2,32]{1,0:T(2,128)S(1)} collective-permute-done((f32[2,32]{1,0:T(2,128)S(1)}, f32[2,32]{1,0:T(2,128)S(1)}, u32[]{:S(2)}, u32[]{:S(2)}) %collective-permute-start.9) | collective-permute-done | bytes 288 | tf_op jit(solution)/shard_map/ppermute | solution.py:16
  41.2 2.0 %collective-permute-done.10 = f32[2,32]{1,0:T(2,128)S(1)} collective-permute-done((f32[2,32]{1,0:T(2,128)S(1)}, f32[2,32]{1,0:T(2,128)S(1)}, u32[]{:S(2)}, u32[]{:S(2)}) %collective-permute-start.10) | collective-permute-done | bytes 288 | tf_op jit(solution)/shard_map/ppermute | solution.py:16
  43.2 3.6 %collective-permute-done.11 = f32[2,32]{1,0:T(2,128)S(1)} collective-permute-done((f32[2,32]{1,0:T(2,128)S(1)}, f32[2,32]{1,0:T(2,128)S(1)}, u32[]{:S(2)}, u32[]{:S(2)}) %collective-permute-start.11) | collective-permute-done | bytes 288 | tf_op jit(solution)/shard_map/ppermute | solution.py:16
  46.9 4.4 %collective-permute-done.12 = f32[2,32]{1,0:T(2,128)S(1)} collective-permute-done((f32[2,32]{1,0:T(2,128)S(1)}, f32[2,32]{1,0:T(2,128)S(1)}, u32[]{:S(2)}, u32[]{:S(2)}) %collective-permute-start.12) | collective-permute-done | bytes 288 | tf_op jit(solution)/shard_map/ppermute | solution.py:16
  54.7 3.1 %collective-permute-done.14 = bf16[32,96]{1,0:T(8,128)(2,1)S(1)} collective-permute-done((bf16[32,96]{1,0:T(8,128)(2,1)S(1)}, bf16[32,96]{1,0:T(8,128)(2,1)S(1)}, u32[]{:S(2)}, u32[]{:S(2)}) %collective-permute-start.14) | collective-permute-done | bytes 6176 | tf_op jit(solution)/shard_map/ppermute | solution.py:16
  59.4 2.2 %collective-permute-done.15 = bf16[32,192]{1,0:T(8,128)(2,1)S(1)} collective-permute-done((bf16[32,192]{1,0:T(8,128)(2,1)S(1)}, bf16[32,192]{1,0:T(8,128)(2,1)S(1)}, u32[]{:S(2)}, u32[]{:S(2)}) %collective-permute-start.15) | collective-permute-done | bytes 12320 | tf_op jit(solution)/shard_map/ppermute | solution.py:16
  62.3 2.2 %bitcast_dynamic-update-slice_fusion.2 = (bf16[32,1,9,1,4,2,2,128]{7,0,6,5,4,3,2,1:T(8,128)(2,1)S(1)}, bf16[32,1,1,4,2,2,128]{6,0,5,4,3,2,1:T(8,128)(2,1)}, f32[32,1,1,4,2,2,128]{6,0,5,4,3,2,1:T(8,128)}) fusion(bf16[1,1,4,2,2,48,128]{6,5,4,3,2,1,0:T(8,128)(2,1)} %param.6, bf16[1,48,384]{2,1,0:T(8,128)(2,1)} %param.7, bf16[32,192]{1,0:T(8,128)(2,1)} %copy-done.8, ...), kind=kOutput, calls=%fused_computation.71 | convolution fusion | flops 7779839 | bytes 1044481 | tf_op jit(solution)/shard_map/tbzyxjk,nj->ntbzyxk/dot_general | solution.py:118
  72.3 1.9 %collective-permute-done.18 = bf16[32,1,1,2,2,2,128]{6,0,5,4,3,2,1:T(8,128)(2,1)S(1)} collective-permute-done((bf16[32,1,1,2,2,2,128]{6,0,5,4,3,2,1:T(8,128)(2,1)S(1)}, bf16[32,1,1,2,2,2,128]{6,0,5,4,3,2,1:T(8,128)(2,1)S(1)}, u32[]{:S(2)}, u32[]{:S(2)}) %collective-permute-start.18) | collective-permute-done | bytes 65568 | tf_op jit(solution)/shard_map/ppermute | solution.py:68
  83.8 2.0 %collective-permute-done.22 = f32[32]{0:T(128)S(1)} collective-permute-done((f32[32]{0:T(128)S(1)}, f32[32]{0:T(128)S(1)}, u32[]{:S(2)}, u32[]{:S(2)}) %collective-permute-start.22) | collective-permute-done | bytes 160 | tf_op jit(solution)/shard_map/ppermute | solution.py:16
  87.4 2.0 %collective-permute-done.23 = f32[32]{0:T(128)S(1)} collective-permute-done((f32[32]{0:T(128)S(1)}, f32[32]{0:T(128)S(1)}, u32[]{:S(2)}, u32[]{:S(2)}) %collective-permute-start.23) | collective-permute-done | bytes 160 | tf_op jit(solution)/shard_map/ppermute | solution.py:16
  89.4 3.5 %collective-permute-done.24 = f32[32]{0:T(128)S(1)} collective-permute-done((f32[32]{0:T(128)S(1)}, f32[32]{0:T(128)S(1)}, u32[]{:S(2)}, u32[]{:S(2)}) %collective-permute-start.24) | collective-permute-done | bytes 160 | tf_op jit(solution)/shard_map/ppermute | solution.py:16
  93.0 4.4 %collective-permute-done.25 = f32[32]{0:T(128)S(1)} collective-permute-done((f32[32]{0:T(128)S(1)}, f32[32]{0:T(128)S(1)}, u32[]{:S(2)}, u32[]{:S(2)}) %collective-permute-start.25) | collective-permute-done | bytes 160 | tf_op jit(solution)/shard_map/ppermute | solution.py:16
  100.4 2.1 %collective-permute-done.27 = f32[2,32]{1,0:T(2,128)S(1)} collective-permute-done((f32[2,32]{1,0:T(2,128)S(1)}, f32[2,32]{1,0:T(2,128)S(1)}, u32[]{:S(2)}, u32[]{:S(2)}) %collective-permute-start.27) | collective-permute-done | bytes 288 | tf_op jit(solution)/shard_map/ppermute | solution.py:16
  104.1 2.0 %collective-permute-done.28 = f32[2,32]{1,0:T(2,128)S(1)} collective-permute-done((f32[2,32]{1,0:T(2,128)S(1)}, f32[2,32]{1,0:T(2,128)S(1)}, u32[]{:S(2)}, u32[]{:S(2)}) %collective-permute-start.28) | collective-permute-done | bytes 288 | tf_op jit(solution)/shard_map/ppermute | solution.py:16
  106.2 3.5 %collective-permute-done.29 = f32[2,32]{1,0:T(2,128)S(1)} collective-permute-done((f32[2,32]{1,0:T(2,128)S(1)}, f32[2,32]{1,0:T(2,128)S(1)}, u32[]{:S(2)}, u32[]{:S(2)}) %collective-permute-start.29) | collective-permute-done | bytes 288 | tf_op jit(solution)/shard_map/ppermute | solution.py:16
  109.8 4.4 %collective-permute-done.30 = f32[2,32]{1,0:T(2,128)S(1)} collective-permute-done((f32[2,32]{1,0:T(2,128)S(1)}, f32[2,32]{1,0:T(2,128)S(1)}, u32[]{:S(2)}, u32[]{:S(2)}) %collective-permute-start.30) | collective-permute-done | bytes 288 | tf_op jit(solution)/shard_map/ppermute | solution.py:16
  (144 shorter events, 49.8 us)
Async XLA Ops:
  4.3 4.5 %collective-permute-start.1 = (bf16[32,96]{1,0:T(8,128)(2,1)S(1)}, bf16[32,96]{1,0:T(8,128)(2,1)S(1)}, u32[]{:S(2)}, u32[]{:S(2)}) collective-permute-start(bf16[32,96]{1,0:T(8,128)(2,1)S(1)} %maximum_select_fusion.8), channel_id=1, source_target_pairs={{0,2},{1,3},{2,0},{3,1},{4,6},{5,7},{6,4},{7,5},{8,10},{9,11},{10,... | collective-permute-start | bytes 18440 | tf_op jit(solution)/shard_map/ppermute | solution.py:16
  8.9 3.9 %collective-permute-start.2 = (bf16[32,192]{1,0:T(8,128)(2,1)S(1)}, bf16[32,192]{1,0:T(8,128)(2,1)}, u32[]{:S(2)}, u32[]{:S(2)}) collective-permute-start(bf16[32,192]{1,0:T(8,128)(2,1)S(1)} %maximum_select_fusion.6), channel_id=1, source_target_pairs={{0,4},{1,5},{2,6},{3,7},{4,0},{5,1},{6,2},{7,3},{8,12},{9,13},{10,... | collective-permute-start | bytes 36872 | tf_op jit(solution)/shard_map/ppermute | solution.py:16
  16.7 11.3 %collective-permute-start.4 = (bf16[32,1,1,4,2,2,128]{6,0,5,4,3,2,1:T(8,128)(2,1)}, bf16[32,1,1,4,2,2,128]{6,0,5,4,3,2,1:T(8,128)(2,1)S(1)}, u32[]{:S(2)}, u32[]{:S(2)}) collective-permute-start(bf16[32,1,1,4,2,2,128]{6,0,5,4,3,2,1:T(8,128)(2,1)} %get-tuple-element.15), channel_id=1, source_target_pairs={{2,0},{3,1},{0,2},{1,3},{6,4},{7,5},{4,6},{5,7},{10,8},{11,9},{8,1... | collective-permute-start | bytes 393224 | tf_op jit(solution)/shard_map/ppermute | solution.py:68
  18.7 9.4 %collective-permute-start.6 = (bf16[32,1,1,4,2,2,128]{6,0,5,4,3,2,1:T(8,128)(2,1)}, bf16[32,1,1,4,2,2,128]{6,0,5,4,3,2,1:T(8,128)(2,1)S(1)}, u32[]{:S(2)}, u32[]{:S(2)}) collective-permute-start(bf16[32,1,1,4,2,2,128]{6,0,5,4,3,2,1:T(8,128)(2,1)} %get-tuple-element.15), channel_id=1, source_target_pairs={{8,0},{16,8},{24,16},{0,24},{9,1},{17,9},{25,17},{1,25},{10,2},{18... | collective-permute-start | bytes 393224 | tf_op jit(solution)/shard_map/ppermute | solution.py:74
  22.4 5.6 %collective-permute-start.3 = (bf16[32,1,1,4,2,2,128]{6,0,5,4,3,2,1:T(8,128)(2,1)}, bf16[32,1,1,4,2,2,128]{6,0,5,4,3,2,1:T(8,128)(2,1)S(1)}, u32[]{:S(2)}, u32[]{:S(2)}) collective-permute-start(bf16[32,1,1,4,2,2,128]{6,0,5,4,3,2,1:T(8,128)(2,1)} %get-tuple-element.15), channel_id=1, source_target_pairs={{1,0},{0,1},{3,2},{2,3},{5,4},{4,5},{7,6},{6,7},{9,8},{8,9},{11,10... | collective-permute-start | bytes 393224 | tf_op jit(solution)/shard_map/ppermute | solution.py:68
  22.4 7.9 %collective-permute-start.7 = (bf16[32,1,1,4,2,2,128]{6,0,5,4,3,2,1:T(8,128)(2,1)}, bf16[32,1,1,4,2,2,128]{6,0,5,4,3,2,1:T(8,128)(2,1)S(1)}, u32[]{:S(2)}, u32[]{:S(2)}) collective-permute-start(bf16[32,1,1,4,2,2,128]{6,0,5,4,3,2,1:T(8,128)(2,1)} %get-tuple-element.15), channel_id=1, source_target_pairs={{24,0},{0,8},{8,16},{16,24},{25,1},{1,9},{9,17},{17,25},{26,2},{2,... | collective-permute-start | bytes 393224 | tf_op jit(solution)/shard_map/ppermute | solution.py:75
  23.4 4.5 %collective-permute-start.5 = (bf16[32,1,1,2,2,2,128]{6,0,5,4,3,2,1:T(8,128)(2,1)S(1)}, bf16[32,1,1,2,2,2,128]{6,0,5,4,3,2,1:T(8,128)(2,1)S(1)}, u32[]{:S(2)}, u32[]{:S(2)}) collective-permute-start(bf16[32,1,1,2,2,2,128]{6,0,5,4,3,2,1:T(8,128)(2,1)S(1)} %pad_maximum_fusion.2), channel_id=1, source_target_pairs={{4,0},{5,1},{6,2},{7,3},{0,4},{1,5},{2,6},{3,7},{12,8},{13,9},{14,... | collective-permute-start | bytes 196616 | tf_op jit(solution)/shard_map/ppermute | solution.py:68
  35.9 3.6 %collective-permute-start.9 = (f32[2,32]{1,0:T(2,128)S(1)}, f32[2,32]{1,0:T(2,128)S(1)}, u32[]{:S(2)}, u32[]{:S(2)}) collective-permute-start(f32[2,32]{1,0:T(2,128)S(1)} %fusion.74), channel_id=1, source_target_pairs={{0,2},{1,3},{2,0},{3,1},{4,6},{5,7},{6,4},{7,5},{8,10},{9,11},{10,... | collective-permute-start | bytes 776 | tf_op jit(solution)/shard_map/ppermute | solution.py:16
  39.6 3.6 %collective-permute-start.10 = (f32[2,32]{1,0:T(2,128)S(1)}, f32[2,32]{1,0:T(2,128)S(1)}, u32[]{:S(2)}, u32[]{:S(2)}) collective-permute-start(f32[2,32]{1,0:T(2,128)S(1)} %fusion.96), channel_id=1, source_target_pairs={{0,4},{1,5},{2,6},{3,7},{4,0},{5,1},{6,2},{7,3},{8,12},{9,13},{10,... | collective-permute-start | bytes 776 | tf_op jit(solution)/shard_map/ppermute | solution.py:16
  43.2 3.6 %collective-permute-start.11 = (f32[2,32]{1,0:T(2,128)S(1)}, f32[2,32]{1,0:T(2,128)S(1)}, u32[]{:S(2)}, u32[]{:S(2)}) collective-permute-start(f32[2,32]{1,0:T(2,128)S(1)} %add.95), channel_id=1, source_target_pairs={{0,8},{8,0},{16,24},{24,16},{1,9},{9,1},{17,25},{25,17},{2,10},{10... | collective-permute-start | bytes 776 | tf_op jit(solution)/shard_map/ppermute | solution.py:16
  46.8 4.5 %collective-permute-start.12 = (f32[2,32]{1,0:T(2,128)S(1)}, f32[2,32]{1,0:T(2,128)S(1)}, u32[]{:S(2)}, u32[]{:S(2)}) collective-permute-start(f32[2,32]{1,0:T(2,128)S(1)} %add.96), channel_id=1, source_target_pairs={{0,16},{8,24},{16,0},{24,8},{1,17},{9,25},{17,1},{25,9},{2,18},{10... | collective-permute-start | bytes 776 | tf_op jit(solution)/shard_map/ppermute | solution.py:16
  54.1 3.7 %collective-permute-start.14 = (bf16[32,96]{1,0:T(8,128)(2,1)S(1)}, bf16[32,96]{1,0:T(8,128)(2,1)S(1)}, u32[]{:S(2)}, u32[]{:S(2)}) collective-permute-start(bf16[32,96]{1,0:T(8,128)(2,1)S(1)} %maximum_select_fusion.9), channel_id=1, source_target_pairs={{0,2},{1,3},{2,0},{3,1},{4,6},{5,7},{6,4},{7,5},{8,10},{9,11},{10,... | collective-permute-start | bytes 18440 | tf_op jit(solution)/shard_map/ppermute | solution.py:16
  57.9 3.8 %collective-permute-start.15 = (bf16[32,192]{1,0:T(8,128)(2,1)S(1)}, bf16[32,192]{1,0:T(8,128)(2,1)S(1)}, u32[]{:S(2)}, u32[]{:S(2)}) collective-permute-start(bf16[32,192]{1,0:T(8,128)(2,1)S(1)} %maximum_select_fusion.7), channel_id=1, source_target_pairs={{0,4},{1,5},{2,6},{3,7},{4,0},{5,1},{6,2},{7,3},{8,12},{9,13},{10,... | collective-permute-start | bytes 36872 | tf_op jit(solution)/shard_map/ppermute | solution.py:16
  66.2 8.0 %collective-permute-start.17 = (bf16[32,1,1,4,2,2,128]{6,0,5,4,3,2,1:T(8,128)(2,1)}, bf16[32,1,1,4,2,2,128]{6,0,5,4,3,2,1:T(8,128)(2,1)S(1)}, u32[]{:S(2)}, u32[]{:S(2)}) collective-permute-start(bf16[32,1,1,4,2,2,128]{6,0,5,4,3,2,1:T(8,128)(2,1)} %get-tuple-element.10), channel_id=1, source_target_pairs={{2,0},{3,1},{0,2},{1,3},{6,4},{7,5},{4,6},{5,7},{10,8},{11,9},{8,1... | collective-permute-start | bytes 393224 | tf_op jit(solution)/shard_map/ppermute | solution.py:68
  66.8 7.6 %collective-permute-start.19 = (bf16[32,1,1,4,2,2,128]{6,0,5,4,3,2,1:T(8,128)(2,1)}, bf16[32,1,1,4,2,2,128]{6,0,5,4,3,2,1:T(8,128)(2,1)S(1)}, u32[]{:S(2)}, u32[]{:S(2)}) collective-permute-start(bf16[32,1,1,4,2,2,128]{6,0,5,4,3,2,1:T(8,128)(2,1)} %get-tuple-element.10), channel_id=1, source_target_pairs={{8,0},{16,8},{24,16},{0,24},{9,1},{17,9},{25,17},{1,25},{10,2},{18... | collective-permute-start | bytes 393224 | tf_op jit(solution)/shard_map/ppermute | solution.py:74
  68.3 5.9 %collective-permute-start.16 = (bf16[32,1,1,4,2,2,128]{6,0,5,4,3,2,1:T(8,128)(2,1)}, bf16[32,1,1,4,2,2,128]{6,0,5,4,3,2,1:T(8,128)(2,1)S(1)}, u32[]{:S(2)}, u32[]{:S(2)}) collective-permute-start(bf16[32,1,1,4,2,2,128]{6,0,5,4,3,2,1:T(8,128)(2,1)} %get-tuple-element.10), channel_id=1, source_target_pairs={{1,0},{0,1},{3,2},{2,3},{5,4},{4,5},{7,6},{6,7},{9,8},{8,9},{11,10... | collective-permute-start | bytes 393224 | tf_op jit(solution)/shard_map/ppermute | solution.py:68
  68.3 7.9 %collective-permute-start.20 = (bf16[32,1,1,4,2,2,128]{6,0,5,4,3,2,1:T(8,128)(2,1)}, bf16[32,1,1,4,2,2,128]{6,0,5,4,3,2,1:T(8,128)(2,1)S(1)}, u32[]{:S(2)}, u32[]{:S(2)}) collective-permute-start(bf16[32,1,1,4,2,2,128]{6,0,5,4,3,2,1:T(8,128)(2,1)} %get-tuple-element.10), channel_id=1, source_target_pairs={{24,0},{0,8},{8,16},{16,24},{25,1},{1,9},{9,17},{17,25},{26,2},{2,... | collective-permute-start | bytes 393224 | tf_op jit(solution)/shard_map/ppermute | solution.py:75
  69.8 4.3 %collective-permute-start.18 = (bf16[32,1,1,2,2,2,128]{6,0,5,4,3,2,1:T(8,128)(2,1)S(1)}, bf16[32,1,1,2,2,2,128]{6,0,5,4,3,2,1:T(8,128)(2,1)S(1)}, u32[]{:S(2)}, u32[]{:S(2)}) collective-permute-start(bf16[32,1,1,2,2,2,128]{6,0,5,4,3,2,1:T(8,128)(2,1)S(1)} %pad_maximum_fusion.3), channel_id=1, source_target_pairs={{4,0},{5,1},{6,2},{7,3},{0,4},{1,5},{2,6},{3,7},{12,8},{13,9},{14,... | collective-permute-start | bytes 196616 | tf_op jit(solution)/shard_map/ppermute | solution.py:68
  89.4 3.5 %collective-permute-start.24 = (f32[32]{0:T(128)S(1)}, f32[32]{0:T(128)S(1)}, u32[]{:S(2)}, u32[]{:S(2)}) collective-permute-start(f32[32]{0:T(128)S(1)} %add.103), channel_id=1, source_target_pairs={{0,8},{8,0},{16,24},{24,16},{1,9},{9,1},{17,25},{25,17},{2,10},{10... | collective-permute-start | bytes 392 | tf_op jit(solution)/shard_map/ppermute | solution.py:16
  92.9 4.4 %collective-permute-start.25 = (f32[32]{0:T(128)S(1)}, f32[32]{0:T(128)S(1)}, u32[]{:S(2)}, u32[]{:S(2)}) collective-permute-start(f32[32]{0:T(128)S(1)} %add.104), channel_id=1, source_target_pairs={{0,16},{8,24},{16,0},{24,8},{1,17},{9,25},{17,1},{25,9},{2,18},{10... | collective-permute-start | bytes 392 | tf_op jit(solution)/shard_map/ppermute | solution.py:16
  98.9 3.6 %collective-permute-start.27 = (f32[2,32]{1,0:T(2,128)S(1)}, f32[2,32]{1,0:T(2,128)S(1)}, u32[]{:S(2)}, u32[]{:S(2)}) collective-permute-start(f32[2,32]{1,0:T(2,128)S(1)} %fusion.73), channel_id=1, source_target_pairs={{0,2},{1,3},{2,0},{3,1},{4,6},{5,7},{6,4},{7,5},{8,10},{9,11},{10,... | collective-permute-start | bytes 776 | tf_op jit(solution)/shard_map/ppermute | solution.py:16
  102.5 3.6 %collective-permute-start.28 = (f32[2,32]{1,0:T(2,128)S(1)}, f32[2,32]{1,0:T(2,128)S(1)}, u32[]{:S(2)}, u32[]{:S(2)}) collective-permute-start(f32[2,32]{1,0:T(2,128)S(1)} %fusion.95), channel_id=1, source_target_pairs={{0,4},{1,5},{2,6},{3,7},{4,0},{5,1},{6,2},{7,3},{8,12},{9,13},{10,... | collective-permute-start | bytes 776 | tf_op jit(solution)/shard_map/ppermute | solution.py:16
  106.1 3.6 %collective-permute-start.29 = (f32[2,32]{1,0:T(2,128)S(1)}, f32[2,32]{1,0:T(2,128)S(1)}, u32[]{:S(2)}, u32[]{:S(2)}) collective-permute-start(f32[2,32]{1,0:T(2,128)S(1)} %add.108), channel_id=1, source_target_pairs={{0,8},{8,0},{16,24},{24,16},{1,9},{9,1},{17,25},{25,17},{2,10},{10... | collective-permute-start | bytes 776 | tf_op jit(solution)/shard_map/ppermute | solution.py:16
  109.7 4.5 %collective-permute-start.30 = (f32[2,32]{1,0:T(2,128)S(1)}, f32[2,32]{1,0:T(2,128)S(1)}, u32[]{:S(2)}, u32[]{:S(2)}) collective-permute-start(f32[2,32]{1,0:T(2,128)S(1)} %add.109), channel_id=1, source_target_pairs={{0,16},{8,24},{16,0},{24,8},{1,17},{9,25},{17,1},{25,9},{2,18},{10... | collective-permute-start | bytes 776 | tf_op jit(solution)/shard_map/ppermute | solution.py:16
  (20 other events, 241.7 us)

commit v2 on v1

--- a/solution.py
+++ b/solution.py
@@ -144,11 +144,26 @@
     residual = residual - scaled(step_a, image_a)
     direction_b = precondition(residual, null_vectors, coarse_inverse)
     image_b = apply_links(coarse_links, direction_b.astype(jnp.bfloat16))
-    projection_sum = total_sum(inner_rows(image_a, image_b))
+    sums = total_sum(
+        jnp.stack(
+            [
+                inner_rows(image_a, image_b),
+                inner_rows(image_b, image_b),
+                inner_rows(image_b, residual),
+                inner_rows(image_a, residual),
+            ]
+        )
+    )
+    projection_sum, square_b, raw_correlation, shared_correlation = (
+        sums[0], sums[1], sums[2], sums[3]
+    )
     beta_coef = projection_sum / (norm_a + EPS)
     image_b = image_b - scaled(beta_coef, image_a)
     direction_b = direction_b - scaled(beta_coef, direction_a)
-    norm_b, correlation_b = pair_products(image_b, residual)
+    norm_b = jnp.maximum(
+        square_b - beta_coef * (2.0 * projection_sum - beta_coef * norm_a), 0.0
+    )
+    correlation_b = raw_correlation - beta_coef * shared_correlation
     step_b = correlation_b / (norm_b + EPS)
     solution = solution + scaled(step_b, direction_b)
     residual = residual - scaled(step_b, image_b)

time: 117 us -> 101 us (0.86)
  waiting for transfers between devices: 59 us -> 46.1 us
  starting transfers between devices: 27.9 us -> 24.7 us
    ppermute x21 -> x16, waiting for transfers between devices: 51.2 us -> 38.2 us  [exchange(): return lax.ppermute(x, axis, [(i, i ^ bit) for i in range(count)])]
    ppermute x21 -> x16, starting transfers between devices: 16.4 us -> 13.2 us  [exchange(): return lax.ppermute(x, axis, [(i, i ^ bit) for i in range(count)])]
  transfers between devices with their start and end apart: 31 -> 26, of which waited for: 25 -> 20; matrix products, arithmetic and copies ran while one was open for 4% -> 4% of each run, Pallas kernels for 0% -> 0%
where the time goes in v2:
time: 101 us; the launch traced here: 99.9 us
  waiting for transfers between devices  46.1 us (46%)
  starting transfers between devices  24.7 us (24%)
  local copies, waits for them, and re-layouts  13.5 us (13%)
  matrix products  7.39 us (7%)
  other arithmetic  7.08 us (7%)
  between operations  1.16 us (1%)
    ppermute x16, waiting for transfers between devices, exchange(): return lax.ppermute(x, axis, [(i, i ^ bit) for i in range(count)])  38.2 us
    ppermute x16, starting transfers between devices, exchange(): return lax.ppermute(x, axis, [(i, i ^ bit) for i in range(count)])  13.2 us
    ppermute x6, starting transfers between devices, both_sides(): pair = lax.ppermute(jnp.concatenate([first, last], which), axis, perm)  5.82 us
    ppermute x2, starting transfers between devices, both_sides(): from_upper = lax.ppermute(first, axis, up)  5.12 us
    slice x6, local copies, waits for them, and re-layouts, both_sides(): first = lax.slice_in_dim(lowered, 0, 1, axis=which)  5.08 us
    unnamed x30, local copies, waits for them, and re-layouts  4.87 us
    dot_general x2, matrix products, precondition(): jnp.einsum('tbzyxjk,nj->ntbzyxk', null_vectors, correction, preferred_ele...  4.44 us
    ppermute x6, waiting for transfers between devices, both_sides(): pair = lax.ppermute(jnp.concatenate([first, last], which), axis, perm)  3.95 us
  transfers between devices with their start and end apart: 26, of which 20 were waited for; matrix products, arithmetic and copies ran while one was open for 4% of the time, Pallas kernels for 0%

profile of v2, /device:TPU:0, one launch (start us, length us, event | category | flops | bytes accessed | tf_op | source)
XLA Modules:
  0.0 99.9 jit_solution(9785503245274071203)
XLA Ops:
  4.3 2.8 %collective-permute-start.1 = (bf16[32,96]{1,0:T(8,128)(2,1)S(1)}, bf16[32,96]{1,0:T(8,128)(2,1)S(1)}, u32[]{:S(2)}, u32[]{:S(2)}) collective-permute-start(bf16[32,96]{1,0:T(8,128)(2,1)S(1)} %maximum_select_fusion.8), channel_id=1, source_target_pairs={{0,2},{1,3},{2,0},{3,1},{4,6},{5,7},{6,4},{7,5},{8,10},{9,11},{10,... | collective-permute-start | bytes 18440 | tf_op jit(solution)/shard_map/ppermute | solution.py:16
  7.2 1.6 %collective-permute-done.1 = bf16[32,96]{1,0:T(8,128)(2,1)S(1)} collective-permute-done((bf16[32,96]{1,0:T(8,128)(2,1)S(1)}, bf16[32,96]{1,0:T(8,128)(2,1)S(1)}, u32[]{:S(2)}, u32[]{:S(2)}) %collective-permute-start.1) | collective-permute-done | bytes 6176 | tf_op jit(solution)/shard_map/ppermute | solution.py:16
  8.9 2.1 %collective-permute-start.2 = (bf16[32,192]{1,0:T(8,128)(2,1)S(1)}, bf16[32,192]{1,0:T(8,128)(2,1)}, u32[]{:S(2)}, u32[]{:S(2)}) collective-permute-start(bf16[32,192]{1,0:T(8,128)(2,1)S(1)} %maximum_select_fusion.6), channel_id=1, source_target_pairs={{0,4},{1,5},{2,6},{3,7},{4,0},{5,1},{6,2},{7,3},{8,12},{9,13},{10,... | collective-permute-start | bytes 36872 | tf_op jit(solution)/shard_map/ppermute | solution.py:16
  11.0 1.8 %collective-permute-done.2 = bf16[32,192]{1,0:T(8,128)(2,1)} collective-permute-done((bf16[32,192]{1,0:T(8,128)(2,1)S(1)}, bf16[32,192]{1,0:T(8,128)(2,1)}, u32[]{:S(2)}, u32[]{:S(2)}) %collective-permute-start.2) | collective-permute-done | bytes 12320 | tf_op jit(solution)/shard_map/ppermute | solution.py:16
  12.8 2.2 %bitcast_dynamic-update-slice_fusion.5 = (bf16[32,1,9,1,4,2,2,128]{7,0,6,5,4,3,2,1:T(8,128)(2,1)S(1)}, bf16[32,1,1,4,2,2,128]{6,0,5,4,3,2,1:T(8,128)(2,1)}, f32[32,1,1,4,2,2,128]{6,0,5,4,3,2,1:T(8,128)}) fusion(bf16[1,1,4,2,2,48,128]{6,5,4,3,2,1,0:T(8,128)(2,1)} %param.6, bf16[1,48,384]{2,1,0:T(8,128)(2,1)} %param.7, ...), kind=kOutput, calls=%fused_computation.74 | convolution fusion | flops 7779839 | bytes 1044481 | tf_op jit(solution)/shard_map/tbzyxjk,nj->ntbzyxk/dot_general | solution.py:118
  16.7 2.1 %collective-permute-start.4 = (bf16[32,1,1,4,2,2,128]{6,0,5,4,3,2,1:T(8,128)(2,1)}, bf16[32,1,1,4,2,2,128]{6,0,5,4,3,2,1:T(8,128)(2,1)S(1)}, u32[]{:S(2)}, u32[]{:S(2)}) collective-permute-start(bf16[32,1,1,4,2,2,128]{6,0,5,4,3,2,1:T(8,128)(2,1)} %get-tuple-element.19), channel_id=1, source_target_pairs={{2,0},{3,1},{0,2},{1,3},{6,4},{7,5},{4,6},{5,7},{10,8},{11,9},{8,1... | collective-permute-start | bytes 393224 | tf_op jit(solution)/shard_map/ppermute | solution.py:68
  18.7 3.6 %collective-permute-start.6 = (bf16[32,1,1,4,2,2,128]{6,0,5,4,3,2,1:T(8,128)(2,1)}, bf16[32,1,1,4,2,2,128]{6,0,5,4,3,2,1:T(8,128)(2,1)S(1)}, u32[]{:S(2)}, u32[]{:S(2)}) collective-permute-start(bf16[32,1,1,4,2,2,128]{6,0,5,4,3,2,1:T(8,128)(2,1)} %get-tuple-element.19), channel_id=1, source_target_pairs={{8,0},{16,8},{24,16},{0,24},{9,1},{17,9},{25,17},{1,25},{10,2},{18... | collective-permute-start | bytes 393224 | tf_op jit(solution)/shard_map/ppermute | solution.py:74
  23.4 1.6 %collective-permute-start.5 = (bf16[32,1,1,2,2,2,128]{6,0,5,4,3,2,1:T(8,128)(2,1)S(1)}, bf16[32,1,1,2,2,2,128]{6,0,5,4,3,2,1:T(8,128)(2,1)S(1)}, u32[]{:S(2)}, u32[]{:S(2)}) collective-permute-start(bf16[32,1,1,2,2,2,128]{6,0,5,4,3,2,1:T(8,128)(2,1)S(1)} %pad_maximum_fusion.2), channel_id=1, source_target_pairs={{4,0},{5,1},{6,2},{7,3},{0,4},{1,5},{2,6},{3,7},{12,8},{13,9},{14,... | collective-permute-start | bytes 196616 | tf_op jit(solution)/shard_map/ppermute | solution.py:68
  25.9 2.1 %collective-permute-done.5 = bf16[32,1,1,2,2,2,128]{6,0,5,4,3,2,1:T(8,128)(2,1)S(1)} collective-permute-done((bf16[32,1,1,2,2,2,128]{6,0,5,4,3,2,1:T(8,128)(2,1)S(1)}, bf16[32,1,1,2,2,2,128]{6,0,5,4,3,2,1:T(8,128)(2,1)S(1)}, u32[]{:S(2)}, u32[]{:S(2)}) %collective-permute-start.5) | collective-permute-done | bytes 65568 | tf_op jit(solution)/shard_map/ppermute | solution.py:68
  28.2 2.1 %collective-permute-done.7 = bf16[32,1,1,4,2,2,128]{6,0,5,4,3,2,1:T(8,128)(2,1)S(1)} collective-permute-done((bf16[32,1,1,4,2,2,128]{6,0,5,4,3,2,1:T(8,128)(2,1)}, bf16[32,1,1,4,2,2,128]{6,0,5,4,3,2,1:T(8,128)(2,1)S(1)}, u32[]{:S(2)}, u32[]{:S(2)}) %collective-permute-start.7) | collective-permute-done | bytes 131104 | tf_op jit(solution)/shard_map/ppermute | solution.py:75
  36.5 3.0 %collective-permute-done.9 = f32[2,32]{1,0:T(2,128)S(1)} collective-permute-done((f32[2,32]{1,0:T(2,128)S(1)}, f32[2,32]{1,0:T(2,128)S(1)}, u32[]{:S(2)}, u32[]{:S(2)}) %collective-permute-start.9) | collective-permute-done | bytes 288 | tf_op jit(solution)/shard_map/ppermute | solution.py:16
  41.2 2.0 %collective-permute-done.10 = f32[2,32]{1,0:T(2,128)S(1)} collective-permute-done((f32[2,32]{1,0:T(2,128)S(1)}, f32[2,32]{1,0:T(2,128)S(1)}, u32[]{:S(2)}, u32[]{:S(2)}) %collective-permute-start.10) | collective-permute-done | bytes 288 | tf_op jit(solution)/shard_map/ppermute | solution.py:16
  43.2 3.6 %collective-permute-done.11 = f32[2,32]{1,0:T(2,128)S(1)} collective-permute-done((f32[2,32]{1,0:T(2,128)S(1)}, f32[2,32]{1,0:T(2,128)S(1)}, u32[]{:S(2)}, u32[]{:S(2)}) %collective-permute-start.11) | collective-permute-done | bytes 288 | tf_op jit(solution)/shard_map/ppermute | solution.py:16
  46.9 4.4 %collective-permute-done.12 = f32[2,32]{1,0:T(2,128)S(1)} collective-permute-done((f32[2,32]{1,0:T(2,128)S(1)}, f32[2,32]{1,0:T(2,128)S(1)}, u32[]{:S(2)}, u32[]{:S(2)}) %collective-permute-start.12) | collective-permute-done | bytes 288 | tf_op jit(solution)/shard_map/ppermute | solution.py:16
  54.7 3.1 %collective-permute-done.14 = bf16[32,96]{1,0:T(8,128)(2,1)S(1)} collective-permute-done((bf16[32,96]{1,0:T(8,128)(2,1)S(1)}, bf16[32,96]{1,0:T(8,128)(2,1)S(1)}, u32[]{:S(2)}, u32[]{:S(2)}) %collective-permute-start.14) | collective-permute-done | bytes 6176 | tf_op jit(solution)/shard_map/ppermute | solution.py:16
  59.4 2.2 %collective-permute-done.15 = bf16[32,192]{1,0:T(8,128)(2,1)S(1)} collective-permute-done((bf16[32,192]{1,0:T(8,128)(2,1)S(1)}, bf16[32,192]{1,0:T(8,128)(2,1)S(1)}, u32[]{:S(2)}, u32[]{:S(2)}) %collective-permute-start.15) | collective-permute-done | bytes 12320 | tf_op jit(solution)/shard_map/ppermute | solution.py:16
  62.3 2.2 %bitcast_dynamic-update-slice_fusion.2 = (bf16[32,1,9,1,4,2,2,128]{7,0,6,5,4,3,2,1:T(8,128)(2,1)S(1)}, bf16[32,1,1,4,2,2,128]{6,0,5,4,3,2,1:T(8,128)(2,1)}, f32[32,1,1,4,2,2,128]{6,0,5,4,3,2,1:T(8,128)}) fusion(bf16[1,1,4,2,2,48,128]{6,5,4,3,2,1,0:T(8,128)(2,1)} %param.6, bf16[1,48,384]{2,1,0:T(8,128)(2,1)} %param.7, bf16[32,192]{1,0:T(8,128)(2,1)} %copy-done.8, ...), kind=kOutput, calls=%fused_computation.71 | convolution fusion | flops 7779839 | bytes 1044481 | tf_op jit(solution)/shard_map/tbzyxjk,nj->ntbzyxk/dot_general | solution.py:118
  72.3 1.9 %collective-permute-done.18 = bf16[32,1,1,2,2,2,128]{6,0,5,4,3,2,1:T(8,128)(2,1)S(1)} collective-permute-done((bf16[32,1,1,2,2,2,128]{6,0,5,4,3,2,1:T(8,128)(2,1)S(1)}, bf16[32,1,1,2,2,2,128]{6,0,5,4,3,2,1:T(8,128)(2,1)S(1)}, u32[]{:S(2)}, u32[]{:S(2)}) %collective-permute-start.18) | collective-permute-done | bytes 65568 | tf_op jit(solution)/shard_map/ppermute | solution.py:68
  74.4 1.8 %collective-permute-done.20 = bf16[32,1,1,4,2,2,128]{6,0,5,4,3,2,1:T(8,128)(2,1)S(1)} collective-permute-done((bf16[32,1,1,4,2,2,128]{6,0,5,4,3,2,1:T(8,128)(2,1)}, bf16[32,1,1,4,2,2,128]{6,0,5,4,3,2,1:T(8,128)(2,1)S(1)}, u32[]{:S(2)}, u32[]{:S(2)}) %collective-permute-start.20) | collective-permute-done | bytes 131104 | tf_op jit(solution)/shard_map/ppermute | solution.py:75
  84.0 2.1 %collective-permute-done.22 = f32[4,32]{1,0:T(4,128)S(1)} collective-permute-done((f32[4,32]{1,0:T(4,128)S(1)}, f32[4,32]{1,0:T(4,128)S(1)}, u32[]{:S(2)}, u32[]{:S(2)}) %collective-permute-start.22) | collective-permute-done | bytes 544 | tf_op jit(solution)/shard_map/ppermute | solution.py:16
  86.1 1.6 %collective-permute-start.23 = (f32[4,32]{1,0:T(4,128)S(1)}, f32[4,32]{1,0:T(4,128)S(1)}, u32[]{:S(2)}, u32[]{:S(2)}) collective-permute-start(f32[4,32]{1,0:T(4,128)S(1)} %fusion.100), channel_id=1, source_target_pairs={{0,4},{1,5},{2,6},{3,7},{4,0},{5,1},{6,2},{7,3},{8,12},{9,13},{10,... | collective-permute-start | bytes 1544 | tf_op jit(solution)/shard_map/ppermute | solution.py:16
  87.7 2.1 %collective-permute-done.23 = f32[4,32]{1,0:T(4,128)S(1)} collective-permute-done((f32[4,32]{1,0:T(4,128)S(1)}, f32[4,32]{1,0:T(4,128)S(1)}, u32[]{:S(2)}, u32[]{:S(2)}) %collective-permute-start.23) | collective-permute-done | bytes 544 | tf_op jit(solution)/shard_map/ppermute | solution.py:16
  89.8 3.5 %collective-permute-done.24 = f32[4,32]{1,0:T(4,128)S(1)} collective-permute-done((f32[4,32]{1,0:T(4,128)S(1)}, f32[4,32]{1,0:T(4,128)S(1)}, u32[]{:S(2)}, u32[]{:S(2)}) %collective-permute-start.24) | collective-permute-done | bytes 544 | tf_op jit(solution)/shard_map/ppermute | solution.py:16
  93.4 4.4 %collective-permute-done.25 = f32[4,32]{1,0:T(4,128)S(1)} collective-permute-done((f32[4,32]{1,0:T(4,128)S(1)}, f32[4,32]{1,0:T(4,128)S(1)}, u32[]{:S(2)}, u32[]{:S(2)}) %collective-permute-start.25) | collective-permute-done | bytes 544 | tf_op jit(solution)/shard_map/ppermute | solution.py:16
  (128 shorter events, 38.7 us)
Async XLA Ops:
  2.9 1.3 %collective-permute-start = (bf16[32,48]{1,0:T(8,128)(2,1)S(1)}, bf16[32,48]{1,0:T(8,128)(2,1)S(1)}, u32[]{:S(2)}, u32[]{:S(2)}) collective-permute-start(bf16[32,48]{1,0:T(8,128)(2,1)S(1)} %fusion.18), channel_id=1, source_target_pairs={{0,1},{1,0},{2,3},{3,2},{4,5},{5,4},{6,7},{7,6},{8,9},{9,8},{10,11... | collective-permute-start | bytes 9224 | tf_op jit(solution)/shard_map/ppermute | solution.py:16
  4.3 4.5 %collective-permute-start.1 = (bf16[32,96]{1,0:T(8,128)(2,1)S(1)}, bf16[32,96]{1,0:T(8,128)(2,1)S(1)}, u32[]{:S(2)}, u32[]{:S(2)}) collective-permute-start(bf16[32,96]{1,0:T(8,128)(2,1)S(1)} %maximum_select_fusion.8), channel_id=1, source_target_pairs={{0,2},{1,3},{2,0},{3,1},{4,6},{5,7},{6,4},{7,5},{8,10},{9,11},{10,... | collective-permute-start | bytes 18440 | tf_op jit(solution)/shard_map/ppermute | solution.py:16
  8.9 3.9 %collective-permute-start.2 = (bf16[32,192]{1,0:T(8,128)(2,1)S(1)}, bf16[32,192]{1,0:T(8,128)(2,1)}, u32[]{:S(2)}, u32[]{:S(2)}) collective-permute-start(bf16[32,192]{1,0:T(8,128)(2,1)S(1)} %maximum_select_fusion.6), channel_id=1, source_target_pairs={{0,4},{1,5},{2,6},{3,7},{4,0},{5,1},{6,2},{7,3},{8,12},{9,13},{10,... | collective-permute-start | bytes 36872 | tf_op jit(solution)/shard_map/ppermute | solution.py:16
  16.7 11.3 %collective-permute-start.4 = (bf16[32,1,1,4,2,2,128]{6,0,5,4,3,2,1:T(8,128)(2,1)}, bf16[32,1,1,4,2,2,128]{6,0,5,4,3,2,1:T(8,128)(2,1)S(1)}, u32[]{:S(2)}, u32[]{:S(2)}) collective-permute-start(bf16[32,1,1,4,2,2,128]{6,0,5,4,3,2,1:T(8,128)(2,1)} %get-tuple-element.19), channel_id=1, source_target_pairs={{2,0},{3,1},{0,2},{1,3},{6,4},{7,5},{4,6},{5,7},{10,8},{11,9},{8,1... | collective-permute-start | bytes 393224 | tf_op jit(solution)/shard_map/ppermute | solution.py:68
  18.7 9.4 %collective-permute-start.6 = (bf16[32,1,1,4,2,2,128]{6,0,5,4,3,2,1:T(8,128)(2,1)}, bf16[32,1,1,4,2,2,128]{6,0,5,4,3,2,1:T(8,128)(2,1)S(1)}, u32[]{:S(2)}, u32[]{:S(2)}) collective-permute-start(bf16[32,1,1,4,2,2,128]{6,0,5,4,3,2,1:T(8,128)(2,1)} %get-tuple-element.19), channel_id=1, source_target_pairs={{8,0},{16,8},{24,16},{0,24},{9,1},{17,9},{25,17},{1,25},{10,2},{18... | collective-permute-start | bytes 393224 | tf_op jit(solution)/shard_map/ppermute | solution.py:74
  22.4 5.6 %collective-permute-start.3 = (bf16[32,1,1,4,2,2,128]{6,0,5,4,3,2,1:T(8,128)(2,1)}, bf16[32,1,1,4,2,2,128]{6,0,5,4,3,2,1:T(8,128)(2,1)S(1)}, u32[]{:S(2)}, u32[]{:S(2)}) collective-permute-start(bf16[32,1,1,4,2,2,128]{6,0,5,4,3,2,1:T(8,128)(2,1)} %get-tuple-element.19), channel_id=1, source_target_pairs={{1,0},{0,1},{3,2},{2,3},{5,4},{4,5},{7,6},{6,7},{9,8},{8,9},{11,10... | collective-permute-start | bytes 393224 | tf_op jit(solution)/shard_map/ppermute | solution.py:68
  22.4 7.9 %collective-permute-start.7 = (bf16[32,1,1,4,2,2,128]{6,0,5,4,3,2,1:T(8,128)(2,1)}, bf16[32,1,1,4,2,2,128]{6,0,5,4,3,2,1:T(8,128)(2,1)S(1)}, u32[]{:S(2)}, u32[]{:S(2)}) collective-permute-start(bf16[32,1,1,4,2,2,128]{6,0,5,4,3,2,1:T(8,128)(2,1)} %get-tuple-element.19), channel_id=1, source_target_pairs={{24,0},{0,8},{8,16},{16,24},{25,1},{1,9},{9,17},{17,25},{26,2},{2,... | collective-permute-start | bytes 393224 | tf_op jit(solution)/shard_map/ppermute | solution.py:75
  23.4 4.5 %collective-permute-start.5 = (bf16[32,1,1,2,2,2,128]{6,0,5,4,3,2,1:T(8,128)(2,1)S(1)}, bf16[32,1,1,2,2,2,128]{6,0,5,4,3,2,1:T(8,128)(2,1)S(1)}, u32[]{:S(2)}, u32[]{:S(2)}) collective-permute-start(bf16[32,1,1,2,2,2,128]{6,0,5,4,3,2,1:T(8,128)(2,1)S(1)} %pad_maximum_fusion.2), channel_id=1, source_target_pairs={{4,0},{5,1},{6,2},{7,3},{0,4},{1,5},{2,6},{3,7},{12,8},{13,9},{14,... | collective-permute-start | bytes 196616 | tf_op jit(solution)/shard_map/ppermute | solution.py:68
  35.9 3.6 %collective-permute-start.9 = (f32[2,32]{1,0:T(2,128)S(1)}, f32[2,32]{1,0:T(2,128)S(1)}, u32[]{:S(2)}, u32[]{:S(2)}) collective-permute-start(f32[2,32]{1,0:T(2,128)S(1)} %fusion.78), channel_id=1, source_target_pairs={{0,2},{1,3},{2,0},{3,1},{4,6},{5,7},{6,4},{7,5},{8,10},{9,11},{10,... | collective-permute-start | bytes 776 | tf_op jit(solution)/shard_map/ppermute | solution.py:16
  39.6 3.6 %collective-permute-start.10 = (f32[2,32]{1,0:T(2,128)S(1)}, f32[2,32]{1,0:T(2,128)S(1)}, u32[]{:S(2)}, u32[]{:S(2)}) collective-permute-start(f32[2,32]{1,0:T(2,128)S(1)} %fusion.101), channel_id=1, source_target_pairs={{0,4},{1,5},{2,6},{3,7},{4,0},{5,1},{6,2},{7,3},{8,12},{9,13},{10,... | collective-permute-start | bytes 776 | tf_op jit(solution)/shard_map/ppermute | solution.py:16
  43.2 3.6 %collective-permute-start.11 = (f32[2,32]{1,0:T(2,128)S(1)}, f32[2,32]{1,0:T(2,128)S(1)}, u32[]{:S(2)}, u32[]{:S(2)}) collective-permute-start(f32[2,32]{1,0:T(2,128)S(1)} %add.82), channel_id=1, source_target_pairs={{0,8},{8,0},{16,24},{24,16},{1,9},{9,1},{17,25},{25,17},{2,10},{10... | collective-permute-start | bytes 776 | tf_op jit(solution)/shard_map/ppermute | solution.py:16
  46.8 4.5 %collective-permute-start.12 = (f32[2,32]{1,0:T(2,128)S(1)}, f32[2,32]{1,0:T(2,128)S(1)}, u32[]{:S(2)}, u32[]{:S(2)}) collective-permute-start(f32[2,32]{1,0:T(2,128)S(1)} %add.83), channel_id=1, source_target_pairs={{0,16},{8,24},{16,0},{24,8},{1,17},{9,25},{17,1},{25,9},{2,18},{10... | collective-permute-start | bytes 776 | tf_op jit(solution)/shard_map/ppermute | solution.py:16
  54.1 3.7 %collective-permute-start.14 = (bf16[32,96]{1,0:T(8,128)(2,1)S(1)}, bf16[32,96]{1,0:T(8,128)(2,1)S(1)}, u32[]{:S(2)}, u32[]{:S(2)}) collective-permute-start(bf16[32,96]{1,0:T(8,128)(2,1)S(1)} %maximum_select_fusion.9), channel_id=1, source_target_pairs={{0,2},{1,3},{2,0},{3,1},{4,6},{5,7},{6,4},{7,5},{8,10},{9,11},{10,... | collective-permute-start | bytes 18440 | tf_op jit(solution)/shard_map/ppermute | solution.py:16
  57.9 3.8 %collective-permute-start.15 = (bf16[32,192]{1,0:T(8,128)(2,1)S(1)}, bf16[32,192]{1,0:T(8,128)(2,1)S(1)}, u32[]{:S(2)}, u32[]{:S(2)}) collective-permute-start(bf16[32,192]{1,0:T(8,128)(2,1)S(1)} %maximum_select_fusion.7), channel_id=1, source_target_pairs={{0,4},{1,5},{2,6},{3,7},{4,0},{5,1},{6,2},{7,3},{8,12},{9,13},{10,... | collective-permute-start | bytes 36872 | tf_op jit(solution)/shard_map/ppermute | solution.py:16
  66.2 8.0 %collective-permute-start.17 = (bf16[32,1,1,4,2,2,128]{6,0,5,4,3,2,1:T(8,128)(2,1)}, bf16[32,1,1,4,2,2,128]{6,0,5,4,3,2,1:T(8,128)(2,1)S(1)}, u32[]{:S(2)}, u32[]{:S(2)}) collective-permute-start(bf16[32,1,1,4,2,2,128]{6,0,5,4,3,2,1:T(8,128)(2,1)} %get-tuple-element.14), channel_id=1, source_target_pairs={{2,0},{3,1},{0,2},{1,3},{6,4},{7,5},{4,6},{5,7},{10,8},{11,9},{8,1... | collective-permute-start | bytes 393224 | tf_op jit(solution)/shard_map/ppermute | solution.py:68
  66.8 7.6 %collective-permute-start.19 = (bf16[32,1,1,4,2,2,128]{6,0,5,4,3,2,1:T(8,128)(2,1)}, bf16[32,1,1,4,2,2,128]{6,0,5,4,3,2,1:T(8,128)(2,1)S(1)}, u32[]{:S(2)}, u32[]{:S(2)}) collective-permute-start(bf16[32,1,1,4,2,2,128]{6,0,5,4,3,2,1:T(8,128)(2,1)} %get-tuple-element.14), channel_id=1, source_target_pairs={{8,0},{16,8},{24,16},{0,24},{9,1},{17,9},{25,17},{1,25},{10,2},{18... | collective-permute-start | bytes 393224 | tf_op jit(solution)/shard_map/ppermute | solution.py:74
  68.3 5.9 %collective-permute-start.16 = (bf16[32,1,1,4,2,2,128]{6,0,5,4,3,2,1:T(8,128)(2,1)}, bf16[32,1,1,4,2,2,128]{6,0,5,4,3,2,1:T(8,128)(2,1)S(1)}, u32[]{:S(2)}, u32[]{:S(2)}) collective-permute-start(bf16[32,1,1,4,2,2,128]{6,0,5,4,3,2,1:T(8,128)(2,1)} %get-tuple-element.14), channel_id=1, source_target_pairs={{1,0},{0,1},{3,2},{2,3},{5,4},{4,5},{7,6},{6,7},{9,8},{8,9},{11,10... | collective-permute-start | bytes 393224 | tf_op jit(solution)/shard_map/ppermute | solution.py:68
  68.3 7.9 %collective-permute-start.20 = (bf16[32,1,1,4,2,2,128]{6,0,5,4,3,2,1:T(8,128)(2,1)}, bf16[32,1,1,4,2,2,128]{6,0,5,4,3,2,1:T(8,128)(2,1)S(1)}, u32[]{:S(2)}, u32[]{:S(2)}) collective-permute-start(bf16[32,1,1,4,2,2,128]{6,0,5,4,3,2,1:T(8,128)(2,1)} %get-tuple-element.14), channel_id=1, source_target_pairs={{24,0},{0,8},{8,16},{16,24},{25,1},{1,9},{9,17},{17,25},{26,2},{2,... | collective-permute-start | bytes 393224 | tf_op jit(solution)/shard_map/ppermute | solution.py:75
  69.8 4.3 %collective-permute-start.18 = (bf16[32,1,1,2,2,2,128]{6,0,5,4,3,2,1:T(8,128)(2,1)S(1)}, bf16[32,1,1,2,2,2,128]{6,0,5,4,3,2,1:T(8,128)(2,1)S(1)}, u32[]{:S(2)}, u32[]{:S(2)}) collective-permute-start(bf16[32,1,1,2,2,2,128]{6,0,5,4,3,2,1:T(8,128)(2,1)S(1)} %pad_maximum_fusion.3), channel_id=1, source_target_pairs={{4,0},{5,1},{6,2},{7,3},{0,4},{1,5},{2,6},{3,7},{12,8},{13,9},{14,... | collective-permute-start | bytes 196616 | tf_op jit(solution)/shard_map/ppermute | solution.py:68
  81.2 1.2 %collective-permute-start.21 = (f32[4,32]{1,0:T(4,128)S(1)}, f32[4,32]{1,0:T(4,128)S(1)}, u32[]{:S(2)}, u32[]{:S(2)}) collective-permute-start(f32[4,32]{1,0:T(4,128)S(1)} %pad_maximum_fusion.4), channel_id=1, source_target_pairs={{0,1},{1,0},{2,3},{3,2},{4,5},{5,4},{6,7},{7,6},{8,9},{9,8},{10,11... | collective-permute-start | bytes 1544 | tf_op jit(solution)/shard_map/ppermute | solution.py:16
  82.5 3.7 %collective-permute-start.22 = (f32[4,32]{1,0:T(4,128)S(1)}, f32[4,32]{1,0:T(4,128)S(1)}, u32[]{:S(2)}, u32[]{:S(2)}) collective-permute-start(f32[4,32]{1,0:T(4,128)S(1)} %fusion.79), channel_id=1, source_target_pairs={{0,2},{1,3},{2,0},{3,1},{4,6},{5,7},{6,4},{7,5},{8,10},{9,11},{10,... | collective-permute-start | bytes 1544 | tf_op jit(solution)/shard_map/ppermute | solution.py:16
  86.1 3.7 %collective-permute-start.23 = (f32[4,32]{1,0:T(4,128)S(1)}, f32[4,32]{1,0:T(4,128)S(1)}, u32[]{:S(2)}, u32[]{:S(2)}) collective-permute-start(f32[4,32]{1,0:T(4,128)S(1)} %fusion.100), channel_id=1, source_target_pairs={{0,4},{1,5},{2,6},{3,7},{4,0},{5,1},{6,2},{7,3},{8,12},{9,13},{10,... | collective-permute-start | bytes 1544 | tf_op jit(solution)/shard_map/ppermute | solution.py:16
  89.8 3.6 %collective-permute-start.24 = (f32[4,32]{1,0:T(4,128)S(1)}, f32[4,32]{1,0:T(4,128)S(1)}, u32[]{:S(2)}, u32[]{:S(2)}) collective-permute-start(f32[4,32]{1,0:T(4,128)S(1)} %add.89), channel_id=1, source_target_pairs={{0,8},{8,0},{16,24},{24,16},{1,9},{9,1},{17,25},{25,17},{2,10},{10... | collective-permute-start | bytes 1544 | tf_op jit(solution)/shard_map/ppermute | solution.py:16
  93.4 4.5 %collective-permute-start.25 = (f32[4,32]{1,0:T(4,128)S(1)}, f32[4,32]{1,0:T(4,128)S(1)}, u32[]{:S(2)}, u32[]{:S(2)}) collective-permute-start(f32[4,32]{1,0:T(4,128)S(1)} %add.90), channel_id=1, source_target_pairs={{0,16},{8,24},{16,0},{24,8},{1,17},{9,25},{17,1},{25,9},{2,18},{10... | collective-permute-start | bytes 1544 | tf_op jit(solution)/shard_map/ppermute | solution.py:16
  (15 other events, 166.2 us)

commit v3 on v2

--- a/solution.py
+++ b/solution.py
@@ -16,8 +16,18 @@
     return lax.ppermute(x, axis, [(i, i ^ bit) for i in range(count)])
 
 
+def shifted(x, axis, shift):
+    count = lax.axis_size(axis)
+    return lax.ppermute(x, axis, [(i, (i + shift) % count) for i in range(count)])
+
+
 def axis_sum(x, axis):
     count = lax.axis_size(axis)
+    if count <= 8:
+        received = [shifted(x, axis, shift) for shift in range(1, count)]
+        for part in received:
+            x = x + part
+        return x
     if not is_power_of_two(count):
         return lax.psum(x, axis)
     bit = 1
@@ -109,8 +119,18 @@
         "tbzyxjk,ntbzyxk->nj", null_vectors, lowered, preferred_element_type=jnp.float32
     ).astype(jnp.bfloat16)
     inverse_rows = coarse_inverse[0]
+    count = lax.axis_size("xyz")
+    if count <= 8:
+        width = coarse.shape[1]
+        me = lax.axis_index("xyz")
+        blocks = [coarse] + [shifted(coarse, "xyz", -shift) for shift in range(1, count)]
+        gathered = jnp.concatenate(blocks, 1)
+        doubled = jnp.concatenate([inverse_rows, inverse_rows], 1)
+        inverse_rows = lax.dynamic_slice_in_dim(doubled, me * width, count * width, axis=1)
+    else:
+        gathered = gather_tiled(coarse, "xyz", 1)
     correction = lax.dot_general(
-        gather_tiled(coarse, "xyz", 1),
+        gathered,
         inverse_rows,
         (((1,), (1,)), ((), ())),
         preferred_element_type=jnp.float32,

time: 101 us -> 104 us (1.030)
  starting transfers between devices: 24.7 us -> 48.1 us
  waiting for transfers between devices: 46.1 us -> 26.1 us
    ppermute x16 -> x34, starting transfers between devices: 13.2 us -> 36.2 us  [shifted(): lax.ppermute(x, axis, [(i, (i + shift) % count) for i in range(count)])]
    ppermute x16 -> x34, waiting for transfers between devices: 38.2 us -> 19.3 us  [shifted(): lax.ppermute(x, axis, [(i, (i + shift) % count) for i in range(count)])]
    ppermute x2, starting transfers between devices: 5.12 us -> 3.63 us  [both_sides(): from_upper = lax.ppermute(first, axis, up)]
    concatenate x0 -> x2, local copies, waits for them, and re-layouts: none -> 1.4 us  [precondition(): gathered = jnp.concatenate(blocks, 1)]
    ppermute x2, starting transfers between devices: 0.51 us -> 1.75 us  [both_sides(): from_lower = lax.ppermute(last, axis, down)]
    ppermute x2, waiting for transfers between devices: 3.9 us -> 2.74 us  [both_sides(): from_lower = lax.ppermute(last, axis, down)]
    unnamed x30 -> x20, local copies, waits for them, and re-layouts: 4.87 us -> 3.71 us
  transfers between devices with their start and end apart: 26 -> 44, of which waited for: 20 -> 16; matrix products, arithmetic and copies ran while one was open for 4% -> 4% of each run, Pallas kernels for 0% -> 0%
where the time goes in v3:
time: 104 us; the launch traced here: 103 us
  starting transfers between devices  48.1 us (46%)
  waiting for transfers between devices  26.1 us (25%)
  local copies, waits for them, and re-layouts  13.8 us (13%)
  matrix products  7.44 us (7%)
  other arithmetic  6.75 us (6%)
  between operations  1.15 us (1%)
    ppermute x34, starting transfers between devices, shifted(): lax.ppermute(x, axis, [(i, (i + shift) % count) for i in range(count)])  36.2 us
    ppermute x34, waiting for transfers between devices, shifted(): lax.ppermute(x, axis, [(i, (i + shift) % count) for i in range(count)])  19.3 us
    ppermute x6, starting transfers between devices, both_sides(): pair = lax.ppermute(jnp.concatenate([first, last], which), axis, perm)  6.53 us
    slice x6, local copies, waits for them, and re-layouts, both_sides(): first = lax.slice_in_dim(lowered, 0, 1, axis=which)  5.08 us
    dot_general x2, matrix products, precondition(): jnp.einsum('tbzyxjk,nj->ntbzyxk', null_vectors, correction, preferred_ele...  4.49 us
    ppermute x6, waiting for transfers between devices, both_sides(): pair = lax.ppermute(jnp.concatenate([first, last], which), axis, perm)  3.97 us
    unnamed x20, local copies, waits for them, and re-layouts  3.71 us
    ppermute x2, starting transfers between devices, both_sides(): from_upper = lax.ppermute(first, axis, up)  3.63 us
  transfers between devices with their start and end apart: 44, of which 16 were waited for; matrix products, arithmetic and copies ran while one was open for 4% of the time, Pallas kernels for 0%

profile of v3, /device:TPU:0, one launch (start us, length us, event | category | flops | bytes accessed | tf_op | source)
XLA Modules:
  0.0 103.2 jit_solution(13059361110834527730)
XLA Ops:
  3.4 2.5 %collective-permute-start.5 = (bf16[32,48]{1,0:T(8,128)(2,1)S(1)}, bf16[32,48]{1,0:T(8,128)(2,1)S(1)}, u32[]{:S(2)}, u32[]{:S(2)}) collective-permute-start(bf16[32,48]{1,0:T(8,128)(2,1)S(1)} %fusion.18), channel_id=1, source_target_pairs={{0,2},{1,3},{2,4},{3,5},{4,6},{5,7},{6,0},{7,1},{8,10},{9,11},{10,... | collective-permute-start | bytes 9224 | tf_op jit(solution)/shard_map/ppermute | solution.py:21
  6.0 2.4 %collective-permute-start.4 = (bf16[32,48]{1,0:T(8,128)(2,1)S(1)}, bf16[32,48]{1,0:T(8,128)(2,1)S(1)}, u32[]{:S(2)}, u32[]{:S(2)}) collective-permute-start(bf16[32,48]{1,0:T(8,128)(2,1)S(1)} %fusion.18), channel_id=1, source_target_pairs={{0,3},{1,4},{2,5},{3,6},{4,7},{5,0},{6,1},{7,2},{8,11},{9,12},{10,... | collective-permute-start | bytes 9224 | tf_op jit(solution)/shard_map/ppermute | solution.py:21
  10.4 2.3 %collective-permute-start = (bf16[32,48]{1,0:T(8,128)(2,1)S(1)}, bf16[32,48]{1,0:T(8,128)(2,1)S(1)}, u32[]{:S(2)}, u32[]{:S(2)}) collective-permute-start(bf16[32,48]{1,0:T(8,128)(2,1)S(1)} %fusion.18), channel_id=1, source_target_pairs={{0,7},{1,0},{2,1},{3,2},{4,3},{5,4},{6,5},{7,6},{8,15},{9,8},{10,9... | collective-permute-start | bytes 9224 | tf_op jit(solution)/shard_map/ppermute | solution.py:21
  14.8 2.2 %bitcast_dynamic-update-slice_fusion.5 = (bf16[32,1,9,1,4,2,2,128]{7,0,6,5,4,3,2,1:T(8,128)(2,1)S(1)}, bf16[32,1,1,4,2,2,128]{6,0,5,4,3,2,1:T(8,128)(2,1)}, f32[32,1,1,4,2,2,128]{6,0,5,4,3,2,1:T(8,128)}) fusion(bf16[1,1,4,2,2,48,128]{6,5,4,3,2,1,0:T(8,128)(2,1)} %param.6, bf16[32,384]{1,0:T(8,128)(2,1)} %concatenate.138, s32[]{:T(128)S(6)} %select_n.4, ...), kind=kOutput, calls=%fused_computation.74 | convolution fusion | flops 7742975 | bytes 1044484 | tf_op jit(solution)/shard_map/tbzyxjk,nj->ntbzyxk/dot_general | solution.py:138
  19.6 3.6 %collective-permute-start.10 = (bf16[32,1,1,4,2,2,128]{6,0,5,4,3,2,1:T(8,128)(2,1)}, bf16[32,1,1,4,2,2,128]{6,0,5,4,3,2,1:T(8,128)(2,1)S(1)}, u32[]{:S(2)}, u32[]{:S(2)}) collective-permute-start(bf16[32,1,1,4,2,2,128]{6,0,5,4,3,2,1:T(8,128)(2,1)} %get-tuple-element.19), channel_id=1, source_target_pairs={{8,0},{16,8},{24,16},{0,24},{9,1},{17,9},{25,17},{1,25},{10,2},{18... | collective-permute-start | bytes 393224 | tf_op jit(solution)/shard_map/ppermute | solution.py:84
  24.8 1.6 %collective-permute-start.9 = (bf16[32,1,1,2,2,2,128]{6,0,5,4,3,2,1:T(8,128)(2,1)S(1)}, bf16[32,1,1,2,2,2,128]{6,0,5,4,3,2,1:T(8,128)(2,1)S(1)}, u32[]{:S(2)}, u32[]{:S(2)}) collective-permute-start(bf16[32,1,1,2,2,2,128]{6,0,5,4,3,2,1:T(8,128)(2,1)S(1)} %pad_maximum_fusion.2), channel_id=1, source_target_pairs={{4,0},{5,1},{6,2},{7,3},{0,4},{1,5},{2,6},{3,7},{12,8},{13,9},{14,... | collective-permute-start | bytes 196616 | tf_op jit(solution)/shard_map/ppermute | solution.py:78
  27.3 1.9 %collective-permute-done.9 = bf16[32,1,1,2,2,2,128]{6,0,5,4,3,2,1:T(8,128)(2,1)S(1)} collective-permute-done((bf16[32,1,1,2,2,2,128]{6,0,5,4,3,2,1:T(8,128)(2,1)S(1)}, bf16[32,1,1,2,2,2,128]{6,0,5,4,3,2,1:T(8,128)(2,1)S(1)}, u32[]{:S(2)}, u32[]{:S(2)}) %collective-permute-start.9) | collective-permute-done | bytes 65568 | tf_op jit(solution)/shard_map/ppermute | solution.py:78
  29.4 1.8 %collective-permute-done.11 = bf16[32,1,1,4,2,2,128]{6,0,5,4,3,2,1:T(8,128)(2,1)S(1)} collective-permute-done((bf16[32,1,1,4,2,2,128]{6,0,5,4,3,2,1:T(8,128)(2,1)}, bf16[32,1,1,4,2,2,128]{6,0,5,4,3,2,1:T(8,128)(2,1)S(1)}, u32[]{:S(2)}, u32[]{:S(2)}) %collective-permute-start.11) | collective-permute-done | bytes 131104 | tf_op jit(solution)/shard_map/ppermute | solution.py:85
  38.3 1.5 %collective-permute-start.14 = (f32[2,32]{1,0:T(2,128)S(1)}, f32[2,32]{1,0:T(2,128)S(1)}, u32[]{:S(2)}, u32[]{:S(2)}) collective-permute-start(f32[2,32]{1,0:T(2,128)S(1)} %pad_maximum_fusion.5), channel_id=1, source_target_pairs={{0,3},{1,4},{2,5},{3,6},{4,7},{5,0},{6,1},{7,2},{8,11},{9,12},{10,... | collective-permute-start | bytes 776 | tf_op jit(solution)/shard_map/ppermute | solution.py:21
  39.7 1.9 %collective-permute-start.13 = (f32[2,32]{1,0:T(2,128)S(1)}, f32[2,32]{1,0:T(2,128)S(1)}, u32[]{:S(2)}, u32[]{:S(2)}) collective-permute-start(f32[2,32]{1,0:T(2,128)S(1)} %pad_maximum_fusion.5), channel_id=1, source_target_pairs={{0,2},{1,3},{2,4},{3,5},{4,6},{5,7},{6,0},{7,1},{8,10},{9,11},{10,... | collective-permute-start | bytes 776 | tf_op jit(solution)/shard_map/ppermute | solution.py:21
  42.2 2.1 %collective-permute-done.13 = f32[2,32]{1,0:T(2,128)S(1)} collective-permute-done((f32[2,32]{1,0:T(2,128)S(1)}, f32[2,32]{1,0:T(2,128)S(1)}, u32[]{:S(2)}, u32[]{:S(2)}) %collective-permute-start.13) | collective-permute-done | bytes 288 | tf_op jit(solution)/shard_map/ppermute | solution.py:21
  45.6 2.1 %collective-permute-start.21 = (f32[2,32]{1,0:T(2,128)S(1)}, f32[2,32]{1,0:T(2,128)S(1)}, u32[]{:S(2)}, u32[]{:S(2)}) collective-permute-start(f32[2,32]{1,0:T(2,128)S(1)} %add_add_fusion.3), channel_id=1, source_target_pairs={{0,24},{8,0},{16,8},{24,16},{1,25},{9,1},{17,9},{25,17},{2,26},{10... | collective-permute-start | bytes 776 | tf_op jit(solution)/shard_map/ppermute | solution.py:21
  49.2 2.9 %collective-permute-done.20 = f32[2,32]{1,0:T(2,128)S(1)} collective-permute-done((f32[2,32]{1,0:T(2,128)S(1)}, f32[2,32]{1,0:T(2,128)S(1)}, u32[]{:S(2)}, u32[]{:S(2)}) %collective-permute-start.20) | collective-permute-done | bytes 288 | tf_op jit(solution)/shard_map/ppermute | solution.py:21
  54.6 2.4 %collective-permute-start.26 = (bf16[32,48]{1,0:T(8,128)(2,1)S(1)}, bf16[32,48]{1,0:T(8,128)(2,1)S(1)}, u32[]{:S(2)}, u32[]{:S(2)}) collective-permute-start(bf16[32,48]{1,0:T(8,128)(2,1)S(1)} %fusion.19), channel_id=1, source_target_pairs={{0,3},{1,4},{2,5},{3,6},{4,7},{5,0},{6,1},{7,2},{8,11},{9,12},{10,... | collective-permute-start | bytes 9224 | tf_op jit(solution)/shard_map/ppermute | solution.py:21
  58.5 1.9 %collective-permute-start.23 = (bf16[32,48]{1,0:T(8,128)(2,1)S(1)}, bf16[32,48]{1,0:T(8,128)(2,1)S(1)}, u32[]{:S(2)}, u32[]{:S(2)}) collective-permute-start(bf16[32,48]{1,0:T(8,128)(2,1)S(1)} %fusion.19), channel_id=1, source_target_pairs={{0,6},{1,7},{2,0},{3,1},{4,2},{5,3},{6,4},{7,5},{8,14},{9,15},{10,... | collective-permute-start | bytes 9224 | tf_op jit(solution)/shard_map/ppermute | solution.py:21
  60.4 2.2 %collective-permute-start.22 = (bf16[32,48]{1,0:T(8,128)(2,1)S(1)}, bf16[32,48]{1,0:T(8,128)(2,1)S(1)}, u32[]{:S(2)}, u32[]{:S(2)}) collective-permute-start(bf16[32,48]{1,0:T(8,128)(2,1)S(1)} %fusion.19), channel_id=1, source_target_pairs={{0,7},{1,0},{2,1},{3,2},{4,3},{5,4},{6,5},{7,6},{8,15},{9,8},{10,9... | collective-permute-start | bytes 9224 | tf_op jit(solution)/shard_map/ppermute | solution.py:21
  64.6 2.3 %bitcast_dynamic-update-slice_fusion.2 = (bf16[32,1,9,1,4,2,2,128]{7,0,6,5,4,3,2,1:T(8,128)(2,1)S(1)}, bf16[32,1,1,4,2,2,128]{6,0,5,4,3,2,1:T(8,128)(2,1)}, f32[32,1,1,4,2,2,128]{6,0,5,4,3,2,1:T(8,128)}) fusion(bf16[1,1,4,2,2,48,128]{6,5,4,3,2,1,0:T(8,128)(2,1)} %param.6, bf16[32,384]{1,0:T(8,128)(2,1)} %concatenate.152, s32[]{:T(128)S(6)} %select_n.4, ...), kind=kOutput, calls=%fused_computation.71 | convolution fusion | flops 7742975 | bytes 1044484 | tf_op jit(solution)/shard_map/tbzyxjk,nj->ntbzyxk/dot_general | solution.py:138
  70.6 1.7 %collective-permute-start.33 = (bf16[32,1,1,4,2,2,128]{6,0,5,4,3,2,1:T(8,128)(2,1)}, bf16[32,1,1,4,2,2,128]{6,0,5,4,3,2,1:T(8,128)(2,1)S(1)}, u32[]{:S(2)}, u32[]{:S(2)}) collective-permute-start(bf16[32,1,1,4,2,2,128]{6,0,5,4,3,2,1:T(8,128)(2,1)} %get-tuple-element.14), channel_id=1, source_target_pairs={{24,0},{0,8},{8,16},{16,24},{25,1},{1,9},{9,17},{17,25},{26,2},{2,... | collective-permute-start | bytes 393224 | tf_op jit(solution)/shard_map/ppermute | solution.py:85
  75.6 2.1 %collective-permute-done.31 = bf16[32,1,1,2,2,2,128]{6,0,5,4,3,2,1:T(8,128)(2,1)S(1)} collective-permute-done((bf16[32,1,1,2,2,2,128]{6,0,5,4,3,2,1:T(8,128)(2,1)S(1)}, bf16[32,1,1,2,2,2,128]{6,0,5,4,3,2,1:T(8,128)(2,1)S(1)}, u32[]{:S(2)}, u32[]{:S(2)}) %collective-permute-start.31) | collective-permute-done | bytes 65568 | tf_op jit(solution)/shard_map/ppermute | solution.py:78
  87.5 1.7 %collective-permute-start.35 = (f32[4,32]{1,0:T(4,128)S(1)}, f32[4,32]{1,0:T(4,128)S(1)}, u32[]{:S(2)}, u32[]{:S(2)}) collective-permute-start(f32[4,32]{1,0:T(4,128)S(1)} %pad_maximum_fusion.4), channel_id=1, source_target_pairs={{0,2},{1,3},{2,4},{3,5},{4,6},{5,7},{6,0},{7,1},{8,10},{9,11},{10,... | collective-permute-start | bytes 1544 | tf_op jit(solution)/shard_map/ppermute | solution.py:21
  89.7 2.3 %collective-permute-done.35 = f32[4,32]{1,0:T(4,128)S(1)} collective-permute-done((f32[4,32]{1,0:T(4,128)S(1)}, f32[4,32]{1,0:T(4,128)S(1)}, u32[]{:S(2)}, u32[]{:S(2)}) %collective-permute-start.35) | collective-permute-done | bytes 544 | tf_op jit(solution)/shard_map/ppermute | solution.py:21
  92.0 1.5 %collective-permute-done.34 = f32[4,32]{1,0:T(4,128)S(1)} collective-permute-done((f32[4,32]{1,0:T(4,128)S(1)}, f32[4,32]{1,0:T(4,128)S(1)}, u32[]{:S(2)}, u32[]{:S(2)}) %collective-permute-start.34) | collective-permute-done | bytes 544 | tf_op jit(solution)/shard_map/ppermute | solution.py:21
  93.5 2.2 %collective-permute-start.43 = (f32[4,32]{1,0:T(4,128)S(1)}, f32[4,32]{1,0:T(4,128)S(1)}, u32[]{:S(2)}, u32[]{:S(2)}) collective-permute-start(f32[4,32]{1,0:T(4,128)S(1)} %add_add_fusion.1), channel_id=1, source_target_pairs={{0,24},{8,0},{16,8},{24,16},{1,25},{9,1},{17,9},{25,17},{2,26},{10... | collective-permute-start | bytes 1544 | tf_op jit(solution)/shard_map/ppermute | solution.py:21
  97.2 3.1 %collective-permute-done.42 = f32[4,32]{1,0:T(4,128)S(1)} collective-permute-done((f32[4,32]{1,0:T(4,128)S(1)}, f32[4,32]{1,0:T(4,128)S(1)}, u32[]{:S(2)}, u32[]{:S(2)}) %collective-permute-start.42) | collective-permute-done | bytes 544 | tf_op jit(solution)/shard_map/ppermute | solution.py:21
  (146 shorter events, 50.0 us)
Async XLA Ops:
  2.9 6.0 %collective-permute-start.6 = (bf16[32,48]{1,0:T(8,128)(2,1)S(1)}, bf16[32,48]{1,0:T(8,128)(2,1)S(1)}, u32[]{:S(2)}, u32[]{:S(2)}) collective-permute-start(bf16[32,48]{1,0:T(8,128)(2,1)S(1)} %fusion.18), channel_id=1, source_target_pairs={{0,1},{1,2},{2,3},{3,4},{4,5},{5,6},{6,7},{7,0},{8,9},{9,10},{10,1... | collective-permute-start | bytes 9224 | tf_op jit(solution)/shard_map/ppermute | solution.py:21
  3.4 7.0 %collective-permute-start.5 = (bf16[32,48]{1,0:T(8,128)(2,1)S(1)}, bf16[32,48]{1,0:T(8,128)(2,1)S(1)}, u32[]{:S(2)}, u32[]{:S(2)}) collective-permute-start(bf16[32,48]{1,0:T(8,128)(2,1)S(1)} %fusion.18), channel_id=1, source_target_pairs={{0,2},{1,3},{2,4},{3,5},{4,6},{5,7},{6,0},{7,1},{8,10},{9,11},{10,... | collective-permute-start | bytes 9224 | tf_op jit(solution)/shard_map/ppermute | solution.py:21
  6.0 6.7 %collective-permute-start.4 = (bf16[32,48]{1,0:T(8,128)(2,1)S(1)}, bf16[32,48]{1,0:T(8,128)(2,1)S(1)}, u32[]{:S(2)}, u32[]{:S(2)}) collective-permute-start(bf16[32,48]{1,0:T(8,128)(2,1)S(1)} %fusion.18), channel_id=1, source_target_pairs={{0,3},{1,4},{2,5},{3,6},{4,7},{5,0},{6,1},{7,2},{8,11},{9,12},{10,... | collective-permute-start | bytes 9224 | tf_op jit(solution)/shard_map/ppermute | solution.py:21
  18.7 10.6 %collective-permute-start.8 = (bf16[32,1,1,4,2,2,128]{6,0,5,4,3,2,1:T(8,128)(2,1)}, bf16[32,1,1,4,2,2,128]{6,0,5,4,3,2,1:T(8,128)(2,1)S(1)}, u32[]{:S(2)}, u32[]{:S(2)}) collective-permute-start(bf16[32,1,1,4,2,2,128]{6,0,5,4,3,2,1:T(8,128)(2,1)} %get-tuple-element.19), channel_id=1, source_target_pairs={{2,0},{3,1},{0,2},{1,3},{6,4},{7,5},{4,6},{5,7},{10,8},{11,9},{8,1... | collective-permute-start | bytes 393224 | tf_op jit(solution)/shard_map/ppermute | solution.py:78
  19.6 9.8 %collective-permute-start.10 = (bf16[32,1,1,4,2,2,128]{6,0,5,4,3,2,1:T(8,128)(2,1)}, bf16[32,1,1,4,2,2,128]{6,0,5,4,3,2,1:T(8,128)(2,1)S(1)}, u32[]{:S(2)}, u32[]{:S(2)}) collective-permute-start(bf16[32,1,1,4,2,2,128]{6,0,5,4,3,2,1:T(8,128)(2,1)} %get-tuple-element.19), channel_id=1, source_target_pairs={{8,0},{16,8},{24,16},{0,24},{9,1},{17,9},{25,17},{1,25},{10,2},{18... | collective-permute-start | bytes 393224 | tf_op jit(solution)/shard_map/ppermute | solution.py:84
  23.2 6.0 %collective-permute-start.7 = (bf16[32,1,1,4,2,2,128]{6,0,5,4,3,2,1:T(8,128)(2,1)}, bf16[32,1,1,4,2,2,128]{6,0,5,4,3,2,1:T(8,128)(2,1)S(1)}, u32[]{:S(2)}, u32[]{:S(2)}) collective-permute-start(bf16[32,1,1,4,2,2,128]{6,0,5,4,3,2,1:T(8,128)(2,1)} %get-tuple-element.19), channel_id=1, source_target_pairs={{1,0},{0,1},{3,2},{2,3},{5,4},{4,5},{7,6},{6,7},{9,8},{8,9},{11,10... | collective-permute-start | bytes 393224 | tf_op jit(solution)/shard_map/ppermute | solution.py:78
  23.8 7.4 %collective-permute-start.11 = (bf16[32,1,1,4,2,2,128]{6,0,5,4,3,2,1:T(8,128)(2,1)}, bf16[32,1,1,4,2,2,128]{6,0,5,4,3,2,1:T(8,128)(2,1)S(1)}, u32[]{:S(2)}, u32[]{:S(2)}) collective-permute-start(bf16[32,1,1,4,2,2,128]{6,0,5,4,3,2,1:T(8,128)(2,1)} %get-tuple-element.19), channel_id=1, source_target_pairs={{24,0},{0,8},{8,16},{16,24},{25,1},{1,9},{9,17},{17,25},{26,2},{2,... | collective-permute-start | bytes 393224 | tf_op jit(solution)/shard_map/ppermute | solution.py:85
  35.7 6.0 %collective-permute-start.17 = (f32[2,32]{1,0:T(2,128)S(1)}, f32[2,32]{1,0:T(2,128)S(1)}, u32[]{:S(2)}, u32[]{:S(2)}) collective-permute-start(f32[2,32]{1,0:T(2,128)S(1)} %pad_maximum_fusion.5), channel_id=1, source_target_pairs={{0,6},{1,7},{2,0},{3,1},{4,2},{5,3},{6,4},{7,5},{8,14},{9,15},{10,... | collective-permute-start | bytes 776 | tf_op jit(solution)/shard_map/ppermute | solution.py:21
  37.0 4.6 %collective-permute-start.16 = (f32[2,32]{1,0:T(2,128)S(1)}, f32[2,32]{1,0:T(2,128)S(1)}, u32[]{:S(2)}, u32[]{:S(2)}) collective-permute-start(f32[2,32]{1,0:T(2,128)S(1)} %pad_maximum_fusion.5), channel_id=1, source_target_pairs={{0,5},{1,6},{2,7},{3,0},{4,1},{5,2},{6,3},{7,4},{8,13},{9,14},{10,... | collective-permute-start | bytes 776 | tf_op jit(solution)/shard_map/ppermute | solution.py:21
  37.3 4.9 %collective-permute-start.15 = (f32[2,32]{1,0:T(2,128)S(1)}, f32[2,32]{1,0:T(2,128)S(1)}, u32[]{:S(2)}, u32[]{:S(2)}) collective-permute-start(f32[2,32]{1,0:T(2,128)S(1)} %pad_maximum_fusion.5), channel_id=1, source_target_pairs={{0,4},{1,5},{2,6},{3,7},{4,0},{5,1},{6,2},{7,3},{8,12},{9,13},{10,... | collective-permute-start | bytes 776 | tf_op jit(solution)/shard_map/ppermute | solution.py:21
  48.1 5.4 %collective-permute-start.19 = (f32[2,32]{1,0:T(2,128)S(1)}, f32[2,32]{1,0:T(2,128)S(1)}, u32[]{:S(2)}, u32[]{:S(2)}) collective-permute-start(f32[2,32]{1,0:T(2,128)S(1)} %add_add_fusion.3), channel_id=1, source_target_pairs={{0,8},{8,16},{16,24},{24,0},{1,9},{9,17},{17,25},{25,1},{2,10},{10... | collective-permute-start | bytes 776 | tf_op jit(solution)/shard_map/ppermute | solution.py:21
  54.5 5.9 %collective-permute-start.27 = (bf16[32,48]{1,0:T(8,128)(2,1)S(1)}, bf16[32,48]{1,0:T(8,128)(2,1)S(1)}, u32[]{:S(2)}, u32[]{:S(2)}) collective-permute-start(bf16[32,48]{1,0:T(8,128)(2,1)S(1)} %fusion.19), channel_id=1, source_target_pairs={{0,2},{1,3},{2,4},{3,5},{4,6},{5,7},{6,0},{7,1},{8,10},{9,11},{10,... | collective-permute-start | bytes 9224 | tf_op jit(solution)/shard_map/ppermute | solution.py:21
  54.6 8.0 %collective-permute-start.26 = (bf16[32,48]{1,0:T(8,128)(2,1)S(1)}, bf16[32,48]{1,0:T(8,128)(2,1)S(1)}, u32[]{:S(2)}, u32[]{:S(2)}) collective-permute-start(bf16[32,48]{1,0:T(8,128)(2,1)S(1)} %fusion.19), channel_id=1, source_target_pairs={{0,3},{1,4},{2,5},{3,6},{4,7},{5,0},{6,1},{7,2},{8,11},{9,12},{10,... | collective-permute-start | bytes 9224 | tf_op jit(solution)/shard_map/ppermute | solution.py:21
  57.0 5.6 %collective-permute-start.25 = (bf16[32,48]{1,0:T(8,128)(2,1)S(1)}, bf16[32,48]{1,0:T(8,128)(2,1)S(1)}, u32[]{:S(2)}, u32[]{:S(2)}) collective-permute-start(bf16[32,48]{1,0:T(8,128)(2,1)S(1)} %fusion.19), channel_id=1, source_target_pairs={{0,4},{1,5},{2,6},{3,7},{4,0},{5,1},{6,2},{7,3},{8,12},{9,13},{10,... | collective-permute-start | bytes 9224 | tf_op jit(solution)/shard_map/ppermute | solution.py:21
  57.8 4.8 %collective-permute-start.24 = (bf16[32,48]{1,0:T(8,128)(2,1)S(1)}, bf16[32,48]{1,0:T(8,128)(2,1)S(1)}, u32[]{:S(2)}, u32[]{:S(2)}) collective-permute-start(bf16[32,48]{1,0:T(8,128)(2,1)S(1)} %fusion.19), channel_id=1, source_target_pairs={{0,5},{1,6},{2,7},{3,0},{4,1},{5,2},{6,3},{7,4},{8,13},{9,14},{10,... | collective-permute-start | bytes 9224 | tf_op jit(solution)/shard_map/ppermute | solution.py:21
  68.6 9.2 %collective-permute-start.30 = (bf16[32,1,1,4,2,2,128]{6,0,5,4,3,2,1:T(8,128)(2,1)}, bf16[32,1,1,4,2,2,128]{6,0,5,4,3,2,1:T(8,128)(2,1)S(1)}, u32[]{:S(2)}, u32[]{:S(2)}) collective-permute-start(bf16[32,1,1,4,2,2,128]{6,0,5,4,3,2,1:T(8,128)(2,1)} %get-tuple-element.14), channel_id=1, source_target_pairs={{2,0},{3,1},{0,2},{1,3},{6,4},{7,5},{4,6},{5,7},{10,8},{11,9},{8,1... | collective-permute-start | bytes 393224 | tf_op jit(solution)/shard_map/ppermute | solution.py:78
  69.5 8.5 %collective-permute-start.32 = (bf16[32,1,1,4,2,2,128]{6,0,5,4,3,2,1:T(8,128)(2,1)}, bf16[32,1,1,4,2,2,128]{6,0,5,4,3,2,1:T(8,128)(2,1)S(1)}, u32[]{:S(2)}, u32[]{:S(2)}) collective-permute-start(bf16[32,1,1,4,2,2,128]{6,0,5,4,3,2,1:T(8,128)(2,1)} %get-tuple-element.14), channel_id=1, source_target_pairs={{8,0},{16,8},{24,16},{0,24},{9,1},{17,9},{25,17},{1,25},{10,2},{18... | collective-permute-start | bytes 393224 | tf_op jit(solution)/shard_map/ppermute | solution.py:84
  69.5 8.2 %collective-permute-start.29 = (bf16[32,1,1,4,2,2,128]{6,0,5,4,3,2,1:T(8,128)(2,1)}, bf16[32,1,1,4,2,2,128]{6,0,5,4,3,2,1:T(8,128)(2,1)S(1)}, u32[]{:S(2)}, u32[]{:S(2)}) collective-permute-start(bf16[32,1,1,4,2,2,128]{6,0,5,4,3,2,1:T(8,128)(2,1)} %get-tuple-element.14), channel_id=1, source_target_pairs={{1,0},{0,1},{3,2},{2,3},{5,4},{4,5},{7,6},{6,7},{9,8},{8,9},{11,10... | collective-permute-start | bytes 393224 | tf_op jit(solution)/shard_map/ppermute | solution.py:78
  70.6 8.3 %collective-permute-start.33 = (bf16[32,1,1,4,2,2,128]{6,0,5,4,3,2,1:T(8,128)(2,1)}, bf16[32,1,1,4,2,2,128]{6,0,5,4,3,2,1:T(8,128)(2,1)S(1)}, u32[]{:S(2)}, u32[]{:S(2)}) collective-permute-start(bf16[32,1,1,4,2,2,128]{6,0,5,4,3,2,1:T(8,128)(2,1)} %get-tuple-element.14), channel_id=1, source_target_pairs={{24,0},{0,8},{8,16},{16,24},{25,1},{1,9},{9,17},{17,25},{26,2},{2,... | collective-permute-start | bytes 393224 | tf_op jit(solution)/shard_map/ppermute | solution.py:85
  83.9 5.3 %collective-permute-start.39 = (f32[4,32]{1,0:T(4,128)S(1)}, f32[4,32]{1,0:T(4,128)S(1)}, u32[]{:S(2)}, u32[]{:S(2)}) collective-permute-start(f32[4,32]{1,0:T(4,128)S(1)} %pad_maximum_fusion.4), channel_id=1, source_target_pairs={{0,6},{1,7},{2,0},{3,1},{4,2},{5,3},{6,4},{7,5},{8,14},{9,15},{10,... | collective-permute-start | bytes 1544 | tf_op jit(solution)/shard_map/ppermute | solution.py:21
  85.2 4.5 %collective-permute-start.37 = (f32[4,32]{1,0:T(4,128)S(1)}, f32[4,32]{1,0:T(4,128)S(1)}, u32[]{:S(2)}, u32[]{:S(2)}) collective-permute-start(f32[4,32]{1,0:T(4,128)S(1)} %pad_maximum_fusion.4), channel_id=1, source_target_pairs={{0,4},{1,5},{2,6},{3,7},{4,0},{5,1},{6,2},{7,3},{8,12},{9,13},{10,... | collective-permute-start | bytes 1544 | tf_op jit(solution)/shard_map/ppermute | solution.py:21
  87.5 4.5 %collective-permute-start.35 = (f32[4,32]{1,0:T(4,128)S(1)}, f32[4,32]{1,0:T(4,128)S(1)}, u32[]{:S(2)}, u32[]{:S(2)}) collective-permute-start(f32[4,32]{1,0:T(4,128)S(1)} %pad_maximum_fusion.4), channel_id=1, source_target_pairs={{0,2},{1,3},{2,4},{3,5},{4,6},{5,7},{6,0},{7,1},{8,10},{9,11},{10,... | collective-permute-start | bytes 1544 | tf_op jit(solution)/shard_map/ppermute | solution.py:21
  95.8 4.5 %collective-permute-start.42 = (f32[4,32]{1,0:T(4,128)S(1)}, f32[4,32]{1,0:T(4,128)S(1)}, u32[]{:S(2)}, u32[]{:S(2)}) collective-permute-start(f32[4,32]{1,0:T(4,128)S(1)} %add_add_fusion.1), channel_id=1, source_target_pairs={{0,16},{8,24},{16,0},{24,8},{1,17},{9,25},{17,1},{25,9},{2,18},{10... | collective-permute-start | bytes 1544 | tf_op jit(solution)/shard_map/ppermute | solution.py:21
  95.8 5.4 %collective-permute-start.41 = (f32[4,32]{1,0:T(4,128)S(1)}, f32[4,32]{1,0:T(4,128)S(1)}, u32[]{:S(2)}, u32[]{:S(2)}) collective-permute-start(f32[4,32]{1,0:T(4,128)S(1)} %add_add_fusion.1), channel_id=1, source_target_pairs={{0,8},{8,16},{16,24},{24,0},{1,9},{9,17},{17,25},{25,1},{2,10},{10... | collective-permute-start | bytes 1544 | tf_op jit(solution)/shard_map/ppermute | solution.py:21
  (28 other events, 188.6 us)

commit v4 on v2

--- a/solution.py
+++ b/solution.py
@@ -28,24 +28,17 @@
 
 
 def total_sum(x):
-    return axis_sum(axis_sum(x, "xyz"), "ta")
+    axes = ("ta", "xyz")
+    count = lax.axis_size("ta") * lax.axis_size("xyz")
+    copies = jnp.broadcast_to(x[None], (count,) + x.shape)
+    return jnp.sum(lax.all_to_all(copies, axes, 0, 0), axis=0)
 
 
 def gather_tiled(x, axis, dim):
     count = lax.axis_size(axis)
-    if not is_power_of_two(count):
-        return lax.all_gather(x, axis, axis=dim, tiled=True)
-    me = lax.axis_index(axis)
-    bit = 1
-    while bit < count:
-        other = exchange(x, axis, bit)
-        x = jnp.where(
-            me // bit % 2 == 0,
-            jnp.concatenate([x, other], dim),
-            jnp.concatenate([other, x], dim),
-        )
-        bit *= 2
-    return x
+    copies = jnp.broadcast_to(x[None], (count,) + x.shape)
+    parts = lax.all_to_all(copies, axis, 0, 0)
+    return jnp.concatenate([parts[i] for i in range(count)], dim)
 
 
 def neighbour_source(device, stride, extent, step):

time: 101 us -> 92 us (0.911)
  blocking collectives: 0 us -> 38.5 us
  waiting for transfers between devices: 46.1 us -> 12.5 us
  starting transfers between devices: 24.7 us -> 8.32 us
  local copies, waits for them, and re-layouts: 13.5 us -> 15.2 us
  other arithmetic: 7.08 us -> 8.44 us
    all_to_all x0 -> x4, blocking collectives: none -> 38.5 us  [the longest x2 21.5 us: total_sum(): return jnp.sum(lax.all_to_all(copies, axes, 0, 0), axis=0)]
    ppermute x16 -> x0, waiting for transfers between devices: 38.2 us -> none  [exchange(): return lax.ppermute(x, axis, [(i, i ^ bit) for i in range(count)])]
    ppermute x16 -> x0, starting transfers between devices: 13.2 us -> none  [exchange(): return lax.ppermute(x, axis, [(i, i ^ bit) for i in range(count)])]
    ppermute x2, waiting for transfers between devices: 0.01 us -> 6.58 us  [both_sides(): from_upper = lax.ppermute(first, axis, up)]
    ppermute x6, starting transfers between devices: 5.82 us -> 2.58 us  [both_sides(): pair = lax.ppermute(jnp.concatenate([first, last], which), axis, perm)]
    ppermute x6, waiting for transfers between devices: 3.95 us -> 0.84 us  [both_sides(): pair = lax.ppermute(jnp.concatenate([first, last], which), axis, perm)]
    concatenate x0 -> x2, local copies, waits for them, and re-layouts: none -> 1.42 us  [gather_tiled(): return jnp.concatenate([parts[i] for i in range(count)], dim)]
    ppermute x2, waiting for transfers between devices: 3.9 us -> 5.05 us  [both_sides(): from_lower = lax.ppermute(last, axis, down)]
  transfers between devices with their start and end apart: 26 -> 10, of which waited for: 20 -> 6; matrix products, arithmetic and copies ran while one was open for 4% -> 7% of each run, Pallas kernels for 0% -> 0%
where the time goes in v4:
time: 92 us; the launch traced here: 91.3 us
  blocking collectives  38.5 us (42%)
  local copies, waits for them, and re-layouts  15.2 us (17%)
  waiting for transfers between devices  12.5 us (14%)
  other arithmetic  8.44 us (9%)
  starting transfers between devices  8.32 us (9%)
  matrix products  7.22 us (8%)
  between operations  1.14 us (1%)
    all_to_all x2, blocking collectives, total_sum(): return jnp.sum(lax.all_to_all(copies, axes, 0, 0), axis=0)  21.5 us
    all_to_all x2, blocking collectives, gather_tiled(): parts = lax.all_to_all(copies, axis, 0, 0)  16.9 us
    ppermute x2, waiting for transfers between devices, both_sides(): from_upper = lax.ppermute(first, axis, up)  6.58 us
    slice x6, local copies, waits for them, and re-layouts, both_sides(): first = lax.slice_in_dim(lowered, 0, 1, axis=which)  5.2 us
    ppermute x2, waiting for transfers between devices, both_sides(): from_lower = lax.ppermute(last, axis, down)  5.05 us
    unnamed x28, local copies, waits for them, and re-layouts  4.4 us
    ppermute x2, starting transfers between devices, both_sides(): from_upper = lax.ppermute(first, axis, up)  4.31 us
    dot_general x2, matrix products, precondition(): jnp.einsum('tbzyxjk,nj->ntbzyxk', null_vectors, correction, preferred_ele...  4.27 us
  transfers between devices with their start and end apart: 10, of which 6 were waited for; matrix products, arithmetic and copies ran while one was open for 7% of the time, Pallas kernels for 0%

profile of v4, /device:TPU:0, one launch (start us, length us, event | category | flops | bytes accessed | tf_op | source)
XLA Modules:
  0.0 91.3 jit_solution(6522534098718664283)
XLA Ops:
  0.6 1.2 %convert_bitcast_fusion.1 = bf16[32,4,2,2,128]{4,3,2,1,0:T(2,128)(2,1)S(1)} fusion(f32[32,1,1,4,2,2,128]{6,5,4,3,2,1,0:T(2,128)} %param.4), kind=kLoop, calls=%fused_computation.78 | loop fusion | flops 65536 | bytes 393216 | tf_op jit(solution)/shard_map/reshape
  1.8 1.1 %fusion.18 = bf16[32,48]{1,0:T(8,128)(2,1)S(1)} fusion(bf16[32,4,2,2,128]{4,3,2,1,0:T(2,128)(2,1)S(1)} %convert_bitcast_fusion.1, bf16[1,1,4,2,2,48,128]{6,5,4,3,2,1,0:T(8,128)(2,1)} %param.6), kind=kOutput, calls=%fused_computation.22 | convolution fusion | flops 6292992 | bytes 330752 | tf_op jit(solution)/shard_map/tbzyxjk,ntbzyxk->nj/dot_general | solution.py:101
  3.1 9.8 %all_to_all.20 = bf16[8,2,768]{2,1,0:T(2,128)(2,1)S(1)} all-to-all(bf16[8,2,768]{2,1,0:T(2,128)(2,1)S(1)} %reshape.357), channel_id=1, replica_groups=mesh['ta'=4,'xyz'=8] {'xyz'}, dimensions={0} | all-to-all | bytes 49152 | tf_op jit(solution)/shard_map/all_to_all | solution.py:40
  13.7 2.1 %bitcast_dynamic-update-slice_fusion.5 = (bf16[32,1,9,1,4,2,2,128]{7,0,6,5,4,3,2,1:T(8,128)(2,1)S(1)}, bf16[32,1,1,4,2,2,128]{6,0,5,4,3,2,1:T(8,128)(2,1)}, f32[32,1,1,4,2,2,128]{6,0,5,4,3,2,1:T(8,128)}) fusion(bf16[1,1,4,2,2,48,128]{6,5,4,3,2,1,0:T(8,128)(2,1)} %param.6, bf16[32,384]{1,0:T(8,128)(2,1)} %concatenate.134, bf16[1,48,384]{2,1,0:T(8,128)(2,1)} %param.7, ...), kind=kOutput, calls=%fused_computation.74 | convolution fusion | flops 7669247 | bytes 1044480 | tf_op jit(solution)/shard_map/tbzyxjk,nj->ntbzyxk/dot_general | solution.py:111
  15.9 0.9 %fusion.63 = (bf16[32,1,1,4,2,1,128]{6,0,5,4,3,2,1:T(8,128)(2,1)S(1)}, bf16[32,1,1,4,2,1,128]{6,0,5,4,3,2,1:T(8,128)(2,1)S(1)}) fusion(bf16[32,1,1,4,2,2,128]{6,0,5,4,3,2,1:T(8,128)(2,1)} %get-tuple-element.23), kind=kLoop, calls=%fused_computation.131 | loop fusion | bytes 262144 | tf_op jit(solution)/shard_map/slice | solution.py:52
  18.2 1.0 %fusion.58 = (bf16[32,1,1,3,2,2,128]{6,0,5,4,3,2,1:T(8,128)(2,1)S(1)}, bf16[32,1,1,3,2,2,128]{6,0,5,4,3,2,1:T(8,128)(2,1)S(1)}) fusion(bf16[32,1,1,4,2,2,128]{6,0,5,4,3,2,1:T(8,128)(2,1)} %get-tuple-element.23), kind=kLoop, calls=%fused_computation.126 | loop fusion | bytes 393216 | tf_op jit(solution)/shard_map/slice | solution.py:71
  19.9 0.9 fusion.61
  20.8 3.7 %collective-permute-start.3 = (bf16[32,1,1,4,2,2,128]{6,0,5,4,3,2,1:T(8,128)(2,1)S(1)}, bf16[32,1,1,4,2,2,128]{6,0,5,4,3,2,1:T(8,128)(2,1)S(1)}, u32[]{:S(2)}, u32[]{:S(2)}) collective-permute-start(bf16[32,1,1,4,2,2,128]{6,0,5,4,3,2,1:T(8,128)(2,1)S(1)} %copy-done.5), channel_id=1, source_target_pairs={{8,0},{16,8},{24,16},{0,24},{9,1},{17,9},{25,17},{1,25},{10,2},{18... | collective-permute-start | bytes 393224 | tf_op jit(solution)/shard_map/ppermute | solution.py:67
  24.7 3.7 %collective-permute-done.3 = bf16[32,1,1,4,2,2,128]{6,0,5,4,3,2,1:T(8,128)(2,1)S(1)} collective-permute-done((bf16[32,1,1,4,2,2,128]{6,0,5,4,3,2,1:T(8,128)(2,1)S(1)}, bf16[32,1,1,4,2,2,128]{6,0,5,4,3,2,1:T(8,128)(2,1)S(1)}, u32[]{:S(2)}, u32[]{:S(2)}) %collective-permute-start.3) | collective-permute-done | bytes 131104 | tf_op jit(solution)/shard_map/ppermute | solution.py:67
  28.3 2.9 %collective-permute-done.4 = bf16[32,1,1,4,2,2,128]{6,0,5,4,3,2,1:T(8,128)(2,1)S(1)} collective-permute-done((bf16[32,1,1,4,2,2,128]{6,0,5,4,3,2,1:T(8,128)(2,1)S(1)}, bf16[32,1,1,4,2,2,128]{6,0,5,4,3,2,1:T(8,128)(2,1)S(1)}, u32[]{:S(2)}, u32[]{:S(2)}) %collective-permute-start.4) | collective-permute-done | bytes 131104 | tf_op jit(solution)/shard_map/ppermute | solution.py:68
  34.5 0.9 copy-done.1
  35.7 10.7 %all_to_all.21 = f32[32,2,32]{2,1,0:T(2,128)S(1)} all-to-all(f32[32,2,32]{2,1,0:T(2,128)S(1)} %broadcast_in_dim.9), channel_id=1, replica_groups=mesh['ta'=4,'xyz'=8] {'ta','xyz'}, dimensions={0} | all-to-all | bytes 16384 | tf_op jit(solution)/shard_map/all_to_all | solution.py:34
  47.6 7.2 %all_to_all.22 = bf16[8,2,768]{2,1,0:T(2,128)(2,1)S(1)} all-to-all(bf16[8,2,768]{2,1,0:T(2,128)(2,1)S(1)} %reshape.359), channel_id=1, replica_groups=mesh['ta'=4,'xyz'=8] {'xyz'}, dimensions={0} | all-to-all | bytes 49152 | tf_op jit(solution)/shard_map/all_to_all | solution.py:40
  55.6 2.1 %bitcast_dynamic-update-slice_fusion.2 = (bf16[32,1,9,1,4,2,2,128]{7,0,6,5,4,3,2,1:T(8,128)(2,1)S(1)}, bf16[32,1,1,4,2,2,128]{6,0,5,4,3,2,1:T(8,128)(2,1)}, f32[32,1,1,4,2,2,128]{6,0,5,4,3,2,1:T(8,128)}) fusion(bf16[1,1,4,2,2,48,128]{6,5,4,3,2,1,0:T(8,128)(2,1)} %param.6, bf16[32,384]{1,0:T(8,128)(2,1)} %concatenate.147, bf16[1,48,384]{2,1,0:T(8,128)(2,1)} %param.7, ...), kind=kOutput, calls=%fused_computation.71 | convolution fusion | flops 7669247 | bytes 1044480 | tf_op jit(solution)/shard_map/tbzyxjk,nj->ntbzyxk/dot_general | solution.py:111
  58.6 0.9 fusion.57
  60.1 1.0 %fusion.52 = (bf16[32,1,1,3,2,2,128]{6,0,5,4,3,2,1:T(8,128)(2,1)S(1)}, bf16[32,1,1,3,2,2,128]{6,0,5,4,3,2,1:T(8,128)(2,1)S(1)}) fusion(bf16[32,1,1,4,2,2,128]{6,0,5,4,3,2,1:T(8,128)(2,1)} %get-tuple-element.18), kind=kLoop, calls=%fused_computation.120 | loop fusion | bytes 393216 | tf_op jit(solution)/shard_map/slice | solution.py:71
  61.8 0.9 fusion.55
  63.3 1.4 %collective-permute-start.9 = (bf16[32,1,1,4,2,2,128]{6,0,5,4,3,2,1:T(8,128)(2,1)S(1)}, bf16[32,1,1,4,2,2,128]{6,0,5,4,3,2,1:T(8,128)(2,1)S(1)}, u32[]{:S(2)}, u32[]{:S(2)}) collective-permute-start(bf16[32,1,1,4,2,2,128]{6,0,5,4,3,2,1:T(8,128)(2,1)S(1)} %copy-done.6), channel_id=1, source_target_pairs={{24,0},{0,8},{8,16},{16,24},{25,1},{1,9},{9,17},{17,25},{26,2},{2,... | collective-permute-start | bytes 393224 | tf_op jit(solution)/shard_map/ppermute | solution.py:68
  65.8 2.9 %collective-permute-done.8 = bf16[32,1,1,4,2,2,128]{6,0,5,4,3,2,1:T(8,128)(2,1)S(1)} collective-permute-done((bf16[32,1,1,4,2,2,128]{6,0,5,4,3,2,1:T(8,128)(2,1)S(1)}, bf16[32,1,1,4,2,2,128]{6,0,5,4,3,2,1:T(8,128)(2,1)S(1)}, u32[]{:S(2)}, u32[]{:S(2)}) %collective-permute-start.8) | collective-permute-done | bytes 131104 | tf_op jit(solution)/shard_map/ppermute | solution.py:67
  68.7 2.2 %collective-permute-done.9 = bf16[32,1,1,4,2,2,128]{6,0,5,4,3,2,1:T(8,128)(2,1)S(1)} collective-permute-done((bf16[32,1,1,4,2,2,128]{6,0,5,4,3,2,1:T(8,128)(2,1)S(1)}, bf16[32,1,1,4,2,2,128]{6,0,5,4,3,2,1:T(8,128)(2,1)S(1)}, u32[]{:S(2)}, u32[]{:S(2)}) %collective-permute-start.9) | collective-permute-done | bytes 131104 | tf_op jit(solution)/shard_map/ppermute | solution.py:68
  76.0 10.9 %all_to_all.23 = f32[32,1,128]{2,1,0:T(1,128)S(1)} all-to-all(f32[32,1,128]{2,1,0:T(1,128)S(1)} %reshape.361), channel_id=1, replica_groups=mesh['ta'=4,'xyz'=8] {'ta','xyz'}, dimensions={0} | all-to-all | bytes 32768 | tf_op jit(solution)/shard_map/all_to_all | solution.py:34
  88.3 1.2 %multiply_subtract_fusion = (f32[32,1,1,4,2,2,128]{6,0,5,4,3,2,1:T(8,128)S(1)}, f32[32,1,1,4,2,2,128]{6,0,5,4,3,2,1:T(8,128)S(1)}) fusion(f32[32,1,1,4,2,2,128]{6,0,5,4,3,2,1:T(8,128)S(1)} %copy-done.4, f32[32,1,1,4,2,2,128]{6,0,5,4,3,2,1:T(8,128)S(1)} %get-tuple-element.16, f32[32,1,1,4,2,2,128]{6,0,5,4,3,2,1:T(8,128)S(1)} %copy-done.3, ...), kind=kLoop, calls=%fused_computation.34 | loop fusion | flops 589824 | bytes 1835392 | tf_op jit(solution)/shard_map/sub | solution.py:162
  89.4 0.9 copy.63
  90.3 0.9 copy.64
  (96 shorter events, 19.0 us)
Async XLA Ops:
  0.6 33.0 %copy-start = (bf16[1,1,4,2,2,9,64,128]{7,6,5,4,3,2,1,0:T(8,128)(2,1)S(1)}, bf16[1,1,4,2,2,9,64,128]{7,6,5,4,3,2,1,0:T(8,128)(2,1)}, u32[]{:S(2)}) copy-start(bf16[1,1,4,2,2,9,64,128]{7,6,5,4,3,2,1,0:T(8,128)(2,1)} %param.5) | copy-start | bytes 7077892
  15.8 4.9 %copy-start.5 = (bf16[32,1,1,4,2,2,128]{6,0,5,4,3,2,1:T(8,128)(2,1)S(1)}, bf16[32,1,1,4,2,2,128]{6,0,5,4,3,2,1:T(8,128)(2,1)}, u32[]{:S(2)}) copy-start(bf16[32,1,1,4,2,2,128]{6,0,5,4,3,2,1:T(8,128)(2,1)} %get-tuple-element.23) | copy-start | bytes 393220
  15.9 8.6 %collective-permute-start = (bf16[32,1,1,4,2,2,128]{6,0,5,4,3,2,1:T(8,128)(2,1)}, bf16[32,1,1,4,2,2,128]{6,0,5,4,3,2,1:T(8,128)(2,1)S(1)}, u32[]{:S(2)}, u32[]{:S(2)}) collective-permute-start(bf16[32,1,1,4,2,2,128]{6,0,5,4,3,2,1:T(8,128)(2,1)} %get-tuple-element.23), channel_id=1, source_target_pairs={{1,0},{0,1},{3,2},{2,3},{5,4},{4,5},{7,6},{6,7},{9,8},{8,9},{11,10... | collective-permute-start | bytes 393224 | tf_op jit(solution)/shard_map/ppermute | solution.py:61
  16.8 7.7 %collective-permute-start.1 = (bf16[32,1,1,4,2,2,128]{6,0,5,4,3,2,1:T(8,128)(2,1)}, bf16[32,1,1,4,2,2,128]{6,0,5,4,3,2,1:T(8,128)(2,1)S(1)}, u32[]{:S(2)}, u32[]{:S(2)}) collective-permute-start(bf16[32,1,1,4,2,2,128]{6,0,5,4,3,2,1:T(8,128)(2,1)} %get-tuple-element.23), channel_id=1, source_target_pairs={{2,0},{3,1},{0,2},{1,3},{6,4},{7,5},{4,6},{5,7},{10,8},{11,9},{8,1... | collective-permute-start | bytes 393224 | tf_op jit(solution)/shard_map/ppermute | solution.py:61
  19.2 5.2 %collective-permute-start.2 = (bf16[32,1,1,2,2,2,128]{6,0,5,4,3,2,1:T(8,128)(2,1)S(1)}, bf16[32,1,1,2,2,2,128]{6,0,5,4,3,2,1:T(8,128)(2,1)S(1)}, u32[]{:S(2)}, u32[]{:S(2)}) collective-permute-start(bf16[32,1,1,2,2,2,128]{6,0,5,4,3,2,1:T(8,128)(2,1)S(1)} %pad_maximum_fusion.2), channel_id=1, source_target_pairs={{4,0},{5,1},{6,2},{7,3},{0,4},{1,5},{2,6},{3,7},{12,8},{13,9},{14,... | collective-permute-start | bytes 196616 | tf_op jit(solution)/shard_map/ppermute | solution.py:61
  20.8 7.6 %collective-permute-start.3 = (bf16[32,1,1,4,2,2,128]{6,0,5,4,3,2,1:T(8,128)(2,1)S(1)}, bf16[32,1,1,4,2,2,128]{6,0,5,4,3,2,1:T(8,128)(2,1)S(1)}, u32[]{:S(2)}, u32[]{:S(2)}) collective-permute-start(bf16[32,1,1,4,2,2,128]{6,0,5,4,3,2,1:T(8,128)(2,1)S(1)} %copy-done.5), channel_id=1, source_target_pairs={{8,0},{16,8},{24,16},{0,24},{9,1},{17,9},{25,17},{1,25},{10,2},{18... | collective-permute-start | bytes 393224 | tf_op jit(solution)/shard_map/ppermute | solution.py:67
  24.4 6.8 %collective-permute-start.4 = (bf16[32,1,1,4,2,2,128]{6,0,5,4,3,2,1:T(8,128)(2,1)S(1)}, bf16[32,1,1,4,2,2,128]{6,0,5,4,3,2,1:T(8,128)(2,1)S(1)}, u32[]{:S(2)}, u32[]{:S(2)}) collective-permute-start(bf16[32,1,1,4,2,2,128]{6,0,5,4,3,2,1:T(8,128)(2,1)S(1)} %copy-done.5), channel_id=1, source_target_pairs={{24,0},{0,8},{8,16},{16,24},{25,1},{1,9},{9,17},{17,25},{26,2},{2,... | collective-permute-start | bytes 393224 | tf_op jit(solution)/shard_map/ppermute | solution.py:68
  34.5 1.0 %copy-start.1 = (f32[32,1,1,4,2,2,128]{6,5,4,3,2,1,0:T(2,128)S(1)}, f32[32,1,1,4,2,2,128]{6,5,4,3,2,1,0:T(2,128)}, u32[]{:S(2)}) copy-start(f32[32,1,1,4,2,2,128]{6,5,4,3,2,1,0:T(2,128)} %param.4) | copy-start | bytes 786436
  34.5 12.7 %copy-start.8 = (bf16[1,1,4,2,2,48,128]{6,5,4,3,2,1,0:T(8,128)(2,1)S(1)}, bf16[1,1,4,2,2,48,128]{6,5,4,3,2,1,0:T(8,128)(2,1)}, u32[]{:S(2)}) copy-start(bf16[1,1,4,2,2,48,128]{6,5,4,3,2,1,0:T(8,128)(2,1)} %param.6) | copy-start | bytes 589828
  35.7 19.9 %copy-start.2 = (f32[32,1,1,4,2,2,128]{6,0,5,4,3,2,1:T(8,128)}, f32[32,1,1,4,2,2,128]{6,0,5,4,3,2,1:T(8,128)S(1)}, u32[]{:S(2)}) copy-start(f32[32,1,1,4,2,2,128]{6,0,5,4,3,2,1:T(8,128)S(1)} %get-tuple-element.21) | copy-start | bytes 786436
  57.7 4.9 %copy-start.6 = (bf16[32,1,1,4,2,2,128]{6,0,5,4,3,2,1:T(8,128)(2,1)S(1)}, bf16[32,1,1,4,2,2,128]{6,0,5,4,3,2,1:T(8,128)(2,1)}, u32[]{:S(2)}) copy-start(bf16[32,1,1,4,2,2,128]{6,0,5,4,3,2,1:T(8,128)(2,1)} %get-tuple-element.18) | copy-start | bytes 393220
  58.6 6.9 %collective-permute-start.5 = (bf16[32,1,1,4,2,2,128]{6,0,5,4,3,2,1:T(8,128)(2,1)}, bf16[32,1,1,4,2,2,128]{6,0,5,4,3,2,1:T(8,128)(2,1)S(1)}, u32[]{:S(2)}, u32[]{:S(2)}) collective-permute-start(bf16[32,1,1,4,2,2,128]{6,0,5,4,3,2,1:T(8,128)(2,1)} %get-tuple-element.18), channel_id=1, source_target_pairs={{1,0},{0,1},{3,2},{2,3},{5,4},{4,5},{7,6},{6,7},{9,8},{8,9},{11,10... | collective-permute-start | bytes 393224 | tf_op jit(solution)/shard_map/ppermute | solution.py:61
  59.5 6.2 %collective-permute-start.6 = (bf16[32,1,1,4,2,2,128]{6,0,5,4,3,2,1:T(8,128)(2,1)}, bf16[32,1,1,4,2,2,128]{6,0,5,4,3,2,1:T(8,128)(2,1)S(1)}, u32[]{:S(2)}, u32[]{:S(2)}) collective-permute-start(bf16[32,1,1,4,2,2,128]{6,0,5,4,3,2,1:T(8,128)(2,1)} %get-tuple-element.18), channel_id=1, source_target_pairs={{2,0},{3,1},{0,2},{1,3},{6,4},{7,5},{4,6},{5,7},{10,8},{11,9},{8,1... | collective-permute-start | bytes 393224 | tf_op jit(solution)/shard_map/ppermute | solution.py:61
  61.1 4.3 %collective-permute-start.7 = (bf16[32,1,1,2,2,2,128]{6,0,5,4,3,2,1:T(8,128)(2,1)S(1)}, bf16[32,1,1,2,2,2,128]{6,0,5,4,3,2,1:T(8,128)(2,1)S(1)}, u32[]{:S(2)}, u32[]{:S(2)}) collective-permute-start(bf16[32,1,1,2,2,2,128]{6,0,5,4,3,2,1:T(8,128)(2,1)S(1)} %pad_maximum_fusion.3), channel_id=1, source_target_pairs={{4,0},{5,1},{6,2},{7,3},{0,4},{1,5},{2,6},{3,7},{12,8},{13,9},{14,... | collective-permute-start | bytes 196616 | tf_op jit(solution)/shard_map/ppermute | solution.py:61
  62.7 6.0 %collective-permute-start.8 = (bf16[32,1,1,4,2,2,128]{6,0,5,4,3,2,1:T(8,128)(2,1)S(1)}, bf16[32,1,1,4,2,2,128]{6,0,5,4,3,2,1:T(8,128)(2,1)S(1)}, u32[]{:S(2)}, u32[]{:S(2)}) collective-permute-start(bf16[32,1,1,4,2,2,128]{6,0,5,4,3,2,1:T(8,128)(2,1)S(1)} %copy-done.6), channel_id=1, source_target_pairs={{8,0},{16,8},{24,16},{0,24},{9,1},{17,9},{25,17},{1,25},{10,2},{18... | collective-permute-start | bytes 393224 | tf_op jit(solution)/shard_map/ppermute | solution.py:67
  63.3 7.6 %collective-permute-start.9 = (bf16[32,1,1,4,2,2,128]{6,0,5,4,3,2,1:T(8,128)(2,1)S(1)}, bf16[32,1,1,4,2,2,128]{6,0,5,4,3,2,1:T(8,128)(2,1)S(1)}, u32[]{:S(2)}, u32[]{:S(2)}) collective-permute-start(bf16[32,1,1,4,2,2,128]{6,0,5,4,3,2,1:T(8,128)(2,1)S(1)} %copy-done.6), channel_id=1, source_target_pairs={{24,0},{0,8},{8,16},{16,24},{25,1},{1,9},{9,17},{17,25},{26,2},{2,... | collective-permute-start | bytes 393224 | tf_op jit(solution)/shard_map/ppermute | solution.py:68
  74.6 1.0 %copy-start.3 = (f32[32,1,1,4,2,2,128]{6,0,5,4,3,2,1:T(8,128)S(1)}, f32[32,1,1,4,2,2,128]{6,0,5,4,3,2,1:T(8,128)}, u32[]{:S(2)}) copy-start(f32[32,1,1,4,2,2,128]{6,0,5,4,3,2,1:T(8,128)} %copy-done.2) | copy-start | bytes 786436
  74.6 1.0 %copy-start.4 = (f32[32,1,1,4,2,2,128]{6,0,5,4,3,2,1:T(8,128)S(1)}, f32[32,1,1,4,2,2,128]{6,0,5,4,3,2,1:T(8,128)}, u32[]{:S(2)}) copy-start(f32[32,1,1,4,2,2,128]{6,0,5,4,3,2,1:T(8,128)} %get-tuple-element.20) | copy-start | bytes 786436
  74.6 13.7 %copy-start.7 = (f32[32,1,1,4,2,2,128]{6,0,5,4,3,2,1:T(8,128)S(1)}, f32[32,1,1,4,2,2,128]{6,0,5,4,3,2,1:T(8,128)}, u32[]{:S(2)}) copy-start(f32[32,1,1,4,2,2,128]{6,0,5,4,3,2,1:T(8,128)} %get-tuple-element.78) | copy-start | bytes 786436

commit v5 on v4

v5 whole, which is shorter than its diff:
```python
import jax
import jax.numpy as jnp
from jax import lax
from jax.sharding import PartitionSpec as P

OMEGA = 0.4
EPS = 1e-06


def total_sum(x):
    axes = ("ta", "xyz")
    count = lax.axis_size("ta") * lax.axis_size("xyz")
    copies = jnp.broadcast_to(x[None], (count,) + x.shape)
    return jnp.sum(lax.all_to_all(copies, axes, 0, 0), axis=0)


def neighbour_source(device, stride, extent, step):
    coord = device // stride % extent
    return device + ((coord + step) % extent - coord) * stride


def neighbour_plan():
    blocks_total = lax.axis_size("xyz")
    across_x = 2 + 2 * min(blocks_total // 64, 1)
    across_z = blocks_total // (across_x * across_x)
    specs = (
        (5, "xyz", 1, across_x),
        (4, "xyz", across_x, across_x),
        (3, "xyz", across_x * across_x, across_z),
        (1, "ta", 1, lax.axis_size("ta")),
    )
    directions = []
    for dim, axis, stride, extent in specs:
        count = lax.axis_size(axis)
        for step in (1, -1):
            perm = tuple((neighbour_source(d, stride, extent, step), d) for d in range(count))
            directions.append((dim, axis, step, perm))
    groups = {}
    order = []
    for k, (dim, axis, step, perm) in enumerate(directions):
        key = (axis, perm)
        if key not in groups:
            groups[key] = []
            order.append(key)
        groups[key].append(k)
    return directions, [(key, groups[key]) for key in order]


def face_of(x, dim, step):
    index = 0 if step > 0 else x.shape[dim] - 1
    return lax.slice_in_dim(x, index, index + 1, axis=dim)


def swap(axis, perm, arrays):
    width = arrays[0].shape[-1]
    flat = jnp.concatenate([a.reshape(-1, width) for a in arrays], 0)
    if any(s != d for s, d in perm):
        flat = lax.ppermute(flat, axis, list(perm))
    out, row = [], 0
    for a in arrays:
        rows = a.size // width
        out.append(flat[row : row + rows].reshape(a.shape))
        row += rows
    return out


def exchange_fields(plan, field):
    directions, groups = plan
    received = [None] * len(directions)
    for (axis, perm), members in groups:
        faces = [face_of(field, directions[k][0], directions[k][2]) for k in members]
        for k, got in zip(members, swap(axis, perm, faces)):
            received[k] = got
    return received


def exchange_static(plan, null_vectors, inverse_rows):
    directions, groups = plan
    nulls = [None] * len(directions)
    rows = [None] * len(directions)
    for (axis, perm), members in groups:
        faces = [face_of(null_vectors, directions[k][0] - 1, directions[k][2]) for k in members]
        got = swap(axis, perm, faces + [inverse_rows])
        for k, null_face in zip(members, got[:-1]):
            nulls[k] = null_face
            rows[k] = got[-1]
    return nulls, rows


def correct(slab, rows):
    return lax.dot_general(
        slab, rows, (((1,), (1,)), ((), ())), preferred_element_type=jnp.float32
    ).astype(jnp.bfloat16)


def prolong(null_vectors, correction):
    return jnp.einsum(
        "tbzyxjk,nj->ntbzyxk", null_vectors, correction, preferred_element_type=jnp.float32
    )


def precondition(plan, vector_in, faces_in, null_vectors, inverse_rows, static):
    directions, _ = plan
    nulls, rows = static
    lowered = vector_in.astype(jnp.bfloat16)
    coarse = jnp.einsum(
        "tbzyxjk,ntbzyxk->nj", null_vectors, lowered, preferred_element_type=jnp.float32
    ).astype(jnp.bfloat16)
    slabs_total = lax.axis_size("ta")
    blocks_total = lax.axis_size("xyz")
    count, width = coarse.shape
    me = lax.axis_index("ta")

    def joined(slab):
        return jnp.transpose(slab, (1, 0, 2)).reshape(count, blocks_total * width)

    if slabs_total * blocks_total <= 64:
        copies = jnp.broadcast_to(coarse[None], (slabs_total * blocks_total, count, width))
        parts = lax.all_to_all(copies, ("ta", "xyz"), 0, 0)
        slabs = parts.reshape(slabs_total, blocks_total, count, width)
        slab_for = {
            step: joined(
                lax.dynamic_index_in_dim(slabs, (me + step) % slabs_total, 0, keepdims=False)
            )
            for step in (0, 1, -1)
        }
    else:
        copies = jnp.broadcast_to(coarse[None], (blocks_total, count, width))
        own = joined(lax.all_to_all(copies, "xyz", 0, 0))
        slab_for = {0: own}
        for step in (1, -1):
            perm = [(neighbour_source(d, 1, slabs_total, step), d) for d in range(slabs_total)]
            slab_for[step] = lax.ppermute(own, "ta", perm)
    own_slab = slab_for[0]
    direction = OMEGA * vector_in + prolong(null_vectors, correct(own_slab, inverse_rows))
    faces = []
    for k, (dim, axis, step, perm) in enumerate(directions):
        slab = own_slab if axis == "xyz" else slab_for[step]
        face = OMEGA * faces_in[k] + prolong(nulls[k], correct(slab, rows[k]))
        faces.append(face.astype(jnp.bfloat16))
    return direction, faces


def apply_links(plan, coarse_links, lowered, faces):
    directions, _ = plan
    shifted = [lowered]
    for k, (dim, axis, step, perm) in enumerate(directions):
        length = lowered.shape[dim]
        if step > 0:
            parts = [lax.slice_in_dim(lowered, 1, length, axis=dim), faces[k]]
        else:
            parts = [faces[k], lax.slice_in_dim(lowered, 0, length - 1, axis=dim)]
        shifted.append(jnp.concatenate(parts, dim))
    stacked = jnp.stack(shifted, 2)
    half_width = lowered.shape[-1] // 2
    real_part = stacked[..., :half_width]
    imag_part = stacked[..., half_width:]
    real_input = jnp.concatenate([real_part, -imag_part], -1)
    imag_input = jnp.concatenate([imag_part, real_part], -1)
    inputs = jnp.stack([real_input, imag_input], 0)
    result = jnp.einsum(
        "tbzyxdik,pntdbzyxk->pntbzyxi", coarse_links, inputs, preferred_element_type=jnp.float32
    )
    return jnp.concatenate([result[0], result[1]], -1)


def inner_rows(left_vec, right_vec):
    return jnp.sum(left_vec * right_vec, axis=(1, 2, 3, 4, 5, 6))


def scaled(weights, vector_in):
    return weights[:, None, None, None, None, None, None] * vector_in


def pair_products(image, residual):
    both = total_sum(jnp.stack([inner_rows(image, image), inner_rows(image, residual)]))
    return (both[0], both[1])


def shards(right_side, coarse_links, null_vectors, coarse_inverse):
    plan = neighbour_plan()
    inverse_rows = coarse_inverse[0]
    static = exchange_static(plan, null_vectors, inverse_rows)
    residual = right_side
    residual_faces = exchange_fields(plan, residual)
    direction_a, faces_a = precondition(
        plan, residual, residual_faces, null_vectors, inverse_rows, static
    )
    image_a = apply_links(plan, coarse_links, direction_a.astype(jnp.bfloat16), faces_a)
    image_faces = exchange_fields(plan, image_a)
    norm_a, correlation_a = pair_products(image_a, residual)
    step_a = correlation_a / (norm_a + EPS)
    solution = scaled(step_a, direction_a)
    residual = residual - scaled(step_a, image_a)
    residual_faces = [
        face - scaled(step_a, image_face)
        for face, image_face in zip(residual_faces, image_faces)
    ]
    direction_b, faces_b = precondition(
        plan, residual, residual_faces, null_vectors, inverse_rows, static
    )
    image_b = apply_links(plan, coarse_links, direction_b.astype(jnp.bfloat16), faces_b)
    sums = total_sum(
        jnp.stack(
            [
                inner_rows(image_a, image_b),
                inner_rows(image_b, image_b),
                inner_rows(image_b, residual),
                inner_rows(image_a, residual),
            ]
        )
    )
    projection_sum, square_b, raw_correlation, shared_correlation = (
        sums[0], sums[1], sums[2], sums[3]
    )
    beta_coef = projection_sum / (norm_a + EPS)
    image_b = image_b - scaled(beta_coef, image_a)
    direction_b = direction_b - scaled(beta_coef, direction_a)
    norm_b = jnp.maximum(
        square_b - beta_coef * (2.0 * projection_sum - beta_coef * norm_a), 0.0
    )
    correlation_b = raw_correlation - beta_coef * shared_correlation
    step_b = correlation_b / (norm_b + EPS)
    solution = solution + scaled(step_b, direction_b)
    residual = residual - scaled(step_b, image_b)
    return (solution, residual)


def solution(mesh):
    in_specs = (
        P(None, "ta", "xyz", None, None, None, None),
        P("ta", "xyz", None, None, None, None, None, None),
        P("ta", "xyz", None, None, None, None, None),
        P("ta", "xyz", None),
    )
    out_specs = (
        P(None, "ta", "xyz", None, None, None, None),
        P(None, "ta", "xyz", None, None, None, None),
    )
    return jax.shard_map(shards, mesh=mesh, in_specs=in_specs, out_specs=out_specs, check_vma=False)
```

time: 92 us -> 166 us (1.80)
  local copies, waits for them, and re-layouts: 15.2 us -> 62.6 us
  blocking collectives: 38.5 us -> 8.84 us
  starting transfers between devices: 8.32 us -> 36 us
  matrix products: 7.22 us -> 24.2 us
  other arithmetic: 8.44 us -> 16 us
  waiting for transfers between devices: 12.5 us -> 14.4 us
    slice x14 -> x34, local copies, waits for them, and re-layouts: 7.22 us -> 28.6 us  [the longest x16 17.4 us: swap(): out.append(flat[row:row + rows].reshape(a.shape))]
    dot_general x2 -> x24, matrix products: 4.27 us -> 22.1 us  [the longest x18 19 us: prolong(): jnp.einsum('tbzyxjk,nj->ntbzyxk', null_vectors, correction, preferred_ele...]
    all_to_all x2 -> x0, blocking collectives: 16.9 us -> none  [gather_tiled(): parts = lax.all_to_all(copies, axis, 0, 0)]
    all_to_all x0 -> x3, starting transfers between devices: none -> 15.3 us  [the longest x2 10.1 us: precondition(): parts = lax.all_to_all(copies, ('ta', 'xyz'), 0, 0)]
    reshape x0 -> x11, local copies, waits for them, and re-layouts: none -> 13.3 us  [the longest x6 7.06 us: joined(): return jnp.transpose(slab, (1, 0, 2)).reshape(count, blocks_total * width)]
    all_to_all x2 -> x1, blocking collectives: 21.5 us -> 8.84 us  [total_sum(): return jnp.sum(lax.all_to_all(copies, axes, 0, 0), axis=0)]
    ppermute x10 -> x15, starting transfers between devices: 8.32 us -> 20.7 us  [swap(): flat = lax.ppermute(flat, axis, list(perm))]
    all_to_all x0 -> x3, waiting for transfers between devices: none -> 10.7 us  [the longest x2 6.97 us: precondition(): parts = lax.all_to_all(copies, ('ta', 'xyz'), 0, 0)]
  transfers between devices with their start and end apart: 10 -> 18, of which waited for: 6 -> 4; matrix products, arithmetic and copies ran while one was open for 7% -> 48% of each run, Pallas kernels for 0% -> 0%
where the time goes in v5:
time: 166 us; the launch traced here: 164 us
  local copies, waits for them, and re-layouts  62.6 us (38%)
  starting transfers between devices  36 us (22%)
  matrix products  24.2 us (15%)
  other arithmetic  16 us (10%)
  waiting for transfers between devices  14.4 us (9%)
  blocking collectives  8.84 us (5%)
  between operations  1.83 us (1%)
    ppermute x15, starting transfers between devices, swap(): flat = lax.ppermute(flat, axis, list(perm))  20.7 us
    dot_general x18, matrix products, prolong(): jnp.einsum('tbzyxjk,nj->ntbzyxk', null_vectors, correction, preferred_ele...  19 us
    slice x16, local copies, waits for them, and re-layouts, swap(): out.append(flat[row:row + rows].reshape(a.shape))  17.4 us
    unnamed x117, local copies, waits for them, and re-layouts  11 us
    all_to_all x2, starting transfers between devices, precondition(): parts = lax.all_to_all(copies, ('ta', 'xyz'), 0, 0)  10.1 us
    all_to_all x1, blocking collectives, total_sum(): return jnp.sum(lax.all_to_all(copies, axes, 0, 0), axis=0)  8.84 us
    reshape x6, local copies, waits for them, and re-layouts, joined(): return jnp.transpose(slab, (1, 0, 2)).reshape(count, blocks_total * width)  7.06 us
    all_to_all x2, waiting for transfers between devices, precondition(): parts = lax.all_to_all(copies, ('ta', 'xyz'), 0, 0)  6.97 us
  transfers between devices with their start and end apart: 18, of which 4 were waited for; matrix products, arithmetic and copies ran while one was open for 48% of the time, Pallas kernels for 0%

profile of v5, /device:TPU:0, one launch (start us, length us, event | category | flops | bytes accessed | tf_op | source)
XLA Modules:
  0.0 163.8 jit_solution(10681561276827120646)
XLA Ops:
  3.6 1.8 %pad_maximum_fusion = (bf16[912,128]{1,0:T(8,128)(2,1)}, bf16[912,128]{1,0:T(8,128)(2,1)}, bf16[912,128]{1,0:T(8,128)(2,1)}) fusion(bf16[144,128]{1,0:T(8,128)(2,1)S(1)} %reshape_squeeze.2, bf16[768,128]{1,0:T(8,128)(2,1)} %bitcast.444, bf16[384,128]{1,0:T(8,128)(2,1)S(1)} %bitcast.492, bf16[384,128]{1,0:T(8,128)(2,1)S(1)} %bitcast.491, ...), kind=kLoop, calls=%fused_computation.52 | loop fusion | flops 1634304 | bytes 1327104 | tf_op jit(solution)/shard_map/concatenate | solution.py:56
  5.4 5.0 %collective-permute-start.7 = (bf16[912,128]{1,0:T(8,128)(2,1)}, bf16[912,128]{1,0:T(8,128)(2,1)}, u32[]{:S(2)}, u32[]{:S(2)}) collective-permute-start(bf16[912,128]{1,0:T(8,128)(2,1)} %get-tuple-element.94), channel_id=1, source_target_pairs={{8,0},{16,8},{24,16},{0,24},{9,1},{17,9},{25,17},{1,25},{10,2},{18... | collective-permute-start | bytes 700424 | tf_op jit(solution)/shard_map/ppermute | solution.py:58
  12.7 6.1 %all-to-all-start = ((bf16[32,2,768]{2,1,0:T(2,128)(2,1)}), bf16[32,2,768]{2,1,0:T(2,128)(2,1)S(1)}, u32[]{:S(2)}, u32[]{:S(2)}) async-start(bf16[32,2,768]{2,1,0:T(2,128)(2,1)} %reshape.740), calls=%async_computation | async-start | bytes 196608 | tf_op jit(solution)/shard_map/all_to_all | solution.py:119
  19.1 1.7 %collective-permute-start.3 = (bf16[912,128]{1,0:T(8,128)(2,1)}, bf16[912,128]{1,0:T(8,128)(2,1)}, u32[]{:S(2)}, u32[]{:S(2)}) collective-permute-start(bf16[912,128]{1,0:T(8,128)(2,1)} %get-tuple-element.95), channel_id=1, source_target_pairs={{2,0},{3,1},{0,2},{1,3},{6,4},{7,5},{4,6},{5,7},{10,8},{11,9},{8,1... | collective-permute-start | bytes 700424 | tf_op jit(solution)/shard_map/ppermute | solution.py:58
  29.6 3.1 %collective-permute-done.5 = bf16[528,128]{1,0:T(8,128)(2,1)S(1)} collective-permute-done((bf16[528,128]{1,0:T(8,128)(2,1)S(1)}, bf16[528,128]{1,0:T(8,128)(2,1)S(1)}, u32[]{:S(2)}, u32[]{:S(2)}) %collective-permute-start.5) | collective-permute-done | bytes 135200 | tf_op jit(solution)/shard_map/ppermute | solution.py:58
  32.7 3.0 %collective-permute-start.6 = (f32[512,128]{1,0:T(8,128)}, f32[512,128]{1,0:T(8,128)}, u32[]{:S(2)}, u32[]{:S(2)}) collective-permute-start(f32[512,128]{1,0:T(8,128)} %bitcast.57), channel_id=1, source_target_pairs={{8,0},{16,8},{24,16},{0,24},{9,1},{17,9},{25,17},{1,25},{10,2},{18... | collective-permute-start | bytes 786440 | tf_op jit(solution)/shard_map/ppermute | solution.py:58
  38.6 2.1 %bitcast_dynamic-update-slice_fusion.1 = (bf16[32,1,9,1,4,2,2,128]{7,0,6,5,4,3,2,1:T(8,128)(2,1)S(1)}, bf16[32,1,1,4,2,2,128]{6,0,5,4,3,2,1:T(8,128)(2,1)}, f32[32,1,1,4,2,2,128]{6,0,5,4,3,2,1:T(8,128)}) fusion(bf16[1,1,4,2,2,48,128]{6,5,4,3,2,1,0:T(8,128)(2,1)} %param.6, bf16[32,384]{1,0:T(8,128)(2,1)} %reshape.663, bf16[1,48,384]{2,1,0:T(8,128)(2,1)} %param.7, ...), kind=kOutput, calls=%fused_computation.132 | convolution fusion | flops 7669247 | bytes 1044480 | tf_op jit(solution)/shard_map/tbzyxjk,nj->ntbzyxk/dot_general | solution.py:97
  43.9 1.7 %fusion.134 = (bf16[32,1,1,3,2,2,128]{6,0,5,4,3,2,1:T(8,128)(2,1)}, bf16[32,1,1,3,2,2,128]{6,0,5,4,3,2,1:T(8,128)(2,1)}) fusion(bf16[32,1,1,4,2,2,128]{6,0,5,4,3,2,1:T(8,128)(2,1)} %get-tuple-element.29), kind=kLoop, calls=%fused_computation.249 | loop fusion | bytes 393216 | tf_op jit(solution)/shard_map/slice | solution.py:152
  46.5 1.6 fusion.103
  54.0 1.7 %fusion.126 = (bf16[384,128]{1,0:T(8,128)(2,1)}, bf16[384,128]{1,0:T(8,128)(2,1)}) fusion(bf16[912,128]{1,0:T(8,128)(2,1)} %collective-permute-done.1), kind=kLoop, calls=%fused_computation.241 | loop fusion | bytes 393216 | tf_op jit(solution)/shard_map/slice | solution.py:62
  69.3 1.7 %slice.298 = bf16[768,128]{1,0:T(8,128)(2,1)} slice(bf16[912,128]{1,0:T(8,128)(2,1)} %collective-permute-done.7), slice={[0:768], [0:128]} | slice | bytes 393216 | tf_op jit(solution)/shard_map/slice | solution.py:62
  86.4 3.8 %collective-permute-start.13 = (f32[512,128]{1,0:T(8,128)}, f32[512,128]{1,0:T(8,128)}, u32[]{:S(2)}, u32[]{:S(2)}) collective-permute-start(f32[512,128]{1,0:T(8,128)} %pad_maximum_fusion.7), channel_id=1, source_target_pairs={{8,0},{16,8},{24,16},{0,24},{9,1},{17,9},{25,17},{1,25},{10,2},{18... | collective-permute-start | bytes 786440 | tf_op jit(solution)/shard_map/ppermute | solution.py:58
  92.4 5.2 %all-to-all-start.1 = ((f32[32,2,32]{2,1,0:T(2,128)}), f32[32,2,32]{2,1,0:T(2,128)S(1)}, u32[]{:S(2)}, u32[]{:S(2)}) async-start(f32[32,2,32]{2,1,0:T(2,128)} %broadcast_in_dim.9), calls=%async_computation.1 | async-start | bytes 65536 | tf_op jit(solution)/shard_map/all_to_all | solution.py:14
  99.7 1.7 %collective-permute-start.11 = (f32[512,128]{1,0:T(8,128)}, f32[512,128]{1,0:T(8,128)}, u32[]{:S(2)}, u32[]{:S(2)}) collective-permute-start(f32[512,128]{1,0:T(8,128)} %pad_maximum_fusion.6), channel_id=1, source_target_pairs={{2,0},{3,1},{0,2},{1,3},{6,4},{7,5},{4,6},{5,7},{10,8},{11,9},{8,1... | collective-permute-start | bytes 786440 | tf_op jit(solution)/shard_map/ppermute | solution.py:58
  101.4 3.7 %all-to-all-done.1 = f32[32,2,32]{2,1,0:T(2,128)S(1)} async-done(((f32[32,2,32]{2,1,0:T(2,128)}), f32[32,2,32]{2,1,0:T(2,128)S(1)}, u32[]{:S(2)}, u32[]{:S(2)}) %all-to-all-start.1) | async-done | bytes 8224 | tf_op jit(solution)/shard_map/all_to_all | solution.py:14
  105.2 1.8 %convert_bitcast_fusion = (bf16[32,4,2,2,128]{4,0,3,2,1:T(8,128)(2,1)S(1)}, f32[32,1,1,4,2,2,128]{6,0,5,4,3,2,1:T(8,128)}) fusion(f32[32,1,1,4,2,2,128]{6,0,5,4,3,2,1:T(8,128)S(1)} %get-tuple-element.27, f32[32]{0:T(128)S(1)} %bitcast_divide_fusion.1, f32[32,1,1,4,2,2,128]{6,5,4,3,2,1,0:T(2,128)} %param.4), kind=kLoop, calls=%fused_computation.162 | loop fusion | flops 196608 | bytes 917632 | tf_op jit(solution)/shard_map/reshape.25
  108.2 4.1 %all-to-all-start.2 = ((bf16[32,2,768]{2,1,0:T(2,128)(2,1)}), bf16[32,2,768]{2,1,0:T(2,128)(2,1)S(1)}, u32[]{:S(2)}, u32[]{:S(2)}) async-start(bf16[32,2,768]{2,1,0:T(2,128)(2,1)} %reshape.742), calls=%async_computation.2 | async-start | bytes 196608 | tf_op jit(solution)/shard_map/all_to_all | solution.py:119
  112.9 7.0 %all-to-all-done.2 = bf16[32,2,768]{2,1,0:T(2,128)(2,1)S(1)} async-done(((bf16[32,2,768]{2,1,0:T(2,128)(2,1)}), bf16[32,2,768]{2,1,0:T(2,128)(2,1)S(1)}, u32[]{:S(2)}, u32[]{:S(2)}) %all-to-all-start.2) | async-done | bytes 98336 | tf_op jit(solution)/shard_map/all_to_all | solution.py:119
  123.0 2.2 %bitcast_dynamic-update-slice_fusion = (bf16[32,1,9,1,4,2,2,128]{7,0,6,5,4,3,2,1:T(8,128)(2,1)S(1)}, bf16[32,1,1,4,2,2,128]{6,0,5,4,3,2,1:T(8,128)(2,1)}, f32[32,1,1,4,2,2,128]{6,0,5,4,3,2,1:T(8,128)}) fusion(bf16[1,1,4,2,2,48,128]{6,5,4,3,2,1,0:T(8,128)(2,1)} %param.6, bf16[32,384]{1,0:T(8,128)(2,1)} %copy-done.17, bf16[1,48,384]{2,1,0:T(8,128)(2,1)} %param.7, ...), kind=kOutput, calls=%fused_computation.131 | convolution fusion | flops 7669247 | bytes 1044480 | tf_op jit(solution)/shard_map/tbzyxjk,nj->ntbzyxk/dot_general | solution.py:97
  125.2 1.6 slice_bitcast_fusion.4
  128.3 1.7 %fusion.132 = (bf16[32,1,1,3,2,2,128]{6,0,5,4,3,2,1:T(8,128)(2,1)}, bf16[32,1,1,3,2,2,128]{6,0,5,4,3,2,1:T(8,128)(2,1)}) fusion(bf16[32,1,1,4,2,2,128]{6,0,5,4,3,2,1:T(8,128)(2,1)} %get-tuple-element.24), kind=kLoop, calls=%fused_computation.247 | loop fusion | bytes 393216 | tf_op jit(solution)/shard_map/slice | solution.py:152
  130.0 1.7 %fusion.142 = f32[32,4,2,128]{3,0,2,1:T(8,128)} fusion(bf16[32,48,1,1]{1,0,3,2:T(8,128)(2,1)S(1)} %fusion.28, bf16[4,2,48,128]{3,2,1,0:T(8,128)(2,1)} %bitcast.464), kind=kOutput, calls=%fused_computation.253 | convolution fusion | flops 3145728 | bytes 232448 | tf_op jit(solution)/shard_map/tbzyxjk,nj->ntbzyxk/dot_general | solution.py:97
  140.0 1.7 %fusion.88 = (bf16[32,1,1,4,1,2,128]{6,0,5,3,4,2,1:T(8,128)(2,1)S(1)}, bf16[32,1,1,4,2,1,128]{6,0,4,3,5,2,1:T(8,128)(2,1)S(1)}, bf16[32,1,1,4,1,2,128]{6,0,5,3,4...) fusion(f32[32,4,2,128]{3,2,1,0:T(2,128)S(1)} %bitcast.483, f32[32,4,2,128]{3,2,1,0:T(2,128)} %bitcast.454, ...), kind=kOutput, calls=%fused_computation.175 | convolution fusion | flops 3801088 | bytes 1805440 | tf_op jit(solution)/shard_map/tbzyxjk,nj->ntbzyxk/dot_general | solution.py:97
  150.6 8.8 %all_to_all.20 = f32[32,1,128]{2,1,0:T(1,128)S(1)} all-to-all(f32[32,1,128]{2,1,0:T(1,128)S(1)} %reshape.744), channel_id=1, replica_groups=mesh['ta'=4,'xyz'=8] {'ta','xyz'}, dimensions={0} | all-to-all | bytes 32768 | tf_op jit(solution)/shard_map/all_to_all | solution.py:14
  (263 shorter events, 87.7 us)
Async XLA Ops:
  0.6 81.9 %copy-start = (bf16[1,1,4,2,2,9,64,128]{7,6,5,4,3,2,1,0:T(8,128)(2,1)S(1)}, bf16[1,1,4,2,2,9,64,128]{7,6,5,4,3,2,1,0:T(8,128)(2,1)}, u32[]{:S(2)}) copy-start(bf16[1,1,4,2,2,9,64,128]{7,6,5,4,3,2,1,0:T(8,128)(2,1)} %param.5) | copy-start | bytes 7077892
  5.4 57.7 %collective-permute-start.7 = (bf16[912,128]{1,0:T(8,128)(2,1)}, bf16[912,128]{1,0:T(8,128)(2,1)}, u32[]{:S(2)}, u32[]{:S(2)}) collective-permute-start(bf16[912,128]{1,0:T(8,128)(2,1)} %get-tuple-element.94), channel_id=1, source_target_pairs={{8,0},{16,8},{24,16},{0,24},{9,1},{17,9},{25,17},{1,25},{10,2},{18... | collective-permute-start | bytes 700424 | tf_op jit(solution)/shard_map/ppermute | solution.py:58
  10.4 56.1 %collective-permute-start.9 = (bf16[912,128]{1,0:T(8,128)(2,1)}, bf16[912,128]{1,0:T(8,128)(2,1)}, u32[]{:S(2)}, u32[]{:S(2)}) collective-permute-start(bf16[912,128]{1,0:T(8,128)(2,1)} %get-tuple-element.94), channel_id=1, source_target_pairs={{24,0},{0,8},{8,16},{16,24},{25,1},{1,9},{9,17},{17,25},{26,2},{2,... | collective-permute-start | bytes 700424 | tf_op jit(solution)/shard_map/ppermute | solution.py:58
  12.7 24.2 %all-to-all-start = ((bf16[32,2,768]{2,1,0:T(2,128)(2,1)}), bf16[32,2,768]{2,1,0:T(2,128)(2,1)S(1)}, u32[]{:S(2)}, u32[]{:S(2)}) async-start(bf16[32,2,768]{2,1,0:T(2,128)(2,1)} %reshape.740), calls=%async_computation | async-start | bytes 196608 | tf_op jit(solution)/shard_map/all_to_all | solution.py:119
  18.8 35.2 %collective-permute-start.1 = (bf16[912,128]{1,0:T(8,128)(2,1)}, bf16[912,128]{1,0:T(8,128)(2,1)}, u32[]{:S(2)}, u32[]{:S(2)}) collective-permute-start(bf16[912,128]{1,0:T(8,128)(2,1)} %get-tuple-element.96), channel_id=1, source_target_pairs={{1,0},{0,1},{3,2},{2,3},{5,4},{4,5},{7,6},{6,7},{9,8},{8,9},{11,10... | collective-permute-start | bytes 700424 | tf_op jit(solution)/shard_map/ppermute | solution.py:58
  19.1 39.4 %collective-permute-start.3 = (bf16[912,128]{1,0:T(8,128)(2,1)}, bf16[912,128]{1,0:T(8,128)(2,1)}, u32[]{:S(2)}, u32[]{:S(2)}) collective-permute-start(bf16[912,128]{1,0:T(8,128)(2,1)} %get-tuple-element.95), channel_id=1, source_target_pairs={{2,0},{3,1},{0,2},{1,3},{6,4},{7,5},{4,6},{5,7},{10,8},{11,9},{8,1... | collective-permute-start | bytes 700424 | tf_op jit(solution)/shard_map/ppermute | solution.py:58
  21.7 6.0 %collective-permute-start.4 = (f32[256,128]{1,0:T(8,128)S(1)}, f32[256,128]{1,0:T(8,128)S(1)}, u32[]{:S(2)}, u32[]{:S(2)}) collective-permute-start(f32[256,128]{1,0:T(8,128)S(1)} %pad_maximum_fusion.11), channel_id=1, source_target_pairs={{4,0},{5,1},{6,2},{7,3},{0,4},{1,5},{2,6},{3,7},{12,8},{13,9},{14,... | collective-permute-start | bytes 393224 | tf_op jit(solution)/shard_map/ppermute | solution.py:58
  27.7 5.0 %collective-permute-start.5 = (bf16[528,128]{1,0:T(8,128)(2,1)S(1)}, bf16[528,128]{1,0:T(8,128)(2,1)S(1)}, u32[]{:S(2)}, u32[]{:S(2)}) collective-permute-start(bf16[528,128]{1,0:T(8,128)(2,1)S(1)} %pad_maximum_fusion.10), channel_id=1, source_target_pairs={{4,0},{5,1},{6,2},{7,3},{0,4},{1,5},{2,6},{3,7},{12,8},{13,9},{14,... | collective-permute-start | bytes 405512 | tf_op jit(solution)/shard_map/ppermute | solution.py:58
  32.7 44.0 %collective-permute-start.6 = (f32[512,128]{1,0:T(8,128)}, f32[512,128]{1,0:T(8,128)}, u32[]{:S(2)}, u32[]{:S(2)}) collective-permute-start(f32[512,128]{1,0:T(8,128)} %bitcast.57), channel_id=1, source_target_pairs={{8,0},{16,8},{24,16},{0,24},{9,1},{17,9},{25,17},{1,25},{10,2},{18... | collective-permute-start | bytes 786440 | tf_op jit(solution)/shard_map/ppermute | solution.py:58
  54.0 24.2 %collective-permute-start.8 = (f32[512,128]{1,0:T(8,128)}, f32[512,128]{1,0:T(8,128)}, u32[]{:S(2)}, u32[]{:S(2)}) collective-permute-start(f32[512,128]{1,0:T(8,128)} %bitcast.57), channel_id=1, source_target_pairs={{24,0},{0,8},{8,16},{16,24},{25,1},{1,9},{9,17},{17,25},{26,2},{2,... | collective-permute-start | bytes 786440 | tf_op jit(solution)/shard_map/ppermute | solution.py:58
  58.5 15.1 %collective-permute-start = (f32[512,128]{1,0:T(8,128)}, f32[512,128]{1,0:T(8,128)}, u32[]{:S(2)}, u32[]{:S(2)}) collective-permute-start(f32[512,128]{1,0:T(8,128)} %pad_maximum_fusion.3), channel_id=1, source_target_pairs={{1,0},{0,1},{3,2},{2,3},{5,4},{4,5},{7,6},{6,7},{9,8},{8,9},{11,10... | collective-permute-start | bytes 786440 | tf_op jit(solution)/shard_map/ppermute | solution.py:58
  63.1 12.0 %collective-permute-start.2 = (f32[512,128]{1,0:T(8,128)}, f32[512,128]{1,0:T(8,128)}, u32[]{:S(2)}, u32[]{:S(2)}) collective-permute-start(f32[512,128]{1,0:T(8,128)} %pad_maximum_fusion.4), channel_id=1, source_target_pairs={{2,0},{3,1},{0,2},{1,3},{6,4},{7,5},{4,6},{5,7},{10,8},{11,9},{8,1... | collective-permute-start | bytes 786440 | tf_op jit(solution)/shard_map/ppermute | solution.py:58
  84.8 20.3 %copy-start.3 = (f32[32,1,1,4,2,2,128]{6,0,5,4,3,2,1:T(8,128)}, f32[32,1,1,4,2,2,128]{6,0,5,4,3,2,1:T(8,128)S(1)}, u32[]{:S(2)}) copy-start(f32[32,1,1,4,2,2,128]{6,0,5,4,3,2,1:T(8,128)S(1)} %get-tuple-element.27) | copy-start | bytes 786436
  86.4 55.6 %collective-permute-start.13 = (f32[512,128]{1,0:T(8,128)}, f32[512,128]{1,0:T(8,128)}, u32[]{:S(2)}, u32[]{:S(2)}) collective-permute-start(f32[512,128]{1,0:T(8,128)} %pad_maximum_fusion.7), channel_id=1, source_target_pairs={{8,0},{16,8},{24,16},{0,24},{9,1},{17,9},{25,17},{1,25},{10,2},{18... | collective-permute-start | bytes 786440 | tf_op jit(solution)/shard_map/ppermute | solution.py:58
  90.2 53.7 %collective-permute-start.14 = (f32[512,128]{1,0:T(8,128)}, f32[512,128]{1,0:T(8,128)}, u32[]{:S(2)}, u32[]{:S(2)}) collective-permute-start(f32[512,128]{1,0:T(8,128)} %pad_maximum_fusion.7), channel_id=1, source_target_pairs={{24,0},{0,8},{8,16},{16,24},{25,1},{1,9},{9,17},{17,25},{26,2},{2,... | collective-permute-start | bytes 786440 | tf_op jit(solution)/shard_map/ppermute | solution.py:58
  90.3 21.9 %collective-permute-start.12 = (f32[256,128]{1,0:T(8,128)S(1)}, f32[256,128]{1,0:T(8,128)S(1)}, u32[]{:S(2)}, u32[]{:S(2)}) collective-permute-start(f32[256,128]{1,0:T(8,128)S(1)} %pad_maximum_fusion.12), channel_id=1, source_target_pairs={{4,0},{5,1},{6,2},{7,3},{0,4},{1,5},{2,6},{3,7},{12,8},{13,9},{14,... | collective-permute-start | bytes 393224 | tf_op jit(solution)/shard_map/ppermute | solution.py:58
  92.4 12.7 %all-to-all-start.1 = ((f32[32,2,32]{2,1,0:T(2,128)}), f32[32,2,32]{2,1,0:T(2,128)S(1)}, u32[]{:S(2)}, u32[]{:S(2)}) async-start(f32[32,2,32]{2,1,0:T(2,128)} %broadcast_in_dim.9), calls=%async_computation.1 | async-start | bytes 65536 | tf_op jit(solution)/shard_map/all_to_all | solution.py:14
  98.5 39.4 %collective-permute-start.10 = (f32[512,128]{1,0:T(8,128)}, f32[512,128]{1,0:T(8,128)}, u32[]{:S(2)}, u32[]{:S(2)}) collective-permute-start(f32[512,128]{1,0:T(8,128)} %pad_maximum_fusion.5), channel_id=1, source_target_pairs={{1,0},{0,1},{3,2},{2,3},{5,4},{4,5},{7,6},{6,7},{9,8},{8,9},{11,10... | collective-permute-start | bytes 786440 | tf_op jit(solution)/shard_map/ppermute | solution.py:58
  99.7 39.2 %collective-permute-start.11 = (f32[512,128]{1,0:T(8,128)}, f32[512,128]{1,0:T(8,128)}, u32[]{:S(2)}, u32[]{:S(2)}) collective-permute-start(f32[512,128]{1,0:T(8,128)} %pad_maximum_fusion.6), channel_id=1, source_target_pairs={{2,0},{3,1},{0,2},{1,3},{6,4},{7,5},{4,6},{5,7},{10,8},{11,9},{8,1... | collective-permute-start | bytes 786440 | tf_op jit(solution)/shard_map/ppermute | solution.py:58
  106.9 14.2 %copy-start.29 = (bf16[48,384]{1,0:T(8,128)(2,1)S(1)}, bf16[48,384]{1,0:T(8,128)(2,1)}, u32[]{:S(2)}) copy-start(bf16[48,384]{1,0:T(8,128)(2,1)} %reshape.669) | copy-start | bytes 110596
  107.1 14.1 %copy-start.30 = (bf16[48,384]{1,0:T(8,128)(2,1)S(1)}, bf16[48,384]{1,0:T(8,128)(2,1)}, u32[]{:S(2)}) copy-start(bf16[48,384]{1,0:T(8,128)(2,1)} %reshape.678) | copy-start | bytes 110596
  107.1 14.3 %copy-start.14 = (bf16[384,128]{1,0:T(8,128)(2,1)S(1)}, bf16[384,128]{1,0:T(8,128)(2,1)}, u32[]{:S(2)}) copy-start(bf16[384,128]{1,0:T(8,128)(2,1)} %get-tuple-element.69) | copy-start | bytes 294916
  107.2 15.0 %copy-start.12 = (bf16[384,128]{1,0:T(8,128)(2,1)S(1)}, bf16[384,128]{1,0:T(8,128)(2,1)}, u32[]{:S(2)}) copy-start(bf16[384,128]{1,0:T(8,128)(2,1)} %get-tuple-element.68) | copy-start | bytes 294916
  108.2 11.7 %all-to-all-start.2 = ((bf16[32,2,768]{2,1,0:T(2,128)(2,1)}), bf16[32,2,768]{2,1,0:T(2,128)(2,1)S(1)}, u32[]{:S(2)}, u32[]{:S(2)}) async-start(bf16[32,2,768]{2,1,0:T(2,128)(2,1)} %reshape.742), calls=%async_computation.2 | async-start | bytes 196608 | tf_op jit(solution)/shard_map/all_to_all | solution.py:119
  (46 other events, 200.5 us)

commit v6 on v4

--- a/solution.py
+++ b/solution.py
@@ -32,13 +32,6 @@
     count = lax.axis_size("ta") * lax.axis_size("xyz")
     copies = jnp.broadcast_to(x[None], (count,) + x.shape)
     return jnp.sum(lax.all_to_all(copies, axes, 0, 0), axis=0)
-
-
-def gather_tiled(x, axis, dim):
-    count = lax.axis_size(axis)
-    copies = jnp.broadcast_to(x[None], (count,) + x.shape)
-    parts = lax.all_to_all(copies, axis, 0, 0)
-    return jnp.concatenate([parts[i] for i in range(count)], dim)
 
 
 def neighbour_source(device, stride, extent, step):
@@ -96,14 +89,23 @@
     return jnp.concatenate([result[0], result[1]], -1)
 
 
-def precondition(vector_in, null_vectors, coarse_inverse):
-    lowered = vector_in.astype(jnp.bfloat16)
-    coarse = jnp.einsum(
-        "tbzyxjk,ntbzyxk->nj", null_vectors, lowered, preferred_element_type=jnp.float32
-    ).astype(jnp.bfloat16)
-    inverse_rows = coarse_inverse[0]
+def restrict_exact(null_vectors, field):
+    return jnp.einsum(
+        "tbzyxjk,ntbzyxk->nj",
+        null_vectors.astype(jnp.float32),
+        field,
+        preferred_element_type=jnp.float32,
+        precision=lax.Precision.HIGHEST,
+    )
+
+
+def slab_columns(parts):
+    return jnp.transpose(parts, (1, 0, 2)).reshape(parts.shape[1], -1)
+
+
+def finish(vector_in, slab, null_vectors, inverse_rows):
     correction = lax.dot_general(
-        gather_tiled(coarse, "xyz", 1),
+        slab,
         inverse_rows,
         (((1,), (1,)), ((), ())),
         preferred_element_type=jnp.float32,
@@ -122,20 +124,61 @@
     return weights[:, None, None, None, None, None, None] * vector_in
 
 
-def pair_products(image, residual):
-    both = total_sum(jnp.stack([inner_rows(image, image), inner_rows(image, residual)]))
-    return (both[0], both[1])
-
-
 def shards(right_side, coarse_links, null_vectors, coarse_inverse):
+    inverse_rows = coarse_inverse[0]
+    slabs_total = lax.axis_size("ta")
+    blocks_total = lax.axis_size("xyz")
     residual = right_side
-    direction_a = precondition(residual, null_vectors, coarse_inverse)
+    coarse = jnp.einsum(
+        "tbzyxjk,ntbzyxk->nj",
+        null_vectors,
+        residual.astype(jnp.bfloat16),
+        preferred_element_type=jnp.float32,
+    ).astype(jnp.bfloat16)
+    width = coarse.shape[1]
+    payload = jnp.concatenate(
+        [coarse.astype(jnp.float32), restrict_exact(null_vectors, residual)], 1
+    )
+    parts = lax.all_to_all(
+        jnp.broadcast_to(payload[None], (blocks_total,) + payload.shape), "xyz", 0, 0
+    )
+    slab_a = slab_columns(parts[:, :, :width]).astype(jnp.bfloat16)
+    slab_residual = slab_columns(parts[:, :, width:])
+    direction_a = finish(residual, slab_a, null_vectors, inverse_rows)
     image_a = apply_links(coarse_links, direction_a.astype(jnp.bfloat16))
-    norm_a, correlation_a = pair_products(image_a, residual)
+    image_coarse = restrict_exact(null_vectors, image_a)
+    pair_local = jnp.stack([inner_rows(image_a, image_a), inner_rows(image_a, residual)], 1)
+    if slabs_total * blocks_total <= 64:
+        local = jnp.concatenate([pair_local, image_coarse], 1)
+        gathered = lax.all_to_all(
+            jnp.broadcast_to(local[None], (slabs_total * blocks_total,) + local.shape),
+            ("ta", "xyz"),
+            0,
+            0,
+        )
+        pair = jnp.sum(gathered[:, :, :2], axis=0)
+        image_slabs = gathered[:, :, 2:].reshape(
+            (slabs_total, blocks_total) + image_coarse.shape
+        )
+        slab_image = slab_columns(
+            lax.dynamic_index_in_dim(image_slabs, lax.axis_index("ta"), 0, keepdims=False)
+        )
+    else:
+        pair = total_sum(pair_local)
+        slab_image = slab_columns(
+            lax.all_to_all(
+                jnp.broadcast_to(image_coarse[None], (blocks_total,) + image_coarse.shape),
+                "xyz",
+                0,
+                0,
+            )
+        )
+    norm_a, correlation_a = pair[:, 0], pair[:, 1]
     step_a = correlation_a / (norm_a + EPS)
     solution = scaled(step_a, direction_a)
     residual = residual - scaled(step_a, image_a)
-    direction_b = precondition(residual, null_vectors, coarse_inverse)
+    slab_b = (slab_residual - step_a[:, None] * slab_image).astype(jnp.bfloat16)
+    direction_b = finish(residual, slab_b, null_vectors, inverse_rows)
     image_b = apply_links(coarse_links, direction_b.astype(jnp.bfloat16))
     sums = total_sum(
         jnp.stack(

time: 92 us -> 81.3 us (0.88)
  blocking collectives: 38.5 us -> 20.5 us
  waiting for transfers between devices: 12.5 us -> 21.7 us
  local copies, waits for them, and re-layouts: 15.2 us -> 8.41 us
  starting transfers between devices: 8.32 us -> 11.7 us
  other arithmetic: 8.44 us -> 10.1 us
    all_to_all x2 -> x1, blocking collectives: 21.5 us -> 10 us  [total_sum(): return jnp.sum(lax.all_to_all(copies, axes, 0, 0), axis=0)]
    all_to_all x0 -> x1, waiting for transfers between devices: none -> 9.37 us  [shards(): lax.all_to_all(jnp.broadcast_to(local[None], (slabs_total * blocks_total,...]
    ppermute x2, waiting for transfers between devices: 6.58 us -> 0.01 us  [both_sides(): from_upper = lax.ppermute(first, axis, up)]
    all_to_all x2 -> x1, blocking collectives: 16.9 us -> 10.5 us  [shards(): lax.all_to_all(jnp.broadcast_to(payload[None], (blocks_total,) + payload....]
    ppermute x6, waiting for transfers between devices: 0.84 us -> 6.84 us  [both_sides(): pair = lax.ppermute(jnp.concatenate([first, last], which), axis, perm)]
    slice x6, local copies, waits for them, and re-layouts: 5.2 us -> 0.05 us  [both_sides(): first = lax.slice_in_dim(lowered, 0, 1, axis=which)]
    all_to_all x0 -> x1, starting transfers between devices: none -> 2.73 us  [shards(): lax.all_to_all(jnp.broadcast_to(local[None], (slabs_total * blocks_total,...]
    slice x2, local copies, waits for them, and re-layouts: 1.96 us -> 0.04 us  [both_sides(): lax.slice_in_dim(lowered, 0, length - 1, axis=which)]
  transfers between devices with their start and end apart: 10 -> 11, of which waited for: 6 -> 5; matrix products, arithmetic and copies ran while one was open for 7% -> 1% of each run, Pallas kernels for 0% -> 0%
where the time goes in v6:
time: 81.3 us; the launch traced here: 80.9 us
  waiting for transfers between devices  21.7 us (27%)
  blocking collectives  20.5 us (25%)
  starting transfers between devices  11.7 us (14%)
  other arithmetic  10.1 us (12%)
  local copies, waits for them, and re-layouts  8.41 us (10%)
  matrix products  7.36 us (9%)
  between operations  1.19 us (1%)
    all_to_all x1, blocking collectives, shards(): lax.all_to_all(jnp.broadcast_to(payload[None], (blocks_total,) + payload....  10.5 us
    all_to_all x1, blocking collectives, total_sum(): return jnp.sum(lax.all_to_all(copies, axes, 0, 0), axis=0)  10 us
    all_to_all x1, waiting for transfers between devices, shards(): lax.all_to_all(jnp.broadcast_to(local[None], (slabs_total * blocks_total,...  9.37 us
    ppermute x6, waiting for transfers between devices, both_sides(): pair = lax.ppermute(jnp.concatenate([first, last], which), axis, perm)  6.84 us
    ppermute x2, waiting for transfers between devices, both_sides(): from_lower = lax.ppermute(last, axis, down)  5.44 us
    ppermute x2, starting transfers between devices, both_sides(): from_upper = lax.ppermute(first, axis, up)  5.19 us
    unnamed x20, local copies, waits for them, and re-layouts  5.11 us
    ppermute x6, starting transfers between devices, both_sides(): pair = lax.ppermute(jnp.concatenate([first, last], which), axis, perm)  3.3 us
  transfers between devices with their start and end apart: 11, of which 5 were waited for; matrix products, arithmetic and copies ran while one was open for 1% of the time, Pallas kernels for 0%

profile of v6, /device:TPU:0, one launch (start us, length us, event | category | flops | bytes accessed | tf_op | source)
XLA Modules:
  0.0 80.9 jit_solution(15030518188696629143)
XLA Ops:
  0.7 1.2 %convert_bitcast_fusion = bf16[32,4,2,2,128]{4,3,2,1,0:T(2,128)(2,1)S(1)} fusion(f32[32,1,1,4,2,2,128]{6,5,4,3,2,1,0:T(2,128)} %param.4), kind=kLoop, calls=%fused_computation.85 | loop fusion | flops 65536 | bytes 393216 | tf_op jit(solution)/shard_map/reshape
  1.9 1.3 %convolution_bitcast_fusion.4 = f32[32,48]{1,0:T(8,128)S(1)} fusion(f32[32,4,2,2,128]{4,3,2,1,0:T(2,128)} %bitcast.238, bf16[1,1,4,2,2,48,128]{6,5,4,3,2,1,0:T(8,128)(2,1)} %param.6), kind=kOutput, calls=%fused_computation.22 | convolution fusion | flops 37748736 | bytes 464896 | tf_op jit(solution)/shard_map/tbzyxjk,ntbzyxk->nj/dot_general | solution.py:93
  3.2 1.1 %fusion.19 = f32[32,48]{1,0:T(8,128)S(1)} fusion(bf16[32,4,2,2,128]{4,3,2,1,0:T(2,128)(2,1)S(1)} %convert_bitcast_fusion, bf16[1,1,4,2,2,48,128]{6,5,4,3,2,1,0:T(8,128)(2,1)} %param.6), kind=kOutput, calls=%fused_computation.24 | convolution fusion | flops 6294528 | bytes 333824 | tf_op jit(solution)/shard_map/tbzyxjk,ntbzyxk->nj/dot_general | solution.py:132
  4.4 10.5 %all_to_all.15 = f32[8,32,96]{2,1,0:T(8,128)S(1)} all-to-all(f32[8,32,96]{2,1,0:T(8,128)S(1)} %broadcast_in_dim.6), channel_id=1, replica_groups=mesh['ta'=4,'xyz'=8] {'xyz'}, dimensions={0} | all-to-all | bytes 196608 | tf_op jit(solution)/shard_map/all_to_all | solution.py:142
  15.1 1.0 %bitcast_dynamic-update-slice_fusion.5 = (bf16[32,1,9,1,4,2,2,128]{7,0,6,5,4,3,2,1:T(8,128)(2,1)}, bf16[32,1,1,4,2,2,128]{6,0,5,4,3,2,1:T(8,128)(2,1)S(1)}, f32[32,1,1,4,2,2,128]{6,0,5,4,3,2,1:T(8,128)}) fusion(bf16[1,1,4,2,2,48,128]{6,5,4,3,2,1,0:T(8,128)(2,1)S(1)} %copy-done.4, bf16[32,384]{1,0:T(8,128)(2,1)S(1)} %convert_element_type.43, ...), kind=kOutput, calls=%fused_computation.83 | convolution fusion | flops 7669247 | bytes 1044480 | tf_op jit(solution)/shard_map/tbzyxjk,nj->ntbzyxk/dot_general | solution.py:113
  16.8 3.6 %collective-permute-start.3 = (bf16[32,1,1,4,2,2,128]{6,0,5,4,3,2,1:T(8,128)(2,1)S(1)}, bf16[32,1,1,4,2,2,128]{6,0,5,4,3,2,1:T(8,128)(2,1)S(1)}, u32[]{:S(2)}, u32[]{:S(2)}) collective-permute-start(bf16[32,1,1,4,2,2,128]{6,0,5,4,3,2,1:T(8,128)(2,1)S(1)} %get-tuple-element.34), channel_id=1, source_target_pairs={{8,0},{16,8},{24,16},{0,24},{9,1},{17,9},{25,17},{1,25},{10,2},{18... | collective-permute-start | bytes 393224 | tf_op jit(solution)/shard_map/ppermute | solution.py:60
  21.1 3.9 %collective-permute-done.2 = bf16[32,1,1,2,2,2,128]{6,0,5,4,3,2,1:T(8,128)(2,1)S(1)} collective-permute-done((bf16[32,1,1,2,2,2,128]{6,0,5,4,3,2,1:T(8,128)(2,1)S(1)}, bf16[32,1,1,2,2,2,128]{6,0,5,4,3,2,1:T(8,128)(2,1)S(1)}, u32[]{:S(2)}, u32[]{:S(2)}) %collective-permute-start.2) | collective-permute-done | bytes 65568 | tf_op jit(solution)/shard_map/ppermute | solution.py:54
  25.3 2.8 %collective-permute-done.4 = bf16[32,1,1,4,2,2,128]{6,0,5,4,3,2,1:T(8,128)(2,1)S(1)} collective-permute-done((bf16[32,1,1,4,2,2,128]{6,0,5,4,3,2,1:T(8,128)(2,1)S(1)}, bf16[32,1,1,4,2,2,128]{6,0,5,4,3,2,1:T(8,128)(2,1)S(1)}, u32[]{:S(2)}, u32[]{:S(2)}) %collective-permute-start.4) | collective-permute-done | bytes 131104 | tf_op jit(solution)/shard_map/ppermute | solution.py:61
  30.5 0.8 %fusion.6 = f32[2,32,1,1,4,2,2,64]{7,1,6,5,4,3,2,0:T(8,128)S(1)} fusion(bf16[1,1,4,2,2,9,64,128]{7,6,5,4,3,2,1,0:T(8,128)(2,1)S(1)} %copy-done, bf16[1,32,1,9,1,4,2,2,128]{8,1,7,6,5,3,4,2,0:T(8,128)(2,1)S(1)} %maximum_bitcast_fusion.3, bf16[1,32,1,9,1,4,2,2,128]{8,1,7,6,5,3,4,2,0:T(8,128)(2,1)S(1)} %maximum_bitcast_fusion.2), kind=kOutput, calls=%fused_computation.8 | convolution fusion | flops 152174592 | bytes 4980736 | tf_op jit(solution)/shard_map/tbzyxdik,pntdbzyxk->pntbzyxi/dot_general | solution.py:86
  32.3 1.4 %reshape.379 = f32[32,1,1600]{2,1,0:T(1,128)} reshape(f32[32,32,50]{2,1,0:T(8,128)S(1)} %broadcast_in_dim.7) | data formatting | bytes 409600
  33.6 2.7 %all-to-all-start.1 = ((f32[32,1,1600]{2,1,0:T(1,128)}), f32[32,1,1600]{2,1,0:T(1,128)S(1)}, u32[]{:S(2)}, u32[]{:S(2)}) async-start(f32[32,1,1600]{2,1,0:T(1,128)} %reshape.379), calls=%async_computation.1 | async-start | bytes 425984 | tf_op jit(solution)/shard_map/all_to_all | solution.py:153
  36.4 9.4 %all-to-all-done.1 = f32[32,1,1600]{2,1,0:T(1,128)S(1)} async-done(((f32[32,1,1600]{2,1,0:T(1,128)}), f32[32,1,1600]{2,1,0:T(1,128)S(1)}, u32[]{:S(2)}, u32[]{:S(2)}) %all-to-all-start.1) | async-done | bytes 204832 | tf_op jit(solution)/shard_map/all_to_all | solution.py:153
  46.3 1.9 %reduce.6 = f32[32,1600]{1,0:T(8,128)} reduce(f32[32,1,1600]{2,1,0:T(1,128)S(1)} %all-to-all-done.1, f32[]{:T(128)} %broadcast.79), dimensions={1}, to_apply=%all_to_all.10.reduce_sub_computation | reduce | bytes 409604 | tf_op jit(solution)/shard_map/all_to_all | solution.py:153
  48.2 1.7 %reshape.380 = f32[32,32,50]{2,1,0:T(8,128)S(1)} reshape(f32[32,1600]{1,0:T(8,128)} %reduce.6) | data formatting | bytes 409600
  50.6 1.9 %bitcast_dynamic-update-slice_fusion.2 = (bf16[32,1,9,1,4,2,2,128]{7,0,6,5,4,3,2,1:T(8,128)(2,1)}, bf16[32,1,1,4,2,2,128]{6,0,5,4,3,2,1:T(8,128)(2,1)S(1)}, f32[32,1,1,4,2,2,128]{6,0,5,4,3,2,1:T(8,128)S(1)}) fusion(bf16[1,1,4,2,2,48,128]{6,5,4,3,2,1,0:T(8,128)(2,1)} %param.6, bf16[32,384]{1,0:T(8,128)(2,1)S(1)} %convert_element_type.48, ...), kind=kOutput, calls=%fused_computation.79 | convolution fusion | flops 7800319 | bytes 1306752 | tf_op jit(solution)/shard_map/tbzyxjk,nj->ntbzyxk/dot_general | solution.py:113
  53.2 1.6 %collective-permute-start.8 = (bf16[32,1,1,4,2,2,128]{6,0,5,4,3,2,1:T(8,128)(2,1)S(1)}, bf16[32,1,1,4,2,2,128]{6,0,5,4,3,2,1:T(8,128)(2,1)S(1)}, u32[]{:S(2)}, u32[]{:S(2)}) collective-permute-start(bf16[32,1,1,4,2,2,128]{6,0,5,4,3,2,1:T(8,128)(2,1)S(1)} %get-tuple-element.31), channel_id=1, source_target_pairs={{8,0},{16,8},{24,16},{0,24},{9,1},{17,9},{25,17},{1,25},{10,2},{18... | collective-permute-start | bytes 393224 | tf_op jit(solution)/shard_map/ppermute | solution.py:60
  55.3 1.4 %collective-permute-start.7 = (bf16[32,1,1,2,2,2,128]{6,0,5,4,3,2,1:T(8,128)(2,1)S(1)}, bf16[32,1,1,2,2,2,128]{6,0,5,4,3,2,1:T(8,128)(2,1)S(1)}, u32[]{:S(2)}, u32[]{:S(2)}) collective-permute-start(bf16[32,1,1,2,2,2,128]{6,0,5,4,3,2,1:T(8,128)(2,1)S(1)} %pad_maximum_fusion.3), channel_id=1, source_target_pairs={{4,0},{5,1},{6,2},{7,3},{0,4},{1,5},{2,6},{3,7},{12,8},{13,9},{14,... | collective-permute-start | bytes 196616 | tf_op jit(solution)/shard_map/ppermute | solution.py:54
  56.7 2.9 %collective-permute-done.7 = bf16[32,1,1,2,2,2,128]{6,0,5,4,3,2,1:T(8,128)(2,1)S(1)} collective-permute-done((bf16[32,1,1,2,2,2,128]{6,0,5,4,3,2,1:T(8,128)(2,1)S(1)}, bf16[32,1,1,2,2,2,128]{6,0,5,4,3,2,1:T(8,128)(2,1)S(1)}, u32[]{:S(2)}, u32[]{:S(2)}) %collective-permute-start.7) | collective-permute-done | bytes 65568 | tf_op jit(solution)/shard_map/ppermute | solution.py:54
  59.9 2.6 %collective-permute-done.9 = bf16[32,1,1,4,2,2,128]{6,0,5,4,3,2,1:T(8,128)(2,1)S(1)} collective-permute-done((bf16[32,1,1,4,2,2,128]{6,0,5,4,3,2,1:T(8,128)(2,1)S(1)}, bf16[32,1,1,4,2,2,128]{6,0,5,4,3,2,1:T(8,128)(2,1)S(1)}, u32[]{:S(2)}, u32[]{:S(2)}) %collective-permute-start.9) | collective-permute-done | bytes 131104 | tf_op jit(solution)/shard_map/ppermute | solution.py:61
  65.6 0.8 %fusion.11 = f32[2,32,1,1,4,2,2,64]{7,1,6,5,4,3,2,0:T(8,128)S(1)} fusion(bf16[1,1,4,2,2,9,64,128]{7,6,5,4,3,2,1,0:T(8,128)(2,1)S(1)} %copy-done, bf16[1,32,1,9,1,4,2,2,128]{8,1,7,6,5,3,4,2,0:T(8,128)(2,1)S(1)} %maximum_bitcast_fusion.5, bf16[1,32,1,9,1,4,2,2,128]{8,1,7,6,5,3,4,2,0:T(8,128)(2,1)S(1)} %maximum_bitcast_fusion.4), kind=kOutput, calls=%fused_computation.9 | convolution fusion | flops 152174592 | bytes 4980736 | tf_op jit(solution)/shard_map/tbzyxdik,pntdbzyxk->pntbzyxi/dot_general | solution.py:86
  67.0 10.0 %all_to_all.16 = f32[32,1,128]{2,1,0:T(1,128)S(1)} all-to-all(f32[32,1,128]{2,1,0:T(1,128)S(1)} %reshape.381), channel_id=1, replica_groups=mesh['ta'=4,'xyz'=8] {'ta','xyz'}, dimensions={0} | all-to-all | bytes 32768 | tf_op jit(solution)/shard_map/all_to_all | solution.py:34
  77.9 1.2 %multiply_subtract_fusion = (f32[32,1,1,4,2,2,128]{6,0,5,4,3,2,1:T(8,128)S(1)}, f32[32,1,1,4,2,2,128]{6,0,5,4,3,2,1:T(8,128)S(1)}) fusion(f32[32,1,1,4,2,2,128]{6,0,5,4,3,2,1:T(8,128)S(1)} %get-tuple-element.29, f32[32,1,1,4,2,2,128]{6,0,5,4,3,2,1:T(8,128)S(1)} %get-tuple-element.32, f32[32]{0:T(128)S(1)} %get-tuple-element.28, f32[32]{0:T(128)S(1)} %get-tuple-element.27, ...), kind=kLoop, calls=%fused_computation.38 | loop fusion | flops 720896 | bytes 1835392 | tf_op jit(solution)/shard_map/sub | solution.py:205
  79.1 0.9 %copy.200 = f32[32,1,1,4,2,2,128]{6,5,4,3,2,1,0:T(2,128)} copy(f32[32,1,1,4,2,2,128]{6,0,5,4,3,2,1:T(8,128)S(1)} %get-tuple-element.71) | data formatting | bytes 524288
  80.0 0.9 %copy.199 = f32[32,1,1,4,2,2,128]{6,5,4,3,2,1,0:T(2,128)} copy(f32[32,1,1,4,2,2,128]{6,0,5,4,3,2,1:T(8,128)S(1)} %get-tuple-element.72) | data formatting | bytes 524288
  (95 shorter events, 12.0 us)
Async XLA Ops:
  0.6 29.9 %copy-start = (bf16[1,1,4,2,2,9,64,128]{7,6,5,4,3,2,1,0:T(8,128)(2,1)S(1)}, bf16[1,1,4,2,2,9,64,128]{7,6,5,4,3,2,1,0:T(8,128)(2,1)}, u32[]{:S(2)}) copy-start(bf16[1,1,4,2,2,9,64,128]{7,6,5,4,3,2,1,0:T(8,128)(2,1)} %param.5) | copy-start | bytes 7077892
  0.6 14.4 %copy-start.1 = (f32[32,1,1,4,2,2,128]{6,5,4,3,2,1,0:T(2,128)S(1)}, f32[32,1,1,4,2,2,128]{6,5,4,3,2,1,0:T(2,128)}, u32[]{:S(2)}) copy-start(f32[32,1,1,4,2,2,128]{6,5,4,3,2,1,0:T(2,128)} %param.4) | copy-start | bytes 786436
  0.7 14.4 %copy-start.4 = (bf16[1,1,4,2,2,48,128]{6,5,4,3,2,1,0:T(8,128)(2,1)S(1)}, bf16[1,1,4,2,2,48,128]{6,5,4,3,2,1,0:T(8,128)(2,1)}, u32[]{:S(2)}) copy-start(bf16[1,1,4,2,2,48,128]{6,5,4,3,2,1,0:T(8,128)(2,1)} %param.6) | copy-start | bytes 589828
  0.7 14.4 %copy-start.5 = (bf16[1,48,384]{2,1,0:T(8,128)(2,1)S(1)}, bf16[1,48,384]{2,1,0:T(8,128)(2,1)}, u32[]{:S(2)}) copy-start(bf16[1,48,384]{2,1,0:T(8,128)(2,1)} %param.7) | copy-start | bytes 110596
  16.2 8.9 %copy-start.3 = (bf16[32,1,9,1,4,2,2,128]{7,0,6,5,4,3,2,1:T(8,128)(2,1)S(1)}, bf16[32,1,9,1,4,2,2,128]{7,0,6,5,4,3,2,1:T(8,128)(2,1)}, u32[]{:S(2)}) copy-start(bf16[32,1,9,1,4,2,2,128]{7,0,6,5,4,3,2,1:T(8,128)(2,1)} %get-tuple-element.33) | copy-start | bytes 3538948
  16.2 8.9 %collective-permute-start.1 = (bf16[32,1,1,4,2,2,128]{6,0,5,4,3,2,1:T(8,128)(2,1)S(1)}, bf16[32,1,1,4,2,2,128]{6,0,5,4,3,2,1:T(8,128)(2,1)S(1)}, u32[]{:S(2)}, u32[]{:S(2)}) collective-permute-start(bf16[32,1,1,4,2,2,128]{6,0,5,4,3,2,1:T(8,128)(2,1)S(1)} %get-tuple-element.34), channel_id=1, source_target_pairs={{2,0},{3,1},{0,2},{1,3},{6,4},{7,5},{4,6},{5,7},{10,8},{11,9},{8,1... | collective-permute-start | bytes 393224 | tf_op jit(solution)/shard_map/ppermute | solution.py:54
  16.8 8.5 %collective-permute-start.3 = (bf16[32,1,1,4,2,2,128]{6,0,5,4,3,2,1:T(8,128)(2,1)S(1)}, bf16[32,1,1,4,2,2,128]{6,0,5,4,3,2,1:T(8,128)(2,1)S(1)}, u32[]{:S(2)}, u32[]{:S(2)}) collective-permute-start(bf16[32,1,1,4,2,2,128]{6,0,5,4,3,2,1:T(8,128)(2,1)S(1)} %get-tuple-element.34), channel_id=1, source_target_pairs={{8,0},{16,8},{24,16},{0,24},{9,1},{17,9},{25,17},{1,25},{10,2},{18... | collective-permute-start | bytes 393224 | tf_op jit(solution)/shard_map/ppermute | solution.py:60
  20.4 4.6 %collective-permute-start = (bf16[32,1,1,4,2,2,128]{6,0,5,4,3,2,1:T(8,128)(2,1)S(1)}, bf16[32,1,1,4,2,2,128]{6,0,5,4,3,2,1:T(8,128)(2,1)S(1)}, u32[]{:S(2)}, u32[]{:S(2)}) collective-permute-start(bf16[32,1,1,4,2,2,128]{6,0,5,4,3,2,1:T(8,128)(2,1)S(1)} %get-tuple-element.34), channel_id=1, source_target_pairs={{1,0},{0,1},{3,2},{2,3},{5,4},{4,5},{7,6},{6,7},{9,8},{8,9},{11,10... | collective-permute-start | bytes 393224 | tf_op jit(solution)/shard_map/ppermute | solution.py:54
  20.4 7.7 %collective-permute-start.4 = (bf16[32,1,1,4,2,2,128]{6,0,5,4,3,2,1:T(8,128)(2,1)S(1)}, bf16[32,1,1,4,2,2,128]{6,0,5,4,3,2,1:T(8,128)(2,1)S(1)}, u32[]{:S(2)}, u32[]{:S(2)}) collective-permute-start(bf16[32,1,1,4,2,2,128]{6,0,5,4,3,2,1:T(8,128)(2,1)S(1)} %get-tuple-element.34), channel_id=1, source_target_pairs={{24,0},{0,8},{8,16},{16,24},{25,1},{1,9},{9,17},{17,25},{26,2},{2,... | collective-permute-start | bytes 393224 | tf_op jit(solution)/shard_map/ppermute | solution.py:61
  20.5 4.6 %collective-permute-start.2 = (bf16[32,1,1,2,2,2,128]{6,0,5,4,3,2,1:T(8,128)(2,1)S(1)}, bf16[32,1,1,2,2,2,128]{6,0,5,4,3,2,1:T(8,128)(2,1)S(1)}, u32[]{:S(2)}, u32[]{:S(2)}) collective-permute-start(bf16[32,1,1,2,2,2,128]{6,0,5,4,3,2,1:T(8,128)(2,1)S(1)} %pad_maximum_fusion.2), channel_id=1, source_target_pairs={{4,0},{5,1},{6,2},{7,3},{0,4},{1,5},{2,6},{3,7},{12,8},{13,9},{14,... | collective-permute-start | bytes 196616 | tf_op jit(solution)/shard_map/ppermute | solution.py:54
  33.6 12.1 %all-to-all-start.1 = ((f32[32,1,1600]{2,1,0:T(1,128)}), f32[32,1,1600]{2,1,0:T(1,128)S(1)}, u32[]{:S(2)}, u32[]{:S(2)}) async-start(f32[32,1,1600]{2,1,0:T(1,128)} %reshape.379), calls=%async_computation.1 | async-start | bytes 425984 | tf_op jit(solution)/shard_map/all_to_all | solution.py:153
  52.5 7.1 %copy-start.2 = (bf16[32,1,9,1,4,2,2,128]{7,0,6,5,4,3,2,1:T(8,128)(2,1)S(1)}, bf16[32,1,9,1,4,2,2,128]{7,0,6,5,4,3,2,1:T(8,128)(2,1)}, u32[]{:S(2)}) copy-start(bf16[32,1,9,1,4,2,2,128]{7,0,6,5,4,3,2,1:T(8,128)(2,1)} %get-tuple-element.30) | copy-start | bytes 3538948
  52.6 7.1 %collective-permute-start.6 = (bf16[32,1,1,4,2,2,128]{6,0,5,4,3,2,1:T(8,128)(2,1)S(1)}, bf16[32,1,1,4,2,2,128]{6,0,5,4,3,2,1:T(8,128)(2,1)S(1)}, u32[]{:S(2)}, u32[]{:S(2)}) collective-permute-start(bf16[32,1,1,4,2,2,128]{6,0,5,4,3,2,1:T(8,128)(2,1)S(1)} %get-tuple-element.31), channel_id=1, source_target_pairs={{2,0},{3,1},{0,2},{1,3},{6,4},{7,5},{4,6},{5,7},{10,8},{11,9},{8,1... | collective-permute-start | bytes 393224 | tf_op jit(solution)/shard_map/ppermute | solution.py:54
  53.2 6.6 %collective-permute-start.8 = (bf16[32,1,1,4,2,2,128]{6,0,5,4,3,2,1:T(8,128)(2,1)S(1)}, bf16[32,1,1,4,2,2,128]{6,0,5,4,3,2,1:T(8,128)(2,1)S(1)}, u32[]{:S(2)}, u32[]{:S(2)}) collective-permute-start(bf16[32,1,1,4,2,2,128]{6,0,5,4,3,2,1:T(8,128)(2,1)S(1)} %get-tuple-element.31), channel_id=1, source_target_pairs={{8,0},{16,8},{24,16},{0,24},{9,1},{17,9},{25,17},{1,25},{10,2},{18... | collective-permute-start | bytes 393224 | tf_op jit(solution)/shard_map/ppermute | solution.py:60
  54.8 4.8 %collective-permute-start.5 = (bf16[32,1,1,4,2,2,128]{6,0,5,4,3,2,1:T(8,128)(2,1)S(1)}, bf16[32,1,1,4,2,2,128]{6,0,5,4,3,2,1:T(8,128)(2,1)S(1)}, u32[]{:S(2)}, u32[]{:S(2)}) collective-permute-start(bf16[32,1,1,4,2,2,128]{6,0,5,4,3,2,1:T(8,128)(2,1)S(1)} %get-tuple-element.31), channel_id=1, source_target_pairs={{1,0},{0,1},{3,2},{2,3},{5,4},{4,5},{7,6},{6,7},{9,8},{8,9},{11,10... | collective-permute-start | bytes 393224 | tf_op jit(solution)/shard_map/ppermute | solution.py:54
  54.8 7.7 %collective-permute-start.9 = (bf16[32,1,1,4,2,2,128]{6,0,5,4,3,2,1:T(8,128)(2,1)S(1)}, bf16[32,1,1,4,2,2,128]{6,0,5,4,3,2,1:T(8,128)(2,1)S(1)}, u32[]{:S(2)}, u32[]{:S(2)}) collective-permute-start(bf16[32,1,1,4,2,2,128]{6,0,5,4,3,2,1:T(8,128)(2,1)S(1)} %get-tuple-element.31), channel_id=1, source_target_pairs={{24,0},{0,8},{8,16},{16,24},{25,1},{1,9},{9,17},{17,25},{26,2},{2,... | collective-permute-start | bytes 393224 | tf_op jit(solution)/shard_map/ppermute | solution.py:61
  55.3 4.3 %collective-permute-start.7 = (bf16[32,1,1,2,2,2,128]{6,0,5,4,3,2,1:T(8,128)(2,1)S(1)}, bf16[32,1,1,2,2,2,128]{6,0,5,4,3,2,1:T(8,128)(2,1)S(1)}, u32[]{:S(2)}, u32[]{:S(2)}) collective-permute-start(bf16[32,1,1,2,2,2,128]{6,0,5,4,3,2,1:T(8,128)(2,1)S(1)} %pad_maximum_fusion.3), channel_id=1, source_target_pairs={{4,0},{5,1},{6,2},{7,3},{0,4},{1,5},{2,6},{3,7},{12,8},{13,9},{14,... | collective-permute-start | bytes 196616 | tf_op jit(solution)/shard_map/ppermute | solution.py:54

commit v7 on v6

--- a/solution.py
+++ b/solution.py
@@ -91,7 +91,7 @@
 
 def restrict_exact(null_vectors, field):
     return jnp.einsum(
-        "tbzyxjk,ntbzyxk->nj",
+        "tbzyxjk,ntbzyxk->jn",
         null_vectors.astype(jnp.float32),
         field,
         preferred_element_type=jnp.float32,
@@ -99,15 +99,11 @@
     )
 
 
-def slab_columns(parts):
-    return jnp.transpose(parts, (1, 0, 2)).reshape(parts.shape[1], -1)
-
-
-def finish(vector_in, slab, null_vectors, inverse_rows):
+def finish(vector_in, slab, null_vectors, inverse_blocks):
     correction = lax.dot_general(
         slab,
-        inverse_rows,
-        (((1,), (1,)), ((), ())),
+        inverse_blocks,
+        (((0, 1), (1, 2)), ((), ())),
         preferred_element_type=jnp.float32,
     ).astype(jnp.bfloat16)
     prolonged = jnp.einsum(
@@ -125,60 +121,61 @@
 
 
 def shards(right_side, coarse_links, null_vectors, coarse_inverse):
-    inverse_rows = coarse_inverse[0]
     slabs_total = lax.axis_size("ta")
     blocks_total = lax.axis_size("xyz")
+    inverse_rows = coarse_inverse[0]
+    inverse_blocks = inverse_rows.reshape(
+        inverse_rows.shape[0], blocks_total, inverse_rows.shape[1] // blocks_total
+    )
     residual = right_side
     coarse = jnp.einsum(
-        "tbzyxjk,ntbzyxk->nj",
+        "tbzyxjk,ntbzyxk->jn",
         null_vectors,
         residual.astype(jnp.bfloat16),
         preferred_element_type=jnp.float32,
     ).astype(jnp.bfloat16)
-    width = coarse.shape[1]
+    width = coarse.shape[0]
     payload = jnp.concatenate(
-        [coarse.astype(jnp.float32), restrict_exact(null_vectors, residual)], 1
+        [coarse.astype(jnp.float32), restrict_exact(null_vectors, residual)], 0
     )
     parts = lax.all_to_all(
         jnp.broadcast_to(payload[None], (blocks_total,) + payload.shape), "xyz", 0, 0
     )
-    slab_a = slab_columns(parts[:, :, :width]).astype(jnp.bfloat16)
-    slab_residual = slab_columns(parts[:, :, width:])
-    direction_a = finish(residual, slab_a, null_vectors, inverse_rows)
+    slab_a = parts[:, :width, :].astype(jnp.bfloat16)
+    slab_residual = parts[:, width:, :]
+    direction_a = finish(residual, slab_a, null_vectors, inverse_blocks)
     image_a = apply_links(coarse_links, direction_a.astype(jnp.bfloat16))
     image_coarse = restrict_exact(null_vectors, image_a)
-    pair_local = jnp.stack([inner_rows(image_a, image_a), inner_rows(image_a, residual)], 1)
+    pair_local = jnp.stack([inner_rows(image_a, image_a), inner_rows(image_a, residual)], 0)
     if slabs_total * blocks_total <= 64:
-        local = jnp.concatenate([pair_local, image_coarse], 1)
+        local = jnp.concatenate([pair_local, image_coarse], 0)
         gathered = lax.all_to_all(
             jnp.broadcast_to(local[None], (slabs_total * blocks_total,) + local.shape),
             ("ta", "xyz"),
             0,
             0,
         )
-        pair = jnp.sum(gathered[:, :, :2], axis=0)
-        image_slabs = gathered[:, :, 2:].reshape(
+        pair = jnp.sum(gathered[:, :2, :], axis=0)
+        image_slabs = gathered[:, 2:, :].reshape(
             (slabs_total, blocks_total) + image_coarse.shape
         )
-        slab_image = slab_columns(
-            lax.dynamic_index_in_dim(image_slabs, lax.axis_index("ta"), 0, keepdims=False)
+        slab_image = lax.dynamic_index_in_dim(
+            image_slabs, lax.axis_index("ta"), 0, keepdims=False
         )
     else:
         pair = total_sum(pair_local)
-        slab_image = slab_columns(
-            lax.all_to_all(
-                jnp.broadcast_to(image_coarse[None], (blocks_total,) + image_coarse.shape),
-                "xyz",
-                0,
-                0,
-            )
-        )
-    norm_a, correlation_a = pair[:, 0], pair[:, 1]
+        slab_image = lax.all_to_all(
+            jnp.broadcast_to(image_coarse[None], (blocks_total,) + image_coarse.shape),
+            "xyz",
+            0,
+            0,
+        )
+    norm_a, correlation_a = pair[0], pair[1]
     step_a = correlation_a / (norm_a + EPS)
     solution = scaled(step_a, direction_a)
     residual = residual - scaled(step_a, image_a)
-    slab_b = (slab_residual - step_a[:, None] * slab_image).astype(jnp.bfloat16)
-    direction_b = finish(residual, slab_b, null_vectors, inverse_rows)
+    slab_b = (slab_residual - step_a[None, None, :] * slab_image).astype(jnp.bfloat16)
+    direction_b = finish(residual, slab_b, null_vectors, inverse_blocks)
     image_b = apply_links(coarse_links, direction_b.astype(jnp.bfloat16))
     sums = total_sum(
         jnp.stack(

time: 81.3 us -> 82.7 us (1.017)
  blocking collectives: 20.5 us -> 10 us
  waiting for transfers between devices: 21.7 us -> 27 us
  starting transfers between devices: 11.7 us -> 16.8 us
  local copies, waits for them, and re-layouts: 8.41 us -> 9.86 us
    all_to_all x1 -> x0, blocking collectives: 10.5 us -> none  [shards(): lax.all_to_all(jnp.broadcast_to(payload[None], (blocks_total,) + payload....]
    all_to_all x0 -> x1, waiting for transfers between devices: none -> 5.39 us  [shards(): lax.all_to_all(jnp.broadcast_to(payload[None], (blocks_total,) + payload....]
    all_to_all x0 -> x1, starting transfers between devices: none -> 5.17 us  [shards(): lax.all_to_all(jnp.broadcast_to(payload[None], (blocks_total,) + payload....]
    another operation x0 -> x1, other arithmetic: none -> 1.2 us
    reshape x1 -> x0, other arithmetic: 1.19 us -> none
    slice x1 -> x2, local copies, waits for them, and re-layouts: 0.2 us -> 1.19 us  [the longest x1 1.02 us: shards(): gathered[:, 2:, :].reshape((slabs_total, blocks_total) + image_coarse.shape)]
    unnamed x20 -> x25, local copies, waits for them, and re-layouts: 5.11 us -> 5.18 us
  transfers between devices with their start and end apart: 11 -> 12, of which waited for: 5 -> 6; matrix products, arithmetic and copies ran while one was open for 1% -> 1% of each run, Pallas kernels for 0% -> 0%
where the time goes in v7:
time: 82.7 us; the launch traced here: 82.3 us
  waiting for transfers between devices  27 us (33%)
  starting transfers between devices  16.8 us (20%)
  blocking collectives  10 us (12%)
  local copies, waits for them, and re-layouts  9.86 us (12%)
  other arithmetic  9.63 us (12%)
  matrix products  7.74 us (9%)
  between operations  1.17 us (1%)
    all_to_all x1, blocking collectives, total_sum(): return jnp.sum(lax.all_to_all(copies, axes, 0, 0), axis=0)  10 us
    all_to_all x1, waiting for transfers between devices, shards(): lax.all_to_all(jnp.broadcast_to(local[None], (slabs_total * blocks_total,...  9.37 us
    ppermute x6, waiting for transfers between devices, both_sides(): pair = lax.ppermute(jnp.concatenate([first, last], which), axis, perm)  6.83 us
    ppermute x2, waiting for transfers between devices, both_sides(): from_lower = lax.ppermute(last, axis, down)  5.44 us
    all_to_all x1, waiting for transfers between devices, shards(): lax.all_to_all(jnp.broadcast_to(payload[None], (blocks_total,) + payload....  5.39 us
    ppermute x2, starting transfers between devices, both_sides(): from_upper = lax.ppermute(first, axis, up)  5.19 us
    unnamed x25, local copies, waits for them, and re-layouts  5.18 us
    all_to_all x1, starting transfers between devices, shards(): lax.all_to_all(jnp.broadcast_to(payload[None], (blocks_total,) + payload....  5.17 us
  transfers between devices with their start and end apart: 12, of which 6 were waited for; matrix products, arithmetic and copies ran while one was open for 1% of the time, Pallas kernels for 0%

profile of v7, /device:TPU:0, one launch (start us, length us, event | category | flops | bytes accessed | tf_op | source)
XLA Modules:
  0.0 82.3 jit_solution(13227252570881848982)
XLA Ops:
  0.7 1.2 %convert_bitcast_fusion = bf16[32,4,2,2,128]{4,3,2,1,0:T(2,128)(2,1)S(1)} fusion(f32[32,1,1,4,2,2,128]{6,5,4,3,2,1,0:T(2,128)} %param.4), kind=kLoop, calls=%fused_computation.87 | loop fusion | flops 65536 | bytes 393216 | tf_op jit(solution)/shard_map/reshape.2
  1.9 1.4 %convolution_bitcast_fusion.6 = f32[48,32]{0,1:T(8,128)S(1)} fusion(f32[32,4,2,2,128]{4,3,2,1,0:T(2,128)} %bitcast.248, bf16[1,1,4,2,2,48,128]{6,5,4,3,2,1,0:T(8,128)(2,1)} %param.6), kind=kOutput, calls=%fused_computation.24 | convolution fusion | flops 37748736 | bytes 464896 | tf_op jit(solution)/shard_map/tbzyxjk,ntbzyxk->jn/dot_general | solution.py:93
  3.3 1.1 %fusion.19 = f32[48,32]{0,1:T(8,128)S(1)} fusion(bf16[32,4,2,2,128]{4,3,2,1,0:T(2,128)(2,1)S(1)} %convert_bitcast_fusion, bf16[1,1,4,2,2,48,128]{6,5,4,3,2,1,0:T(8,128)(2,1)} %param.6), kind=kOutput, calls=%fused_computation.26 | convolution fusion | flops 6294528 | bytes 333824 | tf_op jit(solution)/shard_map/tbzyxjk,ntbzyxk->jn/dot_general | solution.py:131
  5.1 5.2 %all-to-all-start = ((f32[8,96,32]{1,2,0:T(8,128)}), f32[8,96,32]{1,2,0:T(8,128)S(1)}, u32[]{:S(2)}, u32[]{:S(2)}) async-start(f32[8,96,32]{1,2,0:T(8,128)} %broadcast_in_dim.6), calls=%async_computation | async-start | bytes 262144 | tf_op jit(solution)/shard_map/all_to_all | solution.py:141
  10.4 5.4 %all-to-all-done = f32[8,96,32]{1,2,0:T(8,128)S(1)} async-done(((f32[8,96,32]{1,2,0:T(8,128)}), f32[8,96,32]{1,2,0:T(8,128)S(1)}, u32[]{:S(2)}, u32[]{:S(2)}) %all-to-all-start) | async-done | bytes 98336 | tf_op jit(solution)/shard_map/all_to_all | solution.py:141
  15.8 1.1 %bitcast_dynamic-update-slice_fusion.5 = (bf16[32,1,9,1,4,2,2,128]{7,0,6,5,4,3,2,1:T(8,128)(2,1)}, bf16[32,1,1,4,2,2,128]{6,0,5,4,3,2,1:T(8,128)(2,1)S(1)}, f32[32,1,1,4,2,2,128]{6,0,5,4,3,2,1:T(8,128)}) fusion(bf16[1,1,4,2,2,48,128]{6,5,4,3,2,1,0:T(8,128)(2,1)S(1)} %copy-done.4, bf16[48,8,48]{2,1,0:T(8,128)(2,1)S(1)} %reshape_squeeze.3, ...), kind=kOutput, calls=%fused_computation.85 | convolution fusion | flops 7669247 | bytes 1146880 | tf_op jit(solution)/shard_map/tbzyxjk,nj->ntbzyxk/dot_general | solution.py:109
  17.6 3.6 %collective-permute-start.3 = (bf16[32,1,1,4,2,2,128]{6,0,5,4,3,2,1:T(8,128)(2,1)S(1)}, bf16[32,1,1,4,2,2,128]{6,0,5,4,3,2,1:T(8,128)(2,1)S(1)}, u32[]{:S(2)}, u32[]{:S(2)}) collective-permute-start(bf16[32,1,1,4,2,2,128]{6,0,5,4,3,2,1:T(8,128)(2,1)S(1)} %get-tuple-element.29), channel_id=1, source_target_pairs={{8,0},{16,8},{24,16},{0,24},{9,1},{17,9},{25,17},{1,25},{10,2},{18... | collective-permute-start | bytes 393224 | tf_op jit(solution)/shard_map/ppermute | solution.py:60
  21.9 3.9 %collective-permute-done.2 = bf16[32,1,1,2,2,2,128]{6,0,5,4,3,2,1:T(8,128)(2,1)S(1)} collective-permute-done((bf16[32,1,1,2,2,2,128]{6,0,5,4,3,2,1:T(8,128)(2,1)S(1)}, bf16[32,1,1,2,2,2,128]{6,0,5,4,3,2,1:T(8,128)(2,1)S(1)}, u32[]{:S(2)}, u32[]{:S(2)}) %collective-permute-start.2) | collective-permute-done | bytes 65568 | tf_op jit(solution)/shard_map/ppermute | solution.py:54
  26.1 2.8 %collective-permute-done.4 = bf16[32,1,1,4,2,2,128]{6,0,5,4,3,2,1:T(8,128)(2,1)S(1)} collective-permute-done((bf16[32,1,1,4,2,2,128]{6,0,5,4,3,2,1:T(8,128)(2,1)S(1)}, bf16[32,1,1,4,2,2,128]{6,0,5,4,3,2,1:T(8,128)(2,1)S(1)}, u32[]{:S(2)}, u32[]{:S(2)}) %collective-permute-start.4) | collective-permute-done | bytes 131104 | tf_op jit(solution)/shard_map/ppermute | solution.py:61
  33.0 1.4 %reshape.380 = f32[32,1,1600]{2,1,0:T(1,128)} reshape(f32[32,32,50]{2,1,0:T(8,128)S(1)} %broadcast_bitcast_fusion) | data formatting | bytes 409600
  34.4 2.7 %all-to-all-start.1 = ((f32[32,1,1600]{2,1,0:T(1,128)}), f32[32,1,1600]{2,1,0:T(1,128)S(1)}, u32[]{:S(2)}, u32[]{:S(2)}) async-start(f32[32,1,1600]{2,1,0:T(1,128)} %reshape.380), calls=%async_computation.1 | async-start | bytes 425984 | tf_op jit(solution)/shard_map/all_to_all | solution.py:152
  37.2 9.4 %all-to-all-done.1 = f32[32,1,1600]{2,1,0:T(1,128)S(1)} async-done(((f32[32,1,1600]{2,1,0:T(1,128)}), f32[32,1,1600]{2,1,0:T(1,128)S(1)}, u32[]{:S(2)}, u32[]{:S(2)}) %all-to-all-start.1) | async-done | bytes 204832 | tf_op jit(solution)/shard_map/all_to_all | solution.py:152
  47.1 1.8 %reduce.4 = f32[32,1600]{1,0:T(8,128)} reduce(f32[32,1,1600]{2,1,0:T(1,128)S(1)} %all-to-all-done.1, f32[]{:T(128)} %broadcast.72), dimensions={1}, to_apply=%all_to_all.10.reduce_sub_computation | reduce | bytes 409604 | tf_op jit(solution)/shard_map/all_to_all | solution.py:152
  48.9 1.7 %reshape.381 = f32[32,32,50]{2,1,0:T(8,128)S(1)} reshape(f32[32,1600]{1,0:T(8,128)} %reduce.4) | data formatting | bytes 409600
  50.6 1.0 %slice.220 = f32[32,48,32]{1,2,0:T(8,128)} slice(f32[32,50,32]{1,2,0:T(8,128)S(1)} %bitcast.252), slice={[0:32], [2:50], [0:32]} | slice | bytes 393216 | tf_op jit(solution)/shard_map/slice | solution.py:159
  51.8 2.2 %bitcast_dynamic-update-slice_fusion.2 = (bf16[32,1,9,1,4,2,2,128]{7,0,6,5,4,3,2,1:T(8,128)(2,1)}, bf16[32,1,1,4,2,2,128]{6,0,5,4,3,2,1:T(8,128)(2,1)S(1)}, f32[32,1,1,4,2,2,128]{6,0,5,4,3,2,1:T(8,128)}) fusion(bf16[1,1,4,2,2,48,128]{6,5,4,3,2,1,0:T(8,128)(2,1)} %param.6, bf16[48,8,48]{2,1,0:T(8,128)(2,1)} %copy-done.6, f32[8,96,32]{1,2,0:T(8,128)S(1)} %all-to-all-done, ...), kind=kOutput, calls=%fused_computation.81 | convolution fusion | flops 7837183 | bytes 1606660 | tf_op jit(solution)/shard_map/tbzyxjk,nj->ntbzyxk/dot_general | solution.py:109
  54.7 1.6 %collective-permute-start.8 = (bf16[32,1,1,4,2,2,128]{6,0,5,4,3,2,1:T(8,128)(2,1)S(1)}, bf16[32,1,1,4,2,2,128]{6,0,5,4,3,2,1:T(8,128)(2,1)S(1)}, u32[]{:S(2)}, u32[]{:S(2)}) collective-permute-start(bf16[32,1,1,4,2,2,128]{6,0,5,4,3,2,1:T(8,128)(2,1)S(1)} %get-tuple-element.26), channel_id=1, source_target_pairs={{8,0},{16,8},{24,16},{0,24},{9,1},{17,9},{25,17},{1,25},{10,2},{18... | collective-permute-start | bytes 393224 | tf_op jit(solution)/shard_map/ppermute | solution.py:60
  56.7 1.4 %collective-permute-start.7 = (bf16[32,1,1,2,2,2,128]{6,0,5,4,3,2,1:T(8,128)(2,1)S(1)}, bf16[32,1,1,2,2,2,128]{6,0,5,4,3,2,1:T(8,128)(2,1)S(1)}, u32[]{:S(2)}, u32[]{:S(2)}) collective-permute-start(bf16[32,1,1,2,2,2,128]{6,0,5,4,3,2,1:T(8,128)(2,1)S(1)} %pad_maximum_fusion.3), channel_id=1, source_target_pairs={{4,0},{5,1},{6,2},{7,3},{0,4},{1,5},{2,6},{3,7},{12,8},{13,9},{14,... | collective-permute-start | bytes 196616 | tf_op jit(solution)/shard_map/ppermute | solution.py:54
  58.2 2.9 %collective-permute-done.7 = bf16[32,1,1,2,2,2,128]{6,0,5,4,3,2,1:T(8,128)(2,1)S(1)} collective-permute-done((bf16[32,1,1,2,2,2,128]{6,0,5,4,3,2,1:T(8,128)(2,1)S(1)}, bf16[32,1,1,2,2,2,128]{6,0,5,4,3,2,1:T(8,128)(2,1)S(1)}, u32[]{:S(2)}, u32[]{:S(2)}) %collective-permute-start.7) | collective-permute-done | bytes 65568 | tf_op jit(solution)/shard_map/ppermute | solution.py:54
  61.4 2.6 %collective-permute-done.9 = bf16[32,1,1,4,2,2,128]{6,0,5,4,3,2,1:T(8,128)(2,1)S(1)} collective-permute-done((bf16[32,1,1,4,2,2,128]{6,0,5,4,3,2,1:T(8,128)(2,1)S(1)}, bf16[32,1,1,4,2,2,128]{6,0,5,4,3,2,1:T(8,128)(2,1)S(1)}, u32[]{:S(2)}, u32[]{:S(2)}) %collective-permute-start.9) | collective-permute-done | bytes 131104 | tf_op jit(solution)/shard_map/ppermute | solution.py:61
  68.5 10.0 %all_to_all.15 = f32[32,1,128]{2,1,0:T(1,128)S(1)} all-to-all(f32[32,1,128]{2,1,0:T(1,128)S(1)} %reshape.382), channel_id=1, replica_groups=mesh['ta'=4,'xyz'=8] {'ta','xyz'}, dimensions={0} | all-to-all | bytes 32768 | tf_op jit(solution)/shard_map/all_to_all | solution.py:34
  79.3 1.2 %multiply_subtract_fusion = (f32[32,1,1,4,2,2,128]{6,0,5,4,3,2,1:T(8,128)S(1)}, f32[32,1,1,4,2,2,128]{6,0,5,4,3,2,1:T(8,128)S(1)}) fusion(f32[32,1,1,4,2,2,128]{6,0,5,4,3,2,1:T(8,128)S(1)} %get-tuple-element.24, f32[32,1,1,4,2,2,128]{6,0,5,4,3,2,1:T(8,128)S(1)} %get-tuple-element.27, f32[32]{0:T(128)S(1)} %get-tuple-element.23, f32[32]{0:T(128)S(1)} %get-tuple-element.22, ...), kind=kLoop, calls=%fused_computation.40 | loop fusion | flops 720896 | bytes 1835392 | tf_op jit(solution)/shard_map/sub | solution.py:202
  80.5 0.9 %copy.154 = f32[32,1,1,4,2,2,128]{6,5,4,3,2,1,0:T(2,128)} copy(f32[32,1,1,4,2,2,128]{6,0,5,4,3,2,1:T(8,128)S(1)} %get-tuple-element.66) | data formatting | bytes 524288
  81.4 0.9 %copy.153 = f32[32,1,1,4,2,2,128]{6,5,4,3,2,1,0:T(2,128)} copy(f32[32,1,1,4,2,2,128]{6,0,5,4,3,2,1:T(8,128)S(1)} %get-tuple-element.67) | data formatting | bytes 524288
  (95 shorter events, 13.8 us)
Async XLA Ops:
  0.6 30.6 %copy-start = (bf16[1,1,4,2,2,9,64,128]{7,6,5,4,3,2,1,0:T(8,128)(2,1)S(1)}, bf16[1,1,4,2,2,9,64,128]{7,6,5,4,3,2,1,0:T(8,128)(2,1)}, u32[]{:S(2)}) copy-start(bf16[1,1,4,2,2,9,64,128]{7,6,5,4,3,2,1,0:T(8,128)(2,1)} %param.5) | copy-start | bytes 7077892
  0.6 15.2 %copy-start.1 = (f32[32,1,1,4,2,2,128]{6,5,4,3,2,1,0:T(2,128)S(1)}, f32[32,1,1,4,2,2,128]{6,5,4,3,2,1,0:T(2,128)}, u32[]{:S(2)}) copy-start(f32[32,1,1,4,2,2,128]{6,5,4,3,2,1,0:T(2,128)} %param.4) | copy-start | bytes 786436
  0.7 15.2 %copy-start.4 = (bf16[1,1,4,2,2,48,128]{6,5,4,3,2,1,0:T(8,128)(2,1)S(1)}, bf16[1,1,4,2,2,48,128]{6,5,4,3,2,1,0:T(8,128)(2,1)}, u32[]{:S(2)}) copy-start(bf16[1,1,4,2,2,48,128]{6,5,4,3,2,1,0:T(8,128)(2,1)} %param.6) | copy-start | bytes 589828
  0.7 9.6 %copy-start.7 = (bf16[1,48,384]{2,1,0:T(8,128)(2,1)S(1)}, bf16[1,48,384]{2,1,0:T(8,128)(2,1)}, u32[]{:S(2)}) copy-start(bf16[1,48,384]{2,1,0:T(8,128)(2,1)} %param.7) | copy-start | bytes 110596
  5.1 10.7 %all-to-all-start = ((f32[8,96,32]{1,2,0:T(8,128)}), f32[8,96,32]{1,2,0:T(8,128)S(1)}, u32[]{:S(2)}, u32[]{:S(2)}) async-start(f32[8,96,32]{1,2,0:T(8,128)} %broadcast_in_dim.6), calls=%async_computation | async-start | bytes 262144 | tf_op jit(solution)/shard_map/all_to_all | solution.py:141
  10.4 11.5 %copy-start.6 = (bf16[48,8,48]{2,1,0:T(8,128)(2,1)}, bf16[48,8,48]{2,1,0:T(8,128)(2,1)S(1)}, u32[]{:S(2)}) copy-start(bf16[48,8,48]{2,1,0:T(8,128)(2,1)S(1)} %reshape_squeeze.3) | copy-start | bytes 110596
  16.9 8.9 %copy-start.3 = (bf16[32,1,9,1,4,2,2,128]{7,0,6,5,4,3,2,1:T(8,128)(2,1)S(1)}, bf16[32,1,9,1,4,2,2,128]{7,0,6,5,4,3,2,1:T(8,128)(2,1)}, u32[]{:S(2)}) copy-start(bf16[32,1,9,1,4,2,2,128]{7,0,6,5,4,3,2,1:T(8,128)(2,1)} %get-tuple-element.28) | copy-start | bytes 3538948
  17.0 8.9 %collective-permute-start.1 = (bf16[32,1,1,4,2,2,128]{6,0,5,4,3,2,1:T(8,128)(2,1)S(1)}, bf16[32,1,1,4,2,2,128]{6,0,5,4,3,2,1:T(8,128)(2,1)S(1)}, u32[]{:S(2)}, u32[]{:S(2)}) collective-permute-start(bf16[32,1,1,4,2,2,128]{6,0,5,4,3,2,1:T(8,128)(2,1)S(1)} %get-tuple-element.29), channel_id=1, source_target_pairs={{2,0},{3,1},{0,2},{1,3},{6,4},{7,5},{4,6},{5,7},{10,8},{11,9},{8,1... | collective-permute-start | bytes 393224 | tf_op jit(solution)/shard_map/ppermute | solution.py:54
  17.6 8.5 %collective-permute-start.3 = (bf16[32,1,1,4,2,2,128]{6,0,5,4,3,2,1:T(8,128)(2,1)S(1)}, bf16[32,1,1,4,2,2,128]{6,0,5,4,3,2,1:T(8,128)(2,1)S(1)}, u32[]{:S(2)}, u32[]{:S(2)}) collective-permute-start(bf16[32,1,1,4,2,2,128]{6,0,5,4,3,2,1:T(8,128)(2,1)S(1)} %get-tuple-element.29), channel_id=1, source_target_pairs={{8,0},{16,8},{24,16},{0,24},{9,1},{17,9},{25,17},{1,25},{10,2},{18... | collective-permute-start | bytes 393224 | tf_op jit(solution)/shard_map/ppermute | solution.py:60
  21.2 4.6 %collective-permute-start = (bf16[32,1,1,4,2,2,128]{6,0,5,4,3,2,1:T(8,128)(2,1)S(1)}, bf16[32,1,1,4,2,2,128]{6,0,5,4,3,2,1:T(8,128)(2,1)S(1)}, u32[]{:S(2)}, u32[]{:S(2)}) collective-permute-start(bf16[32,1,1,4,2,2,128]{6,0,5,4,3,2,1:T(8,128)(2,1)S(1)} %get-tuple-element.29), channel_id=1, source_target_pairs={{1,0},{0,1},{3,2},{2,3},{5,4},{4,5},{7,6},{6,7},{9,8},{8,9},{11,10... | collective-permute-start | bytes 393224 | tf_op jit(solution)/shard_map/ppermute | solution.py:54
  21.2 7.7 %collective-permute-start.4 = (bf16[32,1,1,4,2,2,128]{6,0,5,4,3,2,1:T(8,128)(2,1)S(1)}, bf16[32,1,1,4,2,2,128]{6,0,5,4,3,2,1:T(8,128)(2,1)S(1)}, u32[]{:S(2)}, u32[]{:S(2)}) collective-permute-start(bf16[32,1,1,4,2,2,128]{6,0,5,4,3,2,1:T(8,128)(2,1)S(1)} %get-tuple-element.29), channel_id=1, source_target_pairs={{24,0},{0,8},{8,16},{16,24},{25,1},{1,9},{9,17},{17,25},{26,2},{2,... | collective-permute-start | bytes 393224 | tf_op jit(solution)/shard_map/ppermute | solution.py:61
  21.2 4.6 %collective-permute-start.2 = (bf16[32,1,1,2,2,2,128]{6,0,5,4,3,2,1:T(8,128)(2,1)S(1)}, bf16[32,1,1,2,2,2,128]{6,0,5,4,3,2,1:T(8,128)(2,1)S(1)}, u32[]{:S(2)}, u32[]{:S(2)}) collective-permute-start(bf16[32,1,1,2,2,2,128]{6,0,5,4,3,2,1:T(8,128)(2,1)S(1)} %pad_maximum_fusion.2), channel_id=1, source_target_pairs={{4,0},{5,1},{6,2},{7,3},{0,4},{1,5},{2,6},{3,7},{12,8},{13,9},{14,... | collective-permute-start | bytes 196616 | tf_op jit(solution)/shard_map/ppermute | solution.py:54
  34.4 12.1 %all-to-all-start.1 = ((f32[32,1,1600]{2,1,0:T(1,128)}), f32[32,1,1600]{2,1,0:T(1,128)S(1)}, u32[]{:S(2)}, u32[]{:S(2)}) async-start(f32[32,1,1600]{2,1,0:T(1,128)} %reshape.380), calls=%async_computation.1 | async-start | bytes 425984 | tf_op jit(solution)/shard_map/all_to_all | solution.py:152
  54.0 7.1 %copy-start.2 = (bf16[32,1,9,1,4,2,2,128]{7,0,6,5,4,3,2,1:T(8,128)(2,1)S(1)}, bf16[32,1,9,1,4,2,2,128]{7,0,6,5,4,3,2,1:T(8,128)(2,1)}, u32[]{:S(2)}) copy-start(bf16[32,1,9,1,4,2,2,128]{7,0,6,5,4,3,2,1:T(8,128)(2,1)} %get-tuple-element.25) | copy-start | bytes 3538948
  54.0 7.1 %collective-permute-start.6 = (bf16[32,1,1,4,2,2,128]{6,0,5,4,3,2,1:T(8,128)(2,1)S(1)}, bf16[32,1,1,4,2,2,128]{6,0,5,4,3,2,1:T(8,128)(2,1)S(1)}, u32[]{:S(2)}, u32[]{:S(2)}) collective-permute-start(bf16[32,1,1,4,2,2,128]{6,0,5,4,3,2,1:T(8,128)(2,1)S(1)} %get-tuple-element.26), channel_id=1, source_target_pairs={{2,0},{3,1},{0,2},{1,3},{6,4},{7,5},{4,6},{5,7},{10,8},{11,9},{8,1... | collective-permute-start | bytes 393224 | tf_op jit(solution)/shard_map/ppermute | solution.py:54
  54.7 6.6 %collective-permute-start.8 = (bf16[32,1,1,4,2,2,128]{6,0,5,4,3,2,1:T(8,128)(2,1)S(1)}, bf16[32,1,1,4,2,2,128]{6,0,5,4,3,2,1:T(8,128)(2,1)S(1)}, u32[]{:S(2)}, u32[]{:S(2)}) collective-permute-start(bf16[32,1,1,4,2,2,128]{6,0,5,4,3,2,1:T(8,128)(2,1)S(1)} %get-tuple-element.26), channel_id=1, source_target_pairs={{8,0},{16,8},{24,16},{0,24},{9,1},{17,9},{25,17},{1,25},{10,2},{18... | collective-permute-start | bytes 393224 | tf_op jit(solution)/shard_map/ppermute | solution.py:60
  56.3 4.8 %collective-permute-start.5 = (bf16[32,1,1,4,2,2,128]{6,0,5,4,3,2,1:T(8,128)(2,1)S(1)}, bf16[32,1,1,4,2,2,128]{6,0,5,4,3,2,1:T(8,128)(2,1)S(1)}, u32[]{:S(2)}, u32[]{:S(2)}) collective-permute-start(bf16[32,1,1,4,2,2,128]{6,0,5,4,3,2,1:T(8,128)(2,1)S(1)} %get-tuple-element.26), channel_id=1, source_target_pairs={{1,0},{0,1},{3,2},{2,3},{5,4},{4,5},{7,6},{6,7},{9,8},{8,9},{11,10... | collective-permute-start | bytes 393224 | tf_op jit(solution)/shard_map/ppermute | solution.py:54
  56.3 7.7 %collective-permute-start.9 = (bf16[32,1,1,4,2,2,128]{6,0,5,4,3,2,1:T(8,128)(2,1)S(1)}, bf16[32,1,1,4,2,2,128]{6,0,5,4,3,2,1:T(8,128)(2,1)S(1)}, u32[]{:S(2)}, u32[]{:S(2)}) collective-permute-start(bf16[32,1,1,4,2,2,128]{6,0,5,4,3,2,1:T(8,128)(2,1)S(1)} %get-tuple-element.26), channel_id=1, source_target_pairs={{24,0},{0,8},{8,16},{16,24},{25,1},{1,9},{9,17},{17,25},{26,2},{2,... | collective-permute-start | bytes 393224 | tf_op jit(solution)/shard_map/ppermute | solution.py:61
  56.7 4.3 %collective-permute-start.7 = (bf16[32,1,1,2,2,2,128]{6,0,5,4,3,2,1:T(8,128)(2,1)S(1)}, bf16[32,1,1,2,2,2,128]{6,0,5,4,3,2,1:T(8,128)(2,1)S(1)}, u32[]{:S(2)}, u32[]{:S(2)}) collective-permute-start(bf16[32,1,1,2,2,2,128]{6,0,5,4,3,2,1:T(8,128)(2,1)S(1)} %pad_maximum_fusion.3), channel_id=1, source_target_pairs={{4,0},{5,1},{6,2},{7,3},{0,4},{1,5},{2,6},{3,7},{12,8},{13,9},{14,... | collective-permute-start | bytes 196616 | tf_op jit(solution)/shard_map/ppermute | solution.py:54
  67.9 11.4 %copy-start.5 = (f32[32,1,1,4,2,2,128]{6,0,5,4,3,2,1:T(8,128)S(1)}, f32[32,1,1,4,2,2,128]{6,0,5,4,3,2,1:T(8,128)}, u32[]{:S(2)}) copy-start(f32[32,1,1,4,2,2,128]{6,0,5,4,3,2,1:T(8,128)} %get-tuple-element.68) | copy-start | bytes 786436

commit v8 on v6

--- a/solution.py
+++ b/solution.py
@@ -66,7 +66,20 @@
     return (upper, lower)
 
 
-def apply_links(coarse_links, lowered):
+def split_links(coarse_links):
+    half_width = coarse_links.shape[-1] // 2
+    real_part = coarse_links[..., :half_width]
+    imag_part = coarse_links[..., half_width:]
+    return jnp.stack(
+        [
+            jnp.concatenate([real_part, -imag_part], -1),
+            jnp.concatenate([imag_part, real_part], -1),
+        ],
+        0,
+    )
+
+
+def apply_links(links_pair, lowered):
     blocks_total = lax.axis_size("xyz")
     across_x = 2 + 2 * min(blocks_total // 64, 1)
     across_z = blocks_total // (across_x * across_x)
@@ -77,14 +90,8 @@
     stacked = jnp.stack(
         [lowered, upper_x, lower_x, upper_y, lower_y, upper_z, lower_z, upper_t, lower_t], 2
     )
-    half_width = lowered.shape[-1] // 2
-    real_part = stacked[..., :half_width]
-    imag_part = stacked[..., half_width:]
-    real_input = jnp.concatenate([real_part, -imag_part], -1)
-    imag_input = jnp.concatenate([imag_part, real_part], -1)
-    inputs = jnp.stack([real_input, imag_input], 0)
     result = jnp.einsum(
-        "tbzyxdik,pntdbzyxk->pntbzyxi", coarse_links, inputs, preferred_element_type=jnp.float32
+        "ptbzyxdik,ntdbzyxk->pntbzyxi", links_pair, stacked, preferred_element_type=jnp.float32
     )
     return jnp.concatenate([result[0], result[1]], -1)
 
@@ -126,6 +133,7 @@
 
 def shards(right_side, coarse_links, null_vectors, coarse_inverse):
     inverse_rows = coarse_inverse[0]
+    links_pair = split_links(coarse_links)
     slabs_total = lax.axis_size("ta")
     blocks_total = lax.axis_size("xyz")
     residual = right_side
@@ -145,7 +153,7 @@
     slab_a = slab_columns(parts[:, :, :width]).astype(jnp.bfloat16)
     slab_residual = slab_columns(parts[:, :, width:])
     direction_a = finish(residual, slab_a, null_vectors, inverse_rows)
-    image_a = apply_links(coarse_links, direction_a.astype(jnp.bfloat16))
+    image_a = apply_links(links_pair, direction_a.astype(jnp.bfloat16))
     image_coarse = restrict_exact(null_vectors, image_a)
     pair_local = jnp.stack([inner_rows(image_a, image_a), inner_rows(image_a, residual)], 1)
     if slabs_total * blocks_total <= 64:
@@ -179,7 +187,7 @@
     residual = residual - scaled(step_a, image_a)
     slab_b = (slab_residual - step_a[:, None] * slab_image).astype(jnp.bfloat16)
     direction_b = finish(residual, slab_b, null_vectors, inverse_rows)
-    image_b = apply_links(coarse_links, direction_b.astype(jnp.bfloat16))
+    image_b = apply_links(links_pair, direction_b.astype(jnp.bfloat16))
     sums = total_sum(
         jnp.stack(
             [

time: 81.3 us -> 82.1 us (level)
  blocking collectives: 20.5 us -> 10.5 us
  starting transfers between devices: 11.7 us -> 19.3 us
  other arithmetic: 10.1 us -> 15.5 us
  waiting for transfers between devices: 21.7 us -> 17.3 us
  matrix products: 7.36 us -> 10.3 us
    all_to_all x1 -> x0, blocking collectives: 10.5 us -> none  [shards(): lax.all_to_all(jnp.broadcast_to(payload[None], (blocks_total,) + payload....]
    ppermute x6, waiting for transfers between devices: 6.84 us -> 1.3 us  [both_sides(): pair = lax.ppermute(jnp.concatenate([first, last], which), axis, perm)]
    all_to_all x0 -> x1, starting transfers between devices: none -> 5.17 us  [shards(): lax.all_to_all(jnp.broadcast_to(payload[None], (blocks_total,) + payload....]
    dot_general x2, matrix products: 1.69 us -> 6.24 us  [apply_links(): jnp.einsum('ptbzyxdik,ntdbzyxk->pntbzyxi', links_pair, stacked, preferred...]
    unnamed x12, other arithmetic: 0.24 us -> 4.09 us
    ppermute x2, waiting for transfers between devices: 0.01 us -> 3.65 us  [both_sides(): from_upper = lax.ppermute(first, axis, up)]
    neg x1, other arithmetic: 0.45 us -> 3.37 us  [split_links(): -imag_part]
    ppermute x6, starting transfers between devices: 3.3 us -> 5.83 us  [both_sides(): pair = lax.ppermute(jnp.concatenate([first, last], which), axis, perm)]
  transfers between devices with their start and end apart: 11 -> 12, of which waited for: 5 -> 5; matrix products, arithmetic and copies ran while one was open for 1% -> 15% of each run, Pallas kernels for 0% -> 0%
where the time goes in v8:
time: 82.1 us; the launch traced here: 81.7 us
  starting transfers between devices  19.3 us (24%)
  waiting for transfers between devices  17.3 us (21%)
  other arithmetic  15.5 us (19%)
  blocking collectives  10.5 us (13%)
  matrix products  10.3 us (13%)
  local copies, waits for them, and re-layouts  7.7 us (9%)
  between operations  1.05 us (1%)
    all_to_all x1, blocking collectives, total_sum(): return jnp.sum(lax.all_to_all(copies, axes, 0, 0), axis=0)  10.5 us
    all_to_all x1, waiting for transfers between devices, shards(): lax.all_to_all(jnp.broadcast_to(local[None], (slabs_total * blocks_total,...  9.37 us
    dot_general x2, matrix products, apply_links(): jnp.einsum('ptbzyxdik,ntdbzyxk->pntbzyxi', links_pair, stacked, preferred...  6.24 us
    ppermute x6, starting transfers between devices, both_sides(): pair = lax.ppermute(jnp.concatenate([first, last], which), axis, perm)  5.83 us
    all_to_all x1, starting transfers between devices, shards(): lax.all_to_all(jnp.broadcast_to(payload[None], (blocks_total,) + payload....  5.17 us
    ppermute x2, starting transfers between devices, both_sides(): from_upper = lax.ppermute(first, axis, up)  5.03 us
    unnamed x26, local copies, waits for them, and re-layouts  4.83 us
    unnamed x12, other arithmetic  4.09 us
  transfers between devices with their start and end apart: 12, of which 5 were waited for; matrix products, arithmetic and copies ran while one was open for 15% of the time, Pallas kernels for 0%

profile of v8, /device:TPU:0, one launch (start us, length us, event | category | flops | bytes accessed | tf_op | source)
XLA Modules:
  0.0 81.7 jit_solution(5771269762147975838)
XLA Ops:
  0.6 1.1 %convert_bitcast_fusion = bf16[32,4,2,2,128]{4,3,2,1,0:T(2,128)(2,1)S(1)} fusion(f32[32,1,1,4,2,2,128]{6,5,4,3,2,1,0:T(2,128)} %param.4), kind=kLoop, calls=%fused_computation.82 | loop fusion | flops 65536 | bytes 393216 | tf_op jit(solution)/shard_map/reshape
  1.7 1.3 %convolution_bitcast_fusion.4 = f32[32,48]{1,0:T(8,128)S(1)} fusion(f32[32,4,2,2,128]{4,3,2,1,0:T(2,128)} %bitcast.227, bf16[1,1,4,2,2,48,128]{6,5,4,3,2,1,0:T(8,128)(2,1)S(1)} %copy-done), kind=kOutput, calls=%fused_computation.19 | convolution fusion | flops 37748736 | bytes 464896 | tf_op jit(solution)/shard_map/tbzyxjk,ntbzyxk->nj/dot_general | solution.py:100
  4.0 5.2 %all-to-all-start = ((f32[8,32,96]{2,1,0:T(8,128)}), f32[8,32,96]{2,1,0:T(8,128)S(1)}, u32[]{:S(2)}, u32[]{:S(2)}) async-start(f32[8,32,96]{2,1,0:T(8,128)} %broadcast_in_dim.6), calls=%async_computation | async-start | bytes 262144 | tf_op jit(solution)/shard_map/all_to_all | solution.py:150
  9.1 3.4 %slice_negate_fusion = (bf16[1,1,4,2,2,9,64,64]{7,6,5,4,3,2,1,0:T(8,128)(2,1)S(1)}, bf16[1,1,4,2,2,9,64,64]{7,6,5,4,3,2,1,0:T(8,128)(2,1)S(1)}, bf16[1,1,4,2,2,9,64,64]{7,6,5,4,3,2,1,0:T(8,128)(2,1)S(1)}) fusion(bf16[1,1,4,2,2,9,64,128]{7,6,5,4,3,2,1,0:T(8,128)(2,1)} %param.5), kind=kLoop, calls=%fused_computation.109 | loop fusion | flops 589824 | bytes 5898240 | tf_op jit(solution)/shard_map/neg | solution.py:75
  12.5 3.7 %maximum_bitcast_fusion.1 = (bf16[1,1,1,4,2,2,9,64,128]{8,7,6,0,5,4,3,2,1:T(8,128)(2,1)S(1)}, bf16[1,1,1,4,2,2,9,64,128]{8,7,6,0,5,4,3,2,1:T(8,128)(2,1)}) fusion(bf16[1,1,4,2,2,9,64,64]{7,6,5,4,3,2,1,0:T(8,128)(2,1)S(1)} %get-tuple-element.37, bf16[1,1,4,2,2,9,64,64]{7,6,5,4,3,2,1,0:T(8,128)(2,1)S(1)} %get-tuple-element.39, ...), kind=kLoop, calls=%fused_computation.5 | loop fusion | flops 9437184 | bytes 8257536 | tf_op jit(solution)/shard_map/stack | solution.py:73
  16.4 1.3 %bitcast_dynamic-update-slice_fusion.5 = (bf16[32,1,9,1,4,2,2,128]{7,0,6,5,4,3,2,1:T(8,128)(2,1)}, bf16[32,1,1,4,2,2,128]{6,0,5,4,3,2,1:T(8,128)(2,1)S(1)}, f32[32,1,1,4,2,2,128]{6,0,5,4,3,2,1:T(8,128)}) fusion(bf16[1,1,4,2,2,48,128]{6,5,4,3,2,1,0:T(8,128)(2,1)S(1)} %copy-done, bf16[32,384]{1,0:T(8,128)(2,1)S(1)} %convert_element_type.43, ...), kind=kOutput, calls=%fused_computation.80 | convolution fusion | flops 7669247 | bytes 1044480 | tf_op jit(solution)/shard_map/tbzyxjk,nj->ntbzyxk/dot_general | solution.py:120
  18.2 1.7 %collective-permute-start.1 = (bf16[32,1,1,4,2,2,128]{6,0,5,4,3,2,1:T(8,128)(2,1)S(1)}, bf16[32,1,1,4,2,2,128]{6,0,5,4,3,2,1:T(8,128)(2,1)S(1)}, u32[]{:S(2)}, u32[]{:S(2)}) collective-permute-start(bf16[32,1,1,4,2,2,128]{6,0,5,4,3,2,1:T(8,128)(2,1)S(1)} %get-tuple-element.34), channel_id=1, source_target_pairs={{2,0},{3,1},{0,2},{1,3},{6,4},{7,5},{4,6},{5,7},{10,8},{11,9},{8,1... | collective-permute-start | bytes 393224 | tf_op jit(solution)/shard_map/ppermute | solution.py:54
  20.0 1.5 %collective-permute-start.2 = (bf16[32,1,1,2,2,2,128]{6,0,5,4,3,2,1:T(8,128)(2,1)S(1)}, bf16[32,1,1,2,2,2,128]{6,0,5,4,3,2,1:T(8,128)(2,1)S(1)}, u32[]{:S(2)}, u32[]{:S(2)}) collective-permute-start(bf16[32,1,1,2,2,2,128]{6,0,5,4,3,2,1:T(8,128)(2,1)S(1)} %pad_maximum_fusion.2), channel_id=1, source_target_pairs={{4,0},{5,1},{6,2},{7,3},{0,4},{1,5},{2,6},{3,7},{12,8},{13,9},{14,... | collective-permute-start | bytes 196616 | tf_op jit(solution)/shard_map/ppermute | solution.py:54
  21.6 3.7 %collective-permute-start.3 = (bf16[32,1,1,4,2,2,128]{6,0,5,4,3,2,1:T(8,128)(2,1)S(1)}, bf16[32,1,1,4,2,2,128]{6,0,5,4,3,2,1:T(8,128)(2,1)S(1)}, u32[]{:S(2)}, u32[]{:S(2)}) collective-permute-start(bf16[32,1,1,4,2,2,128]{6,0,5,4,3,2,1:T(8,128)(2,1)S(1)} %get-tuple-element.34), channel_id=1, source_target_pairs={{8,0},{16,8},{24,16},{0,24},{9,1},{17,9},{25,17},{1,25},{10,2},{18... | collective-permute-start | bytes 393224 | tf_op jit(solution)/shard_map/ppermute | solution.py:60
  25.5 3.6 %collective-permute-done.3 = bf16[32,1,1,4,2,2,128]{6,0,5,4,3,2,1:T(8,128)(2,1)S(1)} collective-permute-done((bf16[32,1,1,4,2,2,128]{6,0,5,4,3,2,1:T(8,128)(2,1)S(1)}, bf16[32,1,1,4,2,2,128]{6,0,5,4,3,2,1:T(8,128)(2,1)S(1)}, u32[]{:S(2)}, u32[]{:S(2)}) %collective-permute-start.3) | collective-permute-done | bytes 131104 | tf_op jit(solution)/shard_map/ppermute | solution.py:60
  29.2 2.8 %collective-permute-done.4 = bf16[32,1,1,4,2,2,128]{6,0,5,4,3,2,1:T(8,128)(2,1)S(1)} collective-permute-done((bf16[32,1,1,4,2,2,128]{6,0,5,4,3,2,1:T(8,128)(2,1)S(1)}, bf16[32,1,1,4,2,2,128]{6,0,5,4,3,2,1:T(8,128)(2,1)S(1)}, u32[]{:S(2)}, u32[]{:S(2)}) %collective-permute-start.4) | collective-permute-done | bytes 131104 | tf_op jit(solution)/shard_map/ppermute | solution.py:61
  32.0 2.6 %fusion.4 = f32[2,32,1,1,4,2,2,64]{7,1,6,5,4,3,2,0:T(8,128)S(1)} fusion(bf16[1,1,1,4,2,2,9,64,128]{8,7,6,0,5,4,3,2,1:T(8,128)(2,1)S(1)} %copy-done.4, bf16[1,1,1,4,2,2,9,64,128]{8,7,6,0,5,4,3,2,1:T(8,128)(2,1)S(1)} %get-tuple-element.35, bf16[32,1,9,1,4,2,2,128]{7,0,6,5,4,3,2,1:T(8,128)(2,1)S(1)} %bitcast_dynamic-update-slice_fusion.3), kind=kOutput, calls=%fused_computation.7 | convolution fusion | flops 153354240 | bytes 6160384 | tf_op jit(solution)/shard_map/ptbzyxdik,ntdbzyxk->pntbzyxi/dot_general | solution.py:93
  35.6 1.4 %reshape.380 = f32[32,1,1600]{2,1,0:T(1,128)} reshape(f32[32,32,50]{2,1,0:T(8,128)S(1)} %broadcast_in_dim.7) | data formatting | bytes 409600
  36.9 2.6 %all-to-all-start.1 = ((f32[32,1,1600]{2,1,0:T(1,128)}), f32[32,1,1600]{2,1,0:T(1,128)S(1)}, u32[]{:S(2)}, u32[]{:S(2)}) async-start(f32[32,1,1600]{2,1,0:T(1,128)} %reshape.380), calls=%async_computation.1 | async-start | bytes 425984 | tf_op jit(solution)/shard_map/all_to_all | solution.py:161
  39.5 9.4 %all-to-all-done.1 = f32[32,1,1600]{2,1,0:T(1,128)S(1)} async-done(((f32[32,1,1600]{2,1,0:T(1,128)}), f32[32,1,1600]{2,1,0:T(1,128)S(1)}, u32[]{:S(2)}, u32[]{:S(2)}) %all-to-all-start.1) | async-done | bytes 204832 | tf_op jit(solution)/shard_map/all_to_all | solution.py:161
  49.4 1.2 %reduce.6 = f32[32,1600]{1,0:T(8,128)S(1)} reduce(f32[32,1,1600]{2,1,0:T(1,128)S(1)} %all-to-all-done.1, f32[]{:T(128)} %broadcast.79), dimensions={1}, to_apply=%all_to_all.10.reduce_sub_computation | reduce | bytes 409604 | tf_op jit(solution)/shard_map/all_to_all | solution.py:161
  52.0 1.0 %bitcast_dynamic-update-slice_fusion.2 = (bf16[32,1,9,1,4,2,2,128]{7,0,6,5,4,3,2,1:T(8,128)(2,1)}, bf16[32,1,1,4,2,2,128]{6,0,5,4,3,2,1:T(8,128)(2,1)S(1)}, f32[32,1,1,4,2,2,128]{6,0,5,4,3,2,1:T(8,128)S(1)}) fusion(bf16[1,1,4,2,2,48,128]{6,5,4,3,2,1,0:T(8,128)(2,1)S(1)} %copy-done, bf16[32,384]{1,0:T(8,128)(2,1)S(1)} %convert_element_type.48, ...), kind=kOutput, calls=%fused_computation.76 | convolution fusion | flops 7800319 | bytes 1306752 | tf_op jit(solution)/shard_map/tbzyxjk,nj->ntbzyxk/dot_general | solution.py:120
  54.2 1.0 %collective-permute-start.7 = (bf16[32,1,1,2,2,2,128]{6,0,5,4,3,2,1:T(8,128)(2,1)S(1)}, bf16[32,1,1,2,2,2,128]{6,0,5,4,3,2,1:T(8,128)(2,1)S(1)}, u32[]{:S(2)}, u32[]{:S(2)}) collective-permute-start(bf16[32,1,1,2,2,2,128]{6,0,5,4,3,2,1:T(8,128)(2,1)S(1)} %pad_maximum_fusion.3), channel_id=1, source_target_pairs={{4,0},{5,1},{6,2},{7,3},{0,4},{1,5},{2,6},{3,7},{12,8},{13,9},{14,... | collective-permute-start | bytes 196616 | tf_op jit(solution)/shard_map/ppermute | solution.py:54
  55.1 1.4 %collective-permute-start.8 = (bf16[32,1,1,4,2,2,128]{6,0,5,4,3,2,1:T(8,128)(2,1)S(1)}, bf16[32,1,1,4,2,2,128]{6,0,5,4,3,2,1:T(8,128)(2,1)S(1)}, u32[]{:S(2)}, u32[]{:S(2)}) collective-permute-start(bf16[32,1,1,4,2,2,128]{6,0,5,4,3,2,1:T(8,128)(2,1)S(1)} %get-tuple-element.31), channel_id=1, source_target_pairs={{8,0},{16,8},{24,16},{0,24},{9,1},{17,9},{25,17},{1,25},{10,2},{18... | collective-permute-start | bytes 393224 | tf_op jit(solution)/shard_map/ppermute | solution.py:60
  57.2 1.3 %collective-permute-done.7 = bf16[32,1,1,2,2,2,128]{6,0,5,4,3,2,1:T(8,128)(2,1)S(1)} collective-permute-done((bf16[32,1,1,2,2,2,128]{6,0,5,4,3,2,1:T(8,128)(2,1)S(1)}, bf16[32,1,1,2,2,2,128]{6,0,5,4,3,2,1:T(8,128)(2,1)S(1)}, u32[]{:S(2)}, u32[]{:S(2)}) %collective-permute-start.7) | collective-permute-done | bytes 65568 | tf_op jit(solution)/shard_map/ppermute | solution.py:54
  64.1 3.6 %fusion.7 = f32[2,32,1,1,4,2,2,64]{7,1,6,5,4,3,2,0:T(8,128)S(1)} fusion(bf16[1,1,1,4,2,2,9,64,128]{8,7,6,0,5,4,3,2,1:T(8,128)(2,1)S(1)} %copy-done.5, bf16[1,1,1,4,2,2,9,64,128]{8,7,6,0,5,4,3,2,1:T(8,128)(2,1)S(1)} %copy-done.3, bf16[32,1,9,1,4,2,2,128]{7,0,6,5,4,3,2,1:T(8,128)(2,1)} %bitcast_dynamic-update-slice_fusion), kind=kOutput, calls=%fused_computation.8 | convolution fusion | flops 153354240 | bytes 6160384 | tf_op jit(solution)/shard_map/ptbzyxdik,ntdbzyxk->pntbzyxi/dot_general | solution.py:93
  68.2 10.5 %all_to_all.15 = f32[32,1,128]{2,1,0:T(1,128)S(1)} all-to-all(f32[32,1,128]{2,1,0:T(1,128)S(1)} %reshape.382), channel_id=1, replica_groups=mesh['ta'=4,'xyz'=8] {'ta','xyz'}, dimensions={0} | all-to-all | bytes 32768 | tf_op jit(solution)/shard_map/all_to_all | solution.py:34
  79.9 0.9 %copy.159 = f32[32,1,1,4,2,2,128]{6,5,4,3,2,1,0:T(2,128)} copy(f32[32,1,1,4,2,2,128]{6,0,5,4,3,2,1:T(8,128)S(1)} %get-tuple-element.73) | data formatting | bytes 524288
  80.8 0.9 %copy.160 = f32[32,1,1,4,2,2,128]{6,5,4,3,2,1,0:T(2,128)} copy(f32[32,1,1,4,2,2,128]{6,0,5,4,3,2,1:T(8,128)S(1)} %get-tuple-element.72) | data formatting | bytes 524288
  (95 shorter events, 13.7 us)
Async XLA Ops:
  0.6 1.1 %copy-start = (bf16[1,1,4,2,2,48,128]{6,5,4,3,2,1,0:T(8,128)(2,1)S(1)}, bf16[1,1,4,2,2,48,128]{6,5,4,3,2,1,0:T(8,128)(2,1)}, u32[]{:S(2)}) copy-start(bf16[1,1,4,2,2,48,128]{6,5,4,3,2,1,0:T(8,128)(2,1)} %param.6) | copy-start | bytes 589828
  4.0 12.3 %all-to-all-start = ((f32[8,32,96]{2,1,0:T(8,128)}), f32[8,32,96]{2,1,0:T(8,128)S(1)}, u32[]{:S(2)}, u32[]{:S(2)}) async-start(f32[8,32,96]{2,1,0:T(8,128)} %broadcast_in_dim.6), calls=%async_computation | async-start | bytes 262144 | tf_op jit(solution)/shard_map/all_to_all | solution.py:150
  12.5 3.9 %copy-start.1 = (f32[32,1,1,4,2,2,128]{6,5,4,3,2,1,0:T(2,128)S(1)}, f32[32,1,1,4,2,2,128]{6,5,4,3,2,1,0:T(2,128)}, u32[]{:S(2)}) copy-start(f32[32,1,1,4,2,2,128]{6,5,4,3,2,1,0:T(2,128)} %param.4) | copy-start | bytes 786436
  12.5 3.9 %copy-start.7 = (bf16[1,48,384]{2,1,0:T(8,128)(2,1)S(1)}, bf16[1,48,384]{2,1,0:T(8,128)(2,1)}, u32[]{:S(2)}) copy-start(bf16[1,48,384]{2,1,0:T(8,128)(2,1)} %param.7) | copy-start | bytes 110596
  16.2 15.8 %copy-start.2 = (bf16[1,1,1,4,2,2,9,64,128]{8,7,6,0,5,4,3,2,1:T(8,128)(2,1)}, bf16[1,1,1,4,2,2,9,64,128]{8,7,6,0,5,4,3,2,1:T(8,128)(2,1)S(1)}, u32[]{:S(2)}) copy-start(bf16[1,1,1,4,2,2,9,64,128]{8,7,6,0,5,4,3,2,1:T(8,128)(2,1)S(1)} %get-tuple-element.35) | copy-start | bytes 7077892
  17.7 7.6 %copy-start.8 = (bf16[32,1,9,1,4,2,2,128]{7,0,6,5,4,3,2,1:T(8,128)(2,1)S(1)}, bf16[32,1,9,1,4,2,2,128]{7,0,6,5,4,3,2,1:T(8,128)(2,1)}, u32[]{:S(2)}) copy-start(bf16[32,1,9,1,4,2,2,128]{7,0,6,5,4,3,2,1:T(8,128)(2,1)} %get-tuple-element.33) | copy-start | bytes 3538948
  17.7 7.5 %collective-permute-start = (bf16[32,1,1,4,2,2,128]{6,0,5,4,3,2,1:T(8,128)(2,1)S(1)}, bf16[32,1,1,4,2,2,128]{6,0,5,4,3,2,1:T(8,128)(2,1)S(1)}, u32[]{:S(2)}, u32[]{:S(2)}) collective-permute-start(bf16[32,1,1,4,2,2,128]{6,0,5,4,3,2,1:T(8,128)(2,1)S(1)} %get-tuple-element.34), channel_id=1, source_target_pairs={{1,0},{0,1},{3,2},{2,3},{5,4},{4,5},{7,6},{6,7},{9,8},{8,9},{11,10... | collective-permute-start | bytes 393224 | tf_op jit(solution)/shard_map/ppermute | solution.py:54
  18.2 7.1 %collective-permute-start.1 = (bf16[32,1,1,4,2,2,128]{6,0,5,4,3,2,1:T(8,128)(2,1)S(1)}, bf16[32,1,1,4,2,2,128]{6,0,5,4,3,2,1:T(8,128)(2,1)S(1)}, u32[]{:S(2)}, u32[]{:S(2)}) collective-permute-start(bf16[32,1,1,4,2,2,128]{6,0,5,4,3,2,1:T(8,128)(2,1)S(1)} %get-tuple-element.34), channel_id=1, source_target_pairs={{2,0},{3,1},{0,2},{1,3},{6,4},{7,5},{4,6},{5,7},{10,8},{11,9},{8,1... | collective-permute-start | bytes 393224 | tf_op jit(solution)/shard_map/ppermute | solution.py:54
  20.0 5.2 %collective-permute-start.2 = (bf16[32,1,1,2,2,2,128]{6,0,5,4,3,2,1:T(8,128)(2,1)S(1)}, bf16[32,1,1,2,2,2,128]{6,0,5,4,3,2,1:T(8,128)(2,1)S(1)}, u32[]{:S(2)}, u32[]{:S(2)}) collective-permute-start(bf16[32,1,1,2,2,2,128]{6,0,5,4,3,2,1:T(8,128)(2,1)S(1)} %pad_maximum_fusion.2), channel_id=1, source_target_pairs={{4,0},{5,1},{6,2},{7,3},{0,4},{1,5},{2,6},{3,7},{12,8},{13,9},{14,... | collective-permute-start | bytes 196616 | tf_op jit(solution)/shard_map/ppermute | solution.py:54
  21.6 7.6 %collective-permute-start.3 = (bf16[32,1,1,4,2,2,128]{6,0,5,4,3,2,1:T(8,128)(2,1)S(1)}, bf16[32,1,1,4,2,2,128]{6,0,5,4,3,2,1:T(8,128)(2,1)S(1)}, u32[]{:S(2)}, u32[]{:S(2)}) collective-permute-start(bf16[32,1,1,4,2,2,128]{6,0,5,4,3,2,1:T(8,128)(2,1)S(1)} %get-tuple-element.34), channel_id=1, source_target_pairs={{8,0},{16,8},{24,16},{0,24},{9,1},{17,9},{25,17},{1,25},{10,2},{18... | collective-permute-start | bytes 393224 | tf_op jit(solution)/shard_map/ppermute | solution.py:60
  25.2 6.8 %collective-permute-start.4 = (bf16[32,1,1,4,2,2,128]{6,0,5,4,3,2,1:T(8,128)(2,1)S(1)}, bf16[32,1,1,4,2,2,128]{6,0,5,4,3,2,1:T(8,128)(2,1)S(1)}, u32[]{:S(2)}, u32[]{:S(2)}) collective-permute-start(bf16[32,1,1,4,2,2,128]{6,0,5,4,3,2,1:T(8,128)(2,1)S(1)} %get-tuple-element.34), channel_id=1, source_target_pairs={{24,0},{0,8},{8,16},{16,24},{25,1},{1,9},{9,17},{17,25},{26,2},{2,... | collective-permute-start | bytes 393224 | tf_op jit(solution)/shard_map/ppermute | solution.py:61
  25.3 6.7 %copy-start.4 = (bf16[1,1,1,4,2,2,9,64,128]{8,7,6,0,5,4,3,2,1:T(8,128)(2,1)S(1)}, bf16[1,1,1,4,2,2,9,64,128]{8,7,6,0,5,4,3,2,1:T(8,128)(2,1)}, u32[]{:S(2)}) copy-start(bf16[1,1,1,4,2,2,9,64,128]{8,7,6,0,5,4,3,2,1:T(8,128)(2,1)} %get-tuple-element.36) | copy-start | bytes 7077892
  36.9 12.0 %all-to-all-start.1 = ((f32[32,1,1600]{2,1,0:T(1,128)}), f32[32,1,1600]{2,1,0:T(1,128)S(1)}, u32[]{:S(2)}, u32[]{:S(2)}) async-start(f32[32,1,1600]{2,1,0:T(1,128)} %reshape.380), calls=%async_computation.1 | async-start | bytes 425984 | tf_op jit(solution)/shard_map/all_to_all | solution.py:161
  52.0 12.0 %copy-start.5 = (bf16[1,1,1,4,2,2,9,64,128]{8,7,6,0,5,4,3,2,1:T(8,128)(2,1)S(1)}, bf16[1,1,1,4,2,2,9,64,128]{8,7,6,0,5,4,3,2,1:T(8,128)(2,1)}, u32[]{:S(2)}) copy-start(bf16[1,1,1,4,2,2,9,64,128]{8,7,6,0,5,4,3,2,1:T(8,128)(2,1)} %get-tuple-element.36) | copy-start | bytes 7077892
  53.0 5.5 %collective-permute-start.5 = (bf16[32,1,1,4,2,2,128]{6,0,5,4,3,2,1:T(8,128)(2,1)S(1)}, bf16[32,1,1,4,2,2,128]{6,0,5,4,3,2,1:T(8,128)(2,1)S(1)}, u32[]{:S(2)}, u32[]{:S(2)}) collective-permute-start(bf16[32,1,1,4,2,2,128]{6,0,5,4,3,2,1:T(8,128)(2,1)S(1)} %get-tuple-element.31), channel_id=1, source_target_pairs={{1,0},{0,1},{3,2},{2,3},{5,4},{4,5},{7,6},{6,7},{9,8},{8,9},{11,10... | collective-permute-start | bytes 393224 | tf_op jit(solution)/shard_map/ppermute | solution.py:54
  53.4 6.5 %collective-permute-start.6 = (bf16[32,1,1,4,2,2,128]{6,0,5,4,3,2,1:T(8,128)(2,1)S(1)}, bf16[32,1,1,4,2,2,128]{6,0,5,4,3,2,1:T(8,128)(2,1)S(1)}, u32[]{:S(2)}, u32[]{:S(2)}) collective-permute-start(bf16[32,1,1,4,2,2,128]{6,0,5,4,3,2,1:T(8,128)(2,1)S(1)} %get-tuple-element.31), channel_id=1, source_target_pairs={{2,0},{3,1},{0,2},{1,3},{6,4},{7,5},{4,6},{5,7},{10,8},{11,9},{8,1... | collective-permute-start | bytes 393224 | tf_op jit(solution)/shard_map/ppermute | solution.py:54
  54.2 4.3 %collective-permute-start.7 = (bf16[32,1,1,2,2,2,128]{6,0,5,4,3,2,1:T(8,128)(2,1)S(1)}, bf16[32,1,1,2,2,2,128]{6,0,5,4,3,2,1:T(8,128)(2,1)S(1)}, u32[]{:S(2)}, u32[]{:S(2)}) collective-permute-start(bf16[32,1,1,2,2,2,128]{6,0,5,4,3,2,1:T(8,128)(2,1)S(1)} %pad_maximum_fusion.3), channel_id=1, source_target_pairs={{4,0},{5,1},{6,2},{7,3},{0,4},{1,5},{2,6},{3,7},{12,8},{13,9},{14,... | collective-permute-start | bytes 196616 | tf_op jit(solution)/shard_map/ppermute | solution.py:54
  55.1 7.4 %collective-permute-start.8 = (bf16[32,1,1,4,2,2,128]{6,0,5,4,3,2,1:T(8,128)(2,1)S(1)}, bf16[32,1,1,4,2,2,128]{6,0,5,4,3,2,1:T(8,128)(2,1)S(1)}, u32[]{:S(2)}, u32[]{:S(2)}) collective-permute-start(bf16[32,1,1,4,2,2,128]{6,0,5,4,3,2,1:T(8,128)(2,1)S(1)} %get-tuple-element.31), channel_id=1, source_target_pairs={{8,0},{16,8},{24,16},{0,24},{9,1},{17,9},{25,17},{1,25},{10,2},{18... | collective-permute-start | bytes 393224 | tf_op jit(solution)/shard_map/ppermute | solution.py:60
  56.5 6.9 %collective-permute-start.9 = (bf16[32,1,1,4,2,2,128]{6,0,5,4,3,2,1:T(8,128)(2,1)S(1)}, bf16[32,1,1,4,2,2,128]{6,0,5,4,3,2,1:T(8,128)(2,1)S(1)}, u32[]{:S(2)}, u32[]{:S(2)}) collective-permute-start(bf16[32,1,1,4,2,2,128]{6,0,5,4,3,2,1:T(8,128)(2,1)S(1)} %get-tuple-element.31), channel_id=1, source_target_pairs={{24,0},{0,8},{8,16},{16,24},{25,1},{1,9},{9,17},{17,25},{26,2},{2,... | collective-permute-start | bytes 393224 | tf_op jit(solution)/shard_map/ppermute | solution.py:61
  58.5 5.5 %copy-start.3 = (bf16[1,1,1,4,2,2,9,64,128]{8,7,6,0,5,4,3,2,1:T(8,128)(2,1)S(1)}, bf16[1,1,1,4,2,2,9,64,128]{8,7,6,0,5,4,3,2,1:T(8,128)(2,1)}, u32[]{:S(2)}) copy-start(bf16[1,1,1,4,2,2,9,64,128]{8,7,6,0,5,4,3,2,1:T(8,128)(2,1)} %copy-done.2) | copy-start | bytes 7077892
  67.7 11.9 %copy-start.6 = (f32[32,1,1,4,2,2,128]{6,0,5,4,3,2,1:T(8,128)S(1)}, f32[32,1,1,4,2,2,128]{6,0,5,4,3,2,1:T(8,128)}, u32[]{:S(2)}) copy-start(f32[32,1,1,4,2,2,128]{6,0,5,4,3,2,1:T(8,128)} %get-tuple-element.74) | copy-start | bytes 786436

commit v9 on v6

--- a/solution.py
+++ b/solution.py
@@ -95,7 +95,7 @@
         null_vectors.astype(jnp.float32),
         field,
         preferred_element_type=jnp.float32,
-        precision=lax.Precision.HIGHEST,
+        precision=lax.Precision.HIGH,
     )
 
 
@@ -135,18 +135,16 @@
         residual.astype(jnp.bfloat16),
         preferred_element_type=jnp.float32,
     ).astype(jnp.bfloat16)
-    width = coarse.shape[1]
-    payload = jnp.concatenate(
-        [coarse.astype(jnp.float32), restrict_exact(null_vectors, residual)], 1
-    )
     parts = lax.all_to_all(
-        jnp.broadcast_to(payload[None], (blocks_total,) + payload.shape), "xyz", 0, 0
-    )
-    slab_a = slab_columns(parts[:, :, :width]).astype(jnp.bfloat16)
-    slab_residual = slab_columns(parts[:, :, width:])
+        jnp.broadcast_to(coarse[None], (blocks_total,) + coarse.shape), "xyz", 0, 0
+    )
+    slab_a = slab_columns(parts)
     direction_a = finish(residual, slab_a, null_vectors, inverse_rows)
     image_a = apply_links(coarse_links, direction_a.astype(jnp.bfloat16))
-    image_coarse = restrict_exact(null_vectors, image_a)
+    image_coarse = jnp.concatenate(
+        [restrict_exact(null_vectors, residual), restrict_exact(null_vectors, image_a)], 1
+    )
+    width = image_coarse.shape[1] // 2
     pair_local = jnp.stack([inner_rows(image_a, image_a), inner_rows(image_a, residual)], 1)
     if slabs_total * blocks_total <= 64:
         local = jnp.concatenate([pair_local, image_coarse], 1)
@@ -157,22 +155,22 @@
             0,
         )
         pair = jnp.sum(gathered[:, :, :2], axis=0)
-        image_slabs = gathered[:, :, 2:].reshape(
-            (slabs_total, blocks_total) + image_coarse.shape
-        )
-        slab_image = slab_columns(
-            lax.dynamic_index_in_dim(image_slabs, lax.axis_index("ta"), 0, keepdims=False)
+        slabs = lax.dynamic_index_in_dim(
+            gathered[:, :, 2:].reshape((slabs_total, blocks_total) + image_coarse.shape),
+            lax.axis_index("ta"),
+            0,
+            keepdims=False,
         )
     else:
         pair = total_sum(pair_local)
-        slab_image = slab_columns(
-            lax.all_to_all(
-                jnp.broadcast_to(image_coarse[None], (blocks_total,) + image_coarse.shape),
-                "xyz",
-                0,
-                0,
-            )
-        )
+        slabs = lax.all_to_all(
+            jnp.broadcast_to(image_coarse[None], (blocks_total,) + image_coarse.shape),
+            "xyz",
+            0,
+            0,
+        )
+    slab_residual = slab_columns(slabs[:, :, :width])
+    slab_image = slab_columns(slabs[:, :, width:])
     norm_a, correlation_a = pair[:, 0], pair[:, 1]
     step_a = correlation_a / (norm_a + EPS)
     solution = scaled(step_a, direction_a)

time: 81.3 us -> 83.7 us (1.030)
  blocking collectives: 20.5 us -> 9.87 us
  waiting for transfers between devices: 21.7 us -> 31.7 us
  starting transfers between devices: 11.7 us -> 18.4 us
  other arithmetic: 10.1 us -> 8.03 us
  local copies, waits for them, and re-layouts: 8.41 us -> 6.99 us
    all_to_all x1 -> x0, blocking collectives: 10.5 us -> none  [shards(): lax.all_to_all(jnp.broadcast_to(payload[None], (blocks_total,) + payload....]
    all_to_all x1, waiting for transfers between devices: 9.37 us -> 15.5 us  [shards(): lax.all_to_all(jnp.broadcast_to(local[None], (slabs_total * blocks_total,...]
    all_to_all x0 -> x1, starting transfers between devices: none -> 5.17 us  [shards(): lax.all_to_all(jnp.broadcast_to(coarse[None], (blocks_total,) + coarse.sh...]
    ppermute x6, waiting for transfers between devices: 6.84 us -> 2.04 us  [both_sides(): pair = lax.ppermute(jnp.concatenate([first, last], which), axis, perm)]
    ppermute x2, waiting for transfers between devices: 0.01 us -> 4.72 us  [both_sides(): from_upper = lax.ppermute(first, axis, up)]
    all_to_all x0 -> x1, waiting for transfers between devices: none -> 3.55 us  [shards(): lax.all_to_all(jnp.broadcast_to(coarse[None], (blocks_total,) + coarse.sh...]
    unnamed x20, local copies, waits for them, and re-layouts: 5.11 us -> 2.93 us
    all_to_all x1 -> x0, other arithmetic: 1.89 us -> none  [shards(): lax.all_to_all(jnp.broadcast_to(local[None], (slabs_total * blocks_total,...]
  transfers between devices with their start and end apart: 11 -> 12, of which waited for: 5 -> 9; matrix products, arithmetic and copies ran while one was open for 1% -> 2% of each run, Pallas kernels for 0% -> 0%
where the time goes in v9:
time: 83.7 us; the launch traced here: 83.3 us
  waiting for transfers between devices  31.7 us (38%)
  starting transfers between devices  18.4 us (22%)
  blocking collectives  9.87 us (12%)
  other arithmetic  8.03 us (10%)
  matrix products  7.18 us (9%)
  local copies, waits for them, and re-layouts  6.99 us (8%)
  between operations  1.13 us (1%)
    all_to_all x1, waiting for transfers between devices, shards(): lax.all_to_all(jnp.broadcast_to(local[None], (slabs_total * blocks_total,...  15.5 us
    all_to_all x1, blocking collectives, total_sum(): return jnp.sum(lax.all_to_all(copies, axes, 0, 0), axis=0)  9.87 us
    ppermute x2, waiting for transfers between devices, both_sides(): from_lower = lax.ppermute(last, axis, down)  5.83 us
    all_to_all x1, starting transfers between devices, shards(): lax.all_to_all(jnp.broadcast_to(coarse[None], (blocks_total,) + coarse.sh...  5.17 us
    ppermute x2, starting transfers between devices, both_sides(): from_upper = lax.ppermute(first, axis, up)  5.14 us
    ppermute x2, waiting for transfers between devices, both_sides(): from_upper = lax.ppermute(first, axis, up)  4.72 us
    ppermute x6, starting transfers between devices, both_sides(): pair = lax.ppermute(jnp.concatenate([first, last], which), axis, perm)  3.92 us
    all_to_all x1, starting transfers between devices, shards(): lax.all_to_all(jnp.broadcast_to(local[None], (slabs_total * blocks_total,...  3.62 us
  transfers between devices with their start and end apart: 12, of which 9 were waited for; matrix products, arithmetic and copies ran while one was open for 2% of the time, Pallas kernels for 0%

profile of v9, /device:TPU:0, one launch (start us, length us, event | category | flops | bytes accessed | tf_op | source)
XLA Modules:
  0.0 83.3 jit_solution(10286005922071168568)
XLA Ops:
  0.7 1.2 %convert_bitcast_fusion = bf16[32,4,2,2,128]{4,3,2,1,0:T(2,128)(2,1)S(1)} fusion(f32[32,1,1,4,2,2,128]{6,5,4,3,2,1,0:T(2,128)} %param.4), kind=kLoop, calls=%fused_computation.84 | loop fusion | flops 65536 | bytes 393216 | tf_op jit(solution)/shard_map/reshape
  1.9 1.1 %fusion.18 = bf16[32,48]{1,0:T(8,128)(2,1)S(1)} fusion(bf16[32,4,2,2,128]{4,3,2,1,0:T(2,128)(2,1)S(1)} %convert_bitcast_fusion, bf16[1,1,4,2,2,48,128]{6,5,4,3,2,1,0:T(8,128)(2,1)} %param.6), kind=kOutput, calls=%fused_computation.23 | convolution fusion | flops 6292992 | bytes 330752 | tf_op jit(solution)/shard_map/tbzyxjk,ntbzyxk->nj/dot_general | solution.py:132
  3.7 5.2 %all-to-all-start = ((bf16[8,2,768]{2,1,0:T(2,128)(2,1)}), bf16[8,2,768]{2,1,0:T(2,128)(2,1)S(1)}, u32[]{:S(2)}, u32[]{:S(2)}) async-start(bf16[8,2,768]{2,1,0:T(2,128)(2,1)} %reshape.381), calls=%async_computation | async-start | bytes 49152 | tf_op jit(solution)/shard_map/all_to_all | solution.py:138
  8.9 1.2 %convolution_bitcast_fusion.4 = f32[32,48]{1,0:T(8,128)S(1)} fusion(f32[32,4,2,2,128]{4,3,2,1,0:T(2,128)} %bitcast.231, bf16[1,1,4,2,2,48,128]{6,5,4,3,2,1,0:T(8,128)(2,1)} %param.6), kind=kOutput, calls=%fused_computation.22 | convolution fusion | flops 18874368 | bytes 464896 | tf_op jit(solution)/shard_map/tbzyxjk,ntbzyxk->nj/dot_general | solution.py:93
  10.2 3.6 %all-to-all-done = bf16[8,2,768]{2,1,0:T(2,128)(2,1)S(1)} async-done(((bf16[8,2,768]{2,1,0:T(2,128)(2,1)}), bf16[8,2,768]{2,1,0:T(2,128)(2,1)S(1)}, u32[]{:S(2)}, u32[]{:S(2)}) %all-to-all-start) | async-done | bytes 24608 | tf_op jit(solution)/shard_map/all_to_all | solution.py:138
  14.0 1.0 %bitcast_dynamic-update-slice_fusion.5 = (bf16[32,1,9,1,4,2,2,128]{7,0,6,5,4,3,2,1:T(8,128)(2,1)}, bf16[32,1,1,4,2,2,128]{6,0,5,4,3,2,1:T(8,128)(2,1)S(1)}, f32[32,1,1,4,2,2,128]{6,0,5,4,3,2,1:T(8,128)}) fusion(bf16[1,1,4,2,2,48,128]{6,5,4,3,2,1,0:T(8,128)(2,1)S(1)} %copy-done.4, bf16[32,384]{1,0:T(8,128)(2,1)S(1)} %reshape.363, ...), kind=kOutput, calls=%fused_computation.81 | convolution fusion | flops 7669247 | bytes 1044480 | tf_op jit(solution)/shard_map/tbzyxjk,nj->ntbzyxk/dot_general | solution.py:113
  16.4 3.7 %collective-permute-start.3 = (bf16[32,1,1,4,2,2,128]{6,0,5,4,3,2,1:T(8,128)(2,1)S(1)}, bf16[32,1,1,4,2,2,128]{6,0,5,4,3,2,1:T(8,128)(2,1)S(1)}, u32[]{:S(2)}, u32[]{:S(2)}) collective-permute-start(bf16[32,1,1,4,2,2,128]{6,0,5,4,3,2,1:T(8,128)(2,1)S(1)} %get-tuple-element.34), channel_id=1, source_target_pairs={{8,0},{16,8},{24,16},{0,24},{9,1},{17,9},{25,17},{1,25},{10,2},{18... | collective-permute-start | bytes 393224 | tf_op jit(solution)/shard_map/ppermute | solution.py:60
  21.2 2.8 %collective-permute-done.3 = bf16[32,1,1,4,2,2,128]{6,0,5,4,3,2,1:T(8,128)(2,1)S(1)} collective-permute-done((bf16[32,1,1,4,2,2,128]{6,0,5,4,3,2,1:T(8,128)(2,1)S(1)}, bf16[32,1,1,4,2,2,128]{6,0,5,4,3,2,1:T(8,128)(2,1)S(1)}, u32[]{:S(2)}, u32[]{:S(2)}) %collective-permute-start.3) | collective-permute-done | bytes 131104 | tf_op jit(solution)/shard_map/ppermute | solution.py:60
  24.0 2.9 %collective-permute-done.4 = bf16[32,1,1,4,2,2,128]{6,0,5,4,3,2,1:T(8,128)(2,1)S(1)} collective-permute-done((bf16[32,1,1,4,2,2,128]{6,0,5,4,3,2,1:T(8,128)(2,1)S(1)}, bf16[32,1,1,4,2,2,128]{6,0,5,4,3,2,1:T(8,128)(2,1)S(1)}, u32[]{:S(2)}, u32[]{:S(2)}) %collective-permute-start.4) | collective-permute-done | bytes 131104 | tf_op jit(solution)/shard_map/ppermute | solution.py:61
  29.3 0.8 %fusion.6 = f32[2,32,1,1,4,2,2,64]{7,1,6,5,4,3,2,0:T(8,128)S(1)} fusion(bf16[1,1,4,2,2,9,64,128]{7,6,5,4,3,2,1,0:T(8,128)(2,1)S(1)} %copy-done, bf16[1,32,1,9,1,4,2,2,128]{8,1,7,6,5,3,4,2,0:T(8,128)(2,1)S(1)} %maximum_bitcast_fusion.3, bf16[1,32,1,9,1,4,2,2,128]{8,1,7,6,5,3,4,2,0:T(8,128)(2,1)S(1)} %maximum_bitcast_fusion.2), kind=kOutput, calls=%fused_computation.8 | convolution fusion | flops 152174592 | bytes 4980736 | tf_op jit(solution)/shard_map/tbzyxdik,pntdbzyxk->pntbzyxi/dot_general | solution.py:86
  30.9 0.9 %broadcast_in_dim.7 = f32[32,32,98]{2,1,0:T(8,128)} broadcast(f32[32,98]{1,0:T(8,128)S(1)} %pad_maximum_fusion.4), dimensions={1,2} | broadcast | bytes 413952 | tf_op jit(solution)/shard_map/broadcast_in_dim | solution.py:152
  31.8 3.6 %all-to-all-start.1 = ((f32[32,32,98]{2,1,0:T(8,128)}), f32[32,32,98]{2,1,0:T(8,128)S(1)}, u32[]{:S(2)}, u32[]{:S(2)}) async-start(f32[32,32,98]{2,1,0:T(8,128)} %broadcast_in_dim.7), calls=%async_computation.1 | async-start | bytes 1048576 | tf_op jit(solution)/shard_map/all_to_all | solution.py:151
  35.4 15.5 %all-to-all-done.1 = f32[32,32,98]{2,1,0:T(8,128)S(1)} async-done(((f32[32,32,98]{2,1,0:T(8,128)}), f32[32,32,98]{2,1,0:T(8,128)S(1)}, u32[]{:S(2)}, u32[]{:S(2)}) %all-to-all-start.1) | async-done | bytes 401440 | tf_op jit(solution)/shard_map/all_to_all | solution.py:151
  51.7 1.9 %bitcast_dynamic-update-slice_fusion.2 = (bf16[32,1,9,1,4,2,2,128]{7,0,6,5,4,3,2,1:T(8,128)(2,1)}, bf16[32,1,1,4,2,2,128]{6,0,5,4,3,2,1:T(8,128)(2,1)S(1)}, f32[32,1,1,4,2,2,128]{6,0,5,4,3,2,1:T(8,128)S(1)}) fusion(bf16[1,1,4,2,2,48,128]{6,5,4,3,2,1,0:T(8,128)(2,1)} %param.6, bf16[32,384]{1,0:T(8,128)(2,1)S(1)} %convert_element_type.35, ...), kind=kOutput, calls=%fused_computation.78 | convolution fusion | flops 7800319 | bytes 1306752 | tf_op jit(solution)/shard_map/tbzyxjk,nj->ntbzyxk/dot_general | solution.py:113
  53.7 1.4 %collective-permute-start.6 = (bf16[32,1,1,4,2,2,128]{6,0,5,4,3,2,1:T(8,128)(2,1)S(1)}, bf16[32,1,1,4,2,2,128]{6,0,5,4,3,2,1:T(8,128)(2,1)S(1)}, u32[]{:S(2)}, u32[]{:S(2)}) collective-permute-start(bf16[32,1,1,4,2,2,128]{6,0,5,4,3,2,1:T(8,128)(2,1)S(1)} %get-tuple-element.31), channel_id=1, source_target_pairs={{2,0},{3,1},{0,2},{1,3},{6,4},{7,5},{4,6},{5,7},{10,8},{11,9},{8,1... | collective-permute-start | bytes 393224 | tf_op jit(solution)/shard_map/ppermute | solution.py:54
  55.1 1.2 %collective-permute-start.7 = (bf16[32,1,1,2,2,2,128]{6,0,5,4,3,2,1:T(8,128)(2,1)S(1)}, bf16[32,1,1,2,2,2,128]{6,0,5,4,3,2,1:T(8,128)(2,1)S(1)}, u32[]{:S(2)}, u32[]{:S(2)}) collective-permute-start(bf16[32,1,1,2,2,2,128]{6,0,5,4,3,2,1:T(8,128)(2,1)S(1)} %pad_maximum_fusion.3), channel_id=1, source_target_pairs={{4,0},{5,1},{6,2},{7,3},{0,4},{1,5},{2,6},{3,7},{12,8},{13,9},{14,... | collective-permute-start | bytes 196616 | tf_op jit(solution)/shard_map/ppermute | solution.py:54
  56.3 1.5 %collective-permute-start.8 = (bf16[32,1,1,4,2,2,128]{6,0,5,4,3,2,1:T(8,128)(2,1)S(1)}, bf16[32,1,1,4,2,2,128]{6,0,5,4,3,2,1:T(8,128)(2,1)S(1)}, u32[]{:S(2)}, u32[]{:S(2)}) collective-permute-start(bf16[32,1,1,4,2,2,128]{6,0,5,4,3,2,1:T(8,128)(2,1)S(1)} %get-tuple-element.31), channel_id=1, source_target_pairs={{8,0},{16,8},{24,16},{0,24},{9,1},{17,9},{25,17},{1,25},{10,2},{18... | collective-permute-start | bytes 393224 | tf_op jit(solution)/shard_map/ppermute | solution.py:60
  58.4 1.1 %collective-permute-done.7 = bf16[32,1,1,2,2,2,128]{6,0,5,4,3,2,1:T(8,128)(2,1)S(1)} collective-permute-done((bf16[32,1,1,2,2,2,128]{6,0,5,4,3,2,1:T(8,128)(2,1)S(1)}, bf16[32,1,1,2,2,2,128]{6,0,5,4,3,2,1:T(8,128)(2,1)S(1)}, u32[]{:S(2)}, u32[]{:S(2)}) %collective-permute-start.7) | collective-permute-done | bytes 65568 | tf_op jit(solution)/shard_map/ppermute | solution.py:54
  59.8 1.9 %collective-permute-done.8 = bf16[32,1,1,4,2,2,128]{6,0,5,4,3,2,1:T(8,128)(2,1)S(1)} collective-permute-done((bf16[32,1,1,4,2,2,128]{6,0,5,4,3,2,1:T(8,128)(2,1)S(1)}, bf16[32,1,1,4,2,2,128]{6,0,5,4,3,2,1:T(8,128)(2,1)S(1)}, u32[]{:S(2)}, u32[]{:S(2)}) %collective-permute-start.8) | collective-permute-done | bytes 131104 | tf_op jit(solution)/shard_map/ppermute | solution.py:60
  61.7 2.9 %collective-permute-done.9 = bf16[32,1,1,4,2,2,128]{6,0,5,4,3,2,1:T(8,128)(2,1)S(1)} collective-permute-done((bf16[32,1,1,4,2,2,128]{6,0,5,4,3,2,1:T(8,128)(2,1)S(1)}, bf16[32,1,1,4,2,2,128]{6,0,5,4,3,2,1:T(8,128)(2,1)S(1)}, u32[]{:S(2)}, u32[]{:S(2)}) %collective-permute-start.9) | collective-permute-done | bytes 131104 | tf_op jit(solution)/shard_map/ppermute | solution.py:61
  69.1 9.9 %all_to_all.15 = f32[32,1,128]{2,1,0:T(1,128)S(1)} all-to-all(f32[32,1,128]{2,1,0:T(1,128)S(1)} %reshape.383), channel_id=1, replica_groups=mesh['ta'=4,'xyz'=8] {'ta','xyz'}, dimensions={0} | all-to-all | bytes 32768 | tf_op jit(solution)/shard_map/all_to_all | solution.py:34
  80.4 1.2 %multiply_subtract_fusion = (f32[32,1,1,4,2,2,128]{6,0,5,4,3,2,1:T(8,128)S(1)}, f32[32,1,1,4,2,2,128]{6,0,5,4,3,2,1:T(8,128)S(1)}) fusion(f32[32,1,1,4,2,2,128]{6,0,5,4,3,2,1:T(8,128)S(1)} %get-tuple-element.29, f32[32,1,1,4,2,2,128]{6,0,5,4,3,2,1:T(8,128)S(1)} %get-tuple-element.32, f32[32]{0:T(128)S(1)} %get-tuple-element.28, f32[32]{0:T(128)S(1)} %get-tuple-element.27, ...), kind=kLoop, calls=%fused_computation.37 | loop fusion | flops 720896 | bytes 1835392 | tf_op jit(solution)/shard_map/sub | solution.py:203
  81.5 0.9 %copy.198 = f32[32,1,1,4,2,2,128]{6,5,4,3,2,1,0:T(2,128)} copy(f32[32,1,1,4,2,2,128]{6,0,5,4,3,2,1:T(8,128)S(1)} %get-tuple-element.72) | data formatting | bytes 524288
  82.4 0.9 %copy.199 = f32[32,1,1,4,2,2,128]{6,5,4,3,2,1,0:T(2,128)} copy(f32[32,1,1,4,2,2,128]{6,0,5,4,3,2,1:T(8,128)S(1)} %get-tuple-element.71) | data formatting | bytes 524288
  (94 shorter events, 14.0 us)
Async XLA Ops:
  0.6 28.6 %copy-start = (bf16[1,1,4,2,2,9,64,128]{7,6,5,4,3,2,1,0:T(8,128)(2,1)S(1)}, bf16[1,1,4,2,2,9,64,128]{7,6,5,4,3,2,1,0:T(8,128)(2,1)}, u32[]{:S(2)}) copy-start(bf16[1,1,4,2,2,9,64,128]{7,6,5,4,3,2,1,0:T(8,128)(2,1)} %param.5) | copy-start | bytes 7077892
  0.6 13.3 %copy-start.1 = (f32[32,1,1,4,2,2,128]{6,5,4,3,2,1,0:T(2,128)S(1)}, f32[32,1,1,4,2,2,128]{6,5,4,3,2,1,0:T(2,128)}, u32[]{:S(2)}) copy-start(f32[32,1,1,4,2,2,128]{6,5,4,3,2,1,0:T(2,128)} %param.4) | copy-start | bytes 786436
  0.7 13.3 %copy-start.4 = (bf16[1,1,4,2,2,48,128]{6,5,4,3,2,1,0:T(8,128)(2,1)S(1)}, bf16[1,1,4,2,2,48,128]{6,5,4,3,2,1,0:T(8,128)(2,1)}, u32[]{:S(2)}) copy-start(bf16[1,1,4,2,2,48,128]{6,5,4,3,2,1,0:T(8,128)(2,1)} %param.6) | copy-start | bytes 589828
  0.7 13.3 %copy-start.5 = (bf16[1,48,384]{2,1,0:T(8,128)(2,1)S(1)}, bf16[1,48,384]{2,1,0:T(8,128)(2,1)}, u32[]{:S(2)}) copy-start(bf16[1,48,384]{2,1,0:T(8,128)(2,1)} %param.7) | copy-start | bytes 110596
  3.7 10.0 %all-to-all-start = ((bf16[8,2,768]{2,1,0:T(2,128)(2,1)}), bf16[8,2,768]{2,1,0:T(2,128)(2,1)S(1)}, u32[]{:S(2)}, u32[]{:S(2)}) async-start(bf16[8,2,768]{2,1,0:T(2,128)(2,1)} %reshape.381), calls=%async_computation | async-start | bytes 49152 | tf_op jit(solution)/shard_map/all_to_all | solution.py:138
  15.0 5.1 %copy-start.3 = (bf16[32,1,9,1,4,2,2,128]{7,0,6,5,4,3,2,1:T(8,128)(2,1)S(1)}, bf16[32,1,9,1,4,2,2,128]{7,0,6,5,4,3,2,1:T(8,128)(2,1)}, u32[]{:S(2)}) copy-start(bf16[32,1,9,1,4,2,2,128]{7,0,6,5,4,3,2,1:T(8,128)(2,1)} %get-tuple-element.33) | copy-start | bytes 3538948
  15.0 5.1 %collective-permute-start = (bf16[32,1,1,4,2,2,128]{6,0,5,4,3,2,1:T(8,128)(2,1)S(1)}, bf16[32,1,1,4,2,2,128]{6,0,5,4,3,2,1:T(8,128)(2,1)S(1)}, u32[]{:S(2)}, u32[]{:S(2)}) collective-permute-start(bf16[32,1,1,4,2,2,128]{6,0,5,4,3,2,1:T(8,128)(2,1)S(1)} %get-tuple-element.34), channel_id=1, source_target_pairs={{1,0},{0,1},{3,2},{2,3},{5,4},{4,5},{7,6},{6,7},{9,8},{8,9},{11,10... | collective-permute-start | bytes 393224 | tf_op jit(solution)/shard_map/ppermute | solution.py:54
  15.1 6.0 %collective-permute-start.1 = (bf16[32,1,1,4,2,2,128]{6,0,5,4,3,2,1:T(8,128)(2,1)S(1)}, bf16[32,1,1,4,2,2,128]{6,0,5,4,3,2,1:T(8,128)(2,1)S(1)}, u32[]{:S(2)}, u32[]{:S(2)}) collective-permute-start(bf16[32,1,1,4,2,2,128]{6,0,5,4,3,2,1:T(8,128)(2,1)S(1)} %get-tuple-element.34), channel_id=1, source_target_pairs={{2,0},{3,1},{0,2},{1,3},{6,4},{7,5},{4,6},{5,7},{10,8},{11,9},{8,1... | collective-permute-start | bytes 393224 | tf_op jit(solution)/shard_map/ppermute | solution.py:54
  15.8 4.3 %collective-permute-start.2 = (bf16[32,1,1,2,2,2,128]{6,0,5,4,3,2,1:T(8,128)(2,1)S(1)}, bf16[32,1,1,2,2,2,128]{6,0,5,4,3,2,1:T(8,128)(2,1)S(1)}, u32[]{:S(2)}, u32[]{:S(2)}) collective-permute-start(bf16[32,1,1,2,2,2,128]{6,0,5,4,3,2,1:T(8,128)(2,1)S(1)} %pad_maximum_fusion.2), channel_id=1, source_target_pairs={{4,0},{5,1},{6,2},{7,3},{0,4},{1,5},{2,6},{3,7},{12,8},{13,9},{14,... | collective-permute-start | bytes 196616 | tf_op jit(solution)/shard_map/ppermute | solution.py:54
  16.4 7.5 %collective-permute-start.3 = (bf16[32,1,1,4,2,2,128]{6,0,5,4,3,2,1:T(8,128)(2,1)S(1)}, bf16[32,1,1,4,2,2,128]{6,0,5,4,3,2,1:T(8,128)(2,1)S(1)}, u32[]{:S(2)}, u32[]{:S(2)}) collective-permute-start(bf16[32,1,1,4,2,2,128]{6,0,5,4,3,2,1:T(8,128)(2,1)S(1)} %get-tuple-element.34), channel_id=1, source_target_pairs={{8,0},{16,8},{24,16},{0,24},{9,1},{17,9},{25,17},{1,25},{10,2},{18... | collective-permute-start | bytes 393224 | tf_op jit(solution)/shard_map/ppermute | solution.py:60
  20.1 6.8 %collective-permute-start.4 = (bf16[32,1,1,4,2,2,128]{6,0,5,4,3,2,1:T(8,128)(2,1)S(1)}, bf16[32,1,1,4,2,2,128]{6,0,5,4,3,2,1:T(8,128)(2,1)S(1)}, u32[]{:S(2)}, u32[]{:S(2)}) collective-permute-start(bf16[32,1,1,4,2,2,128]{6,0,5,4,3,2,1:T(8,128)(2,1)S(1)} %get-tuple-element.34), channel_id=1, source_target_pairs={{24,0},{0,8},{8,16},{16,24},{25,1},{1,9},{9,17},{17,25},{26,2},{2,... | collective-permute-start | bytes 393224 | tf_op jit(solution)/shard_map/ppermute | solution.py:61
  31.8 19.2 %all-to-all-start.1 = ((f32[32,32,98]{2,1,0:T(8,128)}), f32[32,32,98]{2,1,0:T(8,128)S(1)}, u32[]{:S(2)}, u32[]{:S(2)}) async-start(f32[32,32,98]{2,1,0:T(8,128)} %broadcast_in_dim.7), calls=%async_computation.1 | async-start | bytes 1048576 | tf_op jit(solution)/shard_map/all_to_all | solution.py:151
  53.6 5.9 %copy-start.2 = (bf16[32,1,9,1,4,2,2,128]{7,0,6,5,4,3,2,1:T(8,128)(2,1)S(1)}, bf16[32,1,9,1,4,2,2,128]{7,0,6,5,4,3,2,1:T(8,128)(2,1)}, u32[]{:S(2)}) copy-start(bf16[32,1,9,1,4,2,2,128]{7,0,6,5,4,3,2,1:T(8,128)(2,1)} %get-tuple-element.30) | copy-start | bytes 3538948
  53.6 5.8 %collective-permute-start.5 = (bf16[32,1,1,4,2,2,128]{6,0,5,4,3,2,1:T(8,128)(2,1)S(1)}, bf16[32,1,1,4,2,2,128]{6,0,5,4,3,2,1:T(8,128)(2,1)S(1)}, u32[]{:S(2)}, u32[]{:S(2)}) collective-permute-start(bf16[32,1,1,4,2,2,128]{6,0,5,4,3,2,1:T(8,128)(2,1)S(1)} %get-tuple-element.31), channel_id=1, source_target_pairs={{1,0},{0,1},{3,2},{2,3},{5,4},{4,5},{7,6},{6,7},{9,8},{8,9},{11,10... | collective-permute-start | bytes 393224 | tf_op jit(solution)/shard_map/ppermute | solution.py:54
  53.7 6.0 %collective-permute-start.6 = (bf16[32,1,1,4,2,2,128]{6,0,5,4,3,2,1:T(8,128)(2,1)S(1)}, bf16[32,1,1,4,2,2,128]{6,0,5,4,3,2,1:T(8,128)(2,1)S(1)}, u32[]{:S(2)}, u32[]{:S(2)}) collective-permute-start(bf16[32,1,1,4,2,2,128]{6,0,5,4,3,2,1:T(8,128)(2,1)S(1)} %get-tuple-element.31), channel_id=1, source_target_pairs={{2,0},{3,1},{0,2},{1,3},{6,4},{7,5},{4,6},{5,7},{10,8},{11,9},{8,1... | collective-permute-start | bytes 393224 | tf_op jit(solution)/shard_map/ppermute | solution.py:54
  55.1 4.3 %collective-permute-start.7 = (bf16[32,1,1,2,2,2,128]{6,0,5,4,3,2,1:T(8,128)(2,1)S(1)}, bf16[32,1,1,2,2,2,128]{6,0,5,4,3,2,1:T(8,128)(2,1)S(1)}, u32[]{:S(2)}, u32[]{:S(2)}) collective-permute-start(bf16[32,1,1,2,2,2,128]{6,0,5,4,3,2,1:T(8,128)(2,1)S(1)} %pad_maximum_fusion.3), channel_id=1, source_target_pairs={{4,0},{5,1},{6,2},{7,3},{0,4},{1,5},{2,6},{3,7},{12,8},{13,9},{14,... | collective-permute-start | bytes 196616 | tf_op jit(solution)/shard_map/ppermute | solution.py:54
  56.3 5.4 %collective-permute-start.8 = (bf16[32,1,1,4,2,2,128]{6,0,5,4,3,2,1:T(8,128)(2,1)S(1)}, bf16[32,1,1,4,2,2,128]{6,0,5,4,3,2,1:T(8,128)(2,1)S(1)}, u32[]{:S(2)}, u32[]{:S(2)}) collective-permute-start(bf16[32,1,1,4,2,2,128]{6,0,5,4,3,2,1:T(8,128)(2,1)S(1)} %get-tuple-element.31), channel_id=1, source_target_pairs={{8,0},{16,8},{24,16},{0,24},{9,1},{17,9},{25,17},{1,25},{10,2},{18... | collective-permute-start | bytes 393224 | tf_op jit(solution)/shard_map/ppermute | solution.py:60
  57.8 6.9 %collective-permute-start.9 = (bf16[32,1,1,4,2,2,128]{6,0,5,4,3,2,1:T(8,128)(2,1)S(1)}, bf16[32,1,1,4,2,2,128]{6,0,5,4,3,2,1:T(8,128)(2,1)S(1)}, u32[]{:S(2)}, u32[]{:S(2)}) collective-permute-start(bf16[32,1,1,4,2,2,128]{6,0,5,4,3,2,1:T(8,128)(2,1)S(1)} %get-tuple-element.31), channel_id=1, source_target_pairs={{24,0},{0,8},{8,16},{16,24},{25,1},{1,9},{9,17},{17,25},{26,2},{2,... | collective-permute-start | bytes 393224 | tf_op jit(solution)/shard_map/ppermute | solution.py:61

commit v10 on v6

--- a/solution.py
+++ b/solution.py
@@ -149,16 +149,18 @@
     image_coarse = restrict_exact(null_vectors, image_a)
     pair_local = jnp.stack([inner_rows(image_a, image_a), inner_rows(image_a, residual)], 1)
     if slabs_total * blocks_total <= 64:
-        local = jnp.concatenate([pair_local, image_coarse], 1)
+        devices = slabs_total * blocks_total
+        count, width = image_coarse.shape
+        local = jnp.concatenate([pair_local.T.reshape(-1), image_coarse.reshape(-1)])
         gathered = lax.all_to_all(
-            jnp.broadcast_to(local[None], (slabs_total * blocks_total,) + local.shape),
+            jnp.broadcast_to(local[None, None], (devices, 1) + local.shape),
             ("ta", "xyz"),
             0,
             0,
-        )
-        pair = jnp.sum(gathered[:, :, :2], axis=0)
-        image_slabs = gathered[:, :, 2:].reshape(
-            (slabs_total, blocks_total) + image_coarse.shape
+        )[:, 0]
+        pair = jnp.sum(gathered[:, : 2 * count], axis=0).reshape(2, count).T
+        image_slabs = gathered[:, 2 * count :].reshape(
+            (slabs_total, blocks_total, count, width)
         )
         slab_image = slab_columns(
             lax.dynamic_index_in_dim(image_slabs, lax.axis_index("ta"), 0, keepdims=False)

time: 81.3 us -> 79.4 us (0.977)
  local copies, waits for them, and re-layouts: 8.41 us -> 7.07 us
  other arithmetic: 10.1 us -> 8.82 us
  starting transfers between devices: 11.7 us -> 12.7 us
  matrix products: 7.36 us -> 6.45 us
    ppermute x6, waiting for transfers between devices: 6.84 us -> 2.59 us  [both_sides(): pair = lax.ppermute(jnp.concatenate([first, last], which), axis, perm)]
    ppermute x2, waiting for transfers between devices: 0.01 us -> 4.17 us  [both_sides(): from_upper = lax.ppermute(first, axis, up)]
    unnamed x20 -> x19, local copies, waits for them, and re-layouts: 5.11 us -> 2.09 us
    all_to_all x1 -> x0, other arithmetic: 1.89 us -> none  [shards(): lax.all_to_all(jnp.broadcast_to(local[None], (slabs_total * blocks_total,...]
    reshape x0 -> x4, local copies, waits for them, and re-layouts: none -> 1.29 us  [the longest x1 1.04 us: shards(): gathered[:, 2 * count:].reshape((slabs_total, blocks_total, count, width))]
    dot_general x2, matrix products: 2.96 us -> 2.03 us  [finish(): jnp.einsum('tbzyxjk,nj->ntbzyxk', null_vectors, correction, preferred_ele...]
    all_to_all x1, starting transfers between devices: 2.73 us -> 3.62 us  [shards(): lax.all_to_all(jnp.broadcast_to(local[None, None], (devices, 1) + local.s...]
    convert_element_type x1, other arithmetic: 0.11 us -> 1.01 us  [shards(): slab_b = (slab_residual - step_a[:, None] * slab_image).astype(jnp.bfloat16)]
  transfers between devices with their start and end apart: 11 -> 11, of which waited for: 5 -> 8; matrix products, arithmetic and copies ran while one was open for 1% -> 1% of each run, Pallas kernels for 0% -> 0%
where the time goes in v10:
time: 79.4 us; the launch traced here: 79.1 us
  waiting for transfers between devices  22 us (28%)
  blocking collectives  20.9 us (26%)
  starting transfers between devices  12.7 us (16%)
  other arithmetic  8.82 us (11%)
  local copies, waits for them, and re-layouts  7.07 us (9%)
  matrix products  6.45 us (8%)
  between operations  1.11 us (1%)
    all_to_all x1, blocking collectives, shards(): lax.all_to_all(jnp.broadcast_to(payload[None], (blocks_total,) + payload....  10.5 us
    all_to_all x1, blocking collectives, total_sum(): return jnp.sum(lax.all_to_all(copies, axes, 0, 0), axis=0)  10.4 us
    all_to_all x1, waiting for transfers between devices, shards(): lax.all_to_all(jnp.broadcast_to(local[None, None], (devices, 1) + local.s...  9.37 us
    ppermute x2, waiting for transfers between devices, both_sides(): from_lower = lax.ppermute(last, axis, down)  5.88 us
    ppermute x2, starting transfers between devices, both_sides(): from_upper = lax.ppermute(first, axis, up)  5.14 us
    ppermute x2, waiting for transfers between devices, both_sides(): from_upper = lax.ppermute(first, axis, up)  4.17 us
    all_to_all x1, starting transfers between devices, shards(): lax.all_to_all(jnp.broadcast_to(local[None, None], (devices, 1) + local.s...  3.62 us
    ppermute x6, starting transfers between devices, both_sides(): pair = lax.ppermute(jnp.concatenate([first, last], which), axis, perm)  3.38 us
  transfers between devices with their start and end apart: 11, of which 8 were waited for; matrix products, arithmetic and copies ran while one was open for 1% of the time, Pallas kernels for 0%

profile of v10, /device:TPU:0, one launch (start us, length us, event | category | flops | bytes accessed | tf_op | source)
XLA Modules:
  0.0 79.1 jit_solution(17356184985799824195)
XLA Ops:
  0.7 1.2 %convert_bitcast_fusion = bf16[32,4,2,2,128]{4,3,2,1,0:T(2,128)(2,1)S(1)} fusion(f32[32,1,1,4,2,2,128]{6,5,4,3,2,1,0:T(2,128)} %param.4), kind=kLoop, calls=%fused_computation.85 | loop fusion | flops 65536 | bytes 393216 | tf_op jit(solution)/shard_map/reshape
  1.9 1.1 %fusion.19 = f32[32,48]{1,0:T(8,128)S(1)} fusion(bf16[32,4,2,2,128]{4,3,2,1,0:T(2,128)(2,1)S(1)} %convert_bitcast_fusion, bf16[1,1,4,2,2,48,128]{6,5,4,3,2,1,0:T(8,128)(2,1)} %param.6), kind=kOutput, calls=%fused_computation.24 | convolution fusion | flops 6294528 | bytes 333824 | tf_op jit(solution)/shard_map/tbzyxjk,ntbzyxk->nj/dot_general | solution.py:132
  3.0 1.4 %convolution_bitcast_fusion.4 = f32[32,48]{1,0:T(8,128)S(1)} fusion(f32[32,4,2,2,128]{4,3,2,1,0:T(2,128)} %bitcast.257, bf16[1,1,4,2,2,48,128]{6,5,4,3,2,1,0:T(8,128)(2,1)} %param.6), kind=kOutput, calls=%fused_computation.22 | convolution fusion | flops 37748736 | bytes 464896 | tf_op jit(solution)/shard_map/tbzyxjk,ntbzyxk->nj/dot_general | solution.py:93
  4.4 10.5 %all_to_all.15 = f32[8,32,96]{2,1,0:T(8,128)S(1)} all-to-all(f32[8,32,96]{2,1,0:T(8,128)S(1)} %broadcast_in_dim.6), channel_id=1, replica_groups=mesh['ta'=4,'xyz'=8] {'xyz'}, dimensions={0} | all-to-all | bytes 196608 | tf_op jit(solution)/shard_map/all_to_all | solution.py:142
  15.1 1.1 %bitcast_dynamic-update-slice_fusion.5 = (bf16[32,1,9,1,4,2,2,128]{7,0,6,5,4,3,2,1:T(8,128)(2,1)}, bf16[32,1,1,4,2,2,128]{6,0,5,4,3,2,1:T(8,128)(2,1)S(1)}, f32[32,1,1,4,2,2,128]{6,0,5,4,3,2,1:T(8,128)}) fusion(bf16[1,1,4,2,2,48,128]{6,5,4,3,2,1,0:T(8,128)(2,1)S(1)} %copy-done.4, bf16[32,384]{1,0:T(8,128)(2,1)S(1)} %convert_element_type.43, ...), kind=kOutput, calls=%fused_computation.83 | convolution fusion | flops 7669247 | bytes 1044480 | tf_op jit(solution)/shard_map/tbzyxjk,nj->ntbzyxk/dot_general | solution.py:113
  17.5 3.7 %collective-permute-start.3 = (bf16[32,1,1,4,2,2,128]{6,0,5,4,3,2,1:T(8,128)(2,1)S(1)}, bf16[32,1,1,4,2,2,128]{6,0,5,4,3,2,1:T(8,128)(2,1)S(1)}, u32[]{:S(2)}, u32[]{:S(2)}) collective-permute-start(bf16[32,1,1,4,2,2,128]{6,0,5,4,3,2,1:T(8,128)(2,1)S(1)} %get-tuple-element.29), channel_id=1, source_target_pairs={{8,0},{16,8},{24,16},{0,24},{9,1},{17,9},{25,17},{1,25},{10,2},{18... | collective-permute-start | bytes 393224 | tf_op jit(solution)/shard_map/ppermute | solution.py:60
  21.3 0.9 %collective-permute-done.1 = bf16[32,1,1,4,2,2,128]{6,0,5,4,3,2,1:T(8,128)(2,1)S(1)} collective-permute-done((bf16[32,1,1,4,2,2,128]{6,0,5,4,3,2,1:T(8,128)(2,1)S(1)}, bf16[32,1,1,4,2,2,128]{6,0,5,4,3,2,1:T(8,128)(2,1)S(1)}, u32[]{:S(2)}, u32[]{:S(2)}) %collective-permute-start.1) | collective-permute-done | bytes 131104 | tf_op jit(solution)/shard_map/ppermute | solution.py:54
  22.3 2.8 %collective-permute-done.3 = bf16[32,1,1,4,2,2,128]{6,0,5,4,3,2,1:T(8,128)(2,1)S(1)} collective-permute-done((bf16[32,1,1,4,2,2,128]{6,0,5,4,3,2,1:T(8,128)(2,1)S(1)}, bf16[32,1,1,4,2,2,128]{6,0,5,4,3,2,1:T(8,128)(2,1)S(1)}, u32[]{:S(2)}, u32[]{:S(2)}) %collective-permute-start.3) | collective-permute-done | bytes 131104 | tf_op jit(solution)/shard_map/ppermute | solution.py:60
  25.1 3.0 %collective-permute-done.4 = bf16[32,1,1,4,2,2,128]{6,0,5,4,3,2,1:T(8,128)(2,1)S(1)} collective-permute-done((bf16[32,1,1,4,2,2,128]{6,0,5,4,3,2,1:T(8,128)(2,1)S(1)}, bf16[32,1,1,4,2,2,128]{6,0,5,4,3,2,1:T(8,128)(2,1)S(1)}, u32[]{:S(2)}, u32[]{:S(2)}) %collective-permute-start.4) | collective-permute-done | bytes 131104 | tf_op jit(solution)/shard_map/ppermute | solution.py:61
  32.9 3.6 %all-to-all-start.1 = ((f32[32,1,1600]{2,1,0:T(1,128)}), f32[32,1,1600]{2,1,0:T(1,128)S(1)}, u32[]{:S(2)}, u32[]{:S(2)}) async-start(f32[32,1,1600]{2,1,0:T(1,128)} %broadcast_in_dim.7), calls=%async_computation.1 | async-start | bytes 425984 | tf_op jit(solution)/shard_map/all_to_all | solution.py:155
  36.5 9.4 %all-to-all-done.1 = f32[32,1,1600]{2,1,0:T(1,128)S(1)} async-done(((f32[32,1,1600]{2,1,0:T(1,128)}), f32[32,1,1600]{2,1,0:T(1,128)S(1)}, u32[]{:S(2)}, u32[]{:S(2)}) %all-to-all-start.1) | async-done | bytes 204832 | tf_op jit(solution)/shard_map/all_to_all | solution.py:155
  46.2 1.0 %reshape.380 = f32[4,8,32,48]{3,2,1,0:T(8,128)} reshape(f32[32,1536]{1,0:T(8,128)S(1)} %slice.218) | data formatting | bytes 393216 | tf_op jit(solution)/shard_map/reshape | solution.py:162
  47.2 1.0 %fusion.42 = bf16[32,8,48]{2,0,1:T(8,128)(2,1)S(1)} fusion(f32[4,8,32,48]{3,2,1,0:T(8,128)} %reshape.380, s32[]{:T(128)S(6)} %select_n.4, f32[8,32,96]{2,1,0:T(8,128)S(1)} %all_to_all.15, f32[32]{0:T(128)S(1)} %fusion.53), kind=kLoop, calls=%fused_computation.87 | loop fusion | flops 36864 | bytes 123012 | tf_op jit(solution)/shard_map/convert_element_type | solution.py:182
  48.4 1.0 %bitcast_dynamic-update-slice_fusion.2 = (bf16[32,1,9,1,4,2,2,128]{7,0,6,5,4,3,2,1:T(8,128)(2,1)}, bf16[32,1,1,4,2,2,128]{6,0,5,4,3,2,1:T(8,128)(2,1)S(1)}, f32[32,1,1,4,2,2,128]{6,0,5,4,3,2,1:T(8,128)S(1)}) fusion(bf16[1,1,4,2,2,48,128]{6,5,4,3,2,1,0:T(8,128)(2,1)S(1)} %copy-done.4, bf16[32,384]{1,0:T(8,128)(2,1)S(1)} %convert_element_type.48, ...), kind=kOutput, calls=%fused_computation.79 | convolution fusion | flops 7800319 | bytes 1306752 | tf_op jit(solution)/shard_map/tbzyxjk,nj->ntbzyxk/dot_general | solution.py:113
  50.6 1.0 %collective-permute-start.7 = (bf16[32,1,1,2,2,2,128]{6,0,5,4,3,2,1:T(8,128)(2,1)S(1)}, bf16[32,1,1,2,2,2,128]{6,0,5,4,3,2,1:T(8,128)(2,1)S(1)}, u32[]{:S(2)}, u32[]{:S(2)}) collective-permute-start(bf16[32,1,1,2,2,2,128]{6,0,5,4,3,2,1:T(8,128)(2,1)S(1)} %pad_maximum_fusion.3), channel_id=1, source_target_pairs={{4,0},{5,1},{6,2},{7,3},{0,4},{1,5},{2,6},{3,7},{12,8},{13,9},{14,... | collective-permute-start | bytes 196616 | tf_op jit(solution)/shard_map/ppermute | solution.py:54
  51.5 1.5 %collective-permute-start.8 = (bf16[32,1,1,4,2,2,128]{6,0,5,4,3,2,1:T(8,128)(2,1)S(1)}, bf16[32,1,1,4,2,2,128]{6,0,5,4,3,2,1:T(8,128)(2,1)S(1)}, u32[]{:S(2)}, u32[]{:S(2)}) collective-permute-start(bf16[32,1,1,4,2,2,128]{6,0,5,4,3,2,1:T(8,128)(2,1)S(1)} %get-tuple-element.26), channel_id=1, source_target_pairs={{8,0},{16,8},{24,16},{0,24},{9,1},{17,9},{25,17},{1,25},{10,2},{18... | collective-permute-start | bytes 393224 | tf_op jit(solution)/shard_map/ppermute | solution.py:60
  53.6 1.3 %collective-permute-done.7 = bf16[32,1,1,2,2,2,128]{6,0,5,4,3,2,1:T(8,128)(2,1)S(1)} collective-permute-done((bf16[32,1,1,2,2,2,128]{6,0,5,4,3,2,1:T(8,128)(2,1)S(1)}, bf16[32,1,1,2,2,2,128]{6,0,5,4,3,2,1:T(8,128)(2,1)S(1)}, u32[]{:S(2)}, u32[]{:S(2)}) %collective-permute-start.7) | collective-permute-done | bytes 65568 | tf_op jit(solution)/shard_map/ppermute | solution.py:54
  55.5 1.4 %collective-permute-done.8 = bf16[32,1,1,4,2,2,128]{6,0,5,4,3,2,1:T(8,128)(2,1)S(1)} collective-permute-done((bf16[32,1,1,4,2,2,128]{6,0,5,4,3,2,1:T(8,128)(2,1)S(1)}, bf16[32,1,1,4,2,2,128]{6,0,5,4,3,2,1:T(8,128)(2,1)S(1)}, u32[]{:S(2)}, u32[]{:S(2)}) %collective-permute-start.8) | collective-permute-done | bytes 131104 | tf_op jit(solution)/shard_map/ppermute | solution.py:60
  56.9 2.9 %collective-permute-done.9 = bf16[32,1,1,4,2,2,128]{6,0,5,4,3,2,1:T(8,128)(2,1)S(1)} collective-permute-done((bf16[32,1,1,4,2,2,128]{6,0,5,4,3,2,1:T(8,128)(2,1)S(1)}, bf16[32,1,1,4,2,2,128]{6,0,5,4,3,2,1:T(8,128)(2,1)S(1)}, u32[]{:S(2)}, u32[]{:S(2)}) %collective-permute-start.9) | collective-permute-done | bytes 131104 | tf_op jit(solution)/shard_map/ppermute | solution.py:61
  63.0 0.8 %fusion.11 = f32[2,32,1,1,4,2,2,64]{7,1,6,5,4,3,2,0:T(8,128)S(1)} fusion(bf16[1,1,4,2,2,9,64,128]{7,6,5,4,3,2,1,0:T(8,128)(2,1)S(1)} %copy-done, bf16[1,32,1,9,1,4,2,2,128]{8,1,7,6,5,3,4,2,0:T(8,128)(2,1)S(1)} %maximum_bitcast_fusion.5, bf16[1,32,1,9,1,4,2,2,128]{8,1,7,6,5,3,4,2,0:T(8,128)(2,1)S(1)} %maximum_bitcast_fusion.4), kind=kOutput, calls=%fused_computation.9 | convolution fusion | flops 152174592 | bytes 4980736 | tf_op jit(solution)/shard_map/tbzyxdik,pntdbzyxk->pntbzyxi/dot_general | solution.py:86
  64.3 10.4 %all_to_all.16 = f32[32,1,128]{2,1,0:T(1,128)S(1)} all-to-all(f32[32,1,128]{2,1,0:T(1,128)S(1)} %reshape.390), channel_id=1, replica_groups=mesh['ta'=4,'xyz'=8] {'ta','xyz'}, dimensions={0} | all-to-all | bytes 32768 | tf_op jit(solution)/shard_map/all_to_all | solution.py:34
  76.1 1.2 %multiply_subtract_fusion = (f32[32,1,1,4,2,2,128]{6,0,5,4,3,2,1:T(8,128)S(1)}, f32[32,1,1,4,2,2,128]{6,0,5,4,3,2,1:T(8,128)S(1)}) fusion(f32[32,1,1,4,2,2,128]{6,0,5,4,3,2,1:T(8,128)S(1)} %get-tuple-element.24, f32[32,1,1,4,2,2,128]{6,0,5,4,3,2,1:T(8,128)S(1)} %get-tuple-element.27, f32[32]{0:T(128)S(1)} %get-tuple-element.23, f32[32]{0:T(128)S(1)} %get-tuple-element.22, ...), kind=kLoop, calls=%fused_computation.37 | loop fusion | flops 720896 | bytes 1835392 | tf_op jit(solution)/shard_map/sub | solution.py:207
  77.3 0.9 %copy.160 = f32[32,1,1,4,2,2,128]{6,5,4,3,2,1,0:T(2,128)} copy(f32[32,1,1,4,2,2,128]{6,0,5,4,3,2,1:T(8,128)S(1)} %get-tuple-element.67) | data formatting | bytes 524288
  78.2 0.9 %copy.161 = f32[32,1,1,4,2,2,128]{6,5,4,3,2,1,0:T(2,128)} copy(f32[32,1,1,4,2,2,128]{6,0,5,4,3,2,1:T(8,128)S(1)} %get-tuple-element.66) | data formatting | bytes 524288
  (96 shorter events, 14.3 us)
Async XLA Ops:
  0.6 29.8 %copy-start = (bf16[1,1,4,2,2,9,64,128]{7,6,5,4,3,2,1,0:T(8,128)(2,1)S(1)}, bf16[1,1,4,2,2,9,64,128]{7,6,5,4,3,2,1,0:T(8,128)(2,1)}, u32[]{:S(2)}) copy-start(bf16[1,1,4,2,2,9,64,128]{7,6,5,4,3,2,1,0:T(8,128)(2,1)} %param.5) | copy-start | bytes 7077892
  0.6 14.4 %copy-start.1 = (f32[32,1,1,4,2,2,128]{6,5,4,3,2,1,0:T(2,128)S(1)}, f32[32,1,1,4,2,2,128]{6,5,4,3,2,1,0:T(2,128)}, u32[]{:S(2)}) copy-start(f32[32,1,1,4,2,2,128]{6,5,4,3,2,1,0:T(2,128)} %param.4) | copy-start | bytes 786436
  0.7 14.4 %copy-start.4 = (bf16[1,1,4,2,2,48,128]{6,5,4,3,2,1,0:T(8,128)(2,1)S(1)}, bf16[1,1,4,2,2,48,128]{6,5,4,3,2,1,0:T(8,128)(2,1)}, u32[]{:S(2)}) copy-start(bf16[1,1,4,2,2,48,128]{6,5,4,3,2,1,0:T(8,128)(2,1)} %param.6) | copy-start | bytes 589828
  0.7 14.4 %copy-start.5 = (bf16[1,48,384]{2,1,0:T(8,128)(2,1)S(1)}, bf16[1,48,384]{2,1,0:T(8,128)(2,1)}, u32[]{:S(2)}) copy-start(bf16[1,48,384]{2,1,0:T(8,128)(2,1)} %param.7) | copy-start | bytes 110596
  16.2 5.1 %copy-start.3 = (bf16[32,1,9,1,4,2,2,128]{7,0,6,5,4,3,2,1:T(8,128)(2,1)S(1)}, bf16[32,1,9,1,4,2,2,128]{7,0,6,5,4,3,2,1:T(8,128)(2,1)}, u32[]{:S(2)}) copy-start(bf16[32,1,9,1,4,2,2,128]{7,0,6,5,4,3,2,1:T(8,128)(2,1)} %get-tuple-element.28) | copy-start | bytes 3538948
  16.2 5.0 %collective-permute-start = (bf16[32,1,1,4,2,2,128]{6,0,5,4,3,2,1:T(8,128)(2,1)S(1)}, bf16[32,1,1,4,2,2,128]{6,0,5,4,3,2,1:T(8,128)(2,1)S(1)}, u32[]{:S(2)}, u32[]{:S(2)}) collective-permute-start(bf16[32,1,1,4,2,2,128]{6,0,5,4,3,2,1:T(8,128)(2,1)S(1)} %get-tuple-element.29), channel_id=1, source_target_pairs={{1,0},{0,1},{3,2},{2,3},{5,4},{4,5},{7,6},{6,7},{9,8},{8,9},{11,10... | collective-permute-start | bytes 393224 | tf_op jit(solution)/shard_map/ppermute | solution.py:54
  16.2 6.0 %collective-permute-start.1 = (bf16[32,1,1,4,2,2,128]{6,0,5,4,3,2,1:T(8,128)(2,1)S(1)}, bf16[32,1,1,4,2,2,128]{6,0,5,4,3,2,1:T(8,128)(2,1)S(1)}, u32[]{:S(2)}, u32[]{:S(2)}) collective-permute-start(bf16[32,1,1,4,2,2,128]{6,0,5,4,3,2,1:T(8,128)(2,1)S(1)} %get-tuple-element.29), channel_id=1, source_target_pairs={{2,0},{3,1},{0,2},{1,3},{6,4},{7,5},{4,6},{5,7},{10,8},{11,9},{8,1... | collective-permute-start | bytes 393224 | tf_op jit(solution)/shard_map/ppermute | solution.py:54
  16.9 4.3 %collective-permute-start.2 = (bf16[32,1,1,2,2,2,128]{6,0,5,4,3,2,1:T(8,128)(2,1)S(1)}, bf16[32,1,1,2,2,2,128]{6,0,5,4,3,2,1:T(8,128)(2,1)S(1)}, u32[]{:S(2)}, u32[]{:S(2)}) collective-permute-start(bf16[32,1,1,2,2,2,128]{6,0,5,4,3,2,1:T(8,128)(2,1)S(1)} %pad_maximum_fusion.2), channel_id=1, source_target_pairs={{4,0},{5,1},{6,2},{7,3},{0,4},{1,5},{2,6},{3,7},{12,8},{13,9},{14,... | collective-permute-start | bytes 196616 | tf_op jit(solution)/shard_map/ppermute | solution.py:54
  17.5 7.5 %collective-permute-start.3 = (bf16[32,1,1,4,2,2,128]{6,0,5,4,3,2,1:T(8,128)(2,1)S(1)}, bf16[32,1,1,4,2,2,128]{6,0,5,4,3,2,1:T(8,128)(2,1)S(1)}, u32[]{:S(2)}, u32[]{:S(2)}) collective-permute-start(bf16[32,1,1,4,2,2,128]{6,0,5,4,3,2,1:T(8,128)(2,1)S(1)} %get-tuple-element.29), channel_id=1, source_target_pairs={{8,0},{16,8},{24,16},{0,24},{9,1},{17,9},{25,17},{1,25},{10,2},{18... | collective-permute-start | bytes 393224 | tf_op jit(solution)/shard_map/ppermute | solution.py:60
  21.2 6.9 %collective-permute-start.4 = (bf16[32,1,1,4,2,2,128]{6,0,5,4,3,2,1:T(8,128)(2,1)S(1)}, bf16[32,1,1,4,2,2,128]{6,0,5,4,3,2,1:T(8,128)(2,1)S(1)}, u32[]{:S(2)}, u32[]{:S(2)}) collective-permute-start(bf16[32,1,1,4,2,2,128]{6,0,5,4,3,2,1:T(8,128)(2,1)S(1)} %get-tuple-element.29), channel_id=1, source_target_pairs={{24,0},{0,8},{8,16},{16,24},{25,1},{1,9},{9,17},{17,25},{26,2},{2,... | collective-permute-start | bytes 393224 | tf_op jit(solution)/shard_map/ppermute | solution.py:61
  32.9 13.0 %all-to-all-start.1 = ((f32[32,1,1600]{2,1,0:T(1,128)}), f32[32,1,1600]{2,1,0:T(1,128)S(1)}, u32[]{:S(2)}, u32[]{:S(2)}) async-start(f32[32,1,1600]{2,1,0:T(1,128)} %broadcast_in_dim.7), calls=%async_computation.1 | async-start | bytes 425984 | tf_op jit(solution)/shard_map/all_to_all | solution.py:155
  49.3 5.6 %copy-start.2 = (bf16[32,1,9,1,4,2,2,128]{7,0,6,5,4,3,2,1:T(8,128)(2,1)S(1)}, bf16[32,1,9,1,4,2,2,128]{7,0,6,5,4,3,2,1:T(8,128)(2,1)}, u32[]{:S(2)}) copy-start(bf16[32,1,9,1,4,2,2,128]{7,0,6,5,4,3,2,1:T(8,128)(2,1)} %get-tuple-element.25) | copy-start | bytes 3538948
  49.3 5.6 %collective-permute-start.5 = (bf16[32,1,1,4,2,2,128]{6,0,5,4,3,2,1:T(8,128)(2,1)S(1)}, bf16[32,1,1,4,2,2,128]{6,0,5,4,3,2,1:T(8,128)(2,1)S(1)}, u32[]{:S(2)}, u32[]{:S(2)}) collective-permute-start(bf16[32,1,1,4,2,2,128]{6,0,5,4,3,2,1:T(8,128)(2,1)S(1)} %get-tuple-element.26), channel_id=1, source_target_pairs={{1,0},{0,1},{3,2},{2,3},{5,4},{4,5},{7,6},{6,7},{9,8},{8,9},{11,10... | collective-permute-start | bytes 393224 | tf_op jit(solution)/shard_map/ppermute | solution.py:54
  49.8 5.6 %collective-permute-start.6 = (bf16[32,1,1,4,2,2,128]{6,0,5,4,3,2,1:T(8,128)(2,1)S(1)}, bf16[32,1,1,4,2,2,128]{6,0,5,4,3,2,1:T(8,128)(2,1)S(1)}, u32[]{:S(2)}, u32[]{:S(2)}) collective-permute-start(bf16[32,1,1,4,2,2,128]{6,0,5,4,3,2,1:T(8,128)(2,1)S(1)} %get-tuple-element.26), channel_id=1, source_target_pairs={{2,0},{3,1},{0,2},{1,3},{6,4},{7,5},{4,6},{5,7},{10,8},{11,9},{8,1... | collective-permute-start | bytes 393224 | tf_op jit(solution)/shard_map/ppermute | solution.py:54
  50.6 4.3 %collective-permute-start.7 = (bf16[32,1,1,2,2,2,128]{6,0,5,4,3,2,1:T(8,128)(2,1)S(1)}, bf16[32,1,1,2,2,2,128]{6,0,5,4,3,2,1:T(8,128)(2,1)S(1)}, u32[]{:S(2)}, u32[]{:S(2)}) collective-permute-start(bf16[32,1,1,2,2,2,128]{6,0,5,4,3,2,1:T(8,128)(2,1)S(1)} %pad_maximum_fusion.3), channel_id=1, source_target_pairs={{4,0},{5,1},{6,2},{7,3},{0,4},{1,5},{2,6},{3,7},{12,8},{13,9},{14,... | collective-permute-start | bytes 196616 | tf_op jit(solution)/shard_map/ppermute | solution.py:54
  51.5 5.4 %collective-permute-start.8 = (bf16[32,1,1,4,2,2,128]{6,0,5,4,3,2,1:T(8,128)(2,1)S(1)}, bf16[32,1,1,4,2,2,128]{6,0,5,4,3,2,1:T(8,128)(2,1)S(1)}, u32[]{:S(2)}, u32[]{:S(2)}) collective-permute-start(bf16[32,1,1,4,2,2,128]{6,0,5,4,3,2,1:T(8,128)(2,1)S(1)} %get-tuple-element.26), channel_id=1, source_target_pairs={{8,0},{16,8},{24,16},{0,24},{9,1},{17,9},{25,17},{1,25},{10,2},{18... | collective-permute-start | bytes 393224 | tf_op jit(solution)/shard_map/ppermute | solution.py:60
  53.0 6.9 %collective-permute-start.9 = (bf16[32,1,1,4,2,2,128]{6,0,5,4,3,2,1:T(8,128)(2,1)S(1)}, bf16[32,1,1,4,2,2,128]{6,0,5,4,3,2,1:T(8,128)(2,1)S(1)}, u32[]{:S(2)}, u32[]{:S(2)}) collective-permute-start(bf16[32,1,1,4,2,2,128]{6,0,5,4,3,2,1:T(8,128)(2,1)S(1)} %get-tuple-element.26), channel_id=1, source_target_pairs={{24,0},{0,8},{8,16},{16,24},{25,1},{1,9},{9,17},{17,25},{26,2},{2,... | collective-permute-start | bytes 393224 | tf_op jit(solution)/shard_map/ppermute | solution.py:61

commit v11 on v10

--- a/solution.py
+++ b/solution.py
@@ -30,8 +30,9 @@
 def total_sum(x):
     axes = ("ta", "xyz")
     count = lax.axis_size("ta") * lax.axis_size("xyz")
-    copies = jnp.broadcast_to(x[None], (count,) + x.shape)
-    return jnp.sum(lax.all_to_all(copies, axes, 0, 0), axis=0)
+    flat = x.reshape(-1)
+    copies = jnp.broadcast_to(flat[None, None], (count, 1) + flat.shape)
+    return jnp.sum(lax.all_to_all(copies, axes, 0, 0)[:, 0], axis=0).reshape(x.shape)
 
 
 def neighbour_source(device, stride, extent, step):
@@ -95,7 +96,7 @@
         null_vectors.astype(jnp.float32),
         field,
         preferred_element_type=jnp.float32,
-        precision=lax.Precision.HIGHEST,
+        precision=lax.Precision.HIGH,
     )
 
 

time: 79.4 us -> 76.3 us (0.961)
  starting transfers between devices: 12.7 us -> 11.7 us
    ppermute x6, waiting for transfers between devices: 2.59 us -> 6.84 us  [both_sides(): pair = lax.ppermute(jnp.concatenate([first, last], which), axis, perm)]
    ppermute x2, waiting for transfers between devices: 4.17 us -> 0.01 us  [both_sides(): from_upper = lax.ppermute(first, axis, up)]
    all_to_all x1, starting transfers between devices: 3.62 us -> 2.72 us  [shards(): lax.all_to_all(jnp.broadcast_to(local[None, None], (devices, 1) + local.s...]
    unnamed x19 -> x17, local copies, waits for them, and re-layouts: 2.09 us -> 1.9 us
  transfers between devices with their start and end apart: 11 -> 11, of which waited for: 8 -> 5; matrix products, arithmetic and copies ran while one was open for 1% -> 1% of each run, Pallas kernels for 0% -> 0%
where the time goes in v11:
time: 76.3 us; the launch traced here: 76 us
  waiting for transfers between devices  21.7 us (28%)
  blocking collectives  20.5 us (27%)
  starting transfers between devices  11.7 us (15%)
  other arithmetic  8.18 us (11%)
  local copies, waits for them, and re-layouts  6.47 us (8%)
  matrix products  6.31 us (8%)
  between operations  1.14 us (1%)
    all_to_all x1, blocking collectives, shards(): lax.all_to_all(jnp.broadcast_to(payload[None], (blocks_total,) + payload....  10.5 us
    all_to_all x1, blocking collectives, total_sum(): lax.all_to_all(copies, axes, 0, 0)[:, 0]  10 us
    all_to_all x1, waiting for transfers between devices, shards(): lax.all_to_all(jnp.broadcast_to(local[None, None], (devices, 1) + local.s...  9.37 us
    ppermute x6, waiting for transfers between devices, both_sides(): pair = lax.ppermute(jnp.concatenate([first, last], which), axis, perm)  6.84 us
    ppermute x2, waiting for transfers between devices, both_sides(): from_lower = lax.ppermute(last, axis, down)  5.45 us
    ppermute x2, starting transfers between devices, both_sides(): from_upper = lax.ppermute(first, axis, up)  5.2 us
    ppermute x6, starting transfers between devices, both_sides(): pair = lax.ppermute(jnp.concatenate([first, last], which), axis, perm)  3.3 us
    all_to_all x1, starting transfers between devices, shards(): lax.all_to_all(jnp.broadcast_to(local[None, None], (devices, 1) + local.s...  2.72 us
  transfers between devices with their start and end apart: 11, of which 5 were waited for; matrix products, arithmetic and copies ran while one was open for 1% of the time, Pallas kernels for 0%

profile of v11, /device:TPU:0, one launch (start us, length us, event | category | flops | bytes accessed | tf_op | source)
XLA Modules:
  0.0 76.0 jit_solution(6361846885754709754)
XLA Ops:
  0.7 1.2 %convert_bitcast_fusion = bf16[32,4,2,2,128]{4,3,2,1,0:T(2,128)(2,1)S(1)} fusion(f32[32,1,1,4,2,2,128]{6,5,4,3,2,1,0:T(2,128)} %param.4), kind=kLoop, calls=%fused_computation.85 | loop fusion | flops 65536 | bytes 393216 | tf_op jit(solution)/shard_map/reshape
  1.9 1.2 %convolution_bitcast_fusion.4 = f32[32,48]{1,0:T(8,128)S(1)} fusion(f32[32,4,2,2,128]{4,3,2,1,0:T(2,128)} %bitcast.238, bf16[1,1,4,2,2,48,128]{6,5,4,3,2,1,0:T(8,128)(2,1)} %param.6), kind=kOutput, calls=%fused_computation.22 | convolution fusion | flops 18874368 | bytes 464896 | tf_op jit(solution)/shard_map/tbzyxjk,ntbzyxk->nj/dot_general | solution.py:94
  3.1 1.1 %fusion.19 = f32[32,48]{1,0:T(8,128)S(1)} fusion(bf16[32,4,2,2,128]{4,3,2,1,0:T(2,128)(2,1)S(1)} %convert_bitcast_fusion, bf16[1,1,4,2,2,48,128]{6,5,4,3,2,1,0:T(8,128)(2,1)} %param.6), kind=kOutput, calls=%fused_computation.24 | convolution fusion | flops 6294528 | bytes 333824 | tf_op jit(solution)/shard_map/tbzyxjk,ntbzyxk->nj/dot_general | solution.py:133
  4.3 10.5 %all_to_all.15 = f32[8,32,96]{2,1,0:T(8,128)S(1)} all-to-all(f32[8,32,96]{2,1,0:T(8,128)S(1)} %broadcast_in_dim.8), channel_id=1, replica_groups=mesh['ta'=4,'xyz'=8] {'xyz'}, dimensions={0} | all-to-all | bytes 196608 | tf_op jit(solution)/shard_map/all_to_all | solution.py:143
  15.0 1.1 %bitcast_dynamic-update-slice_fusion.5 = (bf16[32,1,9,1,4,2,2,128]{7,0,6,5,4,3,2,1:T(8,128)(2,1)}, bf16[32,1,1,4,2,2,128]{6,0,5,4,3,2,1:T(8,128)(2,1)S(1)}, f32[32,1,1,4,2,2,128]{6,0,5,4,3,2,1:T(8,128)}) fusion(bf16[1,1,4,2,2,48,128]{6,5,4,3,2,1,0:T(8,128)(2,1)S(1)} %copy-done.4, bf16[32,384]{1,0:T(8,128)(2,1)S(1)} %convert_element_type.43, ...), kind=kOutput, calls=%fused_computation.83 | convolution fusion | flops 7669247 | bytes 1044480 | tf_op jit(solution)/shard_map/tbzyxjk,nj->ntbzyxk/dot_general | solution.py:114
  16.7 3.6 %collective-permute-start.3 = (bf16[32,1,1,4,2,2,128]{6,0,5,4,3,2,1:T(8,128)(2,1)S(1)}, bf16[32,1,1,4,2,2,128]{6,0,5,4,3,2,1:T(8,128)(2,1)S(1)}, u32[]{:S(2)}, u32[]{:S(2)}) collective-permute-start(bf16[32,1,1,4,2,2,128]{6,0,5,4,3,2,1:T(8,128)(2,1)S(1)} %get-tuple-element.29), channel_id=1, source_target_pairs={{8,0},{16,8},{24,16},{0,24},{9,1},{17,9},{25,17},{1,25},{10,2},{18... | collective-permute-start | bytes 393224 | tf_op jit(solution)/shard_map/ppermute | solution.py:61
  21.0 3.9 %collective-permute-done.2 = bf16[32,1,1,2,2,2,128]{6,0,5,4,3,2,1:T(8,128)(2,1)S(1)} collective-permute-done((bf16[32,1,1,2,2,2,128]{6,0,5,4,3,2,1:T(8,128)(2,1)S(1)}, bf16[32,1,1,2,2,2,128]{6,0,5,4,3,2,1:T(8,128)(2,1)S(1)}, u32[]{:S(2)}, u32[]{:S(2)}) %collective-permute-start.2) | collective-permute-done | bytes 65568 | tf_op jit(solution)/shard_map/ppermute | solution.py:55
  25.2 2.8 %collective-permute-done.4 = bf16[32,1,1,4,2,2,128]{6,0,5,4,3,2,1:T(8,128)(2,1)S(1)} collective-permute-done((bf16[32,1,1,4,2,2,128]{6,0,5,4,3,2,1:T(8,128)(2,1)S(1)}, bf16[32,1,1,4,2,2,128]{6,0,5,4,3,2,1:T(8,128)(2,1)S(1)}, u32[]{:S(2)}, u32[]{:S(2)}) %collective-permute-start.4) | collective-permute-done | bytes 131104 | tf_op jit(solution)/shard_map/ppermute | solution.py:62
  30.4 0.8 %fusion.6 = f32[2,32,1,1,4,2,2,64]{7,1,6,5,4,3,2,0:T(8,128)S(1)} fusion(bf16[1,1,4,2,2,9,64,128]{7,6,5,4,3,2,1,0:T(8,128)(2,1)S(1)} %copy-done, bf16[1,32,1,9,1,4,2,2,128]{8,1,7,6,5,3,4,2,0:T(8,128)(2,1)S(1)} %maximum_bitcast_fusion.3, bf16[1,32,1,9,1,4,2,2,128]{8,1,7,6,5,3,4,2,0:T(8,128)(2,1)S(1)} %maximum_bitcast_fusion.2), kind=kOutput, calls=%fused_computation.8 | convolution fusion | flops 152174592 | bytes 4980736 | tf_op jit(solution)/shard_map/tbzyxdik,pntdbzyxk->pntbzyxi/dot_general | solution.py:87
  32.9 2.7 %all-to-all-start.1 = ((f32[32,1,1600]{2,1,0:T(1,128)}), f32[32,1,1600]{2,1,0:T(1,128)S(1)}, u32[]{:S(2)}, u32[]{:S(2)}) async-start(f32[32,1,1600]{2,1,0:T(1,128)} %broadcast_in_dim.9), calls=%async_computation.1 | async-start | bytes 425984 | tf_op jit(solution)/shard_map/all_to_all | solution.py:156
  35.6 9.4 %all-to-all-done.1 = f32[32,1,1600]{2,1,0:T(1,128)S(1)} async-done(((f32[32,1,1600]{2,1,0:T(1,128)}), f32[32,1,1600]{2,1,0:T(1,128)S(1)}, u32[]{:S(2)}, u32[]{:S(2)}) %all-to-all-start.1) | async-done | bytes 204832 | tf_op jit(solution)/shard_map/all_to_all | solution.py:156
  45.2 1.1 %reshape.351 = f32[4,8,32,48]{3,2,1,0:T(8,128)} reshape(f32[32,1536]{1,0:T(8,128)S(1)} %slice.222) | data formatting | bytes 393216 | tf_op jit(solution)/shard_map/reshape | solution.py:163
  46.3 1.0 %fusion.42 = bf16[32,8,48]{2,0,1:T(8,128)(2,1)S(1)} fusion(f32[4,8,32,48]{3,2,1,0:T(8,128)} %reshape.351, s32[]{:T(128)S(6)} %select_n.4, f32[8,32,96]{2,1,0:T(8,128)S(1)} %all_to_all.15, f32[32]{0:T(128)S(1)} %fusion.50), kind=kLoop, calls=%fused_computation.87 | loop fusion | flops 36864 | bytes 123012 | tf_op jit(solution)/shard_map/convert_element_type | solution.py:183
  47.5 1.0 %bitcast_dynamic-update-slice_fusion.2 = (bf16[32,1,9,1,4,2,2,128]{7,0,6,5,4,3,2,1:T(8,128)(2,1)}, bf16[32,1,1,4,2,2,128]{6,0,5,4,3,2,1:T(8,128)(2,1)S(1)}, f32[32,1,1,4,2,2,128]{6,0,5,4,3,2,1:T(8,128)S(1)}) fusion(bf16[1,1,4,2,2,48,128]{6,5,4,3,2,1,0:T(8,128)(2,1)S(1)} %copy-done.4, bf16[32,384]{1,0:T(8,128)(2,1)S(1)} %convert_element_type.48, ...), kind=kOutput, calls=%fused_computation.79 | convolution fusion | flops 7800319 | bytes 1306752 | tf_op jit(solution)/shard_map/tbzyxjk,nj->ntbzyxk/dot_general | solution.py:114
  49.1 1.6 %collective-permute-start.8 = (bf16[32,1,1,4,2,2,128]{6,0,5,4,3,2,1:T(8,128)(2,1)S(1)}, bf16[32,1,1,4,2,2,128]{6,0,5,4,3,2,1:T(8,128)(2,1)S(1)}, u32[]{:S(2)}, u32[]{:S(2)}) collective-permute-start(bf16[32,1,1,4,2,2,128]{6,0,5,4,3,2,1:T(8,128)(2,1)S(1)} %get-tuple-element.26), channel_id=1, source_target_pairs={{8,0},{16,8},{24,16},{0,24},{9,1},{17,9},{25,17},{1,25},{10,2},{18... | collective-permute-start | bytes 393224 | tf_op jit(solution)/shard_map/ppermute | solution.py:61
  51.2 1.4 %collective-permute-start.7 = (bf16[32,1,1,2,2,2,128]{6,0,5,4,3,2,1:T(8,128)(2,1)S(1)}, bf16[32,1,1,2,2,2,128]{6,0,5,4,3,2,1:T(8,128)(2,1)S(1)}, u32[]{:S(2)}, u32[]{:S(2)}) collective-permute-start(bf16[32,1,1,2,2,2,128]{6,0,5,4,3,2,1:T(8,128)(2,1)S(1)} %pad_maximum_fusion.3), channel_id=1, source_target_pairs={{4,0},{5,1},{6,2},{7,3},{0,4},{1,5},{2,6},{3,7},{12,8},{13,9},{14,... | collective-permute-start | bytes 196616 | tf_op jit(solution)/shard_map/ppermute | solution.py:55
  52.6 2.9 %collective-permute-done.7 = bf16[32,1,1,2,2,2,128]{6,0,5,4,3,2,1:T(8,128)(2,1)S(1)} collective-permute-done((bf16[32,1,1,2,2,2,128]{6,0,5,4,3,2,1:T(8,128)(2,1)S(1)}, bf16[32,1,1,2,2,2,128]{6,0,5,4,3,2,1:T(8,128)(2,1)S(1)}, u32[]{:S(2)}, u32[]{:S(2)}) %collective-permute-start.7) | collective-permute-done | bytes 65568 | tf_op jit(solution)/shard_map/ppermute | solution.py:55
  55.8 2.6 %collective-permute-done.9 = bf16[32,1,1,4,2,2,128]{6,0,5,4,3,2,1:T(8,128)(2,1)S(1)} collective-permute-done((bf16[32,1,1,4,2,2,128]{6,0,5,4,3,2,1:T(8,128)(2,1)S(1)}, bf16[32,1,1,4,2,2,128]{6,0,5,4,3,2,1:T(8,128)(2,1)S(1)}, u32[]{:S(2)}, u32[]{:S(2)}) %collective-permute-start.9) | collective-permute-done | bytes 131104 | tf_op jit(solution)/shard_map/ppermute | solution.py:62
  59.3 0.8 %fusion.55 = (bf16[32,1,9,1,4,2,2,64]{7,0,6,5,4,2,3,1:T(8,128)(2,1)S(1)}, bf16[32,1,9,1,4,2,2,64]{7,0,6,5,4,3,2,1:T(8,128)(2,1)S(1)}) fusion(bf16[32,1,9,1,4,2,2,128]{7,0,6,5,4,2,3,1:T(8,128)(2,1)S(1)} %bitcast.239), kind=kLoop, calls=%fused_computation.111 | loop fusion | bytes 1769472 | tf_op jit(solution)/shard_map/slice | solution.py:82
  61.5 0.8 %fusion.11 = f32[2,32,1,1,4,2,2,64]{7,1,6,5,4,3,2,0:T(8,128)S(1)} fusion(bf16[1,1,4,2,2,9,64,128]{7,6,5,4,3,2,1,0:T(8,128)(2,1)S(1)} %copy-done, bf16[1,32,1,9,1,4,2,2,128]{8,1,7,6,5,3,4,2,0:T(8,128)(2,1)S(1)} %maximum_bitcast_fusion.5, bf16[1,32,1,9,1,4,2,2,128]{8,1,7,6,5,3,4,2,0:T(8,128)(2,1)S(1)} %maximum_bitcast_fusion.4), kind=kOutput, calls=%fused_computation.9 | convolution fusion | flops 152174592 | bytes 4980736 | tf_op jit(solution)/shard_map/tbzyxdik,pntdbzyxk->pntbzyxi/dot_general | solution.py:87
  62.8 10.0 %all_to_all.16 = f32[32,1,128]{2,1,0:T(1,128)S(1)} all-to-all(f32[32,1,128]{2,1,0:T(1,128)S(1)} %broadcast_in_dim.11), channel_id=1, replica_groups=mesh['ta'=4,'xyz'=8] {'ta','xyz'}, dimensions={0} | all-to-all | bytes 32768 | tf_op jit(solution)/shard_map/all_to_all | solution.py:35
  73.0 1.2 %multiply_subtract_fusion = (f32[32,1,1,4,2,2,128]{6,0,5,4,3,2,1:T(8,128)S(1)}, f32[32,1,1,4,2,2,128]{6,0,5,4,3,2,1:T(8,128)S(1)}) fusion(f32[32,1,1,4,2,2,128]{6,0,5,4,3,2,1:T(8,128)S(1)} %get-tuple-element.24, f32[32,1,1,4,2,2,128]{6,0,5,4,3,2,1:T(8,128)S(1)} %get-tuple-element.27, f32[32]{0:T(128)S(1)} %get-tuple-element.23, f32[32]{0:T(128)S(1)} %get-tuple-element.22, ...), kind=kLoop, calls=%fused_computation.37 | loop fusion | flops 720896 | bytes 1835392 | tf_op jit(solution)/shard_map/sub | solution.py:208
  74.1 0.9 %copy.161 = f32[32,1,1,4,2,2,128]{6,5,4,3,2,1,0:T(2,128)} copy(f32[32,1,1,4,2,2,128]{6,0,5,4,3,2,1:T(8,128)S(1)} %get-tuple-element.66) | data formatting | bytes 524288
  75.0 0.9 %copy.160 = f32[32,1,1,4,2,2,128]{6,5,4,3,2,1,0:T(2,128)} copy(f32[32,1,1,4,2,2,128]{6,0,5,4,3,2,1:T(8,128)S(1)} %get-tuple-element.67) | data formatting | bytes 524288
  (93 shorter events, 10.2 us)
Async XLA Ops:
  0.6 29.8 %copy-start = (bf16[1,1,4,2,2,9,64,128]{7,6,5,4,3,2,1,0:T(8,128)(2,1)S(1)}, bf16[1,1,4,2,2,9,64,128]{7,6,5,4,3,2,1,0:T(8,128)(2,1)}, u32[]{:S(2)}) copy-start(bf16[1,1,4,2,2,9,64,128]{7,6,5,4,3,2,1,0:T(8,128)(2,1)} %param.5) | copy-start | bytes 7077892
  0.6 14.3 %copy-start.1 = (f32[32,1,1,4,2,2,128]{6,5,4,3,2,1,0:T(2,128)S(1)}, f32[32,1,1,4,2,2,128]{6,5,4,3,2,1,0:T(2,128)}, u32[]{:S(2)}) copy-start(f32[32,1,1,4,2,2,128]{6,5,4,3,2,1,0:T(2,128)} %param.4) | copy-start | bytes 786436
  0.7 14.3 %copy-start.4 = (bf16[1,1,4,2,2,48,128]{6,5,4,3,2,1,0:T(8,128)(2,1)S(1)}, bf16[1,1,4,2,2,48,128]{6,5,4,3,2,1,0:T(8,128)(2,1)}, u32[]{:S(2)}) copy-start(bf16[1,1,4,2,2,48,128]{6,5,4,3,2,1,0:T(8,128)(2,1)} %param.6) | copy-start | bytes 589828
  0.7 14.3 %copy-start.5 = (bf16[1,48,384]{2,1,0:T(8,128)(2,1)S(1)}, bf16[1,48,384]{2,1,0:T(8,128)(2,1)}, u32[]{:S(2)}) copy-start(bf16[1,48,384]{2,1,0:T(8,128)(2,1)} %param.7) | copy-start | bytes 110596
  16.1 8.9 %copy-start.3 = (bf16[32,1,9,1,4,2,2,128]{7,0,6,5,4,3,2,1:T(8,128)(2,1)S(1)}, bf16[32,1,9,1,4,2,2,128]{7,0,6,5,4,3,2,1:T(8,128)(2,1)}, u32[]{:S(2)}) copy-start(bf16[32,1,9,1,4,2,2,128]{7,0,6,5,4,3,2,1:T(8,128)(2,1)} %get-tuple-element.28) | copy-start | bytes 3538948
  16.1 8.9 %collective-permute-start.1 = (bf16[32,1,1,4,2,2,128]{6,0,5,4,3,2,1:T(8,128)(2,1)S(1)}, bf16[32,1,1,4,2,2,128]{6,0,5,4,3,2,1:T(8,128)(2,1)S(1)}, u32[]{:S(2)}, u32[]{:S(2)}) collective-permute-start(bf16[32,1,1,4,2,2,128]{6,0,5,4,3,2,1:T(8,128)(2,1)S(1)} %get-tuple-element.29), channel_id=1, source_target_pairs={{2,0},{3,1},{0,2},{1,3},{6,4},{7,5},{4,6},{5,7},{10,8},{11,9},{8,1... | collective-permute-start | bytes 393224 | tf_op jit(solution)/shard_map/ppermute | solution.py:55
  16.7 8.5 %collective-permute-start.3 = (bf16[32,1,1,4,2,2,128]{6,0,5,4,3,2,1:T(8,128)(2,1)S(1)}, bf16[32,1,1,4,2,2,128]{6,0,5,4,3,2,1:T(8,128)(2,1)S(1)}, u32[]{:S(2)}, u32[]{:S(2)}) collective-permute-start(bf16[32,1,1,4,2,2,128]{6,0,5,4,3,2,1:T(8,128)(2,1)S(1)} %get-tuple-element.29), channel_id=1, source_target_pairs={{8,0},{16,8},{24,16},{0,24},{9,1},{17,9},{25,17},{1,25},{10,2},{18... | collective-permute-start | bytes 393224 | tf_op jit(solution)/shard_map/ppermute | solution.py:61
  20.3 4.6 %collective-permute-start = (bf16[32,1,1,4,2,2,128]{6,0,5,4,3,2,1:T(8,128)(2,1)S(1)}, bf16[32,1,1,4,2,2,128]{6,0,5,4,3,2,1:T(8,128)(2,1)S(1)}, u32[]{:S(2)}, u32[]{:S(2)}) collective-permute-start(bf16[32,1,1,4,2,2,128]{6,0,5,4,3,2,1:T(8,128)(2,1)S(1)} %get-tuple-element.29), channel_id=1, source_target_pairs={{1,0},{0,1},{3,2},{2,3},{5,4},{4,5},{7,6},{6,7},{9,8},{8,9},{11,10... | collective-permute-start | bytes 393224 | tf_op jit(solution)/shard_map/ppermute | solution.py:55
  20.4 7.7 %collective-permute-start.4 = (bf16[32,1,1,4,2,2,128]{6,0,5,4,3,2,1:T(8,128)(2,1)S(1)}, bf16[32,1,1,4,2,2,128]{6,0,5,4,3,2,1:T(8,128)(2,1)S(1)}, u32[]{:S(2)}, u32[]{:S(2)}) collective-permute-start(bf16[32,1,1,4,2,2,128]{6,0,5,4,3,2,1:T(8,128)(2,1)S(1)} %get-tuple-element.29), channel_id=1, source_target_pairs={{24,0},{0,8},{8,16},{16,24},{25,1},{1,9},{9,17},{17,25},{26,2},{2,... | collective-permute-start | bytes 393224 | tf_op jit(solution)/shard_map/ppermute | solution.py:62
  20.4 4.6 %collective-permute-start.2 = (bf16[32,1,1,2,2,2,128]{6,0,5,4,3,2,1:T(8,128)(2,1)S(1)}, bf16[32,1,1,2,2,2,128]{6,0,5,4,3,2,1:T(8,128)(2,1)S(1)}, u32[]{:S(2)}, u32[]{:S(2)}) collective-permute-start(bf16[32,1,1,2,2,2,128]{6,0,5,4,3,2,1:T(8,128)(2,1)S(1)} %pad_maximum_fusion.2), channel_id=1, source_target_pairs={{4,0},{5,1},{6,2},{7,3},{0,4},{1,5},{2,6},{3,7},{12,8},{13,9},{14,... | collective-permute-start | bytes 196616 | tf_op jit(solution)/shard_map/ppermute | solution.py:55
  32.9 12.1 %all-to-all-start.1 = ((f32[32,1,1600]{2,1,0:T(1,128)}), f32[32,1,1600]{2,1,0:T(1,128)S(1)}, u32[]{:S(2)}, u32[]{:S(2)}) async-start(f32[32,1,1600]{2,1,0:T(1,128)} %broadcast_in_dim.9), calls=%async_computation.1 | async-start | bytes 425984 | tf_op jit(solution)/shard_map/all_to_all | solution.py:156
  48.4 7.1 %copy-start.2 = (bf16[32,1,9,1,4,2,2,128]{7,0,6,5,4,3,2,1:T(8,128)(2,1)S(1)}, bf16[32,1,9,1,4,2,2,128]{7,0,6,5,4,3,2,1:T(8,128)(2,1)}, u32[]{:S(2)}) copy-start(bf16[32,1,9,1,4,2,2,128]{7,0,6,5,4,3,2,1:T(8,128)(2,1)} %get-tuple-element.25) | copy-start | bytes 3538948
  48.5 7.1 %collective-permute-start.6 = (bf16[32,1,1,4,2,2,128]{6,0,5,4,3,2,1:T(8,128)(2,1)S(1)}, bf16[32,1,1,4,2,2,128]{6,0,5,4,3,2,1:T(8,128)(2,1)S(1)}, u32[]{:S(2)}, u32[]{:S(2)}) collective-permute-start(bf16[32,1,1,4,2,2,128]{6,0,5,4,3,2,1:T(8,128)(2,1)S(1)} %get-tuple-element.26), channel_id=1, source_target_pairs={{2,0},{3,1},{0,2},{1,3},{6,4},{7,5},{4,6},{5,7},{10,8},{11,9},{8,1... | collective-permute-start | bytes 393224 | tf_op jit(solution)/shard_map/ppermute | solution.py:55
  49.1 6.6 %collective-permute-start.8 = (bf16[32,1,1,4,2,2,128]{6,0,5,4,3,2,1:T(8,128)(2,1)S(1)}, bf16[32,1,1,4,2,2,128]{6,0,5,4,3,2,1:T(8,128)(2,1)S(1)}, u32[]{:S(2)}, u32[]{:S(2)}) collective-permute-start(bf16[32,1,1,4,2,2,128]{6,0,5,4,3,2,1:T(8,128)(2,1)S(1)} %get-tuple-element.26), channel_id=1, source_target_pairs={{8,0},{16,8},{24,16},{0,24},{9,1},{17,9},{25,17},{1,25},{10,2},{18... | collective-permute-start | bytes 393224 | tf_op jit(solution)/shard_map/ppermute | solution.py:61
  50.7 4.8 %collective-permute-start.5 = (bf16[32,1,1,4,2,2,128]{6,0,5,4,3,2,1:T(8,128)(2,1)S(1)}, bf16[32,1,1,4,2,2,128]{6,0,5,4,3,2,1:T(8,128)(2,1)S(1)}, u32[]{:S(2)}, u32[]{:S(2)}) collective-permute-start(bf16[32,1,1,4,2,2,128]{6,0,5,4,3,2,1:T(8,128)(2,1)S(1)} %get-tuple-element.26), channel_id=1, source_target_pairs={{1,0},{0,1},{3,2},{2,3},{5,4},{4,5},{7,6},{6,7},{9,8},{8,9},{11,10... | collective-permute-start | bytes 393224 | tf_op jit(solution)/shard_map/ppermute | solution.py:55
  50.7 7.7 %collective-permute-start.9 = (bf16[32,1,1,4,2,2,128]{6,0,5,4,3,2,1:T(8,128)(2,1)S(1)}, bf16[32,1,1,4,2,2,128]{6,0,5,4,3,2,1:T(8,128)(2,1)S(1)}, u32[]{:S(2)}, u32[]{:S(2)}) collective-permute-start(bf16[32,1,1,4,2,2,128]{6,0,5,4,3,2,1:T(8,128)(2,1)S(1)} %get-tuple-element.26), channel_id=1, source_target_pairs={{24,0},{0,8},{8,16},{16,24},{25,1},{1,9},{9,17},{17,25},{26,2},{2,... | collective-permute-start | bytes 393224 | tf_op jit(solution)/shard_map/ppermute | solution.py:62
  51.2 4.3 %collective-permute-start.7 = (bf16[32,1,1,2,2,2,128]{6,0,5,4,3,2,1:T(8,128)(2,1)S(1)}, bf16[32,1,1,2,2,2,128]{6,0,5,4,3,2,1:T(8,128)(2,1)S(1)}, u32[]{:S(2)}, u32[]{:S(2)}) collective-permute-start(bf16[32,1,1,2,2,2,128]{6,0,5,4,3,2,1:T(8,128)(2,1)S(1)} %pad_maximum_fusion.3), channel_id=1, source_target_pairs={{4,0},{5,1},{6,2},{7,3},{0,4},{1,5},{2,6},{3,7},{12,8},{13,9},{14,... | collective-permute-start | bytes 196616 | tf_op jit(solution)/shard_map/ppermute | solution.py:55

commit v12 on v11

--- a/solution.py
+++ b/solution.py
@@ -130,21 +130,15 @@
     slabs_total = lax.axis_size("ta")
     blocks_total = lax.axis_size("xyz")
     residual = right_side
-    coarse = jnp.einsum(
-        "tbzyxjk,ntbzyxk->nj",
-        null_vectors,
-        residual.astype(jnp.bfloat16),
-        preferred_element_type=jnp.float32,
-    ).astype(jnp.bfloat16)
-    width = coarse.shape[1]
-    payload = jnp.concatenate(
-        [coarse.astype(jnp.float32), restrict_exact(null_vectors, residual)], 1
-    )
+    exact_residual = restrict_exact(null_vectors, residual)
     parts = lax.all_to_all(
-        jnp.broadcast_to(payload[None], (blocks_total,) + payload.shape), "xyz", 0, 0
-    )
-    slab_a = slab_columns(parts[:, :, :width]).astype(jnp.bfloat16)
-    slab_residual = slab_columns(parts[:, :, width:])
+        jnp.broadcast_to(exact_residual[None], (blocks_total,) + exact_residual.shape),
+        "xyz",
+        0,
+        0,
+    )
+    slab_residual = slab_columns(parts)
+    slab_a = slab_residual.astype(jnp.bfloat16)
     direction_a = finish(residual, slab_a, null_vectors, inverse_rows)
     image_a = apply_links(coarse_links, direction_a.astype(jnp.bfloat16))
     image_coarse = restrict_exact(null_vectors, image_a)

time: 76.3 us -> 83.2 us (1.090)
  local copies, waits for them, and re-layouts: 6.47 us -> 16.8 us
  waiting for transfers between devices: 21.7 us -> 18.4 us
  other arithmetic: 8.18 us -> 6.74 us
  matrix products: 6.31 us -> 7.66 us
    slice x6, local copies, waits for them, and re-layouts: 0.05 us -> 5.08 us  [both_sides(): first = lax.slice_in_dim(lowered, 0, 1, axis=which)]
    unnamed x17 -> x25, local copies, waits for them, and re-layouts: 1.9 us -> 4.59 us
    dot_general x2, matrix products: 2.06 us -> 4.36 us  [finish(): jnp.einsum('tbzyxjk,nj->ntbzyxk', null_vectors, correction, preferred_ele...]
    slice x2, local copies, waits for them, and re-layouts: 0.04 us -> 1.98 us  [both_sides(): lax.slice_in_dim(lowered, 0, length - 1, axis=which)]
    ppermute x6, waiting for transfers between devices: 6.84 us -> 5.07 us  [both_sides(): pair = lax.ppermute(jnp.concatenate([first, last], which), axis, perm)]
    ppermute x2, waiting for transfers between devices: 5.45 us -> 3.98 us  [both_sides(): from_lower = lax.ppermute(last, axis, down)]
    reshape x1 -> x0, other arithmetic: 1.19 us -> none
    dot_general x1 -> x0, matrix products: 1.09 us -> none  [shards(): jnp.einsum('tbzyxjk,ntbzyxk->nj', null_vectors, residual.astype(jnp.bfloa...]
  transfers between devices with their start and end apart: 11 -> 11, of which waited for: 5 -> 5; matrix products, arithmetic and copies ran while one was open for 1% -> 5% of each run, Pallas kernels for 0% -> 0%
where the time goes in v12:
time: 83.2 us; the launch traced here: 82.4 us
  blocking collectives  19.9 us (24%)
  waiting for transfers between devices  18.4 us (22%)
  local copies, waits for them, and re-layouts  16.8 us (20%)
  starting transfers between devices  11.7 us (14%)
  matrix products  7.66 us (9%)
  other arithmetic  6.74 us (8%)
  between operations  1.18 us (1%)
    all_to_all x1, blocking collectives, total_sum(): lax.all_to_all(copies, axes, 0, 0)[:, 0]  10 us
    all_to_all x1, blocking collectives, shards(): lax.all_to_all(jnp.broadcast_to(exact_residual[None], (blocks_total,) + e...  9.9 us
    all_to_all x1, waiting for transfers between devices, shards(): lax.all_to_all(jnp.broadcast_to(local[None, None], (devices, 1) + local.s...  9.37 us
    ppermute x2, starting transfers between devices, both_sides(): from_upper = lax.ppermute(first, axis, up)  5.2 us
    slice x6, local copies, waits for them, and re-layouts, both_sides(): first = lax.slice_in_dim(lowered, 0, 1, axis=which)  5.08 us
    ppermute x6, waiting for transfers between devices, both_sides(): pair = lax.ppermute(jnp.concatenate([first, last], which), axis, perm)  5.07 us
    unnamed x25, local copies, waits for them, and re-layouts  4.59 us
    dot_general x2, matrix products, finish(): jnp.einsum('tbzyxjk,nj->ntbzyxk', null_vectors, correction, preferred_ele...  4.36 us
  transfers between devices with their start and end apart: 11, of which 5 were waited for; matrix products, arithmetic and copies ran while one was open for 5% of the time, Pallas kernels for 0%

profile of v12, /device:TPU:0, one launch (start us, length us, event | category | flops | bytes accessed | tf_op | source)
XLA Modules:
  0.0 82.4 jit_solution(18073142270918958635)
XLA Ops:
  0.6 1.4 %convolution_bitcast_fusion.3 = f32[32,48]{1,0:T(8,128)S(1)} fusion(f32[32,4,2,2,128]{4,3,2,1,0:T(2,128)} %bitcast.229, bf16[1,1,4,2,2,48,128]{6,5,4,3,2,1,0:T(8,128)(2,1)} %param.6), kind=kOutput, calls=%fused_computation.21 | convolution fusion | flops 18874368 | bytes 464896 | tf_op jit(solution)/shard_map/tbzyxjk,ntbzyxk->nj/dot_general | solution.py:94
  2.2 9.9 %all_to_all.15 = f32[8,1,1536]{2,1,0:T(1,128)S(1)} all-to-all(f32[8,1,1536]{2,1,0:T(1,128)S(1)} %reshape.354), channel_id=1, replica_groups=mesh['ta'=4,'xyz'=8] {'xyz'}, dimensions={0} | all-to-all | bytes 98304 | tf_op jit(solution)/shard_map/all_to_all | solution.py:134
  14.9 2.1 %bitcast_dynamic-update-slice_fusion.5 = (bf16[32,1,9,1,4,2,2,128]{7,0,6,5,4,3,2,1:T(8,128)(2,1)S(1)}, bf16[32,1,1,4,2,2,128]{6,0,5,4,3,2,1:T(8,128)(2,1)}, f32[32,1,1,4,2,2,128]{6,0,5,4,3,2,1:T(8,128)}) fusion(bf16[1,1,4,2,2,48,128]{6,5,4,3,2,1,0:T(8,128)(2,1)} %param.6, bf16[32,384]{1,0:T(8,128)(2,1)} %convert_element_type.34, ...), kind=kOutput, calls=%fused_computation.78 | convolution fusion | flops 7669247 | bytes 1044480 | tf_op jit(solution)/shard_map/tbzyxjk,nj->ntbzyxk/dot_general | solution.py:114
  17.8 0.9 %fusion.62 = (bf16[32,1,1,4,1,2,128]{6,0,5,4,3,2,1:T(8,128)(2,1)S(1)}, bf16[32,1,1,4,1,2,128]{6,0,5,4,3,2,1:T(8,128)(2,1)S(1)}) fusion(bf16[32,1,1,4,2,2,128]{6,0,5,4,3,2,1:T(8,128)(2,1)} %get-tuple-element.29), kind=kLoop, calls=%fused_computation.114 | loop fusion | bytes 262144 | tf_op jit(solution)/shard_map/slice | solution.py:46
  19.3 3.6 %collective-permute-start.3 = (bf16[32,1,1,4,2,2,128]{6,0,5,4,3,2,1:T(8,128)(2,1)}, bf16[32,1,1,4,2,2,128]{6,0,5,4,3,2,1:T(8,128)(2,1)S(1)}, u32[]{:S(2)}, u32[]{:S(2)}) collective-permute-start(bf16[32,1,1,4,2,2,128]{6,0,5,4,3,2,1:T(8,128)(2,1)} %get-tuple-element.29), channel_id=1, source_target_pairs={{8,0},{16,8},{24,16},{0,24},{9,1},{17,9},{25,17},{1,25},{10,2},{18... | collective-permute-start | bytes 393224 | tf_op jit(solution)/shard_map/ppermute | solution.py:61
  22.9 1.0 %fusion.59 = (bf16[32,1,1,3,2,2,128]{6,0,5,4,3,2,1:T(8,128)(2,1)S(1)}, bf16[32,1,1,3,2,2,128]{6,0,5,4,3,2,1:T(8,128)(2,1)S(1)}) fusion(bf16[32,1,1,4,2,2,128]{6,0,5,4,3,2,1:T(8,128)(2,1)} %get-tuple-element.29), kind=kLoop, calls=%fused_computation.111 | loop fusion | bytes 393216 | tf_op jit(solution)/shard_map/slice | solution.py:65
  24.6 0.9 %fusion.64 = (bf16[32,1,1,4,2,1,128]{6,0,5,4,3,2,1:T(8,128)(2,1)S(1)}, bf16[32,1,1,4,2,1,128]{6,0,5,4,3,2,1:T(8,128)(2,1)S(1)}) fusion(bf16[32,1,1,4,2,2,128]{6,0,5,4,3,2,1:T(8,128)(2,1)} %get-tuple-element.29), kind=kLoop, calls=%fused_computation.116 | loop fusion | bytes 262144 | tf_op jit(solution)/shard_map/slice | solution.py:46
  25.4 3.0 %collective-permute-done.2 = bf16[32,1,1,2,2,2,128]{6,0,5,4,3,2,1:T(8,128)(2,1)S(1)} collective-permute-done((bf16[32,1,1,2,2,2,128]{6,0,5,4,3,2,1:T(8,128)(2,1)S(1)}, bf16[32,1,1,2,2,2,128]{6,0,5,4,3,2,1:T(8,128)(2,1)S(1)}, u32[]{:S(2)}, u32[]{:S(2)}) %collective-permute-start.2) | collective-permute-done | bytes 65568 | tf_op jit(solution)/shard_map/ppermute | solution.py:55
  28.7 2.1 %collective-permute-done.4 = bf16[32,1,1,4,2,2,128]{6,0,5,4,3,2,1:T(8,128)(2,1)S(1)} collective-permute-done((bf16[32,1,1,4,2,2,128]{6,0,5,4,3,2,1:T(8,128)(2,1)}, bf16[32,1,1,4,2,2,128]{6,0,5,4,3,2,1:T(8,128)(2,1)S(1)}, u32[]{:S(2)}, u32[]{:S(2)}) %collective-permute-start.4) | collective-permute-done | bytes 131104 | tf_op jit(solution)/shard_map/ppermute | solution.py:62
  34.1 0.9 %copy-done.1 = f32[32,1,1,4,2,2,128]{6,5,4,3,2,1,0:T(2,128)S(1)} copy-done((f32[32,1,1,4,2,2,128]{6,5,4,3,2,1,0:T(2,128)S(1)}, f32[32,1,1,4,2,2,128]{6,5,4,3,2,1,0:T(2,128)}, u32[]{:S(2)}) %copy-start.1) | copy-done | bytes 262168
  36.6 2.8 %all-to-all-start.1 = ((f32[32,1,1600]{2,1,0:T(1,128)}), f32[32,1,1600]{2,1,0:T(1,128)S(1)}, u32[]{:S(2)}, u32[]{:S(2)}) async-start(f32[32,1,1600]{2,1,0:T(1,128)} %broadcast_in_dim.9), calls=%async_computation.1 | async-start | bytes 425984 | tf_op jit(solution)/shard_map/all_to_all | solution.py:150
  39.3 9.4 %all-to-all-done.1 = f32[32,1,1600]{2,1,0:T(1,128)S(1)} async-done(((f32[32,1,1600]{2,1,0:T(1,128)}), f32[32,1,1600]{2,1,0:T(1,128)S(1)}, u32[]{:S(2)}, u32[]{:S(2)}) %all-to-all-start.1) | async-done | bytes 204832 | tf_op jit(solution)/shard_map/all_to_all | solution.py:150
  50.1 2.2 %bitcast_dynamic-update-slice_fusion.2 = (bf16[32,1,9,1,4,2,2,128]{7,0,6,5,4,3,2,1:T(8,128)(2,1)S(1)}, bf16[32,1,1,4,2,2,128]{6,0,5,4,3,2,1:T(8,128)(2,1)}, f32[32,1,1,4,2,2,128]{6,0,5,4,3,2,1:T(8,128)}) fusion(bf16[1,1,4,2,2,48,128]{6,5,4,3,2,1,0:T(8,128)(2,1)} %param.6, bf16[32,384]{1,0:T(8,128)(2,1)} %convert_element_type.39, ...), kind=kOutput, calls=%fused_computation.72 | convolution fusion | flops 7800319 | bytes 1306752 | tf_op jit(solution)/shard_map/tbzyxjk,nj->ntbzyxk/dot_general | solution.py:114
  53.1 0.9 %fusion.56 = (bf16[32,1,1,4,1,2,128]{6,0,5,4,3,2,1:T(8,128)(2,1)S(1)}, bf16[32,1,1,4,1,2,128]{6,0,5,4,3,2,1:T(8,128)(2,1)S(1)}) fusion(bf16[32,1,1,4,2,2,128]{6,0,5,4,3,2,1:T(8,128)(2,1)} %get-tuple-element.26), kind=kLoop, calls=%fused_computation.108 | loop fusion | bytes 262144 | tf_op jit(solution)/shard_map/slice | solution.py:46
  54.6 1.6 %collective-permute-start.8 = (bf16[32,1,1,4,2,2,128]{6,0,5,4,3,2,1:T(8,128)(2,1)}, bf16[32,1,1,4,2,2,128]{6,0,5,4,3,2,1:T(8,128)(2,1)S(1)}, u32[]{:S(2)}, u32[]{:S(2)}) collective-permute-start(bf16[32,1,1,4,2,2,128]{6,0,5,4,3,2,1:T(8,128)(2,1)} %get-tuple-element.26), channel_id=1, source_target_pairs={{8,0},{16,8},{24,16},{0,24},{9,1},{17,9},{25,17},{1,25},{10,2},{18... | collective-permute-start | bytes 393224 | tf_op jit(solution)/shard_map/ppermute | solution.py:61
  56.6 1.0 %fusion.53 = (bf16[32,1,1,3,2,2,128]{6,0,5,4,3,2,1:T(8,128)(2,1)S(1)}, bf16[32,1,1,3,2,2,128]{6,0,5,4,3,2,1:T(8,128)(2,1)S(1)}) fusion(bf16[32,1,1,4,2,2,128]{6,0,5,4,3,2,1:T(8,128)(2,1)} %get-tuple-element.26), kind=kLoop, calls=%fused_computation.105 | loop fusion | bytes 393216 | tf_op jit(solution)/shard_map/slice | solution.py:65
  57.6 1.4 %collective-permute-start.7 = (bf16[32,1,1,2,2,2,128]{6,0,5,4,3,2,1:T(8,128)(2,1)S(1)}, bf16[32,1,1,2,2,2,128]{6,0,5,4,3,2,1:T(8,128)(2,1)S(1)}, u32[]{:S(2)}, u32[]{:S(2)}) collective-permute-start(bf16[32,1,1,2,2,2,128]{6,0,5,4,3,2,1:T(8,128)(2,1)S(1)} %pad_maximum_fusion.3), channel_id=1, source_target_pairs={{4,0},{5,1},{6,2},{7,3},{0,4},{1,5},{2,6},{3,7},{12,8},{13,9},{14,... | collective-permute-start | bytes 196616 | tf_op jit(solution)/shard_map/ppermute | solution.py:55
  59.0 0.9 %fusion.58 = (bf16[32,1,1,4,2,1,128]{6,0,5,4,3,2,1:T(8,128)(2,1)S(1)}, bf16[32,1,1,4,2,1,128]{6,0,5,4,3,2,1:T(8,128)(2,1)S(1)}) fusion(bf16[32,1,1,4,2,2,128]{6,0,5,4,3,2,1:T(8,128)(2,1)} %get-tuple-element.26), kind=kLoop, calls=%fused_computation.110 | loop fusion | bytes 262144 | tf_op jit(solution)/shard_map/slice | solution.py:46
  59.9 2.0 %collective-permute-done.7 = bf16[32,1,1,2,2,2,128]{6,0,5,4,3,2,1:T(8,128)(2,1)S(1)} collective-permute-done((bf16[32,1,1,2,2,2,128]{6,0,5,4,3,2,1:T(8,128)(2,1)S(1)}, bf16[32,1,1,2,2,2,128]{6,0,5,4,3,2,1:T(8,128)(2,1)S(1)}, u32[]{:S(2)}, u32[]{:S(2)}) %collective-permute-start.7) | collective-permute-done | bytes 65568 | tf_op jit(solution)/shard_map/ppermute | solution.py:55
  62.2 1.9 %collective-permute-done.9 = bf16[32,1,1,4,2,2,128]{6,0,5,4,3,2,1:T(8,128)(2,1)S(1)} collective-permute-done((bf16[32,1,1,4,2,2,128]{6,0,5,4,3,2,1:T(8,128)(2,1)}, bf16[32,1,1,4,2,2,128]{6,0,5,4,3,2,1:T(8,128)(2,1)S(1)}, u32[]{:S(2)}, u32[]{:S(2)}) %collective-permute-start.9) | collective-permute-done | bytes 131104 | tf_op jit(solution)/shard_map/ppermute | solution.py:62
  69.3 10.0 %all_to_all.16 = f32[32,1,128]{2,1,0:T(1,128)S(1)} all-to-all(f32[32,1,128]{2,1,0:T(1,128)S(1)} %broadcast_in_dim.11), channel_id=1, replica_groups=mesh['ta'=4,'xyz'=8] {'ta','xyz'}, dimensions={0} | all-to-all | bytes 32768 | tf_op jit(solution)/shard_map/all_to_all | solution.py:35
  79.4 1.2 %multiply_subtract_fusion = (f32[32,1,1,4,2,2,128]{6,0,5,4,3,2,1:T(8,128)S(1)}, f32[32,1,1,4,2,2,128]{6,0,5,4,3,2,1:T(8,128)S(1)}) fusion(f32[32,1,1,4,2,2,128]{6,0,5,4,3,2,1:T(8,128)S(1)} %get-tuple-element.24, f32[32,1,1,4,2,2,128]{6,0,5,4,3,2,1:T(8,128)S(1)} %copy-done.4, f32[32]{0:T(128)S(1)} %get-tuple-element.23, f32[32]{0:T(128)S(1)} %get-tuple-element.22, ...), kind=kLoop, calls=%fused_computation.34 | loop fusion | flops 720896 | bytes 1835392 | tf_op jit(solution)/shard_map/sub | solution.py:202
  80.6 0.9 %copy.147 = f32[32,1,1,4,2,2,128]{6,5,4,3,2,1,0:T(2,128)} copy(f32[32,1,1,4,2,2,128]{6,0,5,4,3,2,1:T(8,128)S(1)} %get-tuple-element.66) | data formatting | bytes 524288
  81.5 0.9 %copy.146 = f32[32,1,1,4,2,2,128]{6,5,4,3,2,1,0:T(2,128)} copy(f32[32,1,1,4,2,2,128]{6,0,5,4,3,2,1:T(8,128)S(1)} %get-tuple-element.67) | data formatting | bytes 524288
  (100 shorter events, 18.4 us)
Async XLA Ops:
  0.6 32.6 %copy-start = (bf16[1,1,4,2,2,9,64,128]{7,6,5,4,3,2,1,0:T(8,128)(2,1)S(1)}, bf16[1,1,4,2,2,9,64,128]{7,6,5,4,3,2,1,0:T(8,128)(2,1)}, u32[]{:S(2)}) copy-start(bf16[1,1,4,2,2,9,64,128]{7,6,5,4,3,2,1,0:T(8,128)(2,1)} %param.5) | copy-start | bytes 7077892
  13.5 0.7 copy-start.6
  18.7 9.9 %collective-permute-start.1 = (bf16[32,1,1,4,2,2,128]{6,0,5,4,3,2,1:T(8,128)(2,1)}, bf16[32,1,1,4,2,2,128]{6,0,5,4,3,2,1:T(8,128)(2,1)S(1)}, u32[]{:S(2)}, u32[]{:S(2)}) collective-permute-start(bf16[32,1,1,4,2,2,128]{6,0,5,4,3,2,1:T(8,128)(2,1)} %get-tuple-element.29), channel_id=1, source_target_pairs={{2,0},{3,1},{0,2},{1,3},{6,4},{7,5},{4,6},{5,7},{10,8},{11,9},{8,1... | collective-permute-start | bytes 393224 | tf_op jit(solution)/shard_map/ppermute | solution.py:55
  19.3 9.4 %collective-permute-start.3 = (bf16[32,1,1,4,2,2,128]{6,0,5,4,3,2,1:T(8,128)(2,1)}, bf16[32,1,1,4,2,2,128]{6,0,5,4,3,2,1:T(8,128)(2,1)S(1)}, u32[]{:S(2)}, u32[]{:S(2)}) collective-permute-start(bf16[32,1,1,4,2,2,128]{6,0,5,4,3,2,1:T(8,128)(2,1)} %get-tuple-element.29), channel_id=1, source_target_pairs={{8,0},{16,8},{24,16},{0,24},{9,1},{17,9},{25,17},{1,25},{10,2},{18... | collective-permute-start | bytes 393224 | tf_op jit(solution)/shard_map/ppermute | solution.py:61
  22.9 5.6 %collective-permute-start = (bf16[32,1,1,4,2,2,128]{6,0,5,4,3,2,1:T(8,128)(2,1)}, bf16[32,1,1,4,2,2,128]{6,0,5,4,3,2,1:T(8,128)(2,1)S(1)}, u32[]{:S(2)}, u32[]{:S(2)}) collective-permute-start(bf16[32,1,1,4,2,2,128]{6,0,5,4,3,2,1:T(8,128)(2,1)} %get-tuple-element.29), channel_id=1, source_target_pairs={{1,0},{0,1},{3,2},{2,3},{5,4},{4,5},{7,6},{6,7},{9,8},{8,9},{11,10... | collective-permute-start | bytes 393224 | tf_op jit(solution)/shard_map/ppermute | solution.py:55
  22.9 7.9 %collective-permute-start.4 = (bf16[32,1,1,4,2,2,128]{6,0,5,4,3,2,1:T(8,128)(2,1)}, bf16[32,1,1,4,2,2,128]{6,0,5,4,3,2,1:T(8,128)(2,1)S(1)}, u32[]{:S(2)}, u32[]{:S(2)}) collective-permute-start(bf16[32,1,1,4,2,2,128]{6,0,5,4,3,2,1:T(8,128)(2,1)} %get-tuple-element.29), channel_id=1, source_target_pairs={{24,0},{0,8},{8,16},{16,24},{25,1},{1,9},{9,17},{17,25},{26,2},{2,... | collective-permute-start | bytes 393224 | tf_op jit(solution)/shard_map/ppermute | solution.py:62
  23.9 4.5 %collective-permute-start.2 = (bf16[32,1,1,2,2,2,128]{6,0,5,4,3,2,1:T(8,128)(2,1)S(1)}, bf16[32,1,1,2,2,2,128]{6,0,5,4,3,2,1:T(8,128)(2,1)S(1)}, u32[]{:S(2)}, u32[]{:S(2)}) collective-permute-start(bf16[32,1,1,2,2,2,128]{6,0,5,4,3,2,1:T(8,128)(2,1)S(1)} %pad_maximum_fusion.2), channel_id=1, source_target_pairs={{4,0},{5,1},{6,2},{7,3},{0,4},{1,5},{2,6},{3,7},{12,8},{13,9},{14,... | collective-permute-start | bytes 196616 | tf_op jit(solution)/shard_map/ppermute | solution.py:55
  34.0 1.0 %copy-start.1 = (f32[32,1,1,4,2,2,128]{6,5,4,3,2,1,0:T(2,128)S(1)}, f32[32,1,1,4,2,2,128]{6,5,4,3,2,1,0:T(2,128)}, u32[]{:S(2)}) copy-start(f32[32,1,1,4,2,2,128]{6,5,4,3,2,1,0:T(2,128)} %param.4) | copy-start | bytes 786436
  34.1 1.3 %copy-start.5 = (bf16[1,1,4,2,2,48,128]{6,5,4,3,2,1,0:T(8,128)(2,1)S(1)}, bf16[1,1,4,2,2,48,128]{6,5,4,3,2,1,0:T(8,128)(2,1)}, u32[]{:S(2)}) copy-start(bf16[1,1,4,2,2,48,128]{6,5,4,3,2,1,0:T(8,128)(2,1)} %param.6) | copy-start | bytes 589828
  35.2 14.0 %copy-start.3 = (f32[32,1,1,4,2,2,128]{6,0,5,4,3,2,1:T(8,128)}, f32[32,1,1,4,2,2,128]{6,0,5,4,3,2,1:T(8,128)S(1)}, u32[]{:S(2)}) copy-start(f32[32,1,1,4,2,2,128]{6,0,5,4,3,2,1:T(8,128)S(1)} %get-tuple-element.27) | copy-start | bytes 786436
  35.6 13.7 %copy-start.7 = (f32[8,32,48]{2,1,0:T(8,128)S(1)}, f32[8,32,48]{2,1,0:T(8,128)}, u32[]{:S(2)}) copy-start(f32[8,32,48]{2,1,0:T(8,128)} %copy-done.6) | copy-start | bytes 147460
  36.6 12.2 %all-to-all-start.1 = ((f32[32,1,1600]{2,1,0:T(1,128)}), f32[32,1,1600]{2,1,0:T(1,128)S(1)}, u32[]{:S(2)}, u32[]{:S(2)}) async-start(f32[32,1,1600]{2,1,0:T(1,128)} %broadcast_in_dim.9), calls=%async_computation.1 | async-start | bytes 425984 | tf_op jit(solution)/shard_map/all_to_all | solution.py:150
  54.0 8.1 %collective-permute-start.6 = (bf16[32,1,1,4,2,2,128]{6,0,5,4,3,2,1:T(8,128)(2,1)}, bf16[32,1,1,4,2,2,128]{6,0,5,4,3,2,1:T(8,128)(2,1)S(1)}, u32[]{:S(2)}, u32[]{:S(2)}) collective-permute-start(bf16[32,1,1,4,2,2,128]{6,0,5,4,3,2,1:T(8,128)(2,1)} %get-tuple-element.26), channel_id=1, source_target_pairs={{2,0},{3,1},{0,2},{1,3},{6,4},{7,5},{4,6},{5,7},{10,8},{11,9},{8,1... | collective-permute-start | bytes 393224 | tf_op jit(solution)/shard_map/ppermute | solution.py:55
  54.6 7.6 %collective-permute-start.8 = (bf16[32,1,1,4,2,2,128]{6,0,5,4,3,2,1:T(8,128)(2,1)}, bf16[32,1,1,4,2,2,128]{6,0,5,4,3,2,1:T(8,128)(2,1)S(1)}, u32[]{:S(2)}, u32[]{:S(2)}) collective-permute-start(bf16[32,1,1,4,2,2,128]{6,0,5,4,3,2,1:T(8,128)(2,1)} %get-tuple-element.26), channel_id=1, source_target_pairs={{8,0},{16,8},{24,16},{0,24},{9,1},{17,9},{25,17},{1,25},{10,2},{18... | collective-permute-start | bytes 393224 | tf_op jit(solution)/shard_map/ppermute | solution.py:61
  56.2 5.8 %collective-permute-start.5 = (bf16[32,1,1,4,2,2,128]{6,0,5,4,3,2,1:T(8,128)(2,1)}, bf16[32,1,1,4,2,2,128]{6,0,5,4,3,2,1:T(8,128)(2,1)S(1)}, u32[]{:S(2)}, u32[]{:S(2)}) collective-permute-start(bf16[32,1,1,4,2,2,128]{6,0,5,4,3,2,1:T(8,128)(2,1)} %get-tuple-element.26), channel_id=1, source_target_pairs={{1,0},{0,1},{3,2},{2,3},{5,4},{4,5},{7,6},{6,7},{9,8},{8,9},{11,10... | collective-permute-start | bytes 393224 | tf_op jit(solution)/shard_map/ppermute | solution.py:55
  56.2 7.9 %collective-permute-start.9 = (bf16[32,1,1,4,2,2,128]{6,0,5,4,3,2,1:T(8,128)(2,1)}, bf16[32,1,1,4,2,2,128]{6,0,5,4,3,2,1:T(8,128)(2,1)S(1)}, u32[]{:S(2)}, u32[]{:S(2)}) collective-permute-start(bf16[32,1,1,4,2,2,128]{6,0,5,4,3,2,1:T(8,128)(2,1)} %get-tuple-element.26), channel_id=1, source_target_pairs={{24,0},{0,8},{8,16},{16,24},{25,1},{1,9},{9,17},{17,25},{26,2},{2,... | collective-permute-start | bytes 393224 | tf_op jit(solution)/shard_map/ppermute | solution.py:62
  57.6 4.3 %collective-permute-start.7 = (bf16[32,1,1,2,2,2,128]{6,0,5,4,3,2,1:T(8,128)(2,1)S(1)}, bf16[32,1,1,2,2,2,128]{6,0,5,4,3,2,1:T(8,128)(2,1)S(1)}, u32[]{:S(2)}, u32[]{:S(2)}) collective-permute-start(bf16[32,1,1,2,2,2,128]{6,0,5,4,3,2,1:T(8,128)(2,1)S(1)} %pad_maximum_fusion.3), channel_id=1, source_target_pairs={{4,0},{5,1},{6,2},{7,3},{0,4},{1,5},{2,6},{3,7},{12,8},{13,9},{14,... | collective-permute-start | bytes 196616 | tf_op jit(solution)/shard_map/ppermute | solution.py:55
  67.8 1.0 %copy-start.2 = (f32[32,1,1,4,2,2,128]{6,5,4,3,2,1,0:T(2,128)S(1)}, f32[32,1,1,4,2,2,128]{6,5,4,3,2,1,0:T(2,128)}, u32[]{:S(2)}) copy-start(f32[32,1,1,4,2,2,128]{6,5,4,3,2,1,0:T(2,128)} %param.4) | copy-start | bytes 786436
  67.8 1.0 %copy-start.4 = (f32[32,1,1,4,2,2,128]{6,0,5,4,3,2,1:T(8,128)S(1)}, f32[32,1,1,4,2,2,128]{6,0,5,4,3,2,1:T(8,128)}, u32[]{:S(2)}) copy-start(f32[32,1,1,4,2,2,128]{6,0,5,4,3,2,1:T(8,128)} %copy-done.3) | copy-start | bytes 786436
  67.8 11.6 %copy-start.8 = (f32[32,1,1,4,2,2,128]{6,0,5,4,3,2,1:T(8,128)S(1)}, f32[32,1,1,4,2,2,128]{6,0,5,4,3,2,1:T(8,128)}, u32[]{:S(2)}) copy-start(f32[32,1,1,4,2,2,128]{6,0,5,4,3,2,1:T(8,128)} %get-tuple-element.69) | copy-start | bytes 786436

commit v13 on v11

--- a/solution.py
+++ b/solution.py
@@ -144,7 +144,7 @@
         jnp.broadcast_to(payload[None], (blocks_total,) + payload.shape), "xyz", 0, 0
     )
     slab_a = slab_columns(parts[:, :, :width]).astype(jnp.bfloat16)
-    slab_residual = slab_columns(parts[:, :, width:])
+    slab_residual = parts[:, :, width:].reshape(blocks_total, -1)
     direction_a = finish(residual, slab_a, null_vectors, inverse_rows)
     image_a = apply_links(coarse_links, direction_a.astype(jnp.bfloat16))
     image_coarse = restrict_exact(null_vectors, image_a)
@@ -161,26 +161,26 @@
         )[:, 0]
         pair = jnp.sum(gathered[:, : 2 * count], axis=0).reshape(2, count).T
         image_slabs = gathered[:, 2 * count :].reshape(
-            (slabs_total, blocks_total, count, width)
+            (slabs_total, blocks_total, count * width)
         )
-        slab_image = slab_columns(
-            lax.dynamic_index_in_dim(image_slabs, lax.axis_index("ta"), 0, keepdims=False)
+        slab_image = lax.dynamic_index_in_dim(
+            image_slabs, lax.axis_index("ta"), 0, keepdims=False
         )
     else:
         pair = total_sum(pair_local)
-        slab_image = slab_columns(
-            lax.all_to_all(
-                jnp.broadcast_to(image_coarse[None], (blocks_total,) + image_coarse.shape),
-                "xyz",
-                0,
-                0,
-            )
-        )
+        slab_image = lax.all_to_all(
+            jnp.broadcast_to(image_coarse[None], (blocks_total,) + image_coarse.shape),
+            "xyz",
+            0,
+            0,
+        ).reshape(blocks_total, -1)
     norm_a, correlation_a = pair[:, 0], pair[:, 1]
     step_a = correlation_a / (norm_a + EPS)
     solution = scaled(step_a, direction_a)
     residual = residual - scaled(step_a, image_a)
-    slab_b = (slab_residual - step_a[:, None] * slab_image).astype(jnp.bfloat16)
+    steps = jnp.repeat(step_a, slab_image.shape[1] // step_a.shape[0])
+    slab_b = (slab_residual - steps[None, :] * slab_image).astype(jnp.bfloat16)
+    slab_b = slab_columns(slab_b.reshape(blocks_total, step_a.shape[0], -1))
     direction_b = finish(residual, slab_b, null_vectors, inverse_rows)
     image_b = apply_links(coarse_links, direction_b.astype(jnp.bfloat16))
     sums = total_sum(

time: 76.3 us -> 74.4 us (0.975)
  local copies, waits for them, and re-layouts: 6.47 us -> 5.52 us
  other arithmetic: 8.18 us -> 7.27 us
    convert_element_type x1 -> x0, other arithmetic: 1.01 us -> none  [shards(): slab_b = (slab_residual - step_a[:, None] * slab_image).astype(jnp.bfloat16)]
    reshape x1 -> x2, local copies, waits for them, and re-layouts: 1.06 us -> 0.22 us  [the longest x1 0.11 us: slab_columns(): return jnp.transpose(parts, (1, 0, 2)).reshape(parts.shape[1], -1)]
where the time goes in v13:
time: 74.4 us; the launch traced here: 74.1 us
  waiting for transfers between devices  21.7 us (29%)
  blocking collectives  20.5 us (28%)
  starting transfers between devices  11.7 us (16%)
  other arithmetic  7.27 us (10%)
  matrix products  6.31 us (8%)
  local copies, waits for them, and re-layouts  5.52 us (7%)
  between operations  1.15 us (2%)
    all_to_all x1, blocking collectives, shards(): lax.all_to_all(jnp.broadcast_to(payload[None], (blocks_total,) + payload....  10.5 us
    all_to_all x1, blocking collectives, total_sum(): lax.all_to_all(copies, axes, 0, 0)[:, 0]  10 us
    all_to_all x1, waiting for transfers between devices, shards(): lax.all_to_all(jnp.broadcast_to(local[None, None], (devices, 1) + local.s...  9.37 us
    ppermute x6, waiting for transfers between devices, both_sides(): pair = lax.ppermute(jnp.concatenate([first, last], which), axis, perm)  6.84 us
    ppermute x2, waiting for transfers between devices, both_sides(): from_lower = lax.ppermute(last, axis, down)  5.45 us
    ppermute x2, starting transfers between devices, both_sides(): from_upper = lax.ppermute(first, axis, up)  5.2 us
    ppermute x6, starting transfers between devices, both_sides(): pair = lax.ppermute(jnp.concatenate([first, last], which), axis, perm)  3.3 us
    all_to_all x1, starting transfers between devices, shards(): lax.all_to_all(jnp.broadcast_to(local[None, None], (devices, 1) + local.s...  2.72 us
  transfers between devices with their start and end apart: 11, of which 5 were waited for; matrix products, arithmetic and copies ran while one was open for 1% of the time, Pallas kernels for 0%

profile of v13, /device:TPU:0, one launch (start us, length us, event | category | flops | bytes accessed | tf_op | source)
XLA Modules:
  0.0 74.1 jit_solution(1992378650685724611)
XLA Ops:
  0.7 1.2 %convert_bitcast_fusion = bf16[32,4,2,2,128]{4,3,2,1,0:T(2,128)(2,1)S(1)} fusion(f32[32,1,1,4,2,2,128]{6,5,4,3,2,1,0:T(2,128)} %param.4), kind=kLoop, calls=%fused_computation.85 | loop fusion | flops 65536 | bytes 393216 | tf_op jit(solution)/shard_map/reshape
  1.9 1.2 %convolution_bitcast_fusion.4 = f32[32,48]{1,0:T(8,128)S(1)} fusion(f32[32,4,2,2,128]{4,3,2,1,0:T(2,128)} %bitcast.232, bf16[1,1,4,2,2,48,128]{6,5,4,3,2,1,0:T(8,128)(2,1)} %param.6), kind=kOutput, calls=%fused_computation.22 | convolution fusion | flops 18874368 | bytes 464896 | tf_op jit(solution)/shard_map/tbzyxjk,ntbzyxk->nj/dot_general | solution.py:94
  3.1 1.1 %fusion.19 = f32[32,48]{1,0:T(8,128)S(1)} fusion(bf16[32,4,2,2,128]{4,3,2,1,0:T(2,128)(2,1)S(1)} %convert_bitcast_fusion, bf16[1,1,4,2,2,48,128]{6,5,4,3,2,1,0:T(8,128)(2,1)} %param.6), kind=kOutput, calls=%fused_computation.24 | convolution fusion | flops 6294528 | bytes 333824 | tf_op jit(solution)/shard_map/tbzyxjk,ntbzyxk->nj/dot_general | solution.py:133
  4.3 10.5 %all_to_all.15 = f32[8,32,96]{2,1,0:T(8,128)S(1)} all-to-all(f32[8,32,96]{2,1,0:T(8,128)S(1)} %broadcast_in_dim.8), channel_id=1, replica_groups=mesh['ta'=4,'xyz'=8] {'xyz'}, dimensions={0} | all-to-all | bytes 196608 | tf_op jit(solution)/shard_map/all_to_all | solution.py:143
  15.0 1.1 %bitcast_dynamic-update-slice_fusion.5 = (bf16[32,1,9,1,4,2,2,128]{7,0,6,5,4,3,2,1:T(8,128)(2,1)}, bf16[32,1,1,4,2,2,128]{6,0,5,4,3,2,1:T(8,128)(2,1)S(1)}, f32[32,1,1,4,2,2,128]{6,0,5,4,3,2,1:T(8,128)}) fusion(bf16[1,1,4,2,2,48,128]{6,5,4,3,2,1,0:T(8,128)(2,1)S(1)} %copy-done.4, bf16[32,384]{1,0:T(8,128)(2,1)S(1)} %convert_element_type.38, ...), kind=kOutput, calls=%fused_computation.83 | convolution fusion | flops 7669247 | bytes 1044480 | tf_op jit(solution)/shard_map/tbzyxjk,nj->ntbzyxk/dot_general | solution.py:114
  16.7 3.6 %collective-permute-start.3 = (bf16[32,1,1,4,2,2,128]{6,0,5,4,3,2,1:T(8,128)(2,1)S(1)}, bf16[32,1,1,4,2,2,128]{6,0,5,4,3,2,1:T(8,128)(2,1)S(1)}, u32[]{:S(2)}, u32[]{:S(2)}) collective-permute-start(bf16[32,1,1,4,2,2,128]{6,0,5,4,3,2,1:T(8,128)(2,1)S(1)} %get-tuple-element.27), channel_id=1, source_target_pairs={{8,0},{16,8},{24,16},{0,24},{9,1},{17,9},{25,17},{1,25},{10,2},{18... | collective-permute-start | bytes 393224 | tf_op jit(solution)/shard_map/ppermute | solution.py:61
  21.0 3.9 %collective-permute-done.2 = bf16[32,1,1,2,2,2,128]{6,0,5,4,3,2,1:T(8,128)(2,1)S(1)} collective-permute-done((bf16[32,1,1,2,2,2,128]{6,0,5,4,3,2,1:T(8,128)(2,1)S(1)}, bf16[32,1,1,2,2,2,128]{6,0,5,4,3,2,1:T(8,128)(2,1)S(1)}, u32[]{:S(2)}, u32[]{:S(2)}) %collective-permute-start.2) | collective-permute-done | bytes 65568 | tf_op jit(solution)/shard_map/ppermute | solution.py:55
  25.2 2.8 %collective-permute-done.4 = bf16[32,1,1,4,2,2,128]{6,0,5,4,3,2,1:T(8,128)(2,1)S(1)} collective-permute-done((bf16[32,1,1,4,2,2,128]{6,0,5,4,3,2,1:T(8,128)(2,1)S(1)}, bf16[32,1,1,4,2,2,128]{6,0,5,4,3,2,1:T(8,128)(2,1)S(1)}, u32[]{:S(2)}, u32[]{:S(2)}) %collective-permute-start.4) | collective-permute-done | bytes 131104 | tf_op jit(solution)/shard_map/ppermute | solution.py:62
  30.4 0.8 %fusion.6 = f32[2,32,1,1,4,2,2,64]{7,1,6,5,4,3,2,0:T(8,128)S(1)} fusion(bf16[1,1,4,2,2,9,64,128]{7,6,5,4,3,2,1,0:T(8,128)(2,1)S(1)} %copy-done, bf16[1,32,1,9,1,4,2,2,128]{8,1,7,6,5,3,4,2,0:T(8,128)(2,1)S(1)} %maximum_bitcast_fusion.3, bf16[1,32,1,9,1,4,2,2,128]{8,1,7,6,5,3,4,2,0:T(8,128)(2,1)S(1)} %maximum_bitcast_fusion.2), kind=kOutput, calls=%fused_computation.8 | convolution fusion | flops 152174592 | bytes 4980736 | tf_op jit(solution)/shard_map/tbzyxdik,pntdbzyxk->pntbzyxi/dot_general | solution.py:87
  32.1 0.8 %broadcast_in_dim.9 = f32[32,1,1600]{2,1,0:T(1,128)} broadcast(f32[1600]{0:T(1024)S(1)} %pad_maximum_fusion.5), dimensions={2} | broadcast | bytes 211200 | tf_op jit(solution)/shard_map/broadcast_in_dim | solution.py:157
  32.9 2.7 %all-to-all-start.1 = ((f32[32,1,1600]{2,1,0:T(1,128)}), f32[32,1,1600]{2,1,0:T(1,128)S(1)}, u32[]{:S(2)}, u32[]{:S(2)}) async-start(f32[32,1,1600]{2,1,0:T(1,128)} %broadcast_in_dim.9), calls=%async_computation.1 | async-start | bytes 425984 | tf_op jit(solution)/shard_map/all_to_all | solution.py:156
  35.6 9.4 %all-to-all-done.1 = f32[32,1,1600]{2,1,0:T(1,128)S(1)} async-done(((f32[32,1,1600]{2,1,0:T(1,128)}), f32[32,1,1600]{2,1,0:T(1,128)S(1)}, u32[]{:S(2)}, u32[]{:S(2)}) %all-to-all-start.1) | async-done | bytes 204832 | tf_op jit(solution)/shard_map/all_to_all | solution.py:156
  45.6 1.0 %bitcast_dynamic-update-slice_fusion.2 = (bf16[32,1,9,1,4,2,2,128]{7,0,6,5,4,3,2,1:T(8,128)(2,1)}, bf16[32,1,1,4,2,2,128]{6,0,5,4,3,2,1:T(8,128)(2,1)S(1)}, f32[32,1,1,4,2,2,128]{6,0,5,4,3,2,1:T(8,128)S(1)}) fusion(bf16[1,1,4,2,2,48,128]{6,5,4,3,2,1,0:T(8,128)(2,1)S(1)} %copy-done.4, bf16[32,384]{1,0:T(8,128)(2,1)S(1)} %reshape.356, ...), kind=kOutput, calls=%fused_computation.80 | convolution fusion | flops 7800319 | bytes 1306752 | tf_op jit(solution)/shard_map/tbzyxjk,nj->ntbzyxk/dot_general | solution.py:114
  47.2 1.6 %collective-permute-start.8 = (bf16[32,1,1,4,2,2,128]{6,0,5,4,3,2,1:T(8,128)(2,1)S(1)}, bf16[32,1,1,4,2,2,128]{6,0,5,4,3,2,1:T(8,128)(2,1)S(1)}, u32[]{:S(2)}, u32[]{:S(2)}) collective-permute-start(bf16[32,1,1,4,2,2,128]{6,0,5,4,3,2,1:T(8,128)(2,1)S(1)} %get-tuple-element.24), channel_id=1, source_target_pairs={{8,0},{16,8},{24,16},{0,24},{9,1},{17,9},{25,17},{1,25},{10,2},{18... | collective-permute-start | bytes 393224 | tf_op jit(solution)/shard_map/ppermute | solution.py:61
  49.3 1.4 %collective-permute-start.7 = (bf16[32,1,1,2,2,2,128]{6,0,5,4,3,2,1:T(8,128)(2,1)S(1)}, bf16[32,1,1,2,2,2,128]{6,0,5,4,3,2,1:T(8,128)(2,1)S(1)}, u32[]{:S(2)}, u32[]{:S(2)}) collective-permute-start(bf16[32,1,1,2,2,2,128]{6,0,5,4,3,2,1:T(8,128)(2,1)S(1)} %pad_maximum_fusion.3), channel_id=1, source_target_pairs={{4,0},{5,1},{6,2},{7,3},{0,4},{1,5},{2,6},{3,7},{12,8},{13,9},{14,... | collective-permute-start | bytes 196616 | tf_op jit(solution)/shard_map/ppermute | solution.py:55
  50.7 2.9 %collective-permute-done.7 = bf16[32,1,1,2,2,2,128]{6,0,5,4,3,2,1:T(8,128)(2,1)S(1)} collective-permute-done((bf16[32,1,1,2,2,2,128]{6,0,5,4,3,2,1:T(8,128)(2,1)S(1)}, bf16[32,1,1,2,2,2,128]{6,0,5,4,3,2,1:T(8,128)(2,1)S(1)}, u32[]{:S(2)}, u32[]{:S(2)}) %collective-permute-start.7) | collective-permute-done | bytes 65568 | tf_op jit(solution)/shard_map/ppermute | solution.py:55
  53.9 2.6 %collective-permute-done.9 = bf16[32,1,1,4,2,2,128]{6,0,5,4,3,2,1:T(8,128)(2,1)S(1)} collective-permute-done((bf16[32,1,1,4,2,2,128]{6,0,5,4,3,2,1:T(8,128)(2,1)S(1)}, bf16[32,1,1,4,2,2,128]{6,0,5,4,3,2,1:T(8,128)(2,1)S(1)}, u32[]{:S(2)}, u32[]{:S(2)}) %collective-permute-start.9) | collective-permute-done | bytes 131104 | tf_op jit(solution)/shard_map/ppermute | solution.py:62
  57.5 0.8 %fusion.54 = (bf16[32,1,9,1,4,2,2,64]{7,0,6,5,4,2,3,1:T(8,128)(2,1)S(1)}, bf16[32,1,9,1,4,2,2,64]{7,0,6,5,4,3,2,1:T(8,128)(2,1)S(1)}) fusion(bf16[32,1,9,1,4,2,2,128]{7,0,6,5,4,2,3,1:T(8,128)(2,1)S(1)} %bitcast.233), kind=kLoop, calls=%fused_computation.110 | loop fusion | bytes 1769472 | tf_op jit(solution)/shard_map/slice | solution.py:82
  58.3 0.7 maximum_bitcast_fusion.4
  59.6 0.9 %fusion.11 = f32[2,32,1,1,4,2,2,64]{7,1,6,5,4,3,2,0:T(8,128)S(1)} fusion(bf16[1,1,4,2,2,9,64,128]{7,6,5,4,3,2,1,0:T(8,128)(2,1)S(1)} %copy-done, bf16[1,32,1,9,1,4,2,2,128]{8,1,7,6,5,3,4,2,0:T(8,128)(2,1)S(1)} %maximum_bitcast_fusion.5, bf16[1,32,1,9,1,4,2,2,128]{8,1,7,6,5,3,4,2,0:T(8,128)(2,1)S(1)} %maximum_bitcast_fusion.4), kind=kOutput, calls=%fused_computation.9 | convolution fusion | flops 152174592 | bytes 4980736 | tf_op jit(solution)/shard_map/tbzyxdik,pntdbzyxk->pntbzyxi/dot_general | solution.py:87
  61.0 10.0 %all_to_all.16 = f32[32,1,128]{2,1,0:T(1,128)S(1)} all-to-all(f32[32,1,128]{2,1,0:T(1,128)S(1)} %broadcast_in_dim.11), channel_id=1, replica_groups=mesh['ta'=4,'xyz'=8] {'ta','xyz'}, dimensions={0} | all-to-all | bytes 32768 | tf_op jit(solution)/shard_map/all_to_all | solution.py:35
  71.1 1.2 %multiply_subtract_fusion = (f32[32,1,1,4,2,2,128]{6,0,5,4,3,2,1:T(8,128)S(1)}, f32[32,1,1,4,2,2,128]{6,0,5,4,3,2,1:T(8,128)S(1)}) fusion(f32[32,1,1,4,2,2,128]{6,0,5,4,3,2,1:T(8,128)S(1)} %get-tuple-element.22, f32[32,1,1,4,2,2,128]{6,0,5,4,3,2,1:T(8,128)S(1)} %get-tuple-element.25, f32[32]{0:T(128)S(1)} %get-tuple-element.21, f32[32]{0:T(128)S(1)} %get-tuple-element.20, ...), kind=kLoop, calls=%fused_computation.37 | loop fusion | flops 720896 | bytes 1835392 | tf_op jit(solution)/shard_map/sub | solution.py:208
  72.3 0.9 %copy.140 = f32[32,1,1,4,2,2,128]{6,5,4,3,2,1,0:T(2,128)} copy(f32[32,1,1,4,2,2,128]{6,0,5,4,3,2,1:T(8,128)S(1)} %get-tuple-element.64) | data formatting | bytes 524288
  73.2 0.9 %copy.139 = f32[32,1,1,4,2,2,128]{6,5,4,3,2,1,0:T(2,128)} copy(f32[32,1,1,4,2,2,128]{6,0,5,4,3,2,1:T(8,128)S(1)} %get-tuple-element.65) | data formatting | bytes 524288
  (93 shorter events, 8.9 us)
Async XLA Ops:
  0.6 29.8 %copy-start = (bf16[1,1,4,2,2,9,64,128]{7,6,5,4,3,2,1,0:T(8,128)(2,1)S(1)}, bf16[1,1,4,2,2,9,64,128]{7,6,5,4,3,2,1,0:T(8,128)(2,1)}, u32[]{:S(2)}) copy-start(bf16[1,1,4,2,2,9,64,128]{7,6,5,4,3,2,1,0:T(8,128)(2,1)} %param.5) | copy-start | bytes 7077892
  0.6 14.3 %copy-start.1 = (f32[32,1,1,4,2,2,128]{6,5,4,3,2,1,0:T(2,128)S(1)}, f32[32,1,1,4,2,2,128]{6,5,4,3,2,1,0:T(2,128)}, u32[]{:S(2)}) copy-start(f32[32,1,1,4,2,2,128]{6,5,4,3,2,1,0:T(2,128)} %param.4) | copy-start | bytes 786436
  0.7 14.3 %copy-start.4 = (bf16[1,1,4,2,2,48,128]{6,5,4,3,2,1,0:T(8,128)(2,1)S(1)}, bf16[1,1,4,2,2,48,128]{6,5,4,3,2,1,0:T(8,128)(2,1)}, u32[]{:S(2)}) copy-start(bf16[1,1,4,2,2,48,128]{6,5,4,3,2,1,0:T(8,128)(2,1)} %param.6) | copy-start | bytes 589828
  0.7 14.3 %copy-start.5 = (bf16[1,48,384]{2,1,0:T(8,128)(2,1)S(1)}, bf16[1,48,384]{2,1,0:T(8,128)(2,1)}, u32[]{:S(2)}) copy-start(bf16[1,48,384]{2,1,0:T(8,128)(2,1)} %param.7) | copy-start | bytes 110596
  16.1 8.9 %copy-start.3 = (bf16[32,1,9,1,4,2,2,128]{7,0,6,5,4,3,2,1:T(8,128)(2,1)S(1)}, bf16[32,1,9,1,4,2,2,128]{7,0,6,5,4,3,2,1:T(8,128)(2,1)}, u32[]{:S(2)}) copy-start(bf16[32,1,9,1,4,2,2,128]{7,0,6,5,4,3,2,1:T(8,128)(2,1)} %get-tuple-element.26) | copy-start | bytes 3538948
  16.1 8.9 %collective-permute-start.1 = (bf16[32,1,1,4,2,2,128]{6,0,5,4,3,2,1:T(8,128)(2,1)S(1)}, bf16[32,1,1,4,2,2,128]{6,0,5,4,3,2,1:T(8,128)(2,1)S(1)}, u32[]{:S(2)}, u32[]{:S(2)}) collective-permute-start(bf16[32,1,1,4,2,2,128]{6,0,5,4,3,2,1:T(8,128)(2,1)S(1)} %get-tuple-element.27), channel_id=1, source_target_pairs={{2,0},{3,1},{0,2},{1,3},{6,4},{7,5},{4,6},{5,7},{10,8},{11,9},{8,1... | collective-permute-start | bytes 393224 | tf_op jit(solution)/shard_map/ppermute | solution.py:55
  16.7 8.5 %collective-permute-start.3 = (bf16[32,1,1,4,2,2,128]{6,0,5,4,3,2,1:T(8,128)(2,1)S(1)}, bf16[32,1,1,4,2,2,128]{6,0,5,4,3,2,1:T(8,128)(2,1)S(1)}, u32[]{:S(2)}, u32[]{:S(2)}) collective-permute-start(bf16[32,1,1,4,2,2,128]{6,0,5,4,3,2,1:T(8,128)(2,1)S(1)} %get-tuple-element.27), channel_id=1, source_target_pairs={{8,0},{16,8},{24,16},{0,24},{9,1},{17,9},{25,17},{1,25},{10,2},{18... | collective-permute-start | bytes 393224 | tf_op jit(solution)/shard_map/ppermute | solution.py:61
  20.3 4.6 %collective-permute-start = (bf16[32,1,1,4,2,2,128]{6,0,5,4,3,2,1:T(8,128)(2,1)S(1)}, bf16[32,1,1,4,2,2,128]{6,0,5,4,3,2,1:T(8,128)(2,1)S(1)}, u32[]{:S(2)}, u32[]{:S(2)}) collective-permute-start(bf16[32,1,1,4,2,2,128]{6,0,5,4,3,2,1:T(8,128)(2,1)S(1)} %get-tuple-element.27), channel_id=1, source_target_pairs={{1,0},{0,1},{3,2},{2,3},{5,4},{4,5},{7,6},{6,7},{9,8},{8,9},{11,10... | collective-permute-start | bytes 393224 | tf_op jit(solution)/shard_map/ppermute | solution.py:55
  20.4 7.7 %collective-permute-start.4 = (bf16[32,1,1,4,2,2,128]{6,0,5,4,3,2,1:T(8,128)(2,1)S(1)}, bf16[32,1,1,4,2,2,128]{6,0,5,4,3,2,1:T(8,128)(2,1)S(1)}, u32[]{:S(2)}, u32[]{:S(2)}) collective-permute-start(bf16[32,1,1,4,2,2,128]{6,0,5,4,3,2,1:T(8,128)(2,1)S(1)} %get-tuple-element.27), channel_id=1, source_target_pairs={{24,0},{0,8},{8,16},{16,24},{25,1},{1,9},{9,17},{17,25},{26,2},{2,... | collective-permute-start | bytes 393224 | tf_op jit(solution)/shard_map/ppermute | solution.py:62
  20.4 4.6 %collective-permute-start.2 = (bf16[32,1,1,2,2,2,128]{6,0,5,4,3,2,1:T(8,128)(2,1)S(1)}, bf16[32,1,1,2,2,2,128]{6,0,5,4,3,2,1:T(8,128)(2,1)S(1)}, u32[]{:S(2)}, u32[]{:S(2)}) collective-permute-start(bf16[32,1,1,2,2,2,128]{6,0,5,4,3,2,1:T(8,128)(2,1)S(1)} %pad_maximum_fusion.2), channel_id=1, source_target_pairs={{4,0},{5,1},{6,2},{7,3},{0,4},{1,5},{2,6},{3,7},{12,8},{13,9},{14,... | collective-permute-start | bytes 196616 | tf_op jit(solution)/shard_map/ppermute | solution.py:55
  32.9 12.1 %all-to-all-start.1 = ((f32[32,1,1600]{2,1,0:T(1,128)}), f32[32,1,1600]{2,1,0:T(1,128)S(1)}, u32[]{:S(2)}, u32[]{:S(2)}) async-start(f32[32,1,1600]{2,1,0:T(1,128)} %broadcast_in_dim.9), calls=%async_computation.1 | async-start | bytes 425984 | tf_op jit(solution)/shard_map/all_to_all | solution.py:156
  46.6 7.1 %copy-start.2 = (bf16[32,1,9,1,4,2,2,128]{7,0,6,5,4,3,2,1:T(8,128)(2,1)S(1)}, bf16[32,1,9,1,4,2,2,128]{7,0,6,5,4,3,2,1:T(8,128)(2,1)}, u32[]{:S(2)}) copy-start(bf16[32,1,9,1,4,2,2,128]{7,0,6,5,4,3,2,1:T(8,128)(2,1)} %get-tuple-element.23) | copy-start | bytes 3538948
  46.6 7.1 %collective-permute-start.6 = (bf16[32,1,1,4,2,2,128]{6,0,5,4,3,2,1:T(8,128)(2,1)S(1)}, bf16[32,1,1,4,2,2,128]{6,0,5,4,3,2,1:T(8,128)(2,1)S(1)}, u32[]{:S(2)}, u32[]{:S(2)}) collective-permute-start(bf16[32,1,1,4,2,2,128]{6,0,5,4,3,2,1:T(8,128)(2,1)S(1)} %get-tuple-element.24), channel_id=1, source_target_pairs={{2,0},{3,1},{0,2},{1,3},{6,4},{7,5},{4,6},{5,7},{10,8},{11,9},{8,1... | collective-permute-start | bytes 393224 | tf_op jit(solution)/shard_map/ppermute | solution.py:55
  47.2 6.6 %collective-permute-start.8 = (bf16[32,1,1,4,2,2,128]{6,0,5,4,3,2,1:T(8,128)(2,1)S(1)}, bf16[32,1,1,4,2,2,128]{6,0,5,4,3,2,1:T(8,128)(2,1)S(1)}, u32[]{:S(2)}, u32[]{:S(2)}) collective-permute-start(bf16[32,1,1,4,2,2,128]{6,0,5,4,3,2,1:T(8,128)(2,1)S(1)} %get-tuple-element.24), channel_id=1, source_target_pairs={{8,0},{16,8},{24,16},{0,24},{9,1},{17,9},{25,17},{1,25},{10,2},{18... | collective-permute-start | bytes 393224 | tf_op jit(solution)/shard_map/ppermute | solution.py:61
  48.8 4.8 %collective-permute-start.5 = (bf16[32,1,1,4,2,2,128]{6,0,5,4,3,2,1:T(8,128)(2,1)S(1)}, bf16[32,1,1,4,2,2,128]{6,0,5,4,3,2,1:T(8,128)(2,1)S(1)}, u32[]{:S(2)}, u32[]{:S(2)}) collective-permute-start(bf16[32,1,1,4,2,2,128]{6,0,5,4,3,2,1:T(8,128)(2,1)S(1)} %get-tuple-element.24), channel_id=1, source_target_pairs={{1,0},{0,1},{3,2},{2,3},{5,4},{4,5},{7,6},{6,7},{9,8},{8,9},{11,10... | collective-permute-start | bytes 393224 | tf_op jit(solution)/shard_map/ppermute | solution.py:55
  48.8 7.7 %collective-permute-start.9 = (bf16[32,1,1,4,2,2,128]{6,0,5,4,3,2,1:T(8,128)(2,1)S(1)}, bf16[32,1,1,4,2,2,128]{6,0,5,4,3,2,1:T(8,128)(2,1)S(1)}, u32[]{:S(2)}, u32[]{:S(2)}) collective-permute-start(bf16[32,1,1,4,2,2,128]{6,0,5,4,3,2,1:T(8,128)(2,1)S(1)} %get-tuple-element.24), channel_id=1, source_target_pairs={{24,0},{0,8},{8,16},{16,24},{25,1},{1,9},{9,17},{17,25},{26,2},{2,... | collective-permute-start | bytes 393224 | tf_op jit(solution)/shard_map/ppermute | solution.py:62
  49.3 4.3 %collective-permute-start.7 = (bf16[32,1,1,2,2,2,128]{6,0,5,4,3,2,1:T(8,128)(2,1)S(1)}, bf16[32,1,1,2,2,2,128]{6,0,5,4,3,2,1:T(8,128)(2,1)S(1)}, u32[]{:S(2)}, u32[]{:S(2)}) collective-permute-start(bf16[32,1,1,2,2,2,128]{6,0,5,4,3,2,1:T(8,128)(2,1)S(1)} %pad_maximum_fusion.3), channel_id=1, source_target_pairs={{4,0},{5,1},{6,2},{7,3},{0,4},{1,5},{2,6},{3,7},{12,8},{13,9},{14,... | collective-permute-start | bytes 196616 | tf_op jit(solution)/shard_map/ppermute | solution.py:55

commit v14 on v13

--- a/solution.py
+++ b/solution.py
@@ -136,15 +136,17 @@
         residual.astype(jnp.bfloat16),
         preferred_element_type=jnp.float32,
     ).astype(jnp.bfloat16)
-    width = coarse.shape[1]
-    payload = jnp.concatenate(
-        [coarse.astype(jnp.float32), restrict_exact(null_vectors, residual)], 1
-    )
     parts = lax.all_to_all(
-        jnp.broadcast_to(payload[None], (blocks_total,) + payload.shape), "xyz", 0, 0
-    )
-    slab_a = slab_columns(parts[:, :, :width]).astype(jnp.bfloat16)
-    slab_residual = parts[:, :, width:].reshape(blocks_total, -1)
+        jnp.broadcast_to(coarse[None], (blocks_total,) + coarse.shape), "xyz", 0, 0
+    )
+    slab_a = slab_columns(parts)
+    exact_residual = restrict_exact(null_vectors, residual)
+    slab_residual = lax.all_to_all(
+        jnp.broadcast_to(exact_residual[None], (blocks_total,) + exact_residual.shape),
+        "xyz",
+        0,
+        0,
+    ).reshape(blocks_total, -1)
     direction_a = finish(residual, slab_a, null_vectors, inverse_rows)
     image_a = apply_links(coarse_links, direction_a.astype(jnp.bfloat16))
     image_coarse = restrict_exact(null_vectors, image_a)

time: 74.4 us -> 79.1 us (1.063)
  starting transfers between devices: 11.7 us -> 22.5 us
  blocking collectives: 20.5 us -> 10 us
  local copies, waits for them, and re-layouts: 5.52 us -> 7.85 us
    all_to_all x1 -> x0, blocking collectives: 10.5 us -> none  [shards(): lax.all_to_all(jnp.broadcast_to(payload[None], (blocks_total,) + payload....]
    all_to_all x0 -> x2, starting transfers between devices: none -> 8.52 us  [the longest x1 5.17 us: shards(): lax.all_to_all(jnp.broadcast_to(coarse[None], (blocks_total,) + coarse.sh...]
    all_to_all x0 -> x2, waiting for transfers between devices: none -> 2.77 us  [the longest x1 2.76 us: shards(): lax.all_to_all(jnp.broadcast_to(coarse[None], (blocks_total,) + coarse.sh...]
    ppermute x6, starting transfers between devices: 3.3 us -> 5.59 us  [both_sides(): pair = lax.ppermute(jnp.concatenate([first, last], which), axis, perm)]
    unnamed x17 -> x21, local copies, waits for them, and re-layouts: 1.9 us -> 3.63 us
    all_to_all x1, waiting for transfers between devices: 9.37 us -> 7.86 us  [shards(): lax.all_to_all(jnp.broadcast_to(local[None, None], (devices, 1) + local.s...]
    ppermute x6, waiting for transfers between devices: 6.84 us -> 5.91 us  [both_sides(): pair = lax.ppermute(jnp.concatenate([first, last], which), axis, perm)]
    all_to_all x0 -> x1, other arithmetic: none -> 0.8 us  [shards(): lax.all_to_all(jnp.broadcast_to(exact_residual[None], (blocks_total,) + e...]
  transfers between devices with their start and end apart: 11 -> 13, of which waited for: 5 -> 6; matrix products, arithmetic and copies ran while one was open for 1% -> 12% of each run, Pallas kernels for 0% -> 0%
where the time goes in v14:
time: 79.1 us; the launch traced here: 78.6 us
  starting transfers between devices  22.5 us (28%)
  waiting for transfers between devices  22 us (28%)
  blocking collectives  10 us (13%)
  other arithmetic  7.97 us (10%)
  local copies, waits for them, and re-layouts  7.85 us (10%)
  matrix products  7.04 us (9%)
  between operations  1.19 us (2%)
    all_to_all x1, blocking collectives, total_sum(): lax.all_to_all(copies, axes, 0, 0)[:, 0]  10 us
    all_to_all x1, waiting for transfers between devices, shards(): lax.all_to_all(jnp.broadcast_to(local[None, None], (devices, 1) + local.s...  7.86 us
    ppermute x6, waiting for transfers between devices, both_sides(): pair = lax.ppermute(jnp.concatenate([first, last], which), axis, perm)  5.91 us
    ppermute x6, starting transfers between devices, both_sides(): pair = lax.ppermute(jnp.concatenate([first, last], which), axis, perm)  5.59 us
    ppermute x2, waiting for transfers between devices, both_sides(): from_lower = lax.ppermute(last, axis, down)  5.44 us
    ppermute x2, starting transfers between devices, both_sides(): from_upper = lax.ppermute(first, axis, up)  5.2 us
    all_to_all x1, starting transfers between devices, shards(): lax.all_to_all(jnp.broadcast_to(coarse[None], (blocks_total,) + coarse.sh...  5.17 us
    unnamed x21, local copies, waits for them, and re-layouts  3.63 us
  transfers between devices with their start and end apart: 13, of which 6 were waited for; matrix products, arithmetic and copies ran while one was open for 12% of the time, Pallas kernels for 0%

profile of v14, /device:TPU:0, one launch (start us, length us, event | category | flops | bytes accessed | tf_op | source)
XLA Modules:
  0.0 78.6 jit_solution(3739515925005455687)
XLA Ops:
  0.7 1.2 %convert_bitcast_fusion = bf16[32,4,2,2,128]{4,3,2,1,0:T(2,128)(2,1)S(1)} fusion(f32[32,1,1,4,2,2,128]{6,5,4,3,2,1,0:T(2,128)} %param.4), kind=kLoop, calls=%fused_computation.82 | loop fusion | flops 65536 | bytes 393216 | tf_op jit(solution)/shard_map/reshape
  1.9 1.1 %fusion.18 = bf16[32,48]{1,0:T(8,128)(2,1)S(1)} fusion(bf16[32,4,2,2,128]{4,3,2,1,0:T(2,128)(2,1)S(1)} %convert_bitcast_fusion, bf16[1,1,4,2,2,48,128]{6,5,4,3,2,1,0:T(8,128)(2,1)} %param.6), kind=kOutput, calls=%fused_computation.23 | convolution fusion | flops 6292992 | bytes 330752 | tf_op jit(solution)/shard_map/tbzyxjk,ntbzyxk->nj/dot_general | solution.py:133
  3.7 5.2 %all-to-all-start = ((bf16[8,2,768]{2,1,0:T(2,128)(2,1)}), bf16[8,2,768]{2,1,0:T(2,128)(2,1)S(1)}, u32[]{:S(2)}, u32[]{:S(2)}) async-start(bf16[8,2,768]{2,1,0:T(2,128)(2,1)} %reshape.371), calls=%async_computation | async-start | bytes 49152 | tf_op jit(solution)/shard_map/all_to_all | solution.py:139
  8.9 1.2 %convolution_bitcast_fusion.3 = f32[32,48]{1,0:T(8,128)S(1)} fusion(f32[32,4,2,2,128]{4,3,2,1,0:T(2,128)} %bitcast.229, bf16[1,1,4,2,2,48,128]{6,5,4,3,2,1,0:T(8,128)(2,1)} %param.6), kind=kOutput, calls=%fused_computation.21 | convolution fusion | flops 18874368 | bytes 464896 | tf_op jit(solution)/shard_map/tbzyxjk,ntbzyxk->nj/dot_general | solution.py:94
  11.0 2.8 %all-to-all-done = bf16[8,2,768]{2,1,0:T(2,128)(2,1)S(1)} async-done(((bf16[8,2,768]{2,1,0:T(2,128)(2,1)}), bf16[8,2,768]{2,1,0:T(2,128)(2,1)S(1)}, u32[]{:S(2)}, u32[]{:S(2)}) %all-to-all-start) | async-done | bytes 24608 | tf_op jit(solution)/shard_map/all_to_all | solution.py:139
  13.7 3.3 %all-to-all-start.2 = ((f32[8,1,1536]{2,1,0:T(1,128)}), f32[8,1,1536]{2,1,0:T(1,128)S(1)}, u32[]{:S(2)}, u32[]{:S(2)}) async-start(f32[8,1,1536]{2,1,0:T(1,128)} %reshape.369), calls=%async_computation.2 | async-start | bytes 98304 | tf_op jit(solution)/shard_map/all_to_all | solution.py:144
  17.4 1.0 %bitcast_dynamic-update-slice_fusion.5 = (bf16[32,1,9,1,4,2,2,128]{7,0,6,5,4,3,2,1:T(8,128)(2,1)}, bf16[32,1,1,4,2,2,128]{6,0,5,4,3,2,1:T(8,128)(2,1)S(1)}, f32[32,1,1,4,2,2,128]{6,0,5,4,3,2,1:T(8,128)}) fusion(bf16[1,1,4,2,2,48,128]{6,5,4,3,2,1,0:T(8,128)(2,1)S(1)} %copy-done.4, bf16[32,384]{1,0:T(8,128)(2,1)S(1)} %reshape.350, ...), kind=kOutput, calls=%fused_computation.79 | convolution fusion | flops 7669247 | bytes 1044480 | tf_op jit(solution)/shard_map/tbzyxjk,nj->ntbzyxk/dot_general | solution.py:114
  18.4 2.0 %collective-permute-start.1 = (bf16[32,1,1,4,2,2,128]{6,0,5,4,3,2,1:T(8,128)(2,1)S(1)}, bf16[32,1,1,4,2,2,128]{6,0,5,4,3,2,1:T(8,128)(2,1)S(1)}, u32[]{:S(2)}, u32[]{:S(2)}) collective-permute-start(bf16[32,1,1,4,2,2,128]{6,0,5,4,3,2,1:T(8,128)(2,1)S(1)} %get-tuple-element.27), channel_id=1, source_target_pairs={{2,0},{3,1},{0,2},{1,3},{6,4},{7,5},{4,6},{5,7},{10,8},{11,9},{8,1... | collective-permute-start | bytes 393224 | tf_op jit(solution)/shard_map/ppermute | solution.py:55
  20.4 3.6 %collective-permute-start.3 = (bf16[32,1,1,4,2,2,128]{6,0,5,4,3,2,1:T(8,128)(2,1)S(1)}, bf16[32,1,1,4,2,2,128]{6,0,5,4,3,2,1:T(8,128)(2,1)S(1)}, u32[]{:S(2)}, u32[]{:S(2)}) collective-permute-start(bf16[32,1,1,4,2,2,128]{6,0,5,4,3,2,1:T(8,128)(2,1)S(1)} %get-tuple-element.27), channel_id=1, source_target_pairs={{8,0},{16,8},{24,16},{0,24},{9,1},{17,9},{25,17},{1,25},{10,2},{18... | collective-permute-start | bytes 393224 | tf_op jit(solution)/shard_map/ppermute | solution.py:61
  24.1 1.6 %collective-permute-start.2 = (bf16[32,1,1,2,2,2,128]{6,0,5,4,3,2,1:T(8,128)(2,1)S(1)}, bf16[32,1,1,2,2,2,128]{6,0,5,4,3,2,1:T(8,128)(2,1)S(1)}, u32[]{:S(2)}, u32[]{:S(2)}) collective-permute-start(bf16[32,1,1,2,2,2,128]{6,0,5,4,3,2,1:T(8,128)(2,1)S(1)} %pad_maximum_fusion.2), channel_id=1, source_target_pairs={{4,0},{5,1},{6,2},{7,3},{0,4},{1,5},{2,6},{3,7},{12,8},{13,9},{14,... | collective-permute-start | bytes 196616 | tf_op jit(solution)/shard_map/ppermute | solution.py:55
  25.7 3.0 %collective-permute-done.2 = bf16[32,1,1,2,2,2,128]{6,0,5,4,3,2,1:T(8,128)(2,1)S(1)} collective-permute-done((bf16[32,1,1,2,2,2,128]{6,0,5,4,3,2,1:T(8,128)(2,1)S(1)}, bf16[32,1,1,2,2,2,128]{6,0,5,4,3,2,1:T(8,128)(2,1)S(1)}, u32[]{:S(2)}, u32[]{:S(2)}) %collective-permute-start.2) | collective-permute-done | bytes 65568 | tf_op jit(solution)/shard_map/ppermute | solution.py:55
  28.9 2.8 %collective-permute-done.4 = bf16[32,1,1,4,2,2,128]{6,0,5,4,3,2,1:T(8,128)(2,1)S(1)} collective-permute-done((bf16[32,1,1,4,2,2,128]{6,0,5,4,3,2,1:T(8,128)(2,1)S(1)}, bf16[32,1,1,4,2,2,128]{6,0,5,4,3,2,1:T(8,128)(2,1)S(1)}, u32[]{:S(2)}, u32[]{:S(2)}) %collective-permute-start.4) | collective-permute-done | bytes 131104 | tf_op jit(solution)/shard_map/ppermute | solution.py:62
  34.1 0.8 %fusion.6 = f32[2,32,1,1,4,2,2,64]{7,1,6,5,4,3,2,0:T(8,128)S(1)} fusion(bf16[1,1,4,2,2,9,64,128]{7,6,5,4,3,2,1,0:T(8,128)(2,1)S(1)} %copy-done, bf16[1,32,1,9,1,4,2,2,128]{8,1,7,6,5,3,4,2,0:T(8,128)(2,1)S(1)} %maximum_bitcast_fusion.3, bf16[1,32,1,9,1,4,2,2,128]{8,1,7,6,5,3,4,2,0:T(8,128)(2,1)S(1)} %maximum_bitcast_fusion.2), kind=kOutput, calls=%fused_computation.8 | convolution fusion | flops 152174592 | bytes 4980736 | tf_op jit(solution)/shard_map/tbzyxdik,pntdbzyxk->pntbzyxi/dot_general | solution.py:87
  36.6 2.7 %all-to-all-start.1 = ((f32[32,1,1600]{2,1,0:T(1,128)}), f32[32,1,1600]{2,1,0:T(1,128)S(1)}, u32[]{:S(2)}, u32[]{:S(2)}) async-start(f32[32,1,1600]{2,1,0:T(1,128)} %broadcast_in_dim.11), calls=%async_computation.1 | async-start | bytes 425984 | tf_op jit(solution)/shard_map/all_to_all | solution.py:158
  40.8 7.9 %all-to-all-done.1 = f32[32,1,1600]{2,1,0:T(1,128)S(1)} async-done(((f32[32,1,1600]{2,1,0:T(1,128)}), f32[32,1,1600]{2,1,0:T(1,128)S(1)}, u32[]{:S(2)}, u32[]{:S(2)}) %all-to-all-start.1) | async-done | bytes 204832 | tf_op jit(solution)/shard_map/all_to_all | solution.py:158
  49.3 1.7 %bitcast_dynamic-update-slice_fusion.2 = (bf16[32,1,9,1,4,2,2,128]{7,0,6,5,4,3,2,1:T(8,128)(2,1)}, bf16[32,1,1,4,2,2,128]{6,0,5,4,3,2,1:T(8,128)(2,1)S(1)}, f32[32,1,1,4,2,2,128]{6,0,5,4,3,2,1:T(8,128)S(1)}) fusion(bf16[1,1,4,2,2,48,128]{6,5,4,3,2,1,0:T(8,128)(2,1)S(1)} %copy-done.4, bf16[32,384]{1,0:T(8,128)(2,1)S(1)} %reshape.359, ...), kind=kOutput, calls=%fused_computation.76 | convolution fusion | flops 7800319 | bytes 1306752 | tf_op jit(solution)/shard_map/tbzyxjk,nj->ntbzyxk/dot_general | solution.py:114
  51.7 1.6 %collective-permute-start.8 = (bf16[32,1,1,4,2,2,128]{6,0,5,4,3,2,1:T(8,128)(2,1)S(1)}, bf16[32,1,1,4,2,2,128]{6,0,5,4,3,2,1:T(8,128)(2,1)S(1)}, u32[]{:S(2)}, u32[]{:S(2)}) collective-permute-start(bf16[32,1,1,4,2,2,128]{6,0,5,4,3,2,1:T(8,128)(2,1)S(1)} %get-tuple-element.24), channel_id=1, source_target_pairs={{8,0},{16,8},{24,16},{0,24},{9,1},{17,9},{25,17},{1,25},{10,2},{18... | collective-permute-start | bytes 393224 | tf_op jit(solution)/shard_map/ppermute | solution.py:61
  53.8 1.4 %collective-permute-start.7 = (bf16[32,1,1,2,2,2,128]{6,0,5,4,3,2,1:T(8,128)(2,1)S(1)}, bf16[32,1,1,2,2,2,128]{6,0,5,4,3,2,1:T(8,128)(2,1)S(1)}, u32[]{:S(2)}, u32[]{:S(2)}) collective-permute-start(bf16[32,1,1,2,2,2,128]{6,0,5,4,3,2,1:T(8,128)(2,1)S(1)} %pad_maximum_fusion.3), channel_id=1, source_target_pairs={{4,0},{5,1},{6,2},{7,3},{0,4},{1,5},{2,6},{3,7},{12,8},{13,9},{14,... | collective-permute-start | bytes 196616 | tf_op jit(solution)/shard_map/ppermute | solution.py:55
  55.2 2.9 %collective-permute-done.7 = bf16[32,1,1,2,2,2,128]{6,0,5,4,3,2,1:T(8,128)(2,1)S(1)} collective-permute-done((bf16[32,1,1,2,2,2,128]{6,0,5,4,3,2,1:T(8,128)(2,1)S(1)}, bf16[32,1,1,2,2,2,128]{6,0,5,4,3,2,1:T(8,128)(2,1)S(1)}, u32[]{:S(2)}, u32[]{:S(2)}) %collective-permute-start.7) | collective-permute-done | bytes 65568 | tf_op jit(solution)/shard_map/ppermute | solution.py:55
  58.4 2.6 %collective-permute-done.9 = bf16[32,1,1,4,2,2,128]{6,0,5,4,3,2,1:T(8,128)(2,1)S(1)} collective-permute-done((bf16[32,1,1,4,2,2,128]{6,0,5,4,3,2,1:T(8,128)(2,1)S(1)}, bf16[32,1,1,4,2,2,128]{6,0,5,4,3,2,1:T(8,128)(2,1)S(1)}, u32[]{:S(2)}, u32[]{:S(2)}) %collective-permute-start.9) | collective-permute-done | bytes 131104 | tf_op jit(solution)/shard_map/ppermute | solution.py:62
  65.5 10.0 %all_to_all.20 = f32[32,1,128]{2,1,0:T(1,128)S(1)} all-to-all(f32[32,1,128]{2,1,0:T(1,128)S(1)} %broadcast_in_dim.14), channel_id=1, replica_groups=mesh['ta'=4,'xyz'=8] {'ta','xyz'}, dimensions={0} | all-to-all | bytes 32768 | tf_op jit(solution)/shard_map/all_to_all | solution.py:35
  75.6 1.2 %multiply_subtract_fusion = (f32[32,1,1,4,2,2,128]{6,0,5,4,3,2,1:T(8,128)S(1)}, f32[32,1,1,4,2,2,128]{6,0,5,4,3,2,1:T(8,128)S(1)}) fusion(f32[32,1,1,4,2,2,128]{6,0,5,4,3,2,1:T(8,128)S(1)} %get-tuple-element.22, f32[32,1,1,4,2,2,128]{6,0,5,4,3,2,1:T(8,128)S(1)} %get-tuple-element.25, f32[32]{0:T(128)S(1)} %get-tuple-element.21, f32[32]{0:T(128)S(1)} %get-tuple-element.20, ...), kind=kLoop, calls=%fused_computation.36 | loop fusion | flops 720896 | bytes 1835392 | tf_op jit(solution)/shard_map/sub | solution.py:210
  76.8 0.9 %copy.139 = f32[32,1,1,4,2,2,128]{6,5,4,3,2,1,0:T(2,128)} copy(f32[32,1,1,4,2,2,128]{6,0,5,4,3,2,1:T(8,128)S(1)} %get-tuple-element.64) | data formatting | bytes 524288
  77.7 0.9 %copy.138 = f32[32,1,1,4,2,2,128]{6,5,4,3,2,1,0:T(2,128)} copy(f32[32,1,1,4,2,2,128]{6,0,5,4,3,2,1:T(8,128)S(1)} %get-tuple-element.65) | data formatting | bytes 524288
  (101 shorter events, 13.8 us)
Async XLA Ops:
  0.6 33.5 %copy-start = (bf16[1,1,4,2,2,9,64,128]{7,6,5,4,3,2,1,0:T(8,128)(2,1)S(1)}, bf16[1,1,4,2,2,9,64,128]{7,6,5,4,3,2,1,0:T(8,128)(2,1)}, u32[]{:S(2)}) copy-start(bf16[1,1,4,2,2,9,64,128]{7,6,5,4,3,2,1,0:T(8,128)(2,1)} %param.5) | copy-start | bytes 7077892
  0.6 16.7 %copy-start.1 = (f32[32,1,1,4,2,2,128]{6,5,4,3,2,1,0:T(2,128)S(1)}, f32[32,1,1,4,2,2,128]{6,5,4,3,2,1,0:T(2,128)}, u32[]{:S(2)}) copy-start(f32[32,1,1,4,2,2,128]{6,5,4,3,2,1,0:T(2,128)} %param.4) | copy-start | bytes 786436
  0.7 16.7 %copy-start.4 = (bf16[1,1,4,2,2,48,128]{6,5,4,3,2,1,0:T(8,128)(2,1)S(1)}, bf16[1,1,4,2,2,48,128]{6,5,4,3,2,1,0:T(8,128)(2,1)}, u32[]{:S(2)}) copy-start(bf16[1,1,4,2,2,48,128]{6,5,4,3,2,1,0:T(8,128)(2,1)} %param.6) | copy-start | bytes 589828
  0.7 16.7 %copy-start.5 = (bf16[1,48,384]{2,1,0:T(8,128)(2,1)S(1)}, bf16[1,48,384]{2,1,0:T(8,128)(2,1)}, u32[]{:S(2)}) copy-start(bf16[1,48,384]{2,1,0:T(8,128)(2,1)} %param.7) | copy-start | bytes 110596
  3.7 10.0 %all-to-all-start = ((bf16[8,2,768]{2,1,0:T(2,128)(2,1)}), bf16[8,2,768]{2,1,0:T(2,128)(2,1)S(1)}, u32[]{:S(2)}, u32[]{:S(2)}) async-start(bf16[8,2,768]{2,1,0:T(2,128)(2,1)} %reshape.371), calls=%async_computation | async-start | bytes 49152 | tf_op jit(solution)/shard_map/all_to_all | solution.py:139
  13.7 22.0 %all-to-all-start.2 = ((f32[8,1,1536]{2,1,0:T(1,128)}), f32[8,1,1536]{2,1,0:T(1,128)S(1)}, u32[]{:S(2)}, u32[]{:S(2)}) async-start(f32[8,1,1536]{2,1,0:T(1,128)} %reshape.369), calls=%async_computation.2 | async-start | bytes 98304 | tf_op jit(solution)/shard_map/all_to_all | solution.py:144
  18.4 10.3 %copy-start.3 = (bf16[32,1,9,1,4,2,2,128]{7,0,6,5,4,3,2,1:T(8,128)(2,1)S(1)}, bf16[32,1,9,1,4,2,2,128]{7,0,6,5,4,3,2,1:T(8,128)(2,1)}, u32[]{:S(2)}) copy-start(bf16[32,1,9,1,4,2,2,128]{7,0,6,5,4,3,2,1:T(8,128)(2,1)} %get-tuple-element.26) | copy-start | bytes 3538948
  18.4 10.3 %collective-permute-start.1 = (bf16[32,1,1,4,2,2,128]{6,0,5,4,3,2,1:T(8,128)(2,1)S(1)}, bf16[32,1,1,4,2,2,128]{6,0,5,4,3,2,1:T(8,128)(2,1)S(1)}, u32[]{:S(2)}, u32[]{:S(2)}) collective-permute-start(bf16[32,1,1,4,2,2,128]{6,0,5,4,3,2,1:T(8,128)(2,1)S(1)} %get-tuple-element.27), channel_id=1, source_target_pairs={{2,0},{3,1},{0,2},{1,3},{6,4},{7,5},{4,6},{5,7},{10,8},{11,9},{8,1... | collective-permute-start | bytes 393224 | tf_op jit(solution)/shard_map/ppermute | solution.py:55
  20.4 8.5 %collective-permute-start.3 = (bf16[32,1,1,4,2,2,128]{6,0,5,4,3,2,1:T(8,128)(2,1)S(1)}, bf16[32,1,1,4,2,2,128]{6,0,5,4,3,2,1:T(8,128)(2,1)S(1)}, u32[]{:S(2)}, u32[]{:S(2)}) collective-permute-start(bf16[32,1,1,4,2,2,128]{6,0,5,4,3,2,1:T(8,128)(2,1)S(1)} %get-tuple-element.27), channel_id=1, source_target_pairs={{8,0},{16,8},{24,16},{0,24},{9,1},{17,9},{25,17},{1,25},{10,2},{18... | collective-permute-start | bytes 393224 | tf_op jit(solution)/shard_map/ppermute | solution.py:61
  24.0 4.6 %collective-permute-start = (bf16[32,1,1,4,2,2,128]{6,0,5,4,3,2,1:T(8,128)(2,1)S(1)}, bf16[32,1,1,4,2,2,128]{6,0,5,4,3,2,1:T(8,128)(2,1)S(1)}, u32[]{:S(2)}, u32[]{:S(2)}) collective-permute-start(bf16[32,1,1,4,2,2,128]{6,0,5,4,3,2,1:T(8,128)(2,1)S(1)} %get-tuple-element.27), channel_id=1, source_target_pairs={{1,0},{0,1},{3,2},{2,3},{5,4},{4,5},{7,6},{6,7},{9,8},{8,9},{11,10... | collective-permute-start | bytes 393224 | tf_op jit(solution)/shard_map/ppermute | solution.py:55
  24.0 7.7 %collective-permute-start.4 = (bf16[32,1,1,4,2,2,128]{6,0,5,4,3,2,1:T(8,128)(2,1)S(1)}, bf16[32,1,1,4,2,2,128]{6,0,5,4,3,2,1:T(8,128)(2,1)S(1)}, u32[]{:S(2)}, u32[]{:S(2)}) collective-permute-start(bf16[32,1,1,4,2,2,128]{6,0,5,4,3,2,1:T(8,128)(2,1)S(1)} %get-tuple-element.27), channel_id=1, source_target_pairs={{24,0},{0,8},{8,16},{16,24},{25,1},{1,9},{9,17},{17,25},{26,2},{2,... | collective-permute-start | bytes 393224 | tf_op jit(solution)/shard_map/ppermute | solution.py:62
  24.1 4.6 %collective-permute-start.2 = (bf16[32,1,1,2,2,2,128]{6,0,5,4,3,2,1:T(8,128)(2,1)S(1)}, bf16[32,1,1,2,2,2,128]{6,0,5,4,3,2,1:T(8,128)(2,1)S(1)}, u32[]{:S(2)}, u32[]{:S(2)}) collective-permute-start(bf16[32,1,1,2,2,2,128]{6,0,5,4,3,2,1:T(8,128)(2,1)S(1)} %pad_maximum_fusion.2), channel_id=1, source_target_pairs={{4,0},{5,1},{6,2},{7,3},{0,4},{1,5},{2,6},{3,7},{12,8},{13,9},{14,... | collective-permute-start | bytes 196616 | tf_op jit(solution)/shard_map/ppermute | solution.py:55
  36.6 12.1 %all-to-all-start.1 = ((f32[32,1,1600]{2,1,0:T(1,128)}), f32[32,1,1600]{2,1,0:T(1,128)S(1)}, u32[]{:S(2)}, u32[]{:S(2)}) async-start(f32[32,1,1600]{2,1,0:T(1,128)} %broadcast_in_dim.11), calls=%async_computation.1 | async-start | bytes 425984 | tf_op jit(solution)/shard_map/all_to_all | solution.py:158
  51.0 7.1 %copy-start.2 = (bf16[32,1,9,1,4,2,2,128]{7,0,6,5,4,3,2,1:T(8,128)(2,1)S(1)}, bf16[32,1,9,1,4,2,2,128]{7,0,6,5,4,3,2,1:T(8,128)(2,1)}, u32[]{:S(2)}) copy-start(bf16[32,1,9,1,4,2,2,128]{7,0,6,5,4,3,2,1:T(8,128)(2,1)} %get-tuple-element.23) | copy-start | bytes 3538948
  51.1 7.1 %collective-permute-start.6 = (bf16[32,1,1,4,2,2,128]{6,0,5,4,3,2,1:T(8,128)(2,1)S(1)}, bf16[32,1,1,4,2,2,128]{6,0,5,4,3,2,1:T(8,128)(2,1)S(1)}, u32[]{:S(2)}, u32[]{:S(2)}) collective-permute-start(bf16[32,1,1,4,2,2,128]{6,0,5,4,3,2,1:T(8,128)(2,1)S(1)} %get-tuple-element.24), channel_id=1, source_target_pairs={{2,0},{3,1},{0,2},{1,3},{6,4},{7,5},{4,6},{5,7},{10,8},{11,9},{8,1... | collective-permute-start | bytes 393224 | tf_op jit(solution)/shard_map/ppermute | solution.py:55
  51.7 6.6 %collective-permute-start.8 = (bf16[32,1,1,4,2,2,128]{6,0,5,4,3,2,1:T(8,128)(2,1)S(1)}, bf16[32,1,1,4,2,2,128]{6,0,5,4,3,2,1:T(8,128)(2,1)S(1)}, u32[]{:S(2)}, u32[]{:S(2)}) collective-permute-start(bf16[32,1,1,4,2,2,128]{6,0,5,4,3,2,1:T(8,128)(2,1)S(1)} %get-tuple-element.24), channel_id=1, source_target_pairs={{8,0},{16,8},{24,16},{0,24},{9,1},{17,9},{25,17},{1,25},{10,2},{18... | collective-permute-start | bytes 393224 | tf_op jit(solution)/shard_map/ppermute | solution.py:61
  53.3 4.8 %collective-permute-start.5 = (bf16[32,1,1,4,2,2,128]{6,0,5,4,3,2,1:T(8,128)(2,1)S(1)}, bf16[32,1,1,4,2,2,128]{6,0,5,4,3,2,1:T(8,128)(2,1)S(1)}, u32[]{:S(2)}, u32[]{:S(2)}) collective-permute-start(bf16[32,1,1,4,2,2,128]{6,0,5,4,3,2,1:T(8,128)(2,1)S(1)} %get-tuple-element.24), channel_id=1, source_target_pairs={{1,0},{0,1},{3,2},{2,3},{5,4},{4,5},{7,6},{6,7},{9,8},{8,9},{11,10... | collective-permute-start | bytes 393224 | tf_op jit(solution)/shard_map/ppermute | solution.py:55
  53.3 7.7 %collective-permute-start.9 = (bf16[32,1,1,4,2,2,128]{6,0,5,4,3,2,1:T(8,128)(2,1)S(1)}, bf16[32,1,1,4,2,2,128]{6,0,5,4,3,2,1:T(8,128)(2,1)S(1)}, u32[]{:S(2)}, u32[]{:S(2)}) collective-permute-start(bf16[32,1,1,4,2,2,128]{6,0,5,4,3,2,1:T(8,128)(2,1)S(1)} %get-tuple-element.24), channel_id=1, source_target_pairs={{24,0},{0,8},{8,16},{16,24},{25,1},{1,9},{9,17},{17,25},{26,2},{2,... | collective-permute-start | bytes 393224 | tf_op jit(solution)/shard_map/ppermute | solution.py:62
  53.8 4.3 %collective-permute-start.7 = (bf16[32,1,1,2,2,2,128]{6,0,5,4,3,2,1:T(8,128)(2,1)S(1)}, bf16[32,1,1,2,2,2,128]{6,0,5,4,3,2,1:T(8,128)(2,1)S(1)}, u32[]{:S(2)}, u32[]{:S(2)}) collective-permute-start(bf16[32,1,1,2,2,2,128]{6,0,5,4,3,2,1:T(8,128)(2,1)S(1)} %pad_maximum_fusion.3), channel_id=1, source_target_pairs={{4,0},{5,1},{6,2},{7,3},{0,4},{1,5},{2,6},{3,7},{12,8},{13,9},{14,... | collective-permute-start | bytes 196616 | tf_op jit(solution)/shard_map/ppermute | solution.py:55

commit v15 on v13

--- a/solution.py
+++ b/solution.py
@@ -130,16 +130,17 @@
     slabs_total = lax.axis_size("ta")
     blocks_total = lax.axis_size("xyz")
     residual = right_side
-    coarse = jnp.einsum(
-        "tbzyxjk,ntbzyxk->nj",
+    high = residual.astype(jnp.bfloat16)
+    low = (residual - high.astype(jnp.float32)).astype(jnp.bfloat16)
+    both = jnp.einsum(
+        "tbzyxjk,sntbzyxk->snj",
         null_vectors,
-        residual.astype(jnp.bfloat16),
+        jnp.stack([high, low]),
         preferred_element_type=jnp.float32,
-    ).astype(jnp.bfloat16)
+    )
+    coarse = both[0].astype(jnp.bfloat16)
     width = coarse.shape[1]
-    payload = jnp.concatenate(
-        [coarse.astype(jnp.float32), restrict_exact(null_vectors, residual)], 1
-    )
+    payload = jnp.concatenate([coarse.astype(jnp.float32), both[0] + both[1]], 1)
     parts = lax.all_to_all(
         jnp.broadcast_to(payload[None], (blocks_total,) + payload.shape), "xyz", 0, 0
     )

time: 74.4 us -> 74.3 us (level)
  matrix products: 6.31 us -> 5.1 us
  local copies, waits for them, and re-layouts: 5.52 us -> 6.56 us
    dot_general x2 -> x1, matrix products: 1.47 us -> 0.23 us  [restrict_exact(): jnp.einsum('tbzyxjk,ntbzyxk->nj', null_vectors.astype(jnp.float32), field...]
    reshape x1 -> x0, other arithmetic: 1.19 us -> none
    another operation x0 -> x1, other arithmetic: none -> 1.19 us  [shards(): jnp.stack([high, low])]
    unnamed x17 -> x18, local copies, waits for them, and re-layouts: 1.9 us -> 2.94 us
where the time goes in v15:
time: 74.3 us; the launch traced here: 73.9 us
  waiting for transfers between devices  21.7 us (29%)
  blocking collectives  20.5 us (28%)
  starting transfers between devices  11.7 us (16%)
  other arithmetic  7.27 us (10%)
  local copies, waits for them, and re-layouts  6.56 us (9%)
  matrix products  5.1 us (7%)
  between operations  1.16 us (2%)
    all_to_all x1, blocking collectives, shards(): lax.all_to_all(jnp.broadcast_to(payload[None], (blocks_total,) + payload....  10.5 us
    all_to_all x1, blocking collectives, total_sum(): lax.all_to_all(copies, axes, 0, 0)[:, 0]  10 us
    all_to_all x1, waiting for transfers between devices, shards(): lax.all_to_all(jnp.broadcast_to(local[None, None], (devices, 1) + local.s...  9.37 us
    ppermute x6, waiting for transfers between devices, both_sides(): pair = lax.ppermute(jnp.concatenate([first, last], which), axis, perm)  6.84 us
    ppermute x2, waiting for transfers between devices, both_sides(): from_lower = lax.ppermute(last, axis, down)  5.45 us
    ppermute x2, starting transfers between devices, both_sides(): from_upper = lax.ppermute(first, axis, up)  5.2 us
    ppermute x6, starting transfers between devices, both_sides(): pair = lax.ppermute(jnp.concatenate([first, last], which), axis, perm)  3.3 us
    unnamed x18, local copies, waits for them, and re-layouts  2.94 us
  transfers between devices with their start and end apart: 11, of which 5 were waited for; matrix products, arithmetic and copies ran while one was open for 1% of the time, Pallas kernels for 0%

profile of v15, /device:TPU:0, one launch (start us, length us, event | category | flops | bytes accessed | tf_op | source)
XLA Modules:
  0.0 73.9 jit_solution(11074778123446941982)
XLA Ops:
  0.7 1.2 %fusion.26 = bf16[1,32,1,1,4,2,2,128]{7,1,4,0,5,6,3,2:T(8,128)(2,1)S(1)} fusion(f32[32,1,1,4,2,2,128]{6,5,4,3,2,1,0:T(2,128)} %param.4), kind=kLoop, calls=%fused_computation.52 | loop fusion | flops 262144 | bytes 393216 | tf_op jit(solution)/shard_map/stack | solution.py:138
  1.9 1.0 %copy.192 = bf16[32,1,1,4,2,2,128]{6,0,3,4,5,2,1:T(8,128)(2,1)S(1)} copy(f32[32,1,1,4,2,2,128]{6,5,4,3,2,1,0:T(2,128)} %param.4) | data formatting | bytes 393216 | tf_op args[0]
  2.9 1.1 %convolution_bitcast_fusion.2 = f32[2,32,48]{2,1,0:T(8,128)S(1)} fusion(bf16[1,32,1,1,4,2,2,128]{7,1,4,0,5,6,3,2:T(8,128)(2,1)S(1)} %fusion.26, bf16[1,32,1,1,4,2,2,128]{7,1,4,0,5,6,3,2:T(8,128)(2,1)S(1)} %bitcast.241, bf16[1,1,4,2,2,48,128]{6,5,4,3,2,1,0:T(8,128)(2,1)} %param.6), kind=kOutput, calls=%fused_computation.20 | convolution fusion | flops 12713984 | bytes 471040 | tf_op jit(solution)/shard_map/tbzyxjk,sntbzyxk->snj/dot_general | solution.py:135
  4.2 10.5 %all_to_all.15 = f32[8,32,96]{2,1,0:T(8,128)S(1)} all-to-all(f32[8,32,96]{2,1,0:T(8,128)S(1)} %broadcast_in_dim.8), channel_id=1, replica_groups=mesh['ta'=4,'xyz'=8] {'xyz'}, dimensions={0} | all-to-all | bytes 196608 | tf_op jit(solution)/shard_map/all_to_all | solution.py:144
  14.9 1.1 %bitcast_dynamic-update-slice_fusion.5 = (bf16[32,1,9,1,4,2,2,128]{7,0,6,5,4,3,2,1:T(8,128)(2,1)}, bf16[32,1,1,4,2,2,128]{6,0,5,4,3,2,1:T(8,128)(2,1)S(1)}, f32[32,1,1,4,2,2,128]{6,0,5,4,3,2,1:T(8,128)}) fusion(bf16[1,1,4,2,2,48,128]{6,5,4,3,2,1,0:T(8,128)(2,1)S(1)} %copy-done.4, bf16[32,384]{1,0:T(8,128)(2,1)S(1)} %convert_element_type.50, ...), kind=kOutput, calls=%fused_computation.85 | convolution fusion | flops 7669247 | bytes 1044480 | tf_op jit(solution)/shard_map/tbzyxjk,nj->ntbzyxk/dot_general | solution.py:114
  16.6 3.6 %collective-permute-start.3 = (bf16[32,1,1,4,2,2,128]{6,0,5,4,3,2,1:T(8,128)(2,1)S(1)}, bf16[32,1,1,4,2,2,128]{6,0,5,4,3,2,1:T(8,128)(2,1)S(1)}, u32[]{:S(2)}, u32[]{:S(2)}) collective-permute-start(bf16[32,1,1,4,2,2,128]{6,0,5,4,3,2,1:T(8,128)(2,1)S(1)} %get-tuple-element.27), channel_id=1, source_target_pairs={{8,0},{16,8},{24,16},{0,24},{9,1},{17,9},{25,17},{1,25},{10,2},{18... | collective-permute-start | bytes 393224 | tf_op jit(solution)/shard_map/ppermute | solution.py:61
  20.9 3.9 %collective-permute-done.2 = bf16[32,1,1,2,2,2,128]{6,0,5,4,3,2,1:T(8,128)(2,1)S(1)} collective-permute-done((bf16[32,1,1,2,2,2,128]{6,0,5,4,3,2,1:T(8,128)(2,1)S(1)}, bf16[32,1,1,2,2,2,128]{6,0,5,4,3,2,1:T(8,128)(2,1)S(1)}, u32[]{:S(2)}, u32[]{:S(2)}) %collective-permute-start.2) | collective-permute-done | bytes 65568 | tf_op jit(solution)/shard_map/ppermute | solution.py:55
  25.1 2.8 %collective-permute-done.4 = bf16[32,1,1,4,2,2,128]{6,0,5,4,3,2,1:T(8,128)(2,1)S(1)} collective-permute-done((bf16[32,1,1,4,2,2,128]{6,0,5,4,3,2,1:T(8,128)(2,1)S(1)}, bf16[32,1,1,4,2,2,128]{6,0,5,4,3,2,1:T(8,128)(2,1)S(1)}, u32[]{:S(2)}, u32[]{:S(2)}) %collective-permute-start.4) | collective-permute-done | bytes 131104 | tf_op jit(solution)/shard_map/ppermute | solution.py:62
  30.3 0.8 %fusion.6 = f32[2,32,1,1,4,2,2,64]{7,1,6,5,4,3,2,0:T(8,128)S(1)} fusion(bf16[1,1,4,2,2,9,64,128]{7,6,5,4,3,2,1,0:T(8,128)(2,1)S(1)} %copy-done, bf16[1,32,1,9,1,4,2,2,128]{8,1,7,6,5,3,4,2,0:T(8,128)(2,1)S(1)} %maximum_bitcast_fusion.3, bf16[1,32,1,9,1,4,2,2,128]{8,1,7,6,5,3,4,2,0:T(8,128)(2,1)S(1)} %maximum_bitcast_fusion.2), kind=kOutput, calls=%fused_computation.8 | convolution fusion | flops 152174592 | bytes 4980736 | tf_op jit(solution)/shard_map/tbzyxdik,pntdbzyxk->pntbzyxi/dot_general | solution.py:87
  31.9 0.8 %broadcast_in_dim.9 = f32[32,1,1600]{2,1,0:T(1,128)} broadcast(f32[1600]{0:T(1024)S(1)} %pad_maximum_fusion.5), dimensions={2} | broadcast | bytes 211200 | tf_op jit(solution)/shard_map/broadcast_in_dim | solution.py:158
  32.7 2.7 %all-to-all-start.1 = ((f32[32,1,1600]{2,1,0:T(1,128)}), f32[32,1,1600]{2,1,0:T(1,128)S(1)}, u32[]{:S(2)}, u32[]{:S(2)}) async-start(f32[32,1,1600]{2,1,0:T(1,128)} %broadcast_in_dim.9), calls=%async_computation.1 | async-start | bytes 425984 | tf_op jit(solution)/shard_map/all_to_all | solution.py:157
  35.4 9.4 %all-to-all-done.1 = f32[32,1,1600]{2,1,0:T(1,128)S(1)} async-done(((f32[32,1,1600]{2,1,0:T(1,128)}), f32[32,1,1600]{2,1,0:T(1,128)S(1)}, u32[]{:S(2)}, u32[]{:S(2)}) %all-to-all-start.1) | async-done | bytes 204832 | tf_op jit(solution)/shard_map/all_to_all | solution.py:157
  45.4 1.0 %bitcast_dynamic-update-slice_fusion.2 = (bf16[32,1,9,1,4,2,2,128]{7,0,6,5,4,3,2,1:T(8,128)(2,1)}, bf16[32,1,1,4,2,2,128]{6,0,5,4,3,2,1:T(8,128)(2,1)S(1)}, f32[32,1,1,4,2,2,128]{6,0,5,4,3,2,1:T(8,128)S(1)}) fusion(bf16[1,1,4,2,2,48,128]{6,5,4,3,2,1,0:T(8,128)(2,1)S(1)} %copy-done.4, bf16[32,384]{1,0:T(8,128)(2,1)S(1)} %reshape.355, ...), kind=kOutput, calls=%fused_computation.82 | convolution fusion | flops 7800319 | bytes 1306752 | tf_op jit(solution)/shard_map/tbzyxjk,nj->ntbzyxk/dot_general | solution.py:114
  47.1 1.6 %collective-permute-start.8 = (bf16[32,1,1,4,2,2,128]{6,0,5,4,3,2,1:T(8,128)(2,1)S(1)}, bf16[32,1,1,4,2,2,128]{6,0,5,4,3,2,1:T(8,128)(2,1)S(1)}, u32[]{:S(2)}, u32[]{:S(2)}) collective-permute-start(bf16[32,1,1,4,2,2,128]{6,0,5,4,3,2,1:T(8,128)(2,1)S(1)} %get-tuple-element.24), channel_id=1, source_target_pairs={{8,0},{16,8},{24,16},{0,24},{9,1},{17,9},{25,17},{1,25},{10,2},{18... | collective-permute-start | bytes 393224 | tf_op jit(solution)/shard_map/ppermute | solution.py:61
  49.2 1.4 %collective-permute-start.7 = (bf16[32,1,1,2,2,2,128]{6,0,5,4,3,2,1:T(8,128)(2,1)S(1)}, bf16[32,1,1,2,2,2,128]{6,0,5,4,3,2,1:T(8,128)(2,1)S(1)}, u32[]{:S(2)}, u32[]{:S(2)}) collective-permute-start(bf16[32,1,1,2,2,2,128]{6,0,5,4,3,2,1:T(8,128)(2,1)S(1)} %pad_maximum_fusion.3), channel_id=1, source_target_pairs={{4,0},{5,1},{6,2},{7,3},{0,4},{1,5},{2,6},{3,7},{12,8},{13,9},{14,... | collective-permute-start | bytes 196616 | tf_op jit(solution)/shard_map/ppermute | solution.py:55
  50.6 2.9 %collective-permute-done.7 = bf16[32,1,1,2,2,2,128]{6,0,5,4,3,2,1:T(8,128)(2,1)S(1)} collective-permute-done((bf16[32,1,1,2,2,2,128]{6,0,5,4,3,2,1:T(8,128)(2,1)S(1)}, bf16[32,1,1,2,2,2,128]{6,0,5,4,3,2,1:T(8,128)(2,1)S(1)}, u32[]{:S(2)}, u32[]{:S(2)}) %collective-permute-start.7) | collective-permute-done | bytes 65568 | tf_op jit(solution)/shard_map/ppermute | solution.py:55
  53.8 2.6 %collective-permute-done.9 = bf16[32,1,1,4,2,2,128]{6,0,5,4,3,2,1:T(8,128)(2,1)S(1)} collective-permute-done((bf16[32,1,1,4,2,2,128]{6,0,5,4,3,2,1:T(8,128)(2,1)S(1)}, bf16[32,1,1,4,2,2,128]{6,0,5,4,3,2,1:T(8,128)(2,1)S(1)}, u32[]{:S(2)}, u32[]{:S(2)}) %collective-permute-start.9) | collective-permute-done | bytes 131104 | tf_op jit(solution)/shard_map/ppermute | solution.py:62
  57.3 0.8 %fusion.57 = (bf16[32,1,9,1,4,2,2,64]{7,0,6,5,4,2,3,1:T(8,128)(2,1)S(1)}, bf16[32,1,9,1,4,2,2,64]{7,0,6,5,4,3,2,1:T(8,128)(2,1)S(1)}) fusion(bf16[32,1,9,1,4,2,2,128]{7,0,6,5,4,2,3,1:T(8,128)(2,1)S(1)} %bitcast.237), kind=kLoop, calls=%fused_computation.116 | loop fusion | bytes 1769472 | tf_op jit(solution)/shard_map/slice | solution.py:82
  58.1 0.7 maximum_bitcast_fusion.4
  59.5 0.8 %fusion.11 = f32[2,32,1,1,4,2,2,64]{7,1,6,5,4,3,2,0:T(8,128)S(1)} fusion(bf16[1,1,4,2,2,9,64,128]{7,6,5,4,3,2,1,0:T(8,128)(2,1)S(1)} %copy-done, bf16[1,32,1,9,1,4,2,2,128]{8,1,7,6,5,3,4,2,0:T(8,128)(2,1)S(1)} %maximum_bitcast_fusion.5, bf16[1,32,1,9,1,4,2,2,128]{8,1,7,6,5,3,4,2,0:T(8,128)(2,1)S(1)} %maximum_bitcast_fusion.4), kind=kOutput, calls=%fused_computation.9 | convolution fusion | flops 152174592 | bytes 4980736 | tf_op jit(solution)/shard_map/tbzyxdik,pntdbzyxk->pntbzyxi/dot_general | solution.py:87
  60.8 10.0 %all_to_all.16 = f32[32,1,128]{2,1,0:T(1,128)S(1)} all-to-all(f32[32,1,128]{2,1,0:T(1,128)S(1)} %broadcast_in_dim.11), channel_id=1, replica_groups=mesh['ta'=4,'xyz'=8] {'ta','xyz'}, dimensions={0} | all-to-all | bytes 32768 | tf_op jit(solution)/shard_map/all_to_all | solution.py:35
  71.0 1.2 %multiply_subtract_fusion = (f32[32,1,1,4,2,2,128]{6,0,5,4,3,2,1:T(8,128)S(1)}, f32[32,1,1,4,2,2,128]{6,0,5,4,3,2,1:T(8,128)S(1)}) fusion(f32[32,1,1,4,2,2,128]{6,0,5,4,3,2,1:T(8,128)S(1)} %get-tuple-element.22, f32[32,1,1,4,2,2,128]{6,0,5,4,3,2,1:T(8,128)S(1)} %get-tuple-element.25, f32[32]{0:T(128)S(1)} %get-tuple-element.21, f32[32]{0:T(128)S(1)} %get-tuple-element.20, ...), kind=kLoop, calls=%fused_computation.36 | loop fusion | flops 720896 | bytes 1835392 | tf_op jit(solution)/shard_map/sub | solution.py:209
  72.1 0.9 %copy.140 = f32[32,1,1,4,2,2,128]{6,5,4,3,2,1,0:T(2,128)} copy(f32[32,1,1,4,2,2,128]{6,0,5,4,3,2,1:T(8,128)S(1)} %get-tuple-element.64) | data formatting | bytes 524288
  73.0 0.9 %copy.139 = f32[32,1,1,4,2,2,128]{6,5,4,3,2,1,0:T(2,128)} copy(f32[32,1,1,4,2,2,128]{6,0,5,4,3,2,1:T(8,128)S(1)} %get-tuple-element.65) | data formatting | bytes 524288
  (95 shorter events, 8.9 us)
Async XLA Ops:
  0.6 29.6 %copy-start = (bf16[1,1,4,2,2,9,64,128]{7,6,5,4,3,2,1,0:T(8,128)(2,1)S(1)}, bf16[1,1,4,2,2,9,64,128]{7,6,5,4,3,2,1,0:T(8,128)(2,1)}, u32[]{:S(2)}) copy-start(bf16[1,1,4,2,2,9,64,128]{7,6,5,4,3,2,1,0:T(8,128)(2,1)} %param.5) | copy-start | bytes 7077892
  0.6 14.2 %copy-start.1 = (f32[32,1,1,4,2,2,128]{6,5,4,3,2,1,0:T(2,128)S(1)}, f32[32,1,1,4,2,2,128]{6,5,4,3,2,1,0:T(2,128)}, u32[]{:S(2)}) copy-start(f32[32,1,1,4,2,2,128]{6,5,4,3,2,1,0:T(2,128)} %param.4) | copy-start | bytes 786436
  0.7 14.2 %copy-start.4 = (bf16[1,1,4,2,2,48,128]{6,5,4,3,2,1,0:T(8,128)(2,1)S(1)}, bf16[1,1,4,2,2,48,128]{6,5,4,3,2,1,0:T(8,128)(2,1)}, u32[]{:S(2)}) copy-start(bf16[1,1,4,2,2,48,128]{6,5,4,3,2,1,0:T(8,128)(2,1)} %param.6) | copy-start | bytes 589828
  0.7 14.2 %copy-start.5 = (bf16[1,48,384]{2,1,0:T(8,128)(2,1)S(1)}, bf16[1,48,384]{2,1,0:T(8,128)(2,1)}, u32[]{:S(2)}) copy-start(bf16[1,48,384]{2,1,0:T(8,128)(2,1)} %param.7) | copy-start | bytes 110596
  15.9 8.9 %copy-start.3 = (bf16[32,1,9,1,4,2,2,128]{7,0,6,5,4,3,2,1:T(8,128)(2,1)S(1)}, bf16[32,1,9,1,4,2,2,128]{7,0,6,5,4,3,2,1:T(8,128)(2,1)}, u32[]{:S(2)}) copy-start(bf16[32,1,9,1,4,2,2,128]{7,0,6,5,4,3,2,1:T(8,128)(2,1)} %get-tuple-element.26) | copy-start | bytes 3538948
  15.9 9.0 %collective-permute-start.1 = (bf16[32,1,1,4,2,2,128]{6,0,5,4,3,2,1:T(8,128)(2,1)S(1)}, bf16[32,1,1,4,2,2,128]{6,0,5,4,3,2,1:T(8,128)(2,1)S(1)}, u32[]{:S(2)}, u32[]{:S(2)}) collective-permute-start(bf16[32,1,1,4,2,2,128]{6,0,5,4,3,2,1:T(8,128)(2,1)S(1)} %get-tuple-element.27), channel_id=1, source_target_pairs={{2,0},{3,1},{0,2},{1,3},{6,4},{7,5},{4,6},{5,7},{10,8},{11,9},{8,1... | collective-permute-start | bytes 393224 | tf_op jit(solution)/shard_map/ppermute | solution.py:55
  16.6 8.5 %collective-permute-start.3 = (bf16[32,1,1,4,2,2,128]{6,0,5,4,3,2,1:T(8,128)(2,1)S(1)}, bf16[32,1,1,4,2,2,128]{6,0,5,4,3,2,1:T(8,128)(2,1)S(1)}, u32[]{:S(2)}, u32[]{:S(2)}) collective-permute-start(bf16[32,1,1,4,2,2,128]{6,0,5,4,3,2,1:T(8,128)(2,1)S(1)} %get-tuple-element.27), channel_id=1, source_target_pairs={{8,0},{16,8},{24,16},{0,24},{9,1},{17,9},{25,17},{1,25},{10,2},{18... | collective-permute-start | bytes 393224 | tf_op jit(solution)/shard_map/ppermute | solution.py:61
  20.2 4.6 %collective-permute-start = (bf16[32,1,1,4,2,2,128]{6,0,5,4,3,2,1:T(8,128)(2,1)S(1)}, bf16[32,1,1,4,2,2,128]{6,0,5,4,3,2,1:T(8,128)(2,1)S(1)}, u32[]{:S(2)}, u32[]{:S(2)}) collective-permute-start(bf16[32,1,1,4,2,2,128]{6,0,5,4,3,2,1:T(8,128)(2,1)S(1)} %get-tuple-element.27), channel_id=1, source_target_pairs={{1,0},{0,1},{3,2},{2,3},{5,4},{4,5},{7,6},{6,7},{9,8},{8,9},{11,10... | collective-permute-start | bytes 393224 | tf_op jit(solution)/shard_map/ppermute | solution.py:55
  20.2 7.7 %collective-permute-start.4 = (bf16[32,1,1,4,2,2,128]{6,0,5,4,3,2,1:T(8,128)(2,1)S(1)}, bf16[32,1,1,4,2,2,128]{6,0,5,4,3,2,1:T(8,128)(2,1)S(1)}, u32[]{:S(2)}, u32[]{:S(2)}) collective-permute-start(bf16[32,1,1,4,2,2,128]{6,0,5,4,3,2,1:T(8,128)(2,1)S(1)} %get-tuple-element.27), channel_id=1, source_target_pairs={{24,0},{0,8},{8,16},{16,24},{25,1},{1,9},{9,17},{17,25},{26,2},{2,... | collective-permute-start | bytes 393224 | tf_op jit(solution)/shard_map/ppermute | solution.py:62
  20.2 4.6 %collective-permute-start.2 = (bf16[32,1,1,2,2,2,128]{6,0,5,4,3,2,1:T(8,128)(2,1)S(1)}, bf16[32,1,1,2,2,2,128]{6,0,5,4,3,2,1:T(8,128)(2,1)S(1)}, u32[]{:S(2)}, u32[]{:S(2)}) collective-permute-start(bf16[32,1,1,2,2,2,128]{6,0,5,4,3,2,1:T(8,128)(2,1)S(1)} %pad_maximum_fusion.2), channel_id=1, source_target_pairs={{4,0},{5,1},{6,2},{7,3},{0,4},{1,5},{2,6},{3,7},{12,8},{13,9},{14,... | collective-permute-start | bytes 196616 | tf_op jit(solution)/shard_map/ppermute | solution.py:55
  32.7 12.1 %all-to-all-start.1 = ((f32[32,1,1600]{2,1,0:T(1,128)}), f32[32,1,1600]{2,1,0:T(1,128)S(1)}, u32[]{:S(2)}, u32[]{:S(2)}) async-start(f32[32,1,1600]{2,1,0:T(1,128)} %broadcast_in_dim.9), calls=%async_computation.1 | async-start | bytes 425984 | tf_op jit(solution)/shard_map/all_to_all | solution.py:157
  46.4 7.1 %copy-start.2 = (bf16[32,1,9,1,4,2,2,128]{7,0,6,5,4,3,2,1:T(8,128)(2,1)S(1)}, bf16[32,1,9,1,4,2,2,128]{7,0,6,5,4,3,2,1:T(8,128)(2,1)}, u32[]{:S(2)}) copy-start(bf16[32,1,9,1,4,2,2,128]{7,0,6,5,4,3,2,1:T(8,128)(2,1)} %get-tuple-element.23) | copy-start | bytes 3538948
  46.5 7.1 %collective-permute-start.6 = (bf16[32,1,1,4,2,2,128]{6,0,5,4,3,2,1:T(8,128)(2,1)S(1)}, bf16[32,1,1,4,2,2,128]{6,0,5,4,3,2,1:T(8,128)(2,1)S(1)}, u32[]{:S(2)}, u32[]{:S(2)}) collective-permute-start(bf16[32,1,1,4,2,2,128]{6,0,5,4,3,2,1:T(8,128)(2,1)S(1)} %get-tuple-element.24), channel_id=1, source_target_pairs={{2,0},{3,1},{0,2},{1,3},{6,4},{7,5},{4,6},{5,7},{10,8},{11,9},{8,1... | collective-permute-start | bytes 393224 | tf_op jit(solution)/shard_map/ppermute | solution.py:55
  47.1 6.6 %collective-permute-start.8 = (bf16[32,1,1,4,2,2,128]{6,0,5,4,3,2,1:T(8,128)(2,1)S(1)}, bf16[32,1,1,4,2,2,128]{6,0,5,4,3,2,1:T(8,128)(2,1)S(1)}, u32[]{:S(2)}, u32[]{:S(2)}) collective-permute-start(bf16[32,1,1,4,2,2,128]{6,0,5,4,3,2,1:T(8,128)(2,1)S(1)} %get-tuple-element.24), channel_id=1, source_target_pairs={{8,0},{16,8},{24,16},{0,24},{9,1},{17,9},{25,17},{1,25},{10,2},{18... | collective-permute-start | bytes 393224 | tf_op jit(solution)/shard_map/ppermute | solution.py:61
  48.7 4.8 %collective-permute-start.5 = (bf16[32,1,1,4,2,2,128]{6,0,5,4,3,2,1:T(8,128)(2,1)S(1)}, bf16[32,1,1,4,2,2,128]{6,0,5,4,3,2,1:T(8,128)(2,1)S(1)}, u32[]{:S(2)}, u32[]{:S(2)}) collective-permute-start(bf16[32,1,1,4,2,2,128]{6,0,5,4,3,2,1:T(8,128)(2,1)S(1)} %get-tuple-element.24), channel_id=1, source_target_pairs={{1,0},{0,1},{3,2},{2,3},{5,4},{4,5},{7,6},{6,7},{9,8},{8,9},{11,10... | collective-permute-start | bytes 393224 | tf_op jit(solution)/shard_map/ppermute | solution.py:55
  48.7 7.7 %collective-permute-start.9 = (bf16[32,1,1,4,2,2,128]{6,0,5,4,3,2,1:T(8,128)(2,1)S(1)}, bf16[32,1,1,4,2,2,128]{6,0,5,4,3,2,1:T(8,128)(2,1)S(1)}, u32[]{:S(2)}, u32[]{:S(2)}) collective-permute-start(bf16[32,1,1,4,2,2,128]{6,0,5,4,3,2,1:T(8,128)(2,1)S(1)} %get-tuple-element.24), channel_id=1, source_target_pairs={{24,0},{0,8},{8,16},{16,24},{25,1},{1,9},{9,17},{17,25},{26,2},{2,... | collective-permute-start | bytes 393224 | tf_op jit(solution)/shard_map/ppermute | solution.py:62
  49.2 4.3 %collective-permute-start.7 = (bf16[32,1,1,2,2,2,128]{6,0,5,4,3,2,1:T(8,128)(2,1)S(1)}, bf16[32,1,1,2,2,2,128]{6,0,5,4,3,2,1:T(8,128)(2,1)S(1)}, u32[]{:S(2)}, u32[]{:S(2)}) collective-permute-start(bf16[32,1,1,2,2,2,128]{6,0,5,4,3,2,1:T(8,128)(2,1)S(1)} %pad_maximum_fusion.3), channel_id=1, source_target_pairs={{4,0},{5,1},{6,2},{7,3},{0,4},{1,5},{2,6},{3,7},{12,8},{13,9},{14,... | collective-permute-start | bytes 196616 | tf_op jit(solution)/shard_map/ppermute | solution.py:55

commit v16 on v13

--- a/solution.py
+++ b/solution.py
@@ -67,7 +67,7 @@
     return (upper, lower)
 
 
-def apply_links(coarse_links, lowered):
+def apply_links(links_pair, lowered):
     blocks_total = lax.axis_size("xyz")
     across_x = 2 + 2 * min(blocks_total // 64, 1)
     across_z = blocks_total // (across_x * across_x)
@@ -78,16 +78,24 @@
     stacked = jnp.stack(
         [lowered, upper_x, lower_x, upper_y, lower_y, upper_z, lower_z, upper_t, lower_t], 2
     )
-    half_width = lowered.shape[-1] // 2
-    real_part = stacked[..., :half_width]
-    imag_part = stacked[..., half_width:]
-    real_input = jnp.concatenate([real_part, -imag_part], -1)
-    imag_input = jnp.concatenate([imag_part, real_part], -1)
-    inputs = jnp.stack([real_input, imag_input], 0)
-    result = jnp.einsum(
-        "tbzyxdik,pntdbzyxk->pntbzyxi", coarse_links, inputs, preferred_element_type=jnp.float32
-    )
-    return jnp.concatenate([result[0], result[1]], -1)
+    real_links, imag_links = links_pair
+    real = jnp.einsum(
+        "tbzyxdik,ntdbzyxk->ntbzyxi", real_links, stacked, preferred_element_type=jnp.float32
+    )
+    imag = jnp.einsum(
+        "tbzyxdik,ntdbzyxk->ntbzyxi", imag_links, stacked, preferred_element_type=jnp.float32
+    )
+    return jnp.concatenate([real, imag], -1)
+
+
+def split_links(coarse_links):
+    half_width = coarse_links.shape[-1] // 2
+    real_part = coarse_links[..., :half_width]
+    imag_part = coarse_links[..., half_width:]
+    return (
+        jnp.concatenate([real_part, -imag_part], -1),
+        jnp.concatenate([imag_part, real_part], -1),
+    )
 
 
 def restrict_exact(null_vectors, field):
@@ -127,6 +135,7 @@
 
 def shards(right_side, coarse_links, null_vectors, coarse_inverse):
     inverse_rows = coarse_inverse[0]
+    links_pair = split_links(coarse_links)
     slabs_total = lax.axis_size("ta")
     blocks_total = lax.axis_size("xyz")
     residual = right_side
@@ -146,7 +155,7 @@
     slab_a = slab_columns(parts[:, :, :width]).astype(jnp.bfloat16)
     slab_residual = parts[:, :, width:].reshape(blocks_total, -1)
     direction_a = finish(residual, slab_a, null_vectors, inverse_rows)
-    image_a = apply_links(coarse_links, direction_a.astype(jnp.bfloat16))
+    image_a = apply_links(links_pair, direction_a.astype(jnp.bfloat16))
     image_coarse = restrict_exact(null_vectors, image_a)
     pair_local = jnp.stack([inner_rows(image_a, image_a), inner_rows(image_a, residual)], 1)
     if slabs_total * blocks_total <= 64:
@@ -182,7 +191,7 @@
     slab_b = (slab_residual - steps[None, :] * slab_image).astype(jnp.bfloat16)
     slab_b = slab_columns(slab_b.reshape(blocks_total, step_a.shape[0], -1))
     direction_b = finish(residual, slab_b, null_vectors, inverse_rows)
-    image_b = apply_links(coarse_links, direction_b.astype(jnp.bfloat16))
+    image_b = apply_links(links_pair, direction_b.astype(jnp.bfloat16))
     sums = total_sum(
         jnp.stack(
             [

time: 74.4 us -> 76.7 us (1.031)
  blocking collectives: 20.5 us -> 10.7 us
  starting transfers between devices: 11.7 us -> 19.9 us
  local copies, waits for them, and re-layouts: 5.52 us -> 8.73 us
  matrix products: 6.31 us -> 8.05 us
  waiting for transfers between devices: 21.7 us -> 20.7 us
    all_to_all x1 -> x0, blocking collectives: 10.5 us -> none  [shards(): lax.all_to_all(jnp.broadcast_to(payload[None], (blocks_total,) + payload....]
    all_to_all x0 -> x1, starting transfers between devices: none -> 5.17 us  [shards(): lax.all_to_all(jnp.broadcast_to(payload[None], (blocks_total,) + payload....]
    concatenate x0 -> x1, other arithmetic: none -> 2.75 us  [split_links(): jnp.concatenate([imag_part, real_part], -1)]
    dot_general x2 -> x4, matrix products: 1.7 us -> 4.45 us  [the longest x2 2.88 us: apply_links(): jnp.einsum('tbzyxdik,ntdbzyxk->ntbzyxi', real_links, stacked, preferred_e...]
    another operation x4 -> x0, other arithmetic: 2.64 us -> none  [apply_links(): inputs = jnp.stack([real_input, imag_input], 0)]
    ppermute x6, starting transfers between devices: 3.3 us -> 5.66 us  [both_sides(): pair = lax.ppermute(jnp.concatenate([first, last], which), axis, perm)]
    slice x3 -> x1, local copies, waits for them, and re-layouts: 1.7 us -> 3.79 us  [split_links(): imag_part = coarse_links[..., half_width:]]
    neg x1, other arithmetic: 0.45 us -> 1.75 us  [split_links(): -imag_part]
  transfers between devices with their start and end apart: 11 -> 12, of which waited for: 5 -> 5; matrix products, arithmetic and copies ran while one was open for 1% -> 11% of each run, Pallas kernels for 0% -> 0%
where the time goes in v16:
time: 76.7 us; the launch traced here: 76.3 us
  waiting for transfers between devices  20.7 us (27%)
  starting transfers between devices  19.9 us (26%)
  blocking collectives  10.7 us (14%)
  local copies, waits for them, and re-layouts  8.73 us (11%)
  matrix products  8.05 us (10%)
  other arithmetic  7.07 us (9%)
  between operations  1.13 us (1%)
    all_to_all x1, blocking collectives, total_sum(): lax.all_to_all(copies, axes, 0, 0)[:, 0]  10.7 us
    all_to_all x1, waiting for transfers between devices, shards(): lax.all_to_all(jnp.broadcast_to(local[None, None], (devices, 1) + local.s...  9.37 us
    ppermute x6, waiting for transfers between devices, both_sides(): pair = lax.ppermute(jnp.concatenate([first, last], which), axis, perm)  5.94 us
    ppermute x6, starting transfers between devices, both_sides(): pair = lax.ppermute(jnp.concatenate([first, last], which), axis, perm)  5.66 us
    ppermute x2, waiting for transfers between devices, both_sides(): from_lower = lax.ppermute(last, axis, down)  5.42 us
    ppermute x2, starting transfers between devices, both_sides(): from_upper = lax.ppermute(first, axis, up)  5.2 us
    all_to_all x1, starting transfers between devices, shards(): lax.all_to_all(jnp.broadcast_to(payload[None], (blocks_total,) + payload....  5.17 us
    slice x1, local copies, waits for them, and re-layouts, split_links(): imag_part = coarse_links[..., half_width:]  3.79 us
  transfers between devices with their start and end apart: 12, of which 5 were waited for; matrix products, arithmetic and copies ran while one was open for 11% of the time, Pallas kernels for 0%

profile of v16, /device:TPU:0, one launch (start us, length us, event | category | flops | bytes accessed | tf_op | source)
XLA Modules:
  0.0 76.3 jit_solution(5785359029365934674)
XLA Ops:
  0.6 1.1 %convert_bitcast_fusion = bf16[32,4,2,2,128]{4,3,2,1,0:T(2,128)(2,1)S(1)} fusion(f32[32,1,1,4,2,2,128]{6,5,4,3,2,1,0:T(2,128)} %param.4), kind=kLoop, calls=%fused_computation.83 | loop fusion | flops 65536 | bytes 393216 | tf_op jit(solution)/shard_map/reshape
  1.7 1.2 %convolution_bitcast_fusion.6 = f32[32,48]{1,0:T(8,128)S(1)} fusion(f32[32,4,2,2,128]{4,3,2,1,0:T(2,128)} %bitcast.227, bf16[1,1,4,2,2,48,128]{6,5,4,3,2,1,0:T(8,128)(2,1)S(1)} %copy-done), kind=kOutput, calls=%fused_computation.16 | convolution fusion | flops 18874368 | bytes 464896 | tf_op jit(solution)/shard_map/tbzyxjk,ntbzyxk->nj/dot_general | solution.py:102
  3.9 5.2 %all-to-all-start = ((f32[8,32,96]{2,1,0:T(8,128)}), f32[8,32,96]{2,1,0:T(8,128)S(1)}, u32[]{:S(2)}, u32[]{:S(2)}) async-start(f32[8,32,96]{2,1,0:T(8,128)} %broadcast_in_dim.8), calls=%async_computation | async-start | bytes 262144 | tf_op jit(solution)/shard_map/all_to_all | solution.py:152
  9.0 3.8 %fusion.48 = (bf16[1,1,4,2,2,9,64,64]{7,6,5,4,3,2,1,0:T(8,128)(2,1)S(1)}, bf16[1,1,4,2,2,9,64,64]{7,6,5,4,3,2,1,0:T(8,128)(2,1)S(1)}) fusion(bf16[1,1,4,2,2,9,64,128]{7,6,5,4,3,2,1,0:T(8,128)(2,1)} %param.5), kind=kLoop, calls=%fused_computation.108 | loop fusion | bytes 4718592 | tf_op jit(solution)/shard_map/slice | solution.py:94
  12.8 1.7 %copy_negate_fusion = bf16[1,1,4,2,2,9,64,64]{7,6,2,4,3,5,1,0:T(8,128)(2,1)} fusion(bf16[1,1,4,2,2,9,64,64]{7,6,5,4,3,2,1,0:T(8,128)(2,1)S(1)} %get-tuple-element.28), kind=kLoop, calls=%fused_computation.3 | loop fusion | flops 589824 | bytes 2359296 | tf_op jit(solution)/shard_map/neg | solution.py:96
  14.6 2.8 %pad_maximum_fusion = bf16[1,1,4,2,2,9,64,128]{7,6,5,4,3,2,1,0:T(8,128)(2,1)} fusion(bf16[1,1,4,2,2,9,64,64]{7,6,5,4,3,2,1,0:T(8,128)(2,1)S(1)} %get-tuple-element.29, bf16[1,1,4,2,2,9,64,64]{7,6,5,4,3,2,1,0:T(8,128)(2,1)S(1)} %get-tuple-element.28), kind=kLoop, calls=%fused_computation.1 | loop fusion | flops 4718592 | bytes 4718592 | tf_op jit(solution)/shard_map/concatenate | solution.py:97
  17.5 1.1 %bitcast_dynamic-update-slice_fusion.5 = (bf16[32,1,9,1,4,2,2,128]{7,0,6,5,4,3,2,1:T(8,128)(2,1)}, bf16[32,1,1,4,2,2,128]{6,0,5,4,3,2,1:T(8,128)(2,1)S(1)}, f32[32,1,1,4,2,2,128]{6,0,5,4,3,2,1:T(8,128)}) fusion(bf16[1,1,4,2,2,48,128]{6,5,4,3,2,1,0:T(8,128)(2,1)S(1)} %copy-done, bf16[32,384]{1,0:T(8,128)(2,1)S(1)} %convert_element_type.38, ...), kind=kOutput, calls=%fused_computation.81 | convolution fusion | flops 7669247 | bytes 1044480 | tf_op jit(solution)/shard_map/tbzyxjk,nj->ntbzyxk/dot_general | solution.py:122
  18.6 2.1 %collective-permute-start.1 = (bf16[32,1,1,4,2,2,128]{6,0,5,4,3,2,1:T(8,128)(2,1)S(1)}, bf16[32,1,1,4,2,2,128]{6,0,5,4,3,2,1:T(8,128)(2,1)S(1)}, u32[]{:S(2)}, u32[]{:S(2)}) collective-permute-start(bf16[32,1,1,4,2,2,128]{6,0,5,4,3,2,1:T(8,128)(2,1)S(1)} %get-tuple-element.27), channel_id=1, source_target_pairs={{2,0},{3,1},{0,2},{1,3},{6,4},{7,5},{4,6},{5,7},{10,8},{11,9},{8,1... | collective-permute-start | bytes 393224 | tf_op jit(solution)/shard_map/ppermute | solution.py:55
  20.7 3.6 %collective-permute-start.3 = (bf16[32,1,1,4,2,2,128]{6,0,5,4,3,2,1:T(8,128)(2,1)S(1)}, bf16[32,1,1,4,2,2,128]{6,0,5,4,3,2,1:T(8,128)(2,1)S(1)}, u32[]{:S(2)}, u32[]{:S(2)}) collective-permute-start(bf16[32,1,1,4,2,2,128]{6,0,5,4,3,2,1:T(8,128)(2,1)S(1)} %get-tuple-element.27), channel_id=1, source_target_pairs={{8,0},{16,8},{24,16},{0,24},{9,1},{17,9},{25,17},{1,25},{10,2},{18... | collective-permute-start | bytes 393224 | tf_op jit(solution)/shard_map/ppermute | solution.py:61
  24.4 1.5 %collective-permute-start.2 = (bf16[32,1,1,2,2,2,128]{6,0,5,4,3,2,1:T(8,128)(2,1)S(1)}, bf16[32,1,1,2,2,2,128]{6,0,5,4,3,2,1:T(8,128)(2,1)S(1)}, u32[]{:S(2)}, u32[]{:S(2)}) collective-permute-start(bf16[32,1,1,2,2,2,128]{6,0,5,4,3,2,1:T(8,128)(2,1)S(1)} %pad_maximum_fusion.3), channel_id=1, source_target_pairs={{4,0},{5,1},{6,2},{7,3},{0,4},{1,5},{2,6},{3,7},{12,8},{13,9},{14,... | collective-permute-start | bytes 196616 | tf_op jit(solution)/shard_map/ppermute | solution.py:55
  25.9 3.0 %collective-permute-done.2 = bf16[32,1,1,2,2,2,128]{6,0,5,4,3,2,1:T(8,128)(2,1)S(1)} collective-permute-done((bf16[32,1,1,2,2,2,128]{6,0,5,4,3,2,1:T(8,128)(2,1)S(1)}, bf16[32,1,1,2,2,2,128]{6,0,5,4,3,2,1:T(8,128)(2,1)S(1)}, u32[]{:S(2)}, u32[]{:S(2)}) %collective-permute-start.2) | collective-permute-done | bytes 65568 | tf_op jit(solution)/shard_map/ppermute | solution.py:55
  29.2 2.8 %collective-permute-done.4 = bf16[32,1,1,4,2,2,128]{6,0,5,4,3,2,1:T(8,128)(2,1)S(1)} collective-permute-done((bf16[32,1,1,4,2,2,128]{6,0,5,4,3,2,1:T(8,128)(2,1)S(1)}, bf16[32,1,1,4,2,2,128]{6,0,5,4,3,2,1:T(8,128)(2,1)S(1)}, u32[]{:S(2)}, u32[]{:S(2)}) %collective-permute-start.4) | collective-permute-done | bytes 131104 | tf_op jit(solution)/shard_map/ppermute | solution.py:62
  32.1 1.4 %convolution_bitcast_fusion.3 = f32[4,2,2,32,64]{4,3,0,2,1:T(8,128)S(1)} fusion(bf16[1,1,4,2,2,9,64,64]{7,6,2,4,3,5,1,0:T(8,128)(2,1)S(1)} %copy-done.4, bf16[1,1,4,2,2,9,64,64]{7,6,5,4,3,2,1,0:T(8,128)(2,1)S(1)} %get-tuple-element.29, bf16[32,1,9,1,4,2,2,128]{7,0,6,5,4,3,2,1:T(8,128)(2,1)S(1)} %bitcast_dynamic-update-slice_fusion.3), kind=kOutput, calls=%fused_computation.11 | convolution fusion | flops 80216064 | bytes 3670016 | tf_op jit(solution)/shard_map/tbzyxdik,ntdbzyxk->ntbzyxi/dot_general | solution.py:82
  36.1 3.4 %all-to-all-start.1 = ((f32[32,1,1600]{2,1,0:T(1,128)}), f32[32,1,1600]{2,1,0:T(1,128)S(1)}, u32[]{:S(2)}, u32[]{:S(2)}) async-start(f32[32,1,1600]{2,1,0:T(1,128)} %broadcast_in_dim.9), calls=%async_computation.1 | async-start | bytes 425984 | tf_op jit(solution)/shard_map/all_to_all | solution.py:165
  39.5 9.4 %all-to-all-done.1 = f32[32,1,1600]{2,1,0:T(1,128)S(1)} async-done(((f32[32,1,1600]{2,1,0:T(1,128)}), f32[32,1,1600]{2,1,0:T(1,128)S(1)}, u32[]{:S(2)}, u32[]{:S(2)}) %all-to-all-start.1) | async-done | bytes 204832 | tf_op jit(solution)/shard_map/all_to_all | solution.py:165
  49.5 1.0 %bitcast_dynamic-update-slice_fusion.2 = (bf16[32,1,9,1,4,2,2,128]{7,0,6,5,4,3,2,1:T(8,128)(2,1)}, bf16[32,1,1,4,2,2,128]{6,0,5,4,3,2,1:T(8,128)(2,1)S(1)}, f32[32,1,1,4,2,2,128]{6,0,5,4,3,2,1:T(8,128)S(1)}) fusion(bf16[1,1,4,2,2,48,128]{6,5,4,3,2,1,0:T(8,128)(2,1)S(1)} %copy-done, bf16[32,384]{1,0:T(8,128)(2,1)S(1)} %reshape.309, ...), kind=kOutput, calls=%fused_computation.78 | convolution fusion | flops 7800319 | bytes 1306752 | tf_op jit(solution)/shard_map/tbzyxjk,nj->ntbzyxk/dot_general | solution.py:122
  51.2 1.6 %collective-permute-start.8 = (bf16[32,1,1,4,2,2,128]{6,0,5,4,3,2,1:T(8,128)(2,1)S(1)}, bf16[32,1,1,4,2,2,128]{6,0,5,4,3,2,1:T(8,128)(2,1)S(1)}, u32[]{:S(2)}, u32[]{:S(2)}) collective-permute-start(bf16[32,1,1,4,2,2,128]{6,0,5,4,3,2,1:T(8,128)(2,1)S(1)} %get-tuple-element.24), channel_id=1, source_target_pairs={{8,0},{16,8},{24,16},{0,24},{9,1},{17,9},{25,17},{1,25},{10,2},{18... | collective-permute-start | bytes 393224 | tf_op jit(solution)/shard_map/ppermute | solution.py:61
  53.2 1.4 %collective-permute-start.7 = (bf16[32,1,1,2,2,2,128]{6,0,5,4,3,2,1:T(8,128)(2,1)S(1)}, bf16[32,1,1,2,2,2,128]{6,0,5,4,3,2,1:T(8,128)(2,1)S(1)}, u32[]{:S(2)}, u32[]{:S(2)}) collective-permute-start(bf16[32,1,1,2,2,2,128]{6,0,5,4,3,2,1:T(8,128)(2,1)S(1)} %pad_maximum_fusion.4), channel_id=1, source_target_pairs={{4,0},{5,1},{6,2},{7,3},{0,4},{1,5},{2,6},{3,7},{12,8},{13,9},{14,... | collective-permute-start | bytes 196616 | tf_op jit(solution)/shard_map/ppermute | solution.py:55
  54.7 2.9 %collective-permute-done.7 = bf16[32,1,1,2,2,2,128]{6,0,5,4,3,2,1:T(8,128)(2,1)S(1)} collective-permute-done((bf16[32,1,1,2,2,2,128]{6,0,5,4,3,2,1:T(8,128)(2,1)S(1)}, bf16[32,1,1,2,2,2,128]{6,0,5,4,3,2,1:T(8,128)(2,1)S(1)}, u32[]{:S(2)}, u32[]{:S(2)}) %collective-permute-start.7) | collective-permute-done | bytes 65568 | tf_op jit(solution)/shard_map/ppermute | solution.py:55
  57.8 2.6 %collective-permute-done.9 = bf16[32,1,1,4,2,2,128]{6,0,5,4,3,2,1:T(8,128)(2,1)S(1)} collective-permute-done((bf16[32,1,1,4,2,2,128]{6,0,5,4,3,2,1:T(8,128)(2,1)S(1)}, bf16[32,1,1,4,2,2,128]{6,0,5,4,3,2,1:T(8,128)(2,1)S(1)}, u32[]{:S(2)}, u32[]{:S(2)}) %collective-permute-start.9) | collective-permute-done | bytes 131104 | tf_op jit(solution)/shard_map/ppermute | solution.py:62
  60.5 1.4 %convolution_bitcast_fusion.2 = f32[4,2,2,32,64]{4,3,0,2,1:T(8,128)S(1)} fusion(bf16[1,1,4,2,2,9,64,64]{7,6,2,4,3,5,1,0:T(8,128)(2,1)S(1)} %copy-done.5, bf16[1,1,4,2,2,9,64,64]{7,6,5,4,3,2,1,0:T(8,128)(2,1)S(1)} %get-tuple-element.29, bf16[32,1,9,1,4,2,2,128]{7,0,6,5,4,3,2,1:T(8,128)(2,1)S(1)} %bitcast_dynamic-update-slice_fusion), kind=kOutput, calls=%fused_computation.10 | convolution fusion | flops 80216064 | bytes 3670016 | tf_op jit(solution)/shard_map/tbzyxdik,ntdbzyxk->ntbzyxi/dot_general | solution.py:82
  63.5 10.7 %all_to_all.15 = f32[32,1,128]{2,1,0:T(1,128)S(1)} all-to-all(f32[32,1,128]{2,1,0:T(1,128)S(1)} %broadcast_in_dim.11), channel_id=1, replica_groups=mesh['ta'=4,'xyz'=8] {'ta','xyz'}, dimensions={0} | all-to-all | bytes 32768 | tf_op jit(solution)/shard_map/all_to_all | solution.py:35
  74.4 0.9 %copy.120 = f32[32,1,1,4,2,2,128]{6,5,4,3,2,1,0:T(2,128)} copy(f32[32,1,1,4,2,2,128]{6,0,5,4,3,2,1:T(8,128)S(1)} %get-tuple-element.58) | data formatting | bytes 524288
  75.4 0.9 %copy.119 = f32[32,1,1,4,2,2,128]{6,5,4,3,2,1,0:T(2,128)} copy(f32[32,1,1,4,2,2,128]{6,0,5,4,3,2,1:T(8,128)S(1)} %get-tuple-element.59) | data formatting | bytes 524288
  (99 shorter events, 7.7 us)
Async XLA Ops:
  0.6 1.1 %copy-start = (bf16[1,1,4,2,2,48,128]{6,5,4,3,2,1,0:T(8,128)(2,1)S(1)}, bf16[1,1,4,2,2,48,128]{6,5,4,3,2,1,0:T(8,128)(2,1)}, u32[]{:S(2)}) copy-start(bf16[1,1,4,2,2,48,128]{6,5,4,3,2,1,0:T(8,128)(2,1)} %param.6) | copy-start | bytes 589828
  3.9 13.5 %all-to-all-start = ((f32[8,32,96]{2,1,0:T(8,128)}), f32[8,32,96]{2,1,0:T(8,128)S(1)}, u32[]{:S(2)}, u32[]{:S(2)}) async-start(f32[8,32,96]{2,1,0:T(8,128)} %broadcast_in_dim.8), calls=%async_computation | async-start | bytes 262144 | tf_op jit(solution)/shard_map/all_to_all | solution.py:152
  14.6 2.9 %copy-start.1 = (f32[32,1,1,4,2,2,128]{6,5,4,3,2,1,0:T(2,128)S(1)}, f32[32,1,1,4,2,2,128]{6,5,4,3,2,1,0:T(2,128)}, u32[]{:S(2)}) copy-start(f32[32,1,1,4,2,2,128]{6,5,4,3,2,1,0:T(2,128)} %param.4) | copy-start | bytes 786436
  14.6 2.9 %copy-start.7 = (bf16[1,48,384]{2,1,0:T(8,128)(2,1)S(1)}, bf16[1,48,384]{2,1,0:T(8,128)(2,1)}, u32[]{:S(2)}) copy-start(bf16[1,48,384]{2,1,0:T(8,128)(2,1)} %param.7) | copy-start | bytes 110596
  18.6 10.4 %copy-start.9 = (bf16[32,1,9,1,4,2,2,128]{7,0,6,5,4,3,2,1:T(8,128)(2,1)S(1)}, bf16[32,1,9,1,4,2,2,128]{7,0,6,5,4,3,2,1:T(8,128)(2,1)}, u32[]{:S(2)}) copy-start(bf16[32,1,9,1,4,2,2,128]{7,0,6,5,4,3,2,1:T(8,128)(2,1)} %get-tuple-element.26) | copy-start | bytes 3538948
  18.6 10.4 %collective-permute-start.1 = (bf16[32,1,1,4,2,2,128]{6,0,5,4,3,2,1:T(8,128)(2,1)S(1)}, bf16[32,1,1,4,2,2,128]{6,0,5,4,3,2,1:T(8,128)(2,1)S(1)}, u32[]{:S(2)}, u32[]{:S(2)}) collective-permute-start(bf16[32,1,1,4,2,2,128]{6,0,5,4,3,2,1:T(8,128)(2,1)S(1)} %get-tuple-element.27), channel_id=1, source_target_pairs={{2,0},{3,1},{0,2},{1,3},{6,4},{7,5},{4,6},{5,7},{10,8},{11,9},{8,1... | collective-permute-start | bytes 393224 | tf_op jit(solution)/shard_map/ppermute | solution.py:55
  20.7 8.5 %collective-permute-start.3 = (bf16[32,1,1,4,2,2,128]{6,0,5,4,3,2,1:T(8,128)(2,1)S(1)}, bf16[32,1,1,4,2,2,128]{6,0,5,4,3,2,1:T(8,128)(2,1)S(1)}, u32[]{:S(2)}, u32[]{:S(2)}) collective-permute-start(bf16[32,1,1,4,2,2,128]{6,0,5,4,3,2,1:T(8,128)(2,1)S(1)} %get-tuple-element.27), channel_id=1, source_target_pairs={{8,0},{16,8},{24,16},{0,24},{9,1},{17,9},{25,17},{1,25},{10,2},{18... | collective-permute-start | bytes 393224 | tf_op jit(solution)/shard_map/ppermute | solution.py:61
  24.3 4.6 %collective-permute-start = (bf16[32,1,1,4,2,2,128]{6,0,5,4,3,2,1:T(8,128)(2,1)S(1)}, bf16[32,1,1,4,2,2,128]{6,0,5,4,3,2,1:T(8,128)(2,1)S(1)}, u32[]{:S(2)}, u32[]{:S(2)}) collective-permute-start(bf16[32,1,1,4,2,2,128]{6,0,5,4,3,2,1:T(8,128)(2,1)S(1)} %get-tuple-element.27), channel_id=1, source_target_pairs={{1,0},{0,1},{3,2},{2,3},{5,4},{4,5},{7,6},{6,7},{9,8},{8,9},{11,10... | collective-permute-start | bytes 393224 | tf_op jit(solution)/shard_map/ppermute | solution.py:55
  24.3 7.7 %collective-permute-start.4 = (bf16[32,1,1,4,2,2,128]{6,0,5,4,3,2,1:T(8,128)(2,1)S(1)}, bf16[32,1,1,4,2,2,128]{6,0,5,4,3,2,1:T(8,128)(2,1)S(1)}, u32[]{:S(2)}, u32[]{:S(2)}) collective-permute-start(bf16[32,1,1,4,2,2,128]{6,0,5,4,3,2,1:T(8,128)(2,1)S(1)} %get-tuple-element.27), channel_id=1, source_target_pairs={{24,0},{0,8},{8,16},{16,24},{25,1},{1,9},{9,17},{17,25},{26,2},{2,... | collective-permute-start | bytes 393224 | tf_op jit(solution)/shard_map/ppermute | solution.py:62
  24.4 4.6 %collective-permute-start.2 = (bf16[32,1,1,2,2,2,128]{6,0,5,4,3,2,1:T(8,128)(2,1)S(1)}, bf16[32,1,1,2,2,2,128]{6,0,5,4,3,2,1:T(8,128)(2,1)S(1)}, u32[]{:S(2)}, u32[]{:S(2)}) collective-permute-start(bf16[32,1,1,2,2,2,128]{6,0,5,4,3,2,1:T(8,128)(2,1)S(1)} %pad_maximum_fusion.3), channel_id=1, source_target_pairs={{4,0},{5,1},{6,2},{7,3},{0,4},{1,5},{2,6},{3,7},{12,8},{13,9},{14,... | collective-permute-start | bytes 196616 | tf_op jit(solution)/shard_map/ppermute | solution.py:55
  29.0 3.1 %copy-start.4 = (bf16[1,1,4,2,2,9,64,64]{7,6,2,4,3,5,1,0:T(8,128)(2,1)S(1)}, bf16[1,1,4,2,2,9,64,64]{7,6,2,4,3,5,1,0:T(8,128)(2,1)}, u32[]{:S(2)}) copy-start(bf16[1,1,4,2,2,9,64,64]{7,6,2,4,3,5,1,0:T(8,128)(2,1)} %copy_negate_fusion) | copy-start | bytes 3538948
  32.0 1.7 %copy-start.2 = (bf16[1,1,4,2,2,9,64,128]{7,6,5,4,3,2,1,0:T(8,128)(2,1)S(1)}, bf16[1,1,4,2,2,9,64,128]{7,6,5,4,3,2,1,0:T(8,128)(2,1)}, u32[]{:S(2)}) copy-start(bf16[1,1,4,2,2,9,64,128]{7,6,5,4,3,2,1,0:T(8,128)(2,1)} %pad_maximum_fusion) | copy-start | bytes 7077892
  36.1 12.8 %all-to-all-start.1 = ((f32[32,1,1600]{2,1,0:T(1,128)}), f32[32,1,1600]{2,1,0:T(1,128)S(1)}, u32[]{:S(2)}, u32[]{:S(2)}) async-start(f32[32,1,1600]{2,1,0:T(1,128)} %broadcast_in_dim.9), calls=%async_computation.1 | async-start | bytes 425984 | tf_op jit(solution)/shard_map/all_to_all | solution.py:165
  50.5 7.1 %copy-start.8 = (bf16[32,1,9,1,4,2,2,128]{7,0,6,5,4,3,2,1:T(8,128)(2,1)S(1)}, bf16[32,1,9,1,4,2,2,128]{7,0,6,5,4,3,2,1:T(8,128)(2,1)}, u32[]{:S(2)}) copy-start(bf16[32,1,9,1,4,2,2,128]{7,0,6,5,4,3,2,1:T(8,128)(2,1)} %get-tuple-element.23) | copy-start | bytes 3538948
  50.5 7.1 %collective-permute-start.6 = (bf16[32,1,1,4,2,2,128]{6,0,5,4,3,2,1:T(8,128)(2,1)S(1)}, bf16[32,1,1,4,2,2,128]{6,0,5,4,3,2,1:T(8,128)(2,1)S(1)}, u32[]{:S(2)}, u32[]{:S(2)}) collective-permute-start(bf16[32,1,1,4,2,2,128]{6,0,5,4,3,2,1:T(8,128)(2,1)S(1)} %get-tuple-element.24), channel_id=1, source_target_pairs={{2,0},{3,1},{0,2},{1,3},{6,4},{7,5},{4,6},{5,7},{10,8},{11,9},{8,1... | collective-permute-start | bytes 393224 | tf_op jit(solution)/shard_map/ppermute | solution.py:55
  51.2 6.7 %collective-permute-start.8 = (bf16[32,1,1,4,2,2,128]{6,0,5,4,3,2,1:T(8,128)(2,1)S(1)}, bf16[32,1,1,4,2,2,128]{6,0,5,4,3,2,1:T(8,128)(2,1)S(1)}, u32[]{:S(2)}, u32[]{:S(2)}) collective-permute-start(bf16[32,1,1,4,2,2,128]{6,0,5,4,3,2,1:T(8,128)(2,1)S(1)} %get-tuple-element.24), channel_id=1, source_target_pairs={{8,0},{16,8},{24,16},{0,24},{9,1},{17,9},{25,17},{1,25},{10,2},{18... | collective-permute-start | bytes 393224 | tf_op jit(solution)/shard_map/ppermute | solution.py:61
  52.7 4.8 %collective-permute-start.5 = (bf16[32,1,1,4,2,2,128]{6,0,5,4,3,2,1:T(8,128)(2,1)S(1)}, bf16[32,1,1,4,2,2,128]{6,0,5,4,3,2,1:T(8,128)(2,1)S(1)}, u32[]{:S(2)}, u32[]{:S(2)}) collective-permute-start(bf16[32,1,1,4,2,2,128]{6,0,5,4,3,2,1:T(8,128)(2,1)S(1)} %get-tuple-element.24), channel_id=1, source_target_pairs={{1,0},{0,1},{3,2},{2,3},{5,4},{4,5},{7,6},{6,7},{9,8},{8,9},{11,10... | collective-permute-start | bytes 393224 | tf_op jit(solution)/shard_map/ppermute | solution.py:55
  52.8 7.7 %collective-permute-start.9 = (bf16[32,1,1,4,2,2,128]{6,0,5,4,3,2,1:T(8,128)(2,1)S(1)}, bf16[32,1,1,4,2,2,128]{6,0,5,4,3,2,1:T(8,128)(2,1)S(1)}, u32[]{:S(2)}, u32[]{:S(2)}) collective-permute-start(bf16[32,1,1,4,2,2,128]{6,0,5,4,3,2,1:T(8,128)(2,1)S(1)} %get-tuple-element.24), channel_id=1, source_target_pairs={{24,0},{0,8},{8,16},{16,24},{25,1},{1,9},{9,17},{17,25},{26,2},{2,... | collective-permute-start | bytes 393224 | tf_op jit(solution)/shard_map/ppermute | solution.py:62
  53.2 4.3 %collective-permute-start.7 = (bf16[32,1,1,2,2,2,128]{6,0,5,4,3,2,1:T(8,128)(2,1)S(1)}, bf16[32,1,1,2,2,2,128]{6,0,5,4,3,2,1:T(8,128)(2,1)S(1)}, u32[]{:S(2)}, u32[]{:S(2)}) collective-permute-start(bf16[32,1,1,2,2,2,128]{6,0,5,4,3,2,1:T(8,128)(2,1)S(1)} %pad_maximum_fusion.4), channel_id=1, source_target_pairs={{4,0},{5,1},{6,2},{7,3},{0,4},{1,5},{2,6},{3,7},{12,8},{13,9},{14,... | collective-permute-start | bytes 196616 | tf_op jit(solution)/shard_map/ppermute | solution.py:55
  57.6 2.9 %copy-start.5 = (bf16[1,1,4,2,2,9,64,64]{7,6,2,4,3,5,1,0:T(8,128)(2,1)S(1)}, bf16[1,1,4,2,2,9,64,64]{7,6,2,4,3,5,1,0:T(8,128)(2,1)}, u32[]{:S(2)}) copy-start(bf16[1,1,4,2,2,9,64,64]{7,6,2,4,3,5,1,0:T(8,128)(2,1)} %copy_negate_fusion) | copy-start | bytes 3538948
  60.5 1.7 %copy-start.3 = (bf16[1,1,4,2,2,9,64,128]{7,6,5,4,3,2,1,0:T(8,128)(2,1)S(1)}, bf16[1,1,4,2,2,9,64,128]{7,6,5,4,3,2,1,0:T(8,128)(2,1)}, u32[]{:S(2)}) copy-start(bf16[1,1,4,2,2,9,64,128]{7,6,5,4,3,2,1,0:T(8,128)(2,1)} %pad_maximum_fusion) | copy-start | bytes 7077892
  62.9 11.3 %copy-start.6 = (f32[32,1,1,4,2,2,128]{6,0,5,4,3,2,1:T(8,128)S(1)}, f32[32,1,1,4,2,2,128]{6,0,5,4,3,2,1:T(8,128)}, u32[]{:S(2)}) copy-start(f32[32,1,1,4,2,2,128]{6,0,5,4,3,2,1:T(8,128)} %get-tuple-element.60) | copy-start | bytes 786436

commit v17 on v13

--- a/solution.py
+++ b/solution.py
@@ -93,10 +93,9 @@
 def restrict_exact(null_vectors, field):
     return jnp.einsum(
         "tbzyxjk,ntbzyxk->nj",
-        null_vectors.astype(jnp.float32),
-        field,
+        null_vectors,
+        field.astype(jnp.bfloat16),
         preferred_element_type=jnp.float32,
-        precision=lax.Precision.HIGH,
     )
 
 
@@ -130,21 +129,14 @@
     slabs_total = lax.axis_size("ta")
     blocks_total = lax.axis_size("xyz")
     residual = right_side
-    coarse = jnp.einsum(
-        "tbzyxjk,ntbzyxk->nj",
-        null_vectors,
-        residual.astype(jnp.bfloat16),
-        preferred_element_type=jnp.float32,
-    ).astype(jnp.bfloat16)
-    width = coarse.shape[1]
-    payload = jnp.concatenate(
-        [coarse.astype(jnp.float32), restrict_exact(null_vectors, residual)], 1
-    )
+    exact_residual = restrict_exact(null_vectors, residual)
+    count, width = exact_residual.shape
+    flat = exact_residual.reshape(-1)
     parts = lax.all_to_all(
-        jnp.broadcast_to(payload[None], (blocks_total,) + payload.shape), "xyz", 0, 0
-    )
-    slab_a = slab_columns(parts[:, :, :width]).astype(jnp.bfloat16)
-    slab_residual = parts[:, :, width:].reshape(blocks_total, -1)
+        jnp.broadcast_to(flat[None, None], (blocks_total, 1) + flat.shape), "xyz", 0, 0
+    )[:, 0]
+    slab_residual = parts
+    slab_a = slab_columns(parts.reshape(blocks_total, count, width)).astype(jnp.bfloat16)
     direction_a = finish(residual, slab_a, null_vectors, inverse_rows)
     image_a = apply_links(coarse_links, direction_a.astype(jnp.bfloat16))
     image_coarse = restrict_exact(null_vectors, image_a)

time: 74.4 us -> 83.4 us (1.12)
  local copies, waits for them, and re-layouts: 5.52 us -> 16.1 us
  waiting for transfers between devices: 21.7 us -> 18.4 us
  matrix products: 6.31 us -> 7.38 us
    slice x6, local copies, waits for them, and re-layouts: 0.05 us -> 5.08 us  [both_sides(): first = lax.slice_in_dim(lowered, 0, 1, axis=which)]
    unnamed x17 -> x21, local copies, waits for them, and re-layouts: 1.9 us -> 4.26 us
    dot_general x2, matrix products: 2.06 us -> 4.35 us  [finish(): jnp.einsum('tbzyxjk,nj->ntbzyxk', null_vectors, correction, preferred_ele...]
    slice x2, local copies, waits for them, and re-layouts: 0.04 us -> 1.98 us  [both_sides(): lax.slice_in_dim(lowered, 0, length - 1, axis=which)]
    ppermute x6, waiting for transfers between devices: 6.84 us -> 5.07 us  [both_sides(): pair = lax.ppermute(jnp.concatenate([first, last], which), axis, perm)]
    ppermute x2, waiting for transfers between devices: 5.45 us -> 3.98 us  [both_sides(): from_lower = lax.ppermute(last, axis, down)]
    dot_general x3 -> x2, matrix products: 2.56 us -> 1.33 us  [restrict_exact(): jnp.einsum('tbzyxjk,ntbzyxk->nj', null_vectors, field.astype(jnp.bfloat16...]
  transfers between devices with their start and end apart: 11 -> 11, of which waited for: 5 -> 5; matrix products, arithmetic and copies ran while one was open for 1% -> 5% of each run, Pallas kernels for 0% -> 0%
where the time goes in v17:
time: 83.4 us; the launch traced here: 82.7 us
  blocking collectives  19.9 us (24%)
  waiting for transfers between devices  18.4 us (22%)
  local copies, waits for them, and re-layouts  16.1 us (19%)
  starting transfers between devices  11.7 us (14%)
  other arithmetic  7.99 us (10%)
  matrix products  7.38 us (9%)
  between operations  1.16 us (1%)
    all_to_all x1, blocking collectives, total_sum(): lax.all_to_all(copies, axes, 0, 0)[:, 0]  10 us
    all_to_all x1, blocking collectives, shards(): lax.all_to_all(jnp.broadcast_to(flat[None, None], (blocks_total, 1) + fla...  9.9 us
    all_to_all x1, waiting for transfers between devices, shards(): lax.all_to_all(jnp.broadcast_to(local[None, None], (devices, 1) + local.s...  9.37 us
    ppermute x2, starting transfers between devices, both_sides(): from_upper = lax.ppermute(first, axis, up)  5.2 us
    slice x6, local copies, waits for them, and re-layouts, both_sides(): first = lax.slice_in_dim(lowered, 0, 1, axis=which)  5.08 us
    ppermute x6, waiting for transfers between devices, both_sides(): pair = lax.ppermute(jnp.concatenate([first, last], which), axis, perm)  5.07 us
    dot_general x2, matrix products, finish(): jnp.einsum('tbzyxjk,nj->ntbzyxk', null_vectors, correction, preferred_ele...  4.35 us
    unnamed x21, local copies, waits for them, and re-layouts  4.26 us
  transfers between devices with their start and end apart: 11, of which 5 were waited for; matrix products, arithmetic and copies ran while one was open for 5% of the time, Pallas kernels for 0%

profile of v17, /device:TPU:0, one launch (start us, length us, event | category | flops | bytes accessed | tf_op | source)
XLA Modules:
  0.0 82.7 jit_solution(6150467938858733567)
XLA Ops:
  0.6 1.2 %convert_bitcast_fusion = bf16[32,4,2,2,128]{4,3,2,1,0:T(2,128)(2,1)S(1)} fusion(f32[32,1,1,4,2,2,128]{6,5,4,3,2,1,0:T(2,128)} %param.4), kind=kLoop, calls=%fused_computation.83 | loop fusion | flops 65536 | bytes 393216 | tf_op jit(solution)/shard_map/reshape
  1.8 1.1 %convolution_bitcast_fusion.3 = f32[32,48]{1,0:T(8,128)S(1)} fusion(bf16[32,4,2,2,128]{4,3,2,1,0:T(2,128)(2,1)S(1)} %convert_bitcast_fusion, bf16[1,1,4,2,2,48,128]{6,5,4,3,2,1,0:T(8,128)(2,1)} %param.6), kind=kOutput, calls=%fused_computation.21 | convolution fusion | flops 6291456 | bytes 333824 | tf_op jit(solution)/shard_map/tbzyxjk,ntbzyxk->nj/dot_general | solution.py:94
  3.1 9.9 %all_to_all.15 = f32[8,1,1536]{2,1,0:T(1,128)S(1)} all-to-all(f32[8,1,1536]{2,1,0:T(1,128)S(1)} %broadcast_in_dim.11), channel_id=1, replica_groups=mesh['ta'=4,'xyz'=8] {'xyz'}, dimensions={0} | all-to-all | bytes 98304 | tf_op jit(solution)/shard_map/all_to_all | solution.py:135
  14.6 2.1 %bitcast_dynamic-update-slice_fusion.5 = (bf16[32,1,9,1,4,2,2,128]{7,0,6,5,4,3,2,1:T(8,128)(2,1)S(1)}, bf16[32,1,1,4,2,2,128]{6,0,5,4,3,2,1:T(8,128)(2,1)}, f32[32,1,1,4,2,2,128]{6,0,5,4,3,2,1:T(8,128)}) fusion(bf16[1,1,4,2,2,48,128]{6,5,4,3,2,1,0:T(8,128)(2,1)} %param.6, bf16[32,384]{1,0:T(8,128)(2,1)} %convert_element_type.35, ...), kind=kOutput, calls=%fused_computation.79 | convolution fusion | flops 7669247 | bytes 1044480 | tf_op jit(solution)/shard_map/tbzyxjk,nj->ntbzyxk/dot_general | solution.py:113
  19.0 3.6 %collective-permute-start.3 = (bf16[32,1,1,4,2,2,128]{6,0,5,4,3,2,1:T(8,128)(2,1)}, bf16[32,1,1,4,2,2,128]{6,0,5,4,3,2,1:T(8,128)(2,1)S(1)}, u32[]{:S(2)}, u32[]{:S(2)}) collective-permute-start(bf16[32,1,1,4,2,2,128]{6,0,5,4,3,2,1:T(8,128)(2,1)} %get-tuple-element.27), channel_id=1, source_target_pairs={{8,0},{16,8},{24,16},{0,24},{9,1},{17,9},{25,17},{1,25},{10,2},{18... | collective-permute-start | bytes 393224 | tf_op jit(solution)/shard_map/ppermute | solution.py:61
  22.6 1.0 %fusion.58 = (bf16[32,1,1,3,2,2,128]{6,0,5,4,3,2,1:T(8,128)(2,1)S(1)}, bf16[32,1,1,3,2,2,128]{6,0,5,4,3,2,1:T(8,128)(2,1)S(1)}) fusion(bf16[32,1,1,4,2,2,128]{6,0,5,4,3,2,1:T(8,128)(2,1)} %get-tuple-element.27), kind=kLoop, calls=%fused_computation.115 | loop fusion | bytes 393216 | tf_op jit(solution)/shard_map/slice | solution.py:65
  24.3 0.9 %fusion.63 = (bf16[32,1,1,4,2,1,128]{6,0,5,4,3,2,1:T(8,128)(2,1)S(1)}, bf16[32,1,1,4,2,1,128]{6,0,5,4,3,2,1:T(8,128)(2,1)S(1)}) fusion(bf16[32,1,1,4,2,2,128]{6,0,5,4,3,2,1:T(8,128)(2,1)} %get-tuple-element.27), kind=kLoop, calls=%fused_computation.120 | loop fusion | bytes 262144 | tf_op jit(solution)/shard_map/slice | solution.py:46
  25.1 3.0 %collective-permute-done.2 = bf16[32,1,1,2,2,2,128]{6,0,5,4,3,2,1:T(8,128)(2,1)S(1)} collective-permute-done((bf16[32,1,1,2,2,2,128]{6,0,5,4,3,2,1:T(8,128)(2,1)S(1)}, bf16[32,1,1,2,2,2,128]{6,0,5,4,3,2,1:T(8,128)(2,1)S(1)}, u32[]{:S(2)}, u32[]{:S(2)}) %collective-permute-start.2) | collective-permute-done | bytes 65568 | tf_op jit(solution)/shard_map/ppermute | solution.py:55
  28.4 2.1 %collective-permute-done.4 = bf16[32,1,1,4,2,2,128]{6,0,5,4,3,2,1:T(8,128)(2,1)S(1)} collective-permute-done((bf16[32,1,1,4,2,2,128]{6,0,5,4,3,2,1:T(8,128)(2,1)}, bf16[32,1,1,4,2,2,128]{6,0,5,4,3,2,1:T(8,128)(2,1)S(1)}, u32[]{:S(2)}, u32[]{:S(2)}) %collective-permute-start.4) | collective-permute-done | bytes 131104 | tf_op jit(solution)/shard_map/ppermute | solution.py:62
  35.0 1.0 %multiply_reduce_fusion.5 = (f32[32]{0:T(128)S(1)}, f32[32]{0:T(128)S(1)}, f32[32,1,1,4,2,2,128]{6,0,5,4,3,2,1:T(8,128)}) fusion(f32[32,1,1,4,2,2,128]{6,5,4,3,2,1,0:T(2,128)S(1)} %copy-done.1, f32[32,1,1,4,2,2,64]{6,0,5,4,3,2,1:T(8,128)S(1)} %get-tuple-element.35, f32[32,1,1,4,2,2,64]{6,0,5,4,3,2,1:T(8,128)S(1)} %get-tuple-element.34), kind=kLoop, calls=%fused_computation.38 | loop fusion | flops 327616 | bytes 786688 | tf_op jit(solution)/shard_map/reduce_sum | solution.py:120
  36.9 2.8 %all-to-all-start.1 = ((f32[32,1,1600]{2,1,0:T(1,128)}), f32[32,1,1600]{2,1,0:T(1,128)S(1)}, u32[]{:S(2)}, u32[]{:S(2)}) async-start(f32[32,1,1600]{2,1,0:T(1,128)} %broadcast_in_dim.12), calls=%async_computation.1 | async-start | bytes 425984 | tf_op jit(solution)/shard_map/all_to_all | solution.py:148
  39.7 9.4 %all-to-all-done.1 = f32[32,1,1600]{2,1,0:T(1,128)S(1)} async-done(((f32[32,1,1600]{2,1,0:T(1,128)}), f32[32,1,1600]{2,1,0:T(1,128)S(1)}, u32[]{:S(2)}, u32[]{:S(2)}) %all-to-all-start.1) | async-done | bytes 204832 | tf_op jit(solution)/shard_map/all_to_all | solution.py:148
  50.3 2.2 %bitcast_dynamic-update-slice_fusion.2 = (bf16[32,1,9,1,4,2,2,128]{7,0,6,5,4,3,2,1:T(8,128)(2,1)S(1)}, bf16[32,1,1,4,2,2,128]{6,0,5,4,3,2,1:T(8,128)(2,1)}, f32[32,1,1,4,2,2,128]{6,0,5,4,3,2,1:T(8,128)}) fusion(bf16[1,1,4,2,2,48,128]{6,5,4,3,2,1,0:T(8,128)(2,1)} %param.6, bf16[32,384]{1,0:T(8,128)(2,1)} %reshape.365, bf16[1,48,384]{2,1,0:T(8,128)(2,1)} %param.7, ...), kind=kOutput, calls=%fused_computation.76 | convolution fusion | flops 7800319 | bytes 1306752 | tf_op jit(solution)/shard_map/tbzyxjk,nj->ntbzyxk/dot_general | solution.py:113
  53.3 0.9 %fusion.55 = (bf16[32,1,1,4,1,2,128]{6,0,5,4,3,2,1:T(8,128)(2,1)S(1)}, bf16[32,1,1,4,1,2,128]{6,0,5,4,3,2,1:T(8,128)(2,1)S(1)}) fusion(bf16[32,1,1,4,2,2,128]{6,0,5,4,3,2,1:T(8,128)(2,1)} %get-tuple-element.24), kind=kLoop, calls=%fused_computation.112 | loop fusion | bytes 262144 | tf_op jit(solution)/shard_map/slice | solution.py:46
  54.8 1.6 %collective-permute-start.8 = (bf16[32,1,1,4,2,2,128]{6,0,5,4,3,2,1:T(8,128)(2,1)}, bf16[32,1,1,4,2,2,128]{6,0,5,4,3,2,1:T(8,128)(2,1)S(1)}, u32[]{:S(2)}, u32[]{:S(2)}) collective-permute-start(bf16[32,1,1,4,2,2,128]{6,0,5,4,3,2,1:T(8,128)(2,1)} %get-tuple-element.24), channel_id=1, source_target_pairs={{8,0},{16,8},{24,16},{0,24},{9,1},{17,9},{25,17},{1,25},{10,2},{18... | collective-permute-start | bytes 393224 | tf_op jit(solution)/shard_map/ppermute | solution.py:61
  56.9 1.0 %fusion.52 = (bf16[32,1,1,3,2,2,128]{6,0,5,4,3,2,1:T(8,128)(2,1)S(1)}, bf16[32,1,1,3,2,2,128]{6,0,5,4,3,2,1:T(8,128)(2,1)S(1)}) fusion(bf16[32,1,1,4,2,2,128]{6,0,5,4,3,2,1:T(8,128)(2,1)} %get-tuple-element.24), kind=kLoop, calls=%fused_computation.109 | loop fusion | bytes 393216 | tf_op jit(solution)/shard_map/slice | solution.py:65
  57.9 1.4 %collective-permute-start.7 = (bf16[32,1,1,2,2,2,128]{6,0,5,4,3,2,1:T(8,128)(2,1)S(1)}, bf16[32,1,1,2,2,2,128]{6,0,5,4,3,2,1:T(8,128)(2,1)S(1)}, u32[]{:S(2)}, u32[]{:S(2)}) collective-permute-start(bf16[32,1,1,2,2,2,128]{6,0,5,4,3,2,1:T(8,128)(2,1)S(1)} %pad_maximum_fusion.4), channel_id=1, source_target_pairs={{4,0},{5,1},{6,2},{7,3},{0,4},{1,5},{2,6},{3,7},{12,8},{13,9},{14,... | collective-permute-start | bytes 196616 | tf_op jit(solution)/shard_map/ppermute | solution.py:55
  59.3 0.9 %fusion.57 = (bf16[32,1,1,4,2,1,128]{6,0,5,4,3,2,1:T(8,128)(2,1)S(1)}, bf16[32,1,1,4,2,1,128]{6,0,5,4,3,2,1:T(8,128)(2,1)S(1)}) fusion(bf16[32,1,1,4,2,2,128]{6,0,5,4,3,2,1:T(8,128)(2,1)} %get-tuple-element.24), kind=kLoop, calls=%fused_computation.114 | loop fusion | bytes 262144 | tf_op jit(solution)/shard_map/slice | solution.py:46
  60.2 2.0 %collective-permute-done.7 = bf16[32,1,1,2,2,2,128]{6,0,5,4,3,2,1:T(8,128)(2,1)S(1)} collective-permute-done((bf16[32,1,1,2,2,2,128]{6,0,5,4,3,2,1:T(8,128)(2,1)S(1)}, bf16[32,1,1,2,2,2,128]{6,0,5,4,3,2,1:T(8,128)(2,1)S(1)}, u32[]{:S(2)}, u32[]{:S(2)}) %collective-permute-start.7) | collective-permute-done | bytes 65568 | tf_op jit(solution)/shard_map/ppermute | solution.py:55
  62.5 1.9 %collective-permute-done.9 = bf16[32,1,1,4,2,2,128]{6,0,5,4,3,2,1:T(8,128)(2,1)S(1)} collective-permute-done((bf16[32,1,1,4,2,2,128]{6,0,5,4,3,2,1:T(8,128)(2,1)}, bf16[32,1,1,4,2,2,128]{6,0,5,4,3,2,1:T(8,128)(2,1)S(1)}, u32[]{:S(2)}, u32[]{:S(2)}) %collective-permute-start.9) | collective-permute-done | bytes 131104 | tf_op jit(solution)/shard_map/ppermute | solution.py:62
  69.5 10.0 %all_to_all.16 = f32[32,1,128]{2,1,0:T(1,128)S(1)} all-to-all(f32[32,1,128]{2,1,0:T(1,128)S(1)} %broadcast_in_dim.14), channel_id=1, replica_groups=mesh['ta'=4,'xyz'=8] {'ta','xyz'}, dimensions={0} | all-to-all | bytes 32768 | tf_op jit(solution)/shard_map/all_to_all | solution.py:35
  79.7 1.2 %multiply_subtract_fusion = (f32[32,1,1,4,2,2,128]{6,0,5,4,3,2,1:T(8,128)S(1)}, f32[32,1,1,4,2,2,128]{6,0,5,4,3,2,1:T(8,128)S(1)}) fusion(f32[32,1,1,4,2,2,128]{6,0,5,4,3,2,1:T(8,128)S(1)} %get-tuple-element.22, f32[32,1,1,4,2,2,128]{6,0,5,4,3,2,1:T(8,128)S(1)} %copy-done.3, f32[32]{0:T(128)S(1)} %get-tuple-element.21, f32[32]{0:T(128)S(1)} %get-tuple-element.20, ...), kind=kLoop, calls=%fused_computation.30 | loop fusion | flops 720896 | bytes 1835392 | tf_op jit(solution)/shard_map/sub | solution.py:200
  80.8 0.9 %copy.128 = f32[32,1,1,4,2,2,128]{6,5,4,3,2,1,0:T(2,128)} copy(f32[32,1,1,4,2,2,128]{6,0,5,4,3,2,1:T(8,128)S(1)} %get-tuple-element.66) | data formatting | bytes 524288
  81.7 0.9 %copy.127 = f32[32,1,1,4,2,2,128]{6,5,4,3,2,1,0:T(2,128)} copy(f32[32,1,1,4,2,2,128]{6,0,5,4,3,2,1:T(8,128)S(1)} %get-tuple-element.67) | data formatting | bytes 524288
  (99 shorter events, 18.6 us)
Async XLA Ops:
  0.6 32.2 %copy-start = (bf16[1,1,4,2,2,9,64,128]{7,6,5,4,3,2,1,0:T(8,128)(2,1)S(1)}, bf16[1,1,4,2,2,9,64,128]{7,6,5,4,3,2,1,0:T(8,128)(2,1)}, u32[]{:S(2)}) copy-start(bf16[1,1,4,2,2,9,64,128]{7,6,5,4,3,2,1,0:T(8,128)(2,1)} %param.5) | copy-start | bytes 7077892
  13.2 0.7 copy-start.4
  18.4 9.9 %collective-permute-start.1 = (bf16[32,1,1,4,2,2,128]{6,0,5,4,3,2,1:T(8,128)(2,1)}, bf16[32,1,1,4,2,2,128]{6,0,5,4,3,2,1:T(8,128)(2,1)S(1)}, u32[]{:S(2)}, u32[]{:S(2)}) collective-permute-start(bf16[32,1,1,4,2,2,128]{6,0,5,4,3,2,1:T(8,128)(2,1)} %get-tuple-element.27), channel_id=1, source_target_pairs={{2,0},{3,1},{0,2},{1,3},{6,4},{7,5},{4,6},{5,7},{10,8},{11,9},{8,1... | collective-permute-start | bytes 393224 | tf_op jit(solution)/shard_map/ppermute | solution.py:55
  19.0 9.4 %collective-permute-start.3 = (bf16[32,1,1,4,2,2,128]{6,0,5,4,3,2,1:T(8,128)(2,1)}, bf16[32,1,1,4,2,2,128]{6,0,5,4,3,2,1:T(8,128)(2,1)S(1)}, u32[]{:S(2)}, u32[]{:S(2)}) collective-permute-start(bf16[32,1,1,4,2,2,128]{6,0,5,4,3,2,1:T(8,128)(2,1)} %get-tuple-element.27), channel_id=1, source_target_pairs={{8,0},{16,8},{24,16},{0,24},{9,1},{17,9},{25,17},{1,25},{10,2},{18... | collective-permute-start | bytes 393224 | tf_op jit(solution)/shard_map/ppermute | solution.py:61
  22.6 5.6 %collective-permute-start = (bf16[32,1,1,4,2,2,128]{6,0,5,4,3,2,1:T(8,128)(2,1)}, bf16[32,1,1,4,2,2,128]{6,0,5,4,3,2,1:T(8,128)(2,1)S(1)}, u32[]{:S(2)}, u32[]{:S(2)}) collective-permute-start(bf16[32,1,1,4,2,2,128]{6,0,5,4,3,2,1:T(8,128)(2,1)} %get-tuple-element.27), channel_id=1, source_target_pairs={{1,0},{0,1},{3,2},{2,3},{5,4},{4,5},{7,6},{6,7},{9,8},{8,9},{11,10... | collective-permute-start | bytes 393224 | tf_op jit(solution)/shard_map/ppermute | solution.py:55
  22.6 7.9 %collective-permute-start.4 = (bf16[32,1,1,4,2,2,128]{6,0,5,4,3,2,1:T(8,128)(2,1)}, bf16[32,1,1,4,2,2,128]{6,0,5,4,3,2,1:T(8,128)(2,1)S(1)}, u32[]{:S(2)}, u32[]{:S(2)}) collective-permute-start(bf16[32,1,1,4,2,2,128]{6,0,5,4,3,2,1:T(8,128)(2,1)} %get-tuple-element.27), channel_id=1, source_target_pairs={{24,0},{0,8},{8,16},{16,24},{25,1},{1,9},{9,17},{17,25},{26,2},{2,... | collective-permute-start | bytes 393224 | tf_op jit(solution)/shard_map/ppermute | solution.py:62
  23.6 4.5 %collective-permute-start.2 = (bf16[32,1,1,2,2,2,128]{6,0,5,4,3,2,1:T(8,128)(2,1)S(1)}, bf16[32,1,1,2,2,2,128]{6,0,5,4,3,2,1:T(8,128)(2,1)S(1)}, u32[]{:S(2)}, u32[]{:S(2)}) collective-permute-start(bf16[32,1,1,2,2,2,128]{6,0,5,4,3,2,1:T(8,128)(2,1)S(1)} %pad_maximum_fusion.3), channel_id=1, source_target_pairs={{4,0},{5,1},{6,2},{7,3},{0,4},{1,5},{2,6},{3,7},{12,8},{13,9},{14,... | collective-permute-start | bytes 196616 | tf_op jit(solution)/shard_map/ppermute | solution.py:55
  33.7 0.9 %copy-start.7 = (bf16[1,1,4,2,2,48,128]{6,5,4,3,2,1,0:T(8,128)(2,1)S(1)}, bf16[1,1,4,2,2,48,128]{6,5,4,3,2,1,0:T(8,128)(2,1)}, u32[]{:S(2)}) copy-start(bf16[1,1,4,2,2,48,128]{6,5,4,3,2,1,0:T(8,128)(2,1)} %param.6) | copy-start | bytes 589828
  33.8 1.2 %copy-start.1 = (f32[32,1,1,4,2,2,128]{6,5,4,3,2,1,0:T(2,128)S(1)}, f32[32,1,1,4,2,2,128]{6,5,4,3,2,1,0:T(2,128)}, u32[]{:S(2)}) copy-start(f32[32,1,1,4,2,2,128]{6,5,4,3,2,1,0:T(2,128)} %param.4) | copy-start | bytes 786436
  35.0 14.5 %copy-start.5 = (f32[8,32,48]{2,1,0:T(8,128)S(1)}, f32[8,32,48]{2,1,0:T(8,128)}, u32[]{:S(2)}) copy-start(f32[8,32,48]{2,1,0:T(8,128)} %copy-done.4) | copy-start | bytes 147460
  36.9 12.2 %all-to-all-start.1 = ((f32[32,1,1600]{2,1,0:T(1,128)}), f32[32,1,1600]{2,1,0:T(1,128)S(1)}, u32[]{:S(2)}, u32[]{:S(2)}) async-start(f32[32,1,1600]{2,1,0:T(1,128)} %broadcast_in_dim.12), calls=%async_computation.1 | async-start | bytes 425984 | tf_op jit(solution)/shard_map/all_to_all | solution.py:148
  54.2 8.1 %collective-permute-start.6 = (bf16[32,1,1,4,2,2,128]{6,0,5,4,3,2,1:T(8,128)(2,1)}, bf16[32,1,1,4,2,2,128]{6,0,5,4,3,2,1:T(8,128)(2,1)S(1)}, u32[]{:S(2)}, u32[]{:S(2)}) collective-permute-start(bf16[32,1,1,4,2,2,128]{6,0,5,4,3,2,1:T(8,128)(2,1)} %get-tuple-element.24), channel_id=1, source_target_pairs={{2,0},{3,1},{0,2},{1,3},{6,4},{7,5},{4,6},{5,7},{10,8},{11,9},{8,1... | collective-permute-start | bytes 393224 | tf_op jit(solution)/shard_map/ppermute | solution.py:55
  54.8 7.6 %collective-permute-start.8 = (bf16[32,1,1,4,2,2,128]{6,0,5,4,3,2,1:T(8,128)(2,1)}, bf16[32,1,1,4,2,2,128]{6,0,5,4,3,2,1:T(8,128)(2,1)S(1)}, u32[]{:S(2)}, u32[]{:S(2)}) collective-permute-start(bf16[32,1,1,4,2,2,128]{6,0,5,4,3,2,1:T(8,128)(2,1)} %get-tuple-element.24), channel_id=1, source_target_pairs={{8,0},{16,8},{24,16},{0,24},{9,1},{17,9},{25,17},{1,25},{10,2},{18... | collective-permute-start | bytes 393224 | tf_op jit(solution)/shard_map/ppermute | solution.py:61
  56.4 5.8 %collective-permute-start.5 = (bf16[32,1,1,4,2,2,128]{6,0,5,4,3,2,1:T(8,128)(2,1)}, bf16[32,1,1,4,2,2,128]{6,0,5,4,3,2,1:T(8,128)(2,1)S(1)}, u32[]{:S(2)}, u32[]{:S(2)}) collective-permute-start(bf16[32,1,1,4,2,2,128]{6,0,5,4,3,2,1:T(8,128)(2,1)} %get-tuple-element.24), channel_id=1, source_target_pairs={{1,0},{0,1},{3,2},{2,3},{5,4},{4,5},{7,6},{6,7},{9,8},{8,9},{11,10... | collective-permute-start | bytes 393224 | tf_op jit(solution)/shard_map/ppermute | solution.py:55
  56.4 7.9 %collective-permute-start.9 = (bf16[32,1,1,4,2,2,128]{6,0,5,4,3,2,1:T(8,128)(2,1)}, bf16[32,1,1,4,2,2,128]{6,0,5,4,3,2,1:T(8,128)(2,1)S(1)}, u32[]{:S(2)}, u32[]{:S(2)}) collective-permute-start(bf16[32,1,1,4,2,2,128]{6,0,5,4,3,2,1:T(8,128)(2,1)} %get-tuple-element.24), channel_id=1, source_target_pairs={{24,0},{0,8},{8,16},{16,24},{25,1},{1,9},{9,17},{17,25},{26,2},{2,... | collective-permute-start | bytes 393224 | tf_op jit(solution)/shard_map/ppermute | solution.py:62
  57.9 4.3 %collective-permute-start.7 = (bf16[32,1,1,2,2,2,128]{6,0,5,4,3,2,1:T(8,128)(2,1)S(1)}, bf16[32,1,1,2,2,2,128]{6,0,5,4,3,2,1:T(8,128)(2,1)S(1)}, u32[]{:S(2)}, u32[]{:S(2)}) collective-permute-start(bf16[32,1,1,2,2,2,128]{6,0,5,4,3,2,1:T(8,128)(2,1)S(1)} %pad_maximum_fusion.4), channel_id=1, source_target_pairs={{4,0},{5,1},{6,2},{7,3},{0,4},{1,5},{2,6},{3,7},{12,8},{13,9},{14,... | collective-permute-start | bytes 196616 | tf_op jit(solution)/shard_map/ppermute | solution.py:55
  68.0 1.0 %copy-start.2 = (f32[32,1,1,4,2,2,128]{6,5,4,3,2,1,0:T(2,128)S(1)}, f32[32,1,1,4,2,2,128]{6,5,4,3,2,1,0:T(2,128)}, u32[]{:S(2)}) copy-start(f32[32,1,1,4,2,2,128]{6,5,4,3,2,1,0:T(2,128)} %param.4) | copy-start | bytes 786436
  68.1 1.0 %copy-start.3 = (f32[32,1,1,4,2,2,128]{6,0,5,4,3,2,1:T(8,128)S(1)}, f32[32,1,1,4,2,2,128]{6,0,5,4,3,2,1:T(8,128)}, u32[]{:S(2)}) copy-start(f32[32,1,1,4,2,2,128]{6,0,5,4,3,2,1:T(8,128)} %get-tuple-element.25) | copy-start | bytes 786436
  68.1 11.6 %copy-start.6 = (f32[32,1,1,4,2,2,128]{6,0,5,4,3,2,1:T(8,128)S(1)}, f32[32,1,1,4,2,2,128]{6,0,5,4,3,2,1:T(8,128)}, u32[]{:S(2)}) copy-start(f32[32,1,1,4,2,2,128]{6,0,5,4,3,2,1:T(8,128)} %get-tuple-element.69) | copy-start | bytes 786436

commit v18 on v13

--- a/solution.py
+++ b/solution.py
@@ -152,15 +152,22 @@
     if slabs_total * blocks_total <= 64:
         devices = slabs_total * blocks_total
         count, width = image_coarse.shape
-        local = jnp.concatenate([pair_local.T.reshape(-1), image_coarse.reshape(-1)])
+        pair_flat = pair_local.T.reshape(-1)
+        high = pair_flat.astype(jnp.bfloat16)
+        low = (pair_flat - high.astype(jnp.float32)).astype(jnp.bfloat16)
+        local = jnp.concatenate([high, low, image_coarse.reshape(-1).astype(jnp.bfloat16)])
         gathered = lax.all_to_all(
             jnp.broadcast_to(local[None, None], (devices, 1) + local.shape),
             ("ta", "xyz"),
             0,
             0,
         )[:, 0]
-        pair = jnp.sum(gathered[:, : 2 * count], axis=0).reshape(2, count).T
-        image_slabs = gathered[:, 2 * count :].reshape(
+        size = pair_flat.shape[0]
+        pair_parts = gathered[:, :size].astype(jnp.float32) + gathered[
+            :, size : 2 * size
+        ].astype(jnp.float32)
+        pair = jnp.sum(pair_parts, axis=0).reshape(2, count).T
+        image_slabs = gathered[:, 2 * size :].astype(jnp.float32).reshape(
             (slabs_total, blocks_total, count * width)
         )
         slab_image = lax.dynamic_index_in_dim(

time: 74.4 us -> 75.2 us (1.011)
  waiting for transfers between devices: 21.7 us -> 20.3 us
  other arithmetic: 7.27 us -> 8.52 us
  local copies, waits for them, and re-layouts: 5.52 us -> 6.49 us
    all_to_all x1, waiting for transfers between devices: 9.37 us -> 8.02 us  [shards(): lax.all_to_all(jnp.broadcast_to(local[None, None], (devices, 1) + local.s...]
    broadcast_in_dim x0 -> x1, other arithmetic: none -> 1.25 us  [shards(): jnp.broadcast_to(local[None, None], (devices, 1) + local.shape)]
    unnamed x17 -> x22, local copies, waits for them, and re-layouts: 1.9 us -> 3.06 us
where the time goes in v18:
time: 75.2 us; the launch traced here: 74.8 us
  blocking collectives  20.9 us (28%)
  waiting for transfers between devices  20.3 us (27%)
  starting transfers between devices  11.1 us (15%)
  other arithmetic  8.52 us (11%)
  local copies, waits for them, and re-layouts  6.49 us (9%)
  matrix products  6.28 us (8%)
  between operations  1.18 us (2%)
    all_to_all x1, blocking collectives, shards(): lax.all_to_all(jnp.broadcast_to(payload[None], (blocks_total,) + payload....  10.5 us
    all_to_all x1, blocking collectives, total_sum(): lax.all_to_all(copies, axes, 0, 0)[:, 0]  10.4 us
    all_to_all x1, waiting for transfers between devices, shards(): lax.all_to_all(jnp.broadcast_to(local[None, None], (devices, 1) + local.s...  8.02 us
    ppermute x6, waiting for transfers between devices, both_sides(): pair = lax.ppermute(jnp.concatenate([first, last], which), axis, perm)  7.19 us
    ppermute x2, waiting for transfers between devices, both_sides(): from_lower = lax.ppermute(last, axis, down)  5.08 us
    ppermute x2, starting transfers between devices, both_sides(): from_upper = lax.ppermute(first, axis, up)  4.83 us
    unnamed x22, local copies, waits for them, and re-layouts  3.06 us
    ppermute x6, starting transfers between devices, both_sides(): pair = lax.ppermute(jnp.concatenate([first, last], which), axis, perm)  2.79 us
  transfers between devices with their start and end apart: 11, of which 5 were waited for; matrix products, arithmetic and copies ran while one was open for 1% of the time, Pallas kernels for 0%

profile of v18, /device:TPU:0, one launch (start us, length us, event | category | flops | bytes accessed | tf_op | source)
XLA Modules:
  0.0 74.8 jit_solution(14227148652202641459)
XLA Ops:
  0.7 1.2 %convert_bitcast_fusion = bf16[32,4,2,2,128]{4,3,2,1,0:T(2,128)(2,1)S(1)} fusion(f32[32,1,1,4,2,2,128]{6,5,4,3,2,1,0:T(2,128)} %param.4), kind=kLoop, calls=%fused_computation.84 | loop fusion | flops 65536 | bytes 393216 | tf_op jit(solution)/shard_map/reshape
  1.9 1.2 %convolution_bitcast_fusion.4 = f32[32,48]{1,0:T(8,128)S(1)} fusion(f32[32,4,2,2,128]{4,3,2,1,0:T(2,128)} %bitcast.235, bf16[1,1,4,2,2,48,128]{6,5,4,3,2,1,0:T(8,128)(2,1)} %param.6), kind=kOutput, calls=%fused_computation.22 | convolution fusion | flops 18874368 | bytes 464896 | tf_op jit(solution)/shard_map/tbzyxjk,ntbzyxk->nj/dot_general | solution.py:94
  3.1 1.1 %fusion.20 = f32[32,48]{1,0:T(8,128)S(1)} fusion(bf16[32,4,2,2,128]{4,3,2,1,0:T(2,128)(2,1)S(1)} %convert_bitcast_fusion, bf16[1,1,4,2,2,48,128]{6,5,4,3,2,1,0:T(8,128)(2,1)} %param.6), kind=kOutput, calls=%fused_computation.25 | convolution fusion | flops 6294528 | bytes 333824 | tf_op jit(solution)/shard_map/tbzyxjk,ntbzyxk->nj/dot_general | solution.py:133
  4.3 10.5 %all_to_all.15 = f32[8,32,96]{2,1,0:T(8,128)S(1)} all-to-all(f32[8,32,96]{2,1,0:T(8,128)S(1)} %broadcast_in_dim.8), channel_id=1, replica_groups=mesh['ta'=4,'xyz'=8] {'xyz'}, dimensions={0} | all-to-all | bytes 196608 | tf_op jit(solution)/shard_map/all_to_all | solution.py:143
  15.0 1.0 %bitcast_dynamic-update-slice_fusion.5 = (bf16[32,1,9,1,4,2,2,128]{7,0,6,5,4,3,2,1:T(8,128)(2,1)}, bf16[32,1,1,4,2,2,128]{6,0,5,4,3,2,1:T(8,128)(2,1)S(1)}, f32[32,1,1,4,2,2,128]{6,0,5,4,3,2,1:T(8,128)}) fusion(bf16[1,1,4,2,2,48,128]{6,5,4,3,2,1,0:T(8,128)(2,1)S(1)} %copy-done.4, bf16[32,384]{1,0:T(8,128)(2,1)S(1)} %convert_element_type.60, ...), kind=kOutput, calls=%fused_computation.82 | convolution fusion | flops 7669247 | bytes 1044480 | tf_op jit(solution)/shard_map/tbzyxjk,nj->ntbzyxk/dot_general | solution.py:114
  16.7 3.6 %collective-permute-start.3 = (bf16[32,1,1,4,2,2,128]{6,0,5,4,3,2,1:T(8,128)(2,1)S(1)}, bf16[32,1,1,4,2,2,128]{6,0,5,4,3,2,1:T(8,128)(2,1)S(1)}, u32[]{:S(2)}, u32[]{:S(2)}) collective-permute-start(bf16[32,1,1,4,2,2,128]{6,0,5,4,3,2,1:T(8,128)(2,1)S(1)} %get-tuple-element.27), channel_id=1, source_target_pairs={{8,0},{16,8},{24,16},{0,24},{9,1},{17,9},{25,17},{1,25},{10,2},{18... | collective-permute-start | bytes 393224 | tf_op jit(solution)/shard_map/ppermute | solution.py:61
  21.0 3.9 %collective-permute-done.2 = bf16[32,1,1,2,2,2,128]{6,0,5,4,3,2,1:T(8,128)(2,1)S(1)} collective-permute-done((bf16[32,1,1,2,2,2,128]{6,0,5,4,3,2,1:T(8,128)(2,1)S(1)}, bf16[32,1,1,2,2,2,128]{6,0,5,4,3,2,1:T(8,128)(2,1)S(1)}, u32[]{:S(2)}, u32[]{:S(2)}) %collective-permute-start.2) | collective-permute-done | bytes 65568 | tf_op jit(solution)/shard_map/ppermute | solution.py:55
  25.2 2.8 %collective-permute-done.4 = bf16[32,1,1,4,2,2,128]{6,0,5,4,3,2,1:T(8,128)(2,1)S(1)} collective-permute-done((bf16[32,1,1,4,2,2,128]{6,0,5,4,3,2,1:T(8,128)(2,1)S(1)}, bf16[32,1,1,4,2,2,128]{6,0,5,4,3,2,1:T(8,128)(2,1)S(1)}, u32[]{:S(2)}, u32[]{:S(2)}) %collective-permute-start.4) | collective-permute-done | bytes 131104 | tf_op jit(solution)/shard_map/ppermute | solution.py:62
  30.4 0.8 %fusion.6 = f32[2,32,1,1,4,2,2,64]{7,1,6,5,4,3,2,0:T(8,128)S(1)} fusion(bf16[1,1,4,2,2,9,64,128]{7,6,5,4,3,2,1,0:T(8,128)(2,1)S(1)} %copy-done, bf16[1,32,1,9,1,4,2,2,128]{8,1,7,6,5,3,4,2,0:T(8,128)(2,1)S(1)} %maximum_bitcast_fusion.3, bf16[1,32,1,9,1,4,2,2,128]{8,1,7,6,5,3,4,2,0:T(8,128)(2,1)S(1)} %maximum_bitcast_fusion.2), kind=kOutput, calls=%fused_computation.8 | convolution fusion | flops 152174592 | bytes 4980736 | tf_op jit(solution)/shard_map/tbzyxdik,pntdbzyxk->pntbzyxi/dot_general | solution.py:87
  32.7 1.2 %reduce.1 = bf16[32,1664]{1,0:T(8,128)(2,1)S(1)} reduce(bf16[32,1,1664]{2,1,0:T(2,128)(2,1)S(1)} %broadcast_in_dim.9, bf16[]{:T(256)} %broadcast.55), dimensions={1}, to_apply=%broadcast_in_dim.9.reduce_sub_computation | reduce | bytes 212994 | tf_op jit(solution)/shard_map/broadcast_in_dim | solution.py:160
  34.0 0.8 %reshape.370 = bf16[32,2,832]{2,1,0:T(2,128)(2,1)} reshape(bf16[32,1664]{1,0:T(8,128)(2,1)S(1)} %reduce.1) | data formatting | bytes 212992
  34.8 2.7 %all-to-all-start.1 = ((bf16[32,2,832]{2,1,0:T(2,128)(2,1)}), bf16[32,2,832]{2,1,0:T(2,128)(2,1)S(1)}, u32[]{:S(2)}, u32[]{:S(2)}) async-start(bf16[32,2,832]{2,1,0:T(2,128)(2,1)} %reshape.370), calls=%async_computation.1 | async-start | bytes 229376 | tf_op jit(solution)/shard_map/all_to_all | solution.py:159
  37.5 8.0 %all-to-all-done.1 = bf16[32,2,832]{2,1,0:T(2,128)(2,1)S(1)} async-done(((bf16[32,2,832]{2,1,0:T(2,128)(2,1)}), bf16[32,2,832]{2,1,0:T(2,128)(2,1)S(1)}, u32[]{:S(2)}, u32[]{:S(2)}) %all-to-all-start.1) | async-done | bytes 106528 | tf_op jit(solution)/shard_map/all_to_all | solution.py:159
  46.5 1.0 %bitcast_dynamic-update-slice_fusion.2 = (bf16[32,1,9,1,4,2,2,128]{7,0,6,5,4,3,2,1:T(8,128)(2,1)}, bf16[32,1,1,4,2,2,128]{6,0,5,4,3,2,1:T(8,128)(2,1)S(1)}, f32[32,1,1,4,2,2,128]{6,0,5,4,3,2,1:T(8,128)S(1)}) fusion(bf16[1,1,4,2,2,48,128]{6,5,4,3,2,1,0:T(8,128)(2,1)S(1)} %copy-done.4, bf16[32,384]{1,0:T(8,128)(2,1)S(1)} %reshape.358, ...), kind=kOutput, calls=%fused_computation.79 | convolution fusion | flops 7800319 | bytes 1306752 | tf_op jit(solution)/shard_map/tbzyxjk,nj->ntbzyxk/dot_general | solution.py:114
  47.9 1.2 %collective-permute-start.8 = (bf16[32,1,1,4,2,2,128]{6,0,5,4,3,2,1:T(8,128)(2,1)S(1)}, bf16[32,1,1,4,2,2,128]{6,0,5,4,3,2,1:T(8,128)(2,1)S(1)}, u32[]{:S(2)}, u32[]{:S(2)}) collective-permute-start(bf16[32,1,1,4,2,2,128]{6,0,5,4,3,2,1:T(8,128)(2,1)S(1)} %get-tuple-element.24), channel_id=1, source_target_pairs={{8,0},{16,8},{24,16},{0,24},{9,1},{17,9},{25,17},{1,25},{10,2},{18... | collective-permute-start | bytes 393224 | tf_op jit(solution)/shard_map/ppermute | solution.py:61
  50.0 1.1 %collective-permute-start.7 = (bf16[32,1,1,2,2,2,128]{6,0,5,4,3,2,1:T(8,128)(2,1)S(1)}, bf16[32,1,1,2,2,2,128]{6,0,5,4,3,2,1:T(8,128)(2,1)S(1)}, u32[]{:S(2)}, u32[]{:S(2)}) collective-permute-start(bf16[32,1,1,2,2,2,128]{6,0,5,4,3,2,1:T(8,128)(2,1)S(1)} %pad_maximum_fusion.3), channel_id=1, source_target_pairs={{4,0},{5,1},{6,2},{7,3},{0,4},{1,5},{2,6},{3,7},{12,8},{13,9},{14,... | collective-permute-start | bytes 196616 | tf_op jit(solution)/shard_map/ppermute | solution.py:55
  51.1 3.2 %collective-permute-done.7 = bf16[32,1,1,2,2,2,128]{6,0,5,4,3,2,1:T(8,128)(2,1)S(1)} collective-permute-done((bf16[32,1,1,2,2,2,128]{6,0,5,4,3,2,1:T(8,128)(2,1)S(1)}, bf16[32,1,1,2,2,2,128]{6,0,5,4,3,2,1:T(8,128)(2,1)S(1)}, u32[]{:S(2)}, u32[]{:S(2)}) %collective-permute-start.7) | collective-permute-done | bytes 65568 | tf_op jit(solution)/shard_map/ppermute | solution.py:55
  54.6 2.3 %collective-permute-done.9 = bf16[32,1,1,4,2,2,128]{6,0,5,4,3,2,1:T(8,128)(2,1)S(1)} collective-permute-done((bf16[32,1,1,4,2,2,128]{6,0,5,4,3,2,1:T(8,128)(2,1)S(1)}, bf16[32,1,1,4,2,2,128]{6,0,5,4,3,2,1:T(8,128)(2,1)S(1)}, u32[]{:S(2)}, u32[]{:S(2)}) %collective-permute-start.9) | collective-permute-done | bytes 131104 | tf_op jit(solution)/shard_map/ppermute | solution.py:62
  57.8 0.8 %fusion.55 = (bf16[32,1,9,1,4,2,2,64]{7,0,6,5,4,2,3,1:T(8,128)(2,1)S(1)}, bf16[32,1,9,1,4,2,2,64]{7,0,6,5,4,3,2,1:T(8,128)(2,1)S(1)}) fusion(bf16[32,1,9,1,4,2,2,128]{7,0,6,5,4,2,3,1:T(8,128)(2,1)S(1)} %bitcast.236), kind=kLoop, calls=%fused_computation.111 | loop fusion | bytes 1769472 | tf_op jit(solution)/shard_map/slice | solution.py:82
  60.0 0.9 %fusion.11 = f32[2,32,1,1,4,2,2,64]{7,1,6,5,4,3,2,0:T(8,128)S(1)} fusion(bf16[1,1,4,2,2,9,64,128]{7,6,5,4,3,2,1,0:T(8,128)(2,1)S(1)} %copy-done, bf16[1,32,1,9,1,4,2,2,128]{8,1,7,6,5,3,4,2,0:T(8,128)(2,1)S(1)} %maximum_bitcast_fusion.5, bf16[1,32,1,9,1,4,2,2,128]{8,1,7,6,5,3,4,2,0:T(8,128)(2,1)S(1)} %maximum_bitcast_fusion.4), kind=kOutput, calls=%fused_computation.9 | convolution fusion | flops 152174592 | bytes 4980736 | tf_op jit(solution)/shard_map/tbzyxdik,pntdbzyxk->pntbzyxi/dot_general | solution.py:87
  61.3 10.4 %all_to_all.16 = f32[32,1,128]{2,1,0:T(1,128)S(1)} all-to-all(f32[32,1,128]{2,1,0:T(1,128)S(1)} %broadcast_in_dim.11), channel_id=1, replica_groups=mesh['ta'=4,'xyz'=8] {'ta','xyz'}, dimensions={0} | all-to-all | bytes 32768 | tf_op jit(solution)/shard_map/all_to_all | solution.py:35
  71.9 1.2 %multiply_subtract_fusion = (f32[32,1,1,4,2,2,128]{6,0,5,4,3,2,1:T(8,128)S(1)}, f32[32,1,1,4,2,2,128]{6,0,5,4,3,2,1:T(8,128)S(1)}) fusion(f32[32,1,1,4,2,2,128]{6,0,5,4,3,2,1:T(8,128)S(1)} %get-tuple-element.22, f32[32,1,1,4,2,2,128]{6,0,5,4,3,2,1:T(8,128)S(1)} %get-tuple-element.25, f32[32]{0:T(128)S(1)} %get-tuple-element.21, f32[32]{0:T(128)S(1)} %get-tuple-element.20, ...), kind=kLoop, calls=%fused_computation.38 | loop fusion | flops 720896 | bytes 1835392 | tf_op jit(solution)/shard_map/sub | solution.py:215
  73.0 0.9 %copy.140 = f32[32,1,1,4,2,2,128]{6,5,4,3,2,1,0:T(2,128)} copy(f32[32,1,1,4,2,2,128]{6,0,5,4,3,2,1:T(8,128)S(1)} %get-tuple-element.64) | data formatting | bytes 524288
  73.9 0.9 %copy.139 = f32[32,1,1,4,2,2,128]{6,5,4,3,2,1,0:T(2,128)} copy(f32[32,1,1,4,2,2,128]{6,0,5,4,3,2,1:T(8,128)S(1)} %get-tuple-element.65) | data formatting | bytes 524288
  (100 shorter events, 10.7 us)
Async XLA Ops:
  0.6 29.8 %copy-start = (bf16[1,1,4,2,2,9,64,128]{7,6,5,4,3,2,1,0:T(8,128)(2,1)S(1)}, bf16[1,1,4,2,2,9,64,128]{7,6,5,4,3,2,1,0:T(8,128)(2,1)}, u32[]{:S(2)}) copy-start(bf16[1,1,4,2,2,9,64,128]{7,6,5,4,3,2,1,0:T(8,128)(2,1)} %param.5) | copy-start | bytes 7077892
  0.6 14.4 %copy-start.1 = (f32[32,1,1,4,2,2,128]{6,5,4,3,2,1,0:T(2,128)S(1)}, f32[32,1,1,4,2,2,128]{6,5,4,3,2,1,0:T(2,128)}, u32[]{:S(2)}) copy-start(f32[32,1,1,4,2,2,128]{6,5,4,3,2,1,0:T(2,128)} %param.4) | copy-start | bytes 786436
  0.7 14.4 %copy-start.4 = (bf16[1,1,4,2,2,48,128]{6,5,4,3,2,1,0:T(8,128)(2,1)S(1)}, bf16[1,1,4,2,2,48,128]{6,5,4,3,2,1,0:T(8,128)(2,1)}, u32[]{:S(2)}) copy-start(bf16[1,1,4,2,2,48,128]{6,5,4,3,2,1,0:T(8,128)(2,1)} %param.6) | copy-start | bytes 589828
  0.7 14.3 %copy-start.5 = (bf16[1,48,384]{2,1,0:T(8,128)(2,1)S(1)}, bf16[1,48,384]{2,1,0:T(8,128)(2,1)}, u32[]{:S(2)}) copy-start(bf16[1,48,384]{2,1,0:T(8,128)(2,1)} %param.7) | copy-start | bytes 110596
  16.1 8.9 %copy-start.3 = (bf16[32,1,9,1,4,2,2,128]{7,0,6,5,4,3,2,1:T(8,128)(2,1)S(1)}, bf16[32,1,9,1,4,2,2,128]{7,0,6,5,4,3,2,1:T(8,128)(2,1)}, u32[]{:S(2)}) copy-start(bf16[32,1,9,1,4,2,2,128]{7,0,6,5,4,3,2,1:T(8,128)(2,1)} %get-tuple-element.26) | copy-start | bytes 3538948
  16.1 8.9 %collective-permute-start.1 = (bf16[32,1,1,4,2,2,128]{6,0,5,4,3,2,1:T(8,128)(2,1)S(1)}, bf16[32,1,1,4,2,2,128]{6,0,5,4,3,2,1:T(8,128)(2,1)S(1)}, u32[]{:S(2)}, u32[]{:S(2)}) collective-permute-start(bf16[32,1,1,4,2,2,128]{6,0,5,4,3,2,1:T(8,128)(2,1)S(1)} %get-tuple-element.27), channel_id=1, source_target_pairs={{2,0},{3,1},{0,2},{1,3},{6,4},{7,5},{4,6},{5,7},{10,8},{11,9},{8,1... | collective-permute-start | bytes 393224 | tf_op jit(solution)/shard_map/ppermute | solution.py:55
  16.7 8.5 %collective-permute-start.3 = (bf16[32,1,1,4,2,2,128]{6,0,5,4,3,2,1:T(8,128)(2,1)S(1)}, bf16[32,1,1,4,2,2,128]{6,0,5,4,3,2,1:T(8,128)(2,1)S(1)}, u32[]{:S(2)}, u32[]{:S(2)}) collective-permute-start(bf16[32,1,1,4,2,2,128]{6,0,5,4,3,2,1:T(8,128)(2,1)S(1)} %get-tuple-element.27), channel_id=1, source_target_pairs={{8,0},{16,8},{24,16},{0,24},{9,1},{17,9},{25,17},{1,25},{10,2},{18... | collective-permute-start | bytes 393224 | tf_op jit(solution)/shard_map/ppermute | solution.py:61
  20.3 4.6 %collective-permute-start = (bf16[32,1,1,4,2,2,128]{6,0,5,4,3,2,1:T(8,128)(2,1)S(1)}, bf16[32,1,1,4,2,2,128]{6,0,5,4,3,2,1:T(8,128)(2,1)S(1)}, u32[]{:S(2)}, u32[]{:S(2)}) collective-permute-start(bf16[32,1,1,4,2,2,128]{6,0,5,4,3,2,1:T(8,128)(2,1)S(1)} %get-tuple-element.27), channel_id=1, source_target_pairs={{1,0},{0,1},{3,2},{2,3},{5,4},{4,5},{7,6},{6,7},{9,8},{8,9},{11,10... | collective-permute-start | bytes 393224 | tf_op jit(solution)/shard_map/ppermute | solution.py:55
  20.3 7.7 %collective-permute-start.4 = (bf16[32,1,1,4,2,2,128]{6,0,5,4,3,2,1:T(8,128)(2,1)S(1)}, bf16[32,1,1,4,2,2,128]{6,0,5,4,3,2,1:T(8,128)(2,1)S(1)}, u32[]{:S(2)}, u32[]{:S(2)}) collective-permute-start(bf16[32,1,1,4,2,2,128]{6,0,5,4,3,2,1:T(8,128)(2,1)S(1)} %get-tuple-element.27), channel_id=1, source_target_pairs={{24,0},{0,8},{8,16},{16,24},{25,1},{1,9},{9,17},{17,25},{26,2},{2,... | collective-permute-start | bytes 393224 | tf_op jit(solution)/shard_map/ppermute | solution.py:62
  20.4 4.6 %collective-permute-start.2 = (bf16[32,1,1,2,2,2,128]{6,0,5,4,3,2,1:T(8,128)(2,1)S(1)}, bf16[32,1,1,2,2,2,128]{6,0,5,4,3,2,1:T(8,128)(2,1)S(1)}, u32[]{:S(2)}, u32[]{:S(2)}) collective-permute-start(bf16[32,1,1,2,2,2,128]{6,0,5,4,3,2,1:T(8,128)(2,1)S(1)} %pad_maximum_fusion.2), channel_id=1, source_target_pairs={{4,0},{5,1},{6,2},{7,3},{0,4},{1,5},{2,6},{3,7},{12,8},{13,9},{14,... | collective-permute-start | bytes 196616 | tf_op jit(solution)/shard_map/ppermute | solution.py:55
  34.8 10.8 %all-to-all-start.1 = ((bf16[32,2,832]{2,1,0:T(2,128)(2,1)}), bf16[32,2,832]{2,1,0:T(2,128)(2,1)S(1)}, u32[]{:S(2)}, u32[]{:S(2)}) async-start(bf16[32,2,832]{2,1,0:T(2,128)(2,1)} %reshape.370), calls=%async_computation.1 | async-start | bytes 229376 | tf_op jit(solution)/shard_map/all_to_all | solution.py:159
  45.7 0.8 %copy-start.6 = (bf16[1,48,384]{2,1,0:T(8,128)(2,1)S(1)}, bf16[1,48,384]{2,1,0:T(8,128)(2,1)}, u32[]{:S(2)}) copy-start(bf16[1,48,384]{2,1,0:T(8,128)(2,1)} %param.7) | copy-start | bytes 110596
  47.5 6.9 %copy-start.2 = (bf16[32,1,9,1,4,2,2,128]{7,0,6,5,4,3,2,1:T(8,128)(2,1)S(1)}, bf16[32,1,9,1,4,2,2,128]{7,0,6,5,4,3,2,1:T(8,128)(2,1)}, u32[]{:S(2)}) copy-start(bf16[32,1,9,1,4,2,2,128]{7,0,6,5,4,3,2,1:T(8,128)(2,1)} %get-tuple-element.23) | copy-start | bytes 3538948
  47.5 7.0 %collective-permute-start.6 = (bf16[32,1,1,4,2,2,128]{6,0,5,4,3,2,1:T(8,128)(2,1)S(1)}, bf16[32,1,1,4,2,2,128]{6,0,5,4,3,2,1:T(8,128)(2,1)S(1)}, u32[]{:S(2)}, u32[]{:S(2)}) collective-permute-start(bf16[32,1,1,4,2,2,128]{6,0,5,4,3,2,1:T(8,128)(2,1)S(1)} %get-tuple-element.24), channel_id=1, source_target_pairs={{2,0},{3,1},{0,2},{1,3},{6,4},{7,5},{4,6},{5,7},{10,8},{11,9},{8,1... | collective-permute-start | bytes 393224 | tf_op jit(solution)/shard_map/ppermute | solution.py:55
  47.9 6.6 %collective-permute-start.8 = (bf16[32,1,1,4,2,2,128]{6,0,5,4,3,2,1:T(8,128)(2,1)S(1)}, bf16[32,1,1,4,2,2,128]{6,0,5,4,3,2,1:T(8,128)(2,1)S(1)}, u32[]{:S(2)}, u32[]{:S(2)}) collective-permute-start(bf16[32,1,1,4,2,2,128]{6,0,5,4,3,2,1:T(8,128)(2,1)S(1)} %get-tuple-element.24), channel_id=1, source_target_pairs={{8,0},{16,8},{24,16},{0,24},{9,1},{17,9},{25,17},{1,25},{10,2},{18... | collective-permute-start | bytes 393224 | tf_op jit(solution)/shard_map/ppermute | solution.py:61
  49.2 5.2 %collective-permute-start.5 = (bf16[32,1,1,4,2,2,128]{6,0,5,4,3,2,1:T(8,128)(2,1)S(1)}, bf16[32,1,1,4,2,2,128]{6,0,5,4,3,2,1:T(8,128)(2,1)S(1)}, u32[]{:S(2)}, u32[]{:S(2)}) collective-permute-start(bf16[32,1,1,4,2,2,128]{6,0,5,4,3,2,1:T(8,128)(2,1)S(1)} %get-tuple-element.24), channel_id=1, source_target_pairs={{1,0},{0,1},{3,2},{2,3},{5,4},{4,5},{7,6},{6,7},{9,8},{8,9},{11,10... | collective-permute-start | bytes 393224 | tf_op jit(solution)/shard_map/ppermute | solution.py:55
  49.2 7.7 %collective-permute-start.9 = (bf16[32,1,1,4,2,2,128]{6,0,5,4,3,2,1:T(8,128)(2,1)S(1)}, bf16[32,1,1,4,2,2,128]{6,0,5,4,3,2,1:T(8,128)(2,1)S(1)}, u32[]{:S(2)}, u32[]{:S(2)}) collective-permute-start(bf16[32,1,1,4,2,2,128]{6,0,5,4,3,2,1:T(8,128)(2,1)S(1)} %get-tuple-element.24), channel_id=1, source_target_pairs={{24,0},{0,8},{8,16},{16,24},{25,1},{1,9},{9,17},{17,25},{26,2},{2,... | collective-permute-start | bytes 393224 | tf_op jit(solution)/shard_map/ppermute | solution.py:62
  50.0 4.3 %collective-permute-start.7 = (bf16[32,1,1,2,2,2,128]{6,0,5,4,3,2,1:T(8,128)(2,1)S(1)}, bf16[32,1,1,2,2,2,128]{6,0,5,4,3,2,1:T(8,128)(2,1)S(1)}, u32[]{:S(2)}, u32[]{:S(2)}) collective-permute-start(bf16[32,1,1,2,2,2,128]{6,0,5,4,3,2,1:T(8,128)(2,1)S(1)} %pad_maximum_fusion.3), channel_id=1, source_target_pairs={{4,0},{5,1},{6,2},{7,3},{0,4},{1,5},{2,6},{3,7},{12,8},{13,9},{14,... | collective-permute-start | bytes 196616 | tf_op jit(solution)/shard_map/ppermute | solution.py:55

commit v19 on v13

--- a/solution.py
+++ b/solution.py
@@ -79,11 +79,9 @@
         [lowered, upper_x, lower_x, upper_y, lower_y, upper_z, lower_z, upper_t, lower_t], 2
     )
     half_width = lowered.shape[-1] // 2
-    real_part = stacked[..., :half_width]
-    imag_part = stacked[..., half_width:]
-    real_input = jnp.concatenate([real_part, -imag_part], -1)
-    imag_input = jnp.concatenate([imag_part, real_part], -1)
-    inputs = jnp.stack([real_input, imag_input], 0)
+    lanes = lax.broadcasted_iota(jnp.int32, (lowered.shape[-1],), 0)
+    signs = jnp.where(lanes < half_width, 1.0, -1.0).astype(stacked.dtype)
+    inputs = jnp.stack([stacked * signs, jnp.roll(stacked, half_width, axis=-1)], 0)
     result = jnp.einsum(
         "tbzyxdik,pntdbzyxk->pntbzyxi", coarse_links, inputs, preferred_element_type=jnp.float32
     )

time: 74.4 us -> 74.9 us (level)
  blocking collectives: 20.5 us -> 9.64 us
  waiting for transfers between devices: 21.7 us -> 26.8 us
  starting transfers between devices: 11.7 us -> 16.7 us
  local copies, waits for them, and re-layouts: 5.52 us -> 7.51 us
  other arithmetic: 7.27 us -> 5.37 us
  matrix products: 6.31 us -> 7.09 us
    all_to_all x1 -> x0, blocking collectives: 10.5 us -> none  [shards(): lax.all_to_all(jnp.broadcast_to(payload[None], (blocks_total,) + payload....]
    all_to_all x0 -> x1, waiting for transfers between devices: none -> 5.52 us  [shards(): lax.all_to_all(jnp.broadcast_to(payload[None], (blocks_total,) + payload....]
    all_to_all x0 -> x1, starting transfers between devices: none -> 5.17 us  [shards(): lax.all_to_all(jnp.broadcast_to(payload[None], (blocks_total,) + payload....]
    another operation x4 -> x2, other arithmetic: 2.64 us -> 1.32 us  [apply_links(): jnp.stack([stacked * signs, jnp.roll(stacked, half_width, axis=-1)], 0)]
    squeeze x1, local copies, waits for them, and re-layouts: 0.11 us -> 0.89 us  [shards(): lax.dynamic_index_in_dim(image_slabs, lax.axis_index('ta'), 0, keepdims=F...]
    slice x3 -> x2, local copies, waits for them, and re-layouts: 1.7 us -> 1.48 us  [apply_links(): jnp.roll(stacked, half_width, axis=-1)]
    unnamed x17 -> x33, local copies, waits for them, and re-layouts: 1.9 us -> 1.99 us
  transfers between devices with their start and end apart: 11 -> 12, of which waited for: 5 -> 6; matrix products, arithmetic and copies ran while one was open for 1% -> 1% of each run, Pallas kernels for 0% -> 0%
where the time goes in v19:
time: 74.9 us; the launch traced here: 74.4 us
  waiting for transfers between devices  26.8 us (36%)
  starting transfers between devices  16.7 us (22%)
  blocking collectives  9.64 us (13%)
  local copies, waits for them, and re-layouts  7.51 us (10%)
  matrix products  7.09 us (9%)
  other arithmetic  5.37 us (7%)
  between operations  1.33 us (2%)
    all_to_all x1, blocking collectives, total_sum(): lax.all_to_all(copies, axes, 0, 0)[:, 0]  9.64 us
    all_to_all x1, waiting for transfers between devices, shards(): lax.all_to_all(jnp.broadcast_to(local[None, None], (devices, 1) + local.s...  9.37 us
    ppermute x6, waiting for transfers between devices, both_sides(): pair = lax.ppermute(jnp.concatenate([first, last], which), axis, perm)  6.84 us
    all_to_all x1, waiting for transfers between devices, shards(): lax.all_to_all(jnp.broadcast_to(payload[None], (blocks_total,) + payload....  5.52 us
    ppermute x2, starting transfers between devices, both_sides(): from_upper = lax.ppermute(first, axis, up)  5.24 us
    all_to_all x1, starting transfers between devices, shards(): lax.all_to_all(jnp.broadcast_to(payload[None], (blocks_total,) + payload....  5.17 us
    ppermute x2, waiting for transfers between devices, both_sides(): from_lower = lax.ppermute(last, axis, down)  5.06 us
    ppermute x6, starting transfers between devices, both_sides(): pair = lax.ppermute(jnp.concatenate([first, last], which), axis, perm)  3.06 us
  transfers between devices with their start and end apart: 12, of which 6 were waited for; matrix products, arithmetic and copies ran while one was open for 1% of the time, Pallas kernels for 0%

profile of v19, /device:TPU:0, one launch (start us, length us, event | category | flops | bytes accessed | tf_op | source)
XLA Modules:
  0.0 74.4 jit_solution(3235698404285816840)
XLA Ops:
  0.7 1.2 %convert_bitcast_fusion = bf16[32,4,2,2,128]{4,3,2,1,0:T(2,128)(2,1)S(1)} fusion(f32[32,1,1,4,2,2,128]{6,5,4,3,2,1,0:T(2,128)} %param.4), kind=kLoop, calls=%fused_computation.101 | loop fusion | flops 65536 | bytes 393216 | tf_op jit(solution)/shard_map/reshape
  1.9 1.2 %convolution_bitcast_fusion.4 = f32[32,48]{1,0:T(8,128)S(1)} fusion(f32[32,4,2,2,128]{4,3,2,1,0:T(2,128)} %bitcast.252, bf16[1,1,4,2,2,48,128]{6,5,4,3,2,1,0:T(8,128)(2,1)} %param.6), kind=kOutput, calls=%fused_computation.19 | convolution fusion | flops 18874368 | bytes 464896 | tf_op jit(solution)/shard_map/tbzyxjk,ntbzyxk->nj/dot_general | solution.py:92
  3.1 1.1 %fusion.19 = f32[32,48]{1,0:T(8,128)S(1)} fusion(bf16[32,4,2,2,128]{4,3,2,1,0:T(2,128)(2,1)S(1)} %convert_bitcast_fusion, bf16[1,1,4,2,2,48,128]{6,5,4,3,2,1,0:T(8,128)(2,1)} %param.6), kind=kOutput, calls=%fused_computation.21 | convolution fusion | flops 6294528 | bytes 333824 | tf_op jit(solution)/shard_map/tbzyxjk,ntbzyxk->nj/dot_general | solution.py:131
  5.0 5.2 %all-to-all-start = ((f32[8,32,96]{2,1,0:T(8,128)}), f32[8,32,96]{2,1,0:T(8,128)S(1)}, u32[]{:S(2)}, u32[]{:S(2)}) async-start(f32[8,32,96]{2,1,0:T(8,128)} %broadcast_in_dim.18), calls=%async_computation | async-start | bytes 262144 | tf_op jit(solution)/shard_map/all_to_all | solution.py:141
  10.2 5.5 %all-to-all-done = f32[8,32,96]{2,1,0:T(8,128)S(1)} async-done(((f32[8,32,96]{2,1,0:T(8,128)}), f32[8,32,96]{2,1,0:T(8,128)S(1)}, u32[]{:S(2)}, u32[]{:S(2)}) %all-to-all-start) | async-done | bytes 98336 | tf_op jit(solution)/shard_map/all_to_all | solution.py:141
  15.9 1.0 %bitcast_dynamic-update-slice_fusion.35 = (bf16[1,32,1,9,1,4,2,2,128]{8,1,7,6,5,4,3,2,0:T(8,128)(2,1)}, bf16[32,1,1,4,2,2,128]{6,0,5,4,3,2,1:T(8,128)(2,1)S(1)}, f32[32,1,1,4,2,2,128]{6,0,5,4,3,2,1:T(8,128)}) fusion(bf16[1,1,4,2,2,48,128]{6,5,4,3,2,1,0:T(8,128)(2,1)S(1)} %copy-done.2, bf16[32,384]{1,0:T(8,128)(2,1)S(1)} %convert_element_type.48, ...), kind=kOutput, calls=%fused_computation.99 | convolution fusion | flops 7669247 | bytes 1044480 | tf_op jit(solution)/shard_map/tbzyxjk,nj->ntbzyxk/dot_general | solution.py:112
  17.0 3.7 %collective-permute-start.3 = (bf16[32,1,1,4,2,2,128]{6,0,5,4,3,2,1:T(8,128)(2,1)S(1)}, bf16[32,1,1,4,2,2,128]{6,0,5,4,3,2,1:T(8,128)(2,1)S(1)}, u32[]{:S(2)}, u32[]{:S(2)}) collective-permute-start(bf16[32,1,1,4,2,2,128]{6,0,5,4,3,2,1:T(8,128)(2,1)S(1)} %get-tuple-element.27), channel_id=1, source_target_pairs={{8,0},{16,8},{24,16},{0,24},{9,1},{17,9},{25,17},{1,25},{10,2},{18... | collective-permute-start | bytes 393224 | tf_op jit(solution)/shard_map/ppermute | solution.py:61
  21.9 3.9 %collective-permute-done.2 = bf16[32,1,1,2,2,2,128]{6,0,5,4,3,2,1:T(8,128)(2,1)S(1)} collective-permute-done((bf16[32,1,1,2,2,2,128]{6,0,5,4,3,2,1:T(8,128)(2,1)S(1)}, bf16[32,1,1,2,2,2,128]{6,0,5,4,3,2,1:T(8,128)(2,1)S(1)}, u32[]{:S(2)}, u32[]{:S(2)}) %collective-permute-start.2) | collective-permute-done | bytes 65568 | tf_op jit(solution)/shard_map/ppermute | solution.py:55
  26.3 2.6 %collective-permute-done.4 = bf16[32,1,1,4,2,2,128]{6,0,5,4,3,2,1:T(8,128)(2,1)S(1)} collective-permute-done((bf16[32,1,1,4,2,2,128]{6,0,5,4,3,2,1:T(8,128)(2,1)S(1)}, bf16[32,1,1,4,2,2,128]{6,0,5,4,3,2,1:T(8,128)(2,1)S(1)}, u32[]{:S(2)}, u32[]{:S(2)}) %collective-permute-start.4) | collective-permute-done | bytes 131104 | tf_op jit(solution)/shard_map/ppermute | solution.py:62
  30.5 0.9 %fusion.6 = f32[2,32,1,1,4,2,2,64]{7,1,6,5,4,3,2,0:T(8,128)S(1)} fusion(bf16[1,1,4,2,2,9,64,128]{7,6,5,4,3,2,1,0:T(8,128)(2,1)S(1)} %copy-done, bf16[1,32,1,9,1,4,2,2,128]{8,1,7,6,5,3,4,2,0:T(8,128)(2,1)S(1)} %maximum_bitcast_fusion.2, bf16[1,32,1,9,1,4,2,2,128]{8,1,7,6,5,3,4,2,0:T(8,128)(2,1)S(1)} %bitcast_multiply_fusion), kind=kOutput, calls=%fused_computation.8 | convolution fusion | flops 152174592 | bytes 4980736 | tf_op jit(solution)/shard_map/tbzyxdik,pntdbzyxk->pntbzyxi/dot_general | solution.py:85
  32.1 0.8 %broadcast_in_dim.21 = f32[32,1,1600]{2,1,0:T(1,128)} broadcast(f32[1600]{0:T(1024)S(1)} %pad_maximum_fusion.17), dimensions={2} | broadcast | bytes 211200 | tf_op jit(solution)/shard_map/broadcast_in_dim | solution.py:155
  32.9 2.6 %all-to-all-start.1 = ((f32[32,1,1600]{2,1,0:T(1,128)}), f32[32,1,1600]{2,1,0:T(1,128)S(1)}, u32[]{:S(2)}, u32[]{:S(2)}) async-start(f32[32,1,1600]{2,1,0:T(1,128)} %broadcast_in_dim.21), calls=%async_computation.1 | async-start | bytes 425984 | tf_op jit(solution)/shard_map/all_to_all | solution.py:154
  35.5 9.4 %all-to-all-done.1 = f32[32,1,1600]{2,1,0:T(1,128)S(1)} async-done(((f32[32,1,1600]{2,1,0:T(1,128)}), f32[32,1,1600]{2,1,0:T(1,128)S(1)}, u32[]{:S(2)}, u32[]{:S(2)}) %all-to-all-start.1) | async-done | bytes 204832 | tf_op jit(solution)/shard_map/all_to_all | solution.py:154
  45.8 0.9 %squeeze.29 = f32[8,32,48]{2,1,0:T(8,128)S(1)} reshape(f32[1,8,1536]{2,1,0:T(8,128)} %constant_dynamic-slice_fusion) | data formatting | bytes 98304 | tf_op jit(solution)/shard_map/jit(dynamic_index_in_dim)/squeeze | solution.py:164
  47.0 1.7 %bitcast_dynamic-update-slice_fusion.25 = (bf16[1,32,1,9,1,4,2,2,128]{8,1,7,6,5,3,4,2,0:T(8,128)(2,1)}, bf16[32,1,1,4,2,2,128]{6,0,5,4,3,2,1:T(8,128)(2,1)S(1)}, f32[32,1,1,4,2,2,128]{6,0,5,4,3,2,1:T(8,128)S(1)}) fusion(bf16[1,1,4,2,2,48,128]{6,5,4,3,2,1,0:T(8,128)(2,1)S(1)} %copy-done.2, bf16[32,384]{1,0:T(8,128)(2,1)S(1)} %reshape.696, ...), kind=kOutput, calls=%fused_computation.89 | convolution fusion | flops 7800319 | bytes 1306752 | tf_op jit(solution)/shard_map/tbzyxjk,nj->ntbzyxk/dot_general | solution.py:112
  48.7 1.6 %collective-permute-start.8 = (bf16[32,1,1,4,2,2,128]{6,0,5,4,3,2,1:T(8,128)(2,1)S(1)}, bf16[32,1,1,4,2,2,128]{6,0,5,4,3,2,1:T(8,128)(2,1)S(1)}, u32[]{:S(2)}, u32[]{:S(2)}) collective-permute-start(bf16[32,1,1,4,2,2,128]{6,0,5,4,3,2,1:T(8,128)(2,1)S(1)} %get-tuple-element.24), channel_id=1, source_target_pairs={{8,0},{16,8},{24,16},{0,24},{9,1},{17,9},{25,17},{1,25},{10,2},{18... | collective-permute-start | bytes 393224 | tf_op jit(solution)/shard_map/ppermute | solution.py:61
  51.5 1.4 %collective-permute-start.7 = (bf16[32,1,1,2,2,2,128]{6,0,5,4,3,2,1:T(8,128)(2,1)S(1)}, bf16[32,1,1,2,2,2,128]{6,0,5,4,3,2,1:T(8,128)(2,1)S(1)}, u32[]{:S(2)}, u32[]{:S(2)}) collective-permute-start(bf16[32,1,1,2,2,2,128]{6,0,5,4,3,2,1:T(8,128)(2,1)S(1)} %pad_maximum_fusion.15), channel_id=1, source_target_pairs={{4,0},{5,1},{6,2},{7,3},{0,4},{1,5},{2,6},{3,7},{12,8},{13,9},{14,... | collective-permute-start | bytes 196616 | tf_op jit(solution)/shard_map/ppermute | solution.py:55
  52.9 2.9 %collective-permute-done.7 = bf16[32,1,1,2,2,2,128]{6,0,5,4,3,2,1:T(8,128)(2,1)S(1)} collective-permute-done((bf16[32,1,1,2,2,2,128]{6,0,5,4,3,2,1:T(8,128)(2,1)S(1)}, bf16[32,1,1,2,2,2,128]{6,0,5,4,3,2,1:T(8,128)(2,1)S(1)}, u32[]{:S(2)}, u32[]{:S(2)}) %collective-permute-start.7) | collective-permute-done | bytes 65568 | tf_op jit(solution)/shard_map/ppermute | solution.py:55
  56.1 2.4 %collective-permute-done.9 = bf16[32,1,1,4,2,2,128]{6,0,5,4,3,2,1:T(8,128)(2,1)S(1)} collective-permute-done((bf16[32,1,1,4,2,2,128]{6,0,5,4,3,2,1:T(8,128)(2,1)S(1)}, bf16[32,1,1,4,2,2,128]{6,0,5,4,3,2,1:T(8,128)(2,1)S(1)}, u32[]{:S(2)}, u32[]{:S(2)}) %collective-permute-start.9) | collective-permute-done | bytes 131104 | tf_op jit(solution)/shard_map/ppermute | solution.py:62
  60.3 0.9 %fusion.11 = f32[2,32,1,1,4,2,2,64]{7,1,6,5,4,3,2,0:T(8,128)S(1)} fusion(bf16[1,1,4,2,2,9,64,128]{7,6,5,4,3,2,1,0:T(8,128)(2,1)S(1)} %copy-done, bf16[1,32,1,9,1,4,2,2,128]{8,1,7,6,5,3,4,2,0:T(8,128)(2,1)S(1)} %maximum_bitcast_fusion.3, bf16[1,32,1,9,1,4,2,2,128]{8,1,7,6,5,3,4,2,0:T(8,128)(2,1)S(1)} %broadcast_multiply_fusion), kind=kOutput, calls=%fused_computation.9 | convolution fusion | flops 152174592 | bytes 4980736 | tf_op jit(solution)/shard_map/tbzyxdik,pntdbzyxk->pntbzyxi/dot_general | solution.py:85
  61.7 9.6 %all_to_all.15 = f32[32,1,128]{2,1,0:T(1,128)S(1)} all-to-all(f32[32,1,128]{2,1,0:T(1,128)S(1)} %broadcast_in_dim.23), channel_id=1, replica_groups=mesh['ta'=4,'xyz'=8] {'ta','xyz'}, dimensions={0} | all-to-all | bytes 32768 | tf_op jit(solution)/shard_map/all_to_all | solution.py:35
  71.4 1.2 %multiply_subtract_fusion = (f32[32,1,1,4,2,2,128]{6,0,5,4,3,2,1:T(8,128)S(1)}, f32[32,1,1,4,2,2,128]{6,0,5,4,3,2,1:T(8,128)S(1)}) fusion(f32[32,1,1,4,2,2,128]{6,0,5,4,3,2,1:T(8,128)S(1)} %get-tuple-element.22, f32[32,1,1,4,2,2,128]{6,0,5,4,3,2,1:T(8,128)S(1)} %get-tuple-element.25, f32[32]{0:T(128)S(1)} %get-tuple-element.21, f32[32]{0:T(128)S(1)} %get-tuple-element.20, ...), kind=kLoop, calls=%fused_computation.35 | loop fusion | flops 720896 | bytes 1835392 | tf_op jit(solution)/shard_map/sub | solution.py:206
  72.6 0.9 %copy.170 = f32[32,1,1,4,2,2,128]{6,5,4,3,2,1,0:T(2,128)} copy(f32[32,1,1,4,2,2,128]{6,0,5,4,3,2,1:T(8,128)S(1)} %get-tuple-element.64) | data formatting | bytes 524288
  73.5 0.9 %copy.169 = f32[32,1,1,4,2,2,128]{6,5,4,3,2,1,0:T(2,128)} copy(f32[32,1,1,4,2,2,128]{6,0,5,4,3,2,1:T(8,128)S(1)} %get-tuple-element.65) | data formatting | bytes 524288
  (122 shorter events, 9.5 us)
Async XLA Ops:
  0.6 29.8 %copy-start = (bf16[1,1,4,2,2,9,64,128]{7,6,5,4,3,2,1,0:T(8,128)(2,1)S(1)}, bf16[1,1,4,2,2,9,64,128]{7,6,5,4,3,2,1,0:T(8,128)(2,1)}, u32[]{:S(2)}) copy-start(bf16[1,1,4,2,2,9,64,128]{7,6,5,4,3,2,1,0:T(8,128)(2,1)} %param.5) | copy-start | bytes 7077892
  0.6 15.2 %copy-start.1 = (f32[32,1,1,4,2,2,128]{6,5,4,3,2,1,0:T(2,128)S(1)}, f32[32,1,1,4,2,2,128]{6,5,4,3,2,1,0:T(2,128)}, u32[]{:S(2)}) copy-start(f32[32,1,1,4,2,2,128]{6,5,4,3,2,1,0:T(2,128)} %param.4) | copy-start | bytes 786436
  0.7 15.2 %copy-start.2 = (bf16[1,1,4,2,2,48,128]{6,5,4,3,2,1,0:T(8,128)(2,1)S(1)}, bf16[1,1,4,2,2,48,128]{6,5,4,3,2,1,0:T(8,128)(2,1)}, u32[]{:S(2)}) copy-start(bf16[1,1,4,2,2,48,128]{6,5,4,3,2,1,0:T(8,128)(2,1)} %param.6) | copy-start | bytes 589828
  0.7 15.2 %copy-start.5 = (bf16[1,48,384]{2,1,0:T(8,128)(2,1)S(1)}, bf16[1,48,384]{2,1,0:T(8,128)(2,1)}, u32[]{:S(2)}) copy-start(bf16[1,48,384]{2,1,0:T(8,128)(2,1)} %param.7) | copy-start | bytes 110596
  5.0 10.7 %all-to-all-start = ((f32[8,32,96]{2,1,0:T(8,128)}), f32[8,32,96]{2,1,0:T(8,128)S(1)}, u32[]{:S(2)}, u32[]{:S(2)}) async-start(f32[8,32,96]{2,1,0:T(8,128)} %broadcast_in_dim.18), calls=%async_computation | async-start | bytes 262144 | tf_op jit(solution)/shard_map/all_to_all | solution.py:141
  10.2 19.5 %copy-start.8 = (bf16[128]{0:T(256)(128)(2,1)}, bf16[128]{0:T(256)(128)(2,1)S(1)}, u32[]{:S(2)}) copy-start(bf16[128]{0:T(256)(128)(2,1)S(1)} %fusion.35) | copy-start | bytes 772
  16.9 8.9 %copy-start.4 = (bf16[1,32,1,9,1,4,2,2,128]{8,1,7,6,5,4,3,2,0:T(8,128)(2,1)S(1)}, bf16[1,32,1,9,1,4,2,2,128]{8,1,7,6,5,4,3,2,0:T(8,128)(2,1)}, u32[]{:S(2)}) copy-start(bf16[1,32,1,9,1,4,2,2,128]{8,1,7,6,5,4,3,2,0:T(8,128)(2,1)} %get-tuple-element.26) | copy-start | bytes 3538948
  17.0 9.2 %collective-permute-start.3 = (bf16[32,1,1,4,2,2,128]{6,0,5,4,3,2,1:T(8,128)(2,1)S(1)}, bf16[32,1,1,4,2,2,128]{6,0,5,4,3,2,1:T(8,128)(2,1)S(1)}, u32[]{:S(2)}, u32[]{:S(2)}) collective-permute-start(bf16[32,1,1,4,2,2,128]{6,0,5,4,3,2,1:T(8,128)(2,1)S(1)} %get-tuple-element.27), channel_id=1, source_target_pairs={{8,0},{16,8},{24,16},{0,24},{9,1},{17,9},{25,17},{1,25},{10,2},{18... | collective-permute-start | bytes 393224 | tf_op jit(solution)/shard_map/ppermute | solution.py:61
  20.6 5.4 %collective-permute-start.1 = (bf16[32,1,1,4,2,2,128]{6,0,5,4,3,2,1:T(8,128)(2,1)S(1)}, bf16[32,1,1,4,2,2,128]{6,0,5,4,3,2,1:T(8,128)(2,1)S(1)}, u32[]{:S(2)}, u32[]{:S(2)}) collective-permute-start(bf16[32,1,1,4,2,2,128]{6,0,5,4,3,2,1:T(8,128)(2,1)S(1)} %get-tuple-element.27), channel_id=1, source_target_pairs={{2,0},{3,1},{0,2},{1,3},{6,4},{7,5},{4,6},{5,7},{10,8},{11,9},{8,1... | collective-permute-start | bytes 393224 | tf_op jit(solution)/shard_map/ppermute | solution.py:55
  21.2 4.6 %collective-permute-start = (bf16[32,1,1,4,2,2,128]{6,0,5,4,3,2,1:T(8,128)(2,1)S(1)}, bf16[32,1,1,4,2,2,128]{6,0,5,4,3,2,1:T(8,128)(2,1)S(1)}, u32[]{:S(2)}, u32[]{:S(2)}) collective-permute-start(bf16[32,1,1,4,2,2,128]{6,0,5,4,3,2,1:T(8,128)(2,1)S(1)} %get-tuple-element.27), channel_id=1, source_target_pairs={{1,0},{0,1},{3,2},{2,3},{5,4},{4,5},{7,6},{6,7},{9,8},{8,9},{11,10... | collective-permute-start | bytes 393224 | tf_op jit(solution)/shard_map/ppermute | solution.py:55
  21.2 7.7 %collective-permute-start.4 = (bf16[32,1,1,4,2,2,128]{6,0,5,4,3,2,1:T(8,128)(2,1)S(1)}, bf16[32,1,1,4,2,2,128]{6,0,5,4,3,2,1:T(8,128)(2,1)S(1)}, u32[]{:S(2)}, u32[]{:S(2)}) collective-permute-start(bf16[32,1,1,4,2,2,128]{6,0,5,4,3,2,1:T(8,128)(2,1)S(1)} %get-tuple-element.27), channel_id=1, source_target_pairs={{24,0},{0,8},{8,16},{16,24},{25,1},{1,9},{9,17},{17,25},{26,2},{2,... | collective-permute-start | bytes 393224 | tf_op jit(solution)/shard_map/ppermute | solution.py:62
  21.2 4.6 %collective-permute-start.2 = (bf16[32,1,1,2,2,2,128]{6,0,5,4,3,2,1:T(8,128)(2,1)S(1)}, bf16[32,1,1,2,2,2,128]{6,0,5,4,3,2,1:T(8,128)(2,1)S(1)}, u32[]{:S(2)}, u32[]{:S(2)}) collective-permute-start(bf16[32,1,1,2,2,2,128]{6,0,5,4,3,2,1:T(8,128)(2,1)S(1)} %pad_maximum_fusion.14), channel_id=1, source_target_pairs={{4,0},{5,1},{6,2},{7,3},{0,4},{1,5},{2,6},{3,7},{12,8},{13,9},{14,... | collective-permute-start | bytes 196616 | tf_op jit(solution)/shard_map/ppermute | solution.py:55
  32.9 12.0 %all-to-all-start.1 = ((f32[32,1,1600]{2,1,0:T(1,128)}), f32[32,1,1600]{2,1,0:T(1,128)S(1)}, u32[]{:S(2)}, u32[]{:S(2)}) async-start(f32[32,1,1600]{2,1,0:T(1,128)} %broadcast_in_dim.21), calls=%async_computation.1 | async-start | bytes 425984 | tf_op jit(solution)/shard_map/all_to_all | solution.py:154
  45.1 1.7 %copy-start.10 = (f32[2,32]{1,0:T(2,128)}, f32[2,32]{1,0:T(2,128)S(1)}, u32[]{:S(2)}) copy-start(f32[2,32]{1,0:T(2,128)S(1)} %reshape.694) | copy-start | bytes 772
  45.2 1.7 %copy-start.6 = (f32[32]{0:T(128)}, f32[32]{0:T(128)S(1)}, u32[]{:S(2)}) copy-start(f32[32]{0:T(128)S(1)} %bitcast_divide_fusion) | copy-start | bytes 388
  48.7 7.1 %copy-start.3 = (bf16[1,32,1,9,1,4,2,2,128]{8,1,7,6,5,3,4,2,0:T(8,128)(2,1)S(1)}, bf16[1,32,1,9,1,4,2,2,128]{8,1,7,6,5,3,4,2,0:T(8,128)(2,1)}, u32[]{:S(2)}) copy-start(bf16[1,32,1,9,1,4,2,2,128]{8,1,7,6,5,3,4,2,0:T(8,128)(2,1)} %get-tuple-element.23) | copy-start | bytes 3538948
  48.7 7.3 %collective-permute-start.8 = (bf16[32,1,1,4,2,2,128]{6,0,5,4,3,2,1:T(8,128)(2,1)S(1)}, bf16[32,1,1,4,2,2,128]{6,0,5,4,3,2,1:T(8,128)(2,1)S(1)}, u32[]{:S(2)}, u32[]{:S(2)}) collective-permute-start(bf16[32,1,1,4,2,2,128]{6,0,5,4,3,2,1:T(8,128)(2,1)S(1)} %get-tuple-element.24), channel_id=1, source_target_pairs={{8,0},{16,8},{24,16},{0,24},{9,1},{17,9},{25,17},{1,25},{10,2},{18... | collective-permute-start | bytes 393224 | tf_op jit(solution)/shard_map/ppermute | solution.py:61
  50.3 5.6 %collective-permute-start.6 = (bf16[32,1,1,4,2,2,128]{6,0,5,4,3,2,1:T(8,128)(2,1)S(1)}, bf16[32,1,1,4,2,2,128]{6,0,5,4,3,2,1:T(8,128)(2,1)S(1)}, u32[]{:S(2)}, u32[]{:S(2)}) collective-permute-start(bf16[32,1,1,4,2,2,128]{6,0,5,4,3,2,1:T(8,128)(2,1)S(1)} %get-tuple-element.24), channel_id=1, source_target_pairs={{2,0},{3,1},{0,2},{1,3},{6,4},{7,5},{4,6},{5,7},{10,8},{11,9},{8,1... | collective-permute-start | bytes 393224 | tf_op jit(solution)/shard_map/ppermute | solution.py:55
  50.8 5.0 %collective-permute-start.5 = (bf16[32,1,1,4,2,2,128]{6,0,5,4,3,2,1:T(8,128)(2,1)S(1)}, bf16[32,1,1,4,2,2,128]{6,0,5,4,3,2,1:T(8,128)(2,1)S(1)}, u32[]{:S(2)}, u32[]{:S(2)}) collective-permute-start(bf16[32,1,1,4,2,2,128]{6,0,5,4,3,2,1:T(8,128)(2,1)S(1)} %get-tuple-element.24), channel_id=1, source_target_pairs={{1,0},{0,1},{3,2},{2,3},{5,4},{4,5},{7,6},{6,7},{9,8},{8,9},{11,10... | collective-permute-start | bytes 393224 | tf_op jit(solution)/shard_map/ppermute | solution.py:55
  50.8 7.7 %collective-permute-start.9 = (bf16[32,1,1,4,2,2,128]{6,0,5,4,3,2,1:T(8,128)(2,1)S(1)}, bf16[32,1,1,4,2,2,128]{6,0,5,4,3,2,1:T(8,128)(2,1)S(1)}, u32[]{:S(2)}, u32[]{:S(2)}) collective-permute-start(bf16[32,1,1,4,2,2,128]{6,0,5,4,3,2,1:T(8,128)(2,1)S(1)} %get-tuple-element.24), channel_id=1, source_target_pairs={{24,0},{0,8},{8,16},{16,24},{25,1},{1,9},{9,17},{17,25},{26,2},{2,... | collective-permute-start | bytes 393224 | tf_op jit(solution)/shard_map/ppermute | solution.py:62
  51.5 4.3 %collective-permute-start.7 = (bf16[32,1,1,2,2,2,128]{6,0,5,4,3,2,1:T(8,128)(2,1)S(1)}, bf16[32,1,1,2,2,2,128]{6,0,5,4,3,2,1:T(8,128)(2,1)S(1)}, u32[]{:S(2)}, u32[]{:S(2)}) collective-permute-start(bf16[32,1,1,2,2,2,128]{6,0,5,4,3,2,1:T(8,128)(2,1)S(1)} %pad_maximum_fusion.15), channel_id=1, source_target_pairs={{4,0},{5,1},{6,2},{7,3},{0,4},{1,5},{2,6},{3,7},{12,8},{13,9},{14,... | collective-permute-start | bytes 196616 | tf_op jit(solution)/shard_map/ppermute | solution.py:55
  55.8 2.7 %copy-start.9 = (bf16[128]{0:T(256)(128)(2,1)S(1)}, bf16[128]{0:T(256)(128)(2,1)}, u32[]{:S(2)}) copy-start(bf16[128]{0:T(256)(128)(2,1)} %copy-done.8) | copy-start | bytes 772
  60.2 0.9 %copy-start.7 = (f32[32]{0:T(128)S(1)}, f32[32]{0:T(128)}, u32[]{:S(2)}) copy-start(f32[32]{0:T(128)} %copy-done.6) | copy-start | bytes 388
  61.1 10.2 %copy-start.11 = (f32[2,32]{1,0:T(2,128)S(1)}, f32[2,32]{1,0:T(2,128)}, u32[]{:S(2)}) copy-start(f32[2,32]{1,0:T(2,128)} %copy-done.10) | copy-start | bytes 772
